TPU v7x, 32 devices: a whole 2x2x4 slice. The times are simulated.
32 devices in a mesh: fsdp: 8 (over y, x, core), tp: 4 (over z).
Axes of the slice: x: 2, y: 2, z: 4, core: 2. Of those that a mesh axis runs over, the one named last changes fastest.
Arguments:
- layer_in: bfloat16 [8192, 2048], P(('fsdp', 'tp')), may hold values from -8 to 8
- query_proj: bfloat16 [2048, 4096], P('fsdp', 'tp'), may hold values from -0.125 to 0.125
- key_proj: bfloat16 [2048, 512], P(('fsdp', 'tp')), may hold values from -0.125 to 0.125
- value_proj: bfloat16 [2048, 512], P(('fsdp', 'tp')), may hold values from -0.125 to 0.125
- output_proj: bfloat16 [4096, 2048], P('tp', 'fsdp'), may hold values from -0.75 to 0.75
- attn_gain: bfloat16 [2048], P(('fsdp', 'tp')), may hold values from 0.25 to 1.75
- query_gain: bfloat16 [128], P(('fsdp', 'tp')), may hold values from 0.25 to 1.75
- key_gain: bfloat16 [128], P(('fsdp', 'tp')), may hold values from 0.25 to 1.75
- ffn_gain: bfloat16 [2048], P(('fsdp', 'tp')), may hold values from 0.25 to 1.75
- expert_gate: bfloat16 [16, 2048, 768], P('fsdp', None, 'tp'), may hold values from -0.125 to 0.125
- expert_up: bfloat16 [16, 2048, 768], P('fsdp', None, 'tp'), may hold values from -0.125 to 0.125
- expert_down: bfloat16 [16, 768, 2048], P('fsdp', 'tp'), may hold values from -0.21875 to 0.21875
- routes: int32 [8192, 8], P('fsdp'), may hold values from 0 to 15, all different within a row; in each aligned block of 1024 rows (0 to 1023, 1024 to 2047, ...) at most 576 rows name the same one
- route_weights: float32 [8192, 8], P('fsdp'), may hold values from 0.05 to 0.3
- prefix_len: int32 [8], P('fsdp'), may hold values from 1 to 512
- out_grad: bfloat16 [8192, 2048], P(('fsdp', 'tp')), may hold values from -12 to 12
Outputs:
- layer_out: bfloat16 [8192, 2048], P(('fsdp', 'tp'))
- in_grad: float32 [8192, 2048], P(('fsdp', 'tp'))
- query_proj_grad: float32 [2048, 4096], P('fsdp', 'tp')
- key_proj_grad: float32 [2048, 512], P(('fsdp', 'tp'))
- value_proj_grad: float32 [2048, 512], P(('fsdp', 'tp'))
- output_proj_grad: float32 [4096, 2048], P('tp', 'fsdp')
- attn_gain_grad: float32 [2048], P(('fsdp', 'tp'))
- query_gain_grad: float32 [128], P(('fsdp', 'tp'))
- key_gain_grad: float32 [128], P(('fsdp', 'tp'))
- ffn_gain_grad: float32 [2048], P(('fsdp', 'tp'))
- gate_grad: float32 [16, 2048, 768], P('fsdp', None, 'tp')
- up_grad: float32 [16, 2048, 768], P('fsdp', None, 'tp')
- down_grad: float32 [16, 768, 2048], P('fsdp', 'tp')
Inputs may be any that keep to these rules, and one draw needn't show every extreme that they name: `routes`: the 8 experts of a token differ. Within each aligned block of 1024 rows (the tokens of one index of fsdp) no expert is chosen by more than 576 tokens, and in every draw some expert of some block is chosen by exactly 576.
All inputs are finite; a program needn't handle non-finite values.
Results may differ from a plain program's by a relative error of at most 0.019.
Values may be sent and summed in bfloat16 or wider, within the bound.
No kernel may reach another device: no remote copies, remote signals or barrier semaphores. Data moves between devices by JAX's collectives and lax.ppermute only.
A program may use at most 448 MiB of HBM per device.

v0:
```python
import math

import jax
import jax.numpy as jnp
from jax import lax
from jax.sharding import PartitionSpec as P

HQ = 32
HK = 4
HD = 128
TOP = 8
SEQ = 1024


EPSILON = 1e-06


def rms_norm(values, weight):
    return values * lax.rsqrt(jnp.mean(values * values, axis=-1, keepdims=True) + EPSILON) * weight


def rotate(values, cosine, sine):
    half_width = values.shape[-1] // 2
    first_half = values[..., :half_width]
    second_half = values[..., half_width:]
    return jnp.concatenate(
        [first_half * cosine - second_half * sine, second_half * cosine + first_half * sine],
        axis=-1,
    )


def rotary_tables(positions, width):
    half_width = width // 2
    inverse = jnp.exp(
        -math.log(1000000.0) * 2.0 * jnp.arange(half_width, dtype=jnp.float32) / width
    )
    angles = positions[:, None] * inverse[None, :]
    return (jnp.cos(angles), jnp.sin(angles))


def masked_scores(queries, keys_b, prefix_end, factor):
    scores = jnp.einsum("qhd,kd->hqk", queries, keys_b, preferred_element_type=jnp.float32) * factor
    position = lax.iota(jnp.int32, queries.shape[0])
    allowed = (position[None, :] <= position[:, None]) | (position[None, :] < prefix_end)
    return jnp.where(allowed[None], scores, -1e30)


def body(
    layer_in,
    query_proj,
    key_proj,
    value_proj,
    output_proj,
    attn_gain,
    query_gain,
    key_gain,
    ffn_gain,
    expert_gate,
    expert_up,
    expert_down,
    routes,
    route_weights,
    prefix_len,
    out_grad,
):
    tok_rows = layer_in.shape[0]
    width = layer_in.shape[1]
    group_rows = tok_rows * lax.axis_size("tp")
    seq_count = group_rows // SEQ
    factor = 1.0 / math.sqrt(HD)
    key_all, value_all, gain_attn, gain_query, gain_key, gain_ffn = (
        lax.all_gather(key_proj, ("fsdp", "tp"), axis=0, tiled=True),
        lax.all_gather(value_proj, ("fsdp", "tp"), axis=0, tiled=True),
        lax.all_gather(attn_gain, ("fsdp", "tp"), axis=0, tiled=True),
        lax.all_gather(query_gain, ("fsdp", "tp"), axis=0, tiled=True),
        lax.all_gather(key_gain, ("fsdp", "tp"), axis=0, tiled=True),
        lax.all_gather(ffn_gain, ("fsdp", "tp"), axis=0, tiled=True),
    )
    gain_attn = gain_attn.astype(jnp.float32)
    gain_query = gain_query.astype(jnp.float32)
    gain_key = gain_key.astype(jnp.float32)
    gain_ffn = gain_ffn.astype(jnp.float32)
    query_w, out_w, gate_w, up_w, down_w = (
        lax.all_gather(query_proj, "fsdp", axis=0, tiled=True),
        lax.all_gather(output_proj, "fsdp", axis=1, tiled=True),
        lax.all_gather(expert_gate, "fsdp", axis=0, tiled=True),
        lax.all_gather(expert_up, "fsdp", axis=0, tiled=True),
        lax.all_gather(expert_down, "fsdp", axis=0, tiled=True),
    )
    per_dev = query_w.shape[1] // HD
    kv_head = lax.axis_index("tp") * per_dev // (HQ // HK)
    key_w = lax.dynamic_slice_in_dim(key_all, kv_head * HD, HD, 1)
    value_w = lax.dynamic_slice_in_dim(value_all, kv_head * HD, HD, 1)
    tokens_f = layer_in.astype(jnp.float32)
    attn_in = rms_norm(tokens_f, gain_attn).astype(jnp.bfloat16)
    attn_rows = lax.all_gather(attn_in, "tp", axis=0, tiled=True)
    query_raw = jnp.dot(attn_rows, query_w, preferred_element_type=jnp.float32)
    key_raw = jnp.dot(attn_rows, key_w, preferred_element_type=jnp.float32)
    value_rows = jnp.dot(attn_rows, value_w, preferred_element_type=jnp.float32).astype(
        jnp.bfloat16
    )
    cosine, sine = rotary_tables((lax.iota(jnp.int32, group_rows) % SEQ).astype(jnp.float32), HD)

    def prepare(query_in, key_in, weight_query, weight_key):
        query_heads = rms_norm(query_in.reshape(group_rows, per_dev, HD), weight_query)
        return (
            rotate(query_heads, cosine[:, None, :], sine[:, None, :]),
            rotate(rms_norm(key_in, weight_key), cosine, sine),
        )

    (query_norm, key_norm), prepare_back = jax.vjp(
        prepare, query_raw, key_raw, gain_query, gain_key
    )
    query_seq = query_norm.astype(jnp.bfloat16).reshape(seq_count, SEQ, per_dev, HD)
    key_seq = key_norm.astype(jnp.bfloat16).reshape(seq_count, SEQ, HD)
    value_seq = value_rows.reshape(seq_count, SEQ, HD)

    def attend(operands):
        queries, keys_b, values_b, prefix_end = operands
        scores = masked_scores(queries, keys_b, prefix_end, factor)
        highest = jnp.max(scores, axis=-1, keepdims=True)
        expo = jnp.exp(scores - highest)
        denom = jnp.sum(expo, axis=-1, keepdims=True)
        attn_probs = (expo / denom).astype(jnp.bfloat16)
        context = jnp.einsum(
            "hqk,kd->qhd", attn_probs, values_b, preferred_element_type=jnp.float32
        )
        return (context, (highest + jnp.log(denom))[..., 0])

    context_all, log_sums = lax.map(attend, (query_seq, key_seq, value_seq, prefix_len))
    context_b = context_all.reshape(group_rows, per_dev * HD).astype(jnp.bfloat16)
    attn_out = lax.psum_scatter(
        jnp.dot(context_b, out_w, preferred_element_type=jnp.float32).astype(jnp.bfloat16),
        "tp",
        scatter_dimension=0,
        tiled=True,
    ).astype(jnp.float32)
    residual = tokens_f + attn_out
    ffn_in = rms_norm(residual, gain_ffn).astype(jnp.bfloat16)
    ffn_rows = lax.all_gather(ffn_in, "tp", axis=0, tiled=True)
    padded = jnp.concatenate([ffn_rows, jnp.zeros((1, width), jnp.bfloat16)], axis=0)
    expert_count = gate_w.shape[0]
    capacity = 9 * TOP * group_rows // (8 * expert_count)
    route_flat = routes.reshape(-1)
    one_hot = (route_flat[:, None] == lax.iota(jnp.int32, expert_count)[None, :]).astype(jnp.int32)
    slot_rank = jnp.sum((jnp.cumsum(one_hot, axis=0) - one_hot) * one_hot, axis=1)
    slot_index = route_flat * capacity + slot_rank
    token_of = (
        jnp.full((expert_count * capacity,), group_rows, jnp.int32)
        .at[slot_index]
        .set(lax.iota(jnp.int32, route_flat.shape[0]) // TOP)
        .reshape(expert_count, capacity)
    )
    share_of = (
        jnp.zeros((expert_count * capacity,), jnp.float32)
        .at[slot_index]
        .set(route_weights.reshape(-1))
        .reshape(expert_count, capacity)
    )
    block_size = math.gcd(expert_count, 4)
    block_count = expert_count // block_size

    def ffn_block(accum, block_id):
        first_exp = block_id * block_size
        slot_rows = lax.dynamic_slice_in_dim(token_of, first_exp, block_size, 0)
        slot_share = lax.dynamic_slice_in_dim(share_of, first_exp, block_size, 0)
        inputs = padded[slot_rows]
        gate_val = jnp.einsum(
            "ecd,edf->ecf",
            inputs,
            lax.dynamic_slice_in_dim(gate_w, first_exp, block_size, 0),
            preferred_element_type=jnp.float32,
        )
        up_val = jnp.einsum(
            "ecd,edf->ecf",
            inputs,
            lax.dynamic_slice_in_dim(up_w, first_exp, block_size, 0),
            preferred_element_type=jnp.float32,
        )
        hidden = (jax.nn.silu(gate_val) * up_val).astype(jnp.bfloat16)
        expert_out = (
            jnp.einsum(
                "ecf,efd->ecd",
                hidden,
                lax.dynamic_slice_in_dim(down_w, first_exp, block_size, 0),
                preferred_element_type=jnp.float32,
            )
            * slot_share[..., None]
        )
        accum = accum.at[slot_rows.reshape(-1)].add(expert_out.reshape(-1, width))
        return (accum, (gate_val, up_val, hidden))

    mixture, (gate_all, up_all, hidden_all) = lax.scan(
        ffn_block, jnp.zeros((group_rows + 1, width), jnp.float32), lax.iota(jnp.int32, block_count)
    )
    mixture_own = lax.psum_scatter(
        mixture[:group_rows].astype(jnp.bfloat16), "tp", scatter_dimension=0, tiled=True
    ).astype(jnp.float32)
    layer_out = (residual + mixture_own).astype(jnp.bfloat16)
    grad_out = out_grad.astype(jnp.float32)
    grad_rows = lax.all_gather(out_grad, "tp", axis=0, tiled=True)
    grad_pad = jnp.concatenate([grad_rows, jnp.zeros((1, width), jnp.bfloat16)], axis=0)

    def ffn_back(accum, block_id):
        first_exp = block_id * block_size
        slot_rows = lax.dynamic_slice_in_dim(token_of, first_exp, block_size, 0)
        slot_share = lax.dynamic_slice_in_dim(share_of, first_exp, block_size, 0)
        gate_val = gate_all[block_id]
        up_val = up_all[block_id]
        sigma = jax.nn.sigmoid(gate_val)
        active = gate_val * sigma
        slot_grad = (grad_pad[slot_rows].astype(jnp.float32) * slot_share[..., None]).astype(
            jnp.bfloat16
        )
        hidden_grad = jnp.einsum(
            "ecd,efd->ecf",
            slot_grad,
            lax.dynamic_slice_in_dim(down_w, first_exp, block_size, 0),
            preferred_element_type=jnp.float32,
        )
        gate_back = (hidden_grad * up_val * sigma * (1.0 + gate_val * (1.0 - sigma))).astype(
            jnp.bfloat16
        )
        up_back = (hidden_grad * active).astype(jnp.bfloat16)
        input_grad = jnp.einsum(
            "ecf,edf->ecd",
            gate_back,
            lax.dynamic_slice_in_dim(gate_w, first_exp, block_size, 0),
            preferred_element_type=jnp.float32,
        )
        input_grad = input_grad + jnp.einsum(
            "ecf,edf->ecd",
            up_back,
            lax.dynamic_slice_in_dim(up_w, first_exp, block_size, 0),
            preferred_element_type=jnp.float32,
        )
        accum = accum.at[slot_rows.reshape(-1)].add(input_grad.reshape(-1, width))
        return (accum, (gate_back, up_back))

    ffn_in_grad, (gate_back_all, up_back_all) = lax.scan(
        ffn_back, jnp.zeros((group_rows + 1, width), jnp.float32), lax.iota(jnp.int32, block_count)
    )
    hidden_width = gate_w.shape[2]
    gate_back_all = gate_back_all.reshape(expert_count, capacity, hidden_width)
    up_back_all = up_back_all.reshape(expert_count, capacity, hidden_width)
    hidden_all = hidden_all.reshape(expert_count, capacity, hidden_width)
    owners = lax.axis_size("fsdp")
    local_count = expert_count // owners
    rows_split = token_of.reshape(owners, local_count, capacity)
    share_split = share_of.reshape(owners, local_count, capacity)
    gate_split = gate_back_all.reshape(owners, local_count, capacity, hidden_width)
    up_split = up_back_all.reshape(owners, local_count, capacity, hidden_width)
    hidden_split = hidden_all.reshape(owners, local_count, capacity, hidden_width)
    gate_list = []
    up_list = []
    down_list = []
    for local_id in range(local_count):
        slot_rows = rows_split[:, local_id]
        inputs = padded[slot_rows]
        slot_grad = (
            grad_pad[slot_rows].astype(jnp.float32) * share_split[:, local_id][..., None]
        ).astype(jnp.bfloat16)
        got_in, got_grad, got_gate, got_up, got_hidden = (
            lax.all_to_all(inputs, "fsdp", split_axis=0, concat_axis=1, tiled=True),
            lax.all_to_all(slot_grad, "fsdp", split_axis=0, concat_axis=1, tiled=True),
            lax.all_to_all(
                gate_split[:, local_id], "fsdp", split_axis=0, concat_axis=1, tiled=True
            ),
            lax.all_to_all(up_split[:, local_id], "fsdp", split_axis=0, concat_axis=1, tiled=True),
            lax.all_to_all(
                hidden_split[:, local_id], "fsdp", split_axis=0, concat_axis=1, tiled=True
            ),
        )
        gate_list.append(
            jnp.einsum("ecd,ecf->edf", got_in, got_gate, preferred_element_type=jnp.float32)[0]
        )
        up_list.append(
            jnp.einsum("ecd,ecf->edf", got_in, got_up, preferred_element_type=jnp.float32)[0]
        )
        down_list.append(
            jnp.einsum("ecf,ecd->efd", got_hidden, got_grad, preferred_element_type=jnp.float32)[0]
        )
    gate_grad = jnp.stack(gate_list, axis=0)
    up_grad = jnp.stack(up_list, axis=0)
    down_grad = jnp.stack(down_list, axis=0)
    ffn_in_own = lax.psum_scatter(
        ffn_in_grad[:group_rows].astype(jnp.bfloat16), "tp", scatter_dimension=0, tiled=True
    ).astype(jnp.float32)
    _, second_back = jax.vjp(rms_norm, residual, gain_ffn)
    residual_norm_grad, ffn_gain_part = second_back(ffn_in_own)
    residual_grad = grad_out + residual_norm_grad
    attn_out_grad = lax.all_gather(residual_grad.astype(jnp.bfloat16), "tp", axis=0, tiled=True)
    output_part = jnp.einsum(
        "gq,gd->qd", context_b, attn_out_grad, preferred_element_type=jnp.float32
    )
    context_grad = (
        jnp.einsum("gd,qd->gq", attn_out_grad, out_w, preferred_element_type=jnp.float32)
        .astype(jnp.bfloat16)
        .reshape(seq_count, SEQ, per_dev, HD)
    )

    def attend_back(operands):
        queries, keys_b, values_b, prefix_end, log_sum, ctx_grad = operands
        scores = masked_scores(queries, keys_b, prefix_end, factor)
        attn_probs = jnp.exp(scores - log_sum[..., None])
        value_grad = jnp.einsum(
            "hqk,qhd->kd",
            attn_probs.astype(jnp.bfloat16),
            ctx_grad,
            preferred_element_type=jnp.float32,
        )
        probs_grad = jnp.einsum(
            "qhd,kd->hqk", ctx_grad, values_b, preferred_element_type=jnp.float32
        )
        scores_grad = (
            attn_probs * (probs_grad - jnp.sum(attn_probs * probs_grad, axis=-1, keepdims=True))
        ).astype(jnp.bfloat16)
        query_grad = (
            jnp.einsum("hqk,kd->qhd", scores_grad, keys_b, preferred_element_type=jnp.float32)
            * factor
        )
        key_grad = (
            jnp.einsum("hqk,qhd->kd", scores_grad, queries, preferred_element_type=jnp.float32)
            * factor
        )
        return (query_grad, key_grad, value_grad)

    query_norm_grad, key_norm_grad, value_grad = lax.map(
        attend_back, (query_seq, key_seq, value_seq, prefix_len, log_sums, context_grad)
    )
    query_raw_grad, key_raw_grad, query_gain_part, key_gain_part = prepare_back(
        (query_norm_grad.reshape(group_rows, per_dev, HD), key_norm_grad.reshape(group_rows, HD))
    )
    query_back = query_raw_grad.astype(jnp.bfloat16)
    key_back = key_raw_grad.astype(jnp.bfloat16)
    value_back = value_grad.reshape(group_rows, HD).astype(jnp.bfloat16)
    result = jnp.einsum("gq,dq->gd", query_back, query_w, preferred_element_type=jnp.float32)
    result = result + jnp.einsum("gk,dk->gd", key_back, key_w, preferred_element_type=jnp.float32)
    attn_in_grad = lax.psum_scatter(
        (
            result
            + jnp.einsum("gk,dk->gd", value_back, value_w, preferred_element_type=jnp.float32)
        ).astype(jnp.bfloat16),
        "tp",
        scatter_dimension=0,
        tiled=True,
    ).astype(jnp.float32)
    query_part = jnp.einsum("gd,gq->dq", attn_rows, query_back, preferred_element_type=jnp.float32)
    kv_width = key_all.shape[1]
    key_head_part = jnp.einsum("gd,gk->dk", attn_rows, key_back, preferred_element_type=jnp.float32)
    value_head_part = jnp.einsum(
        "gd,gk->dk", attn_rows, value_back, preferred_element_type=jnp.float32
    )
    key_part = lax.dynamic_update_slice_in_dim(
        jnp.zeros((width, kv_width), jnp.float32), key_head_part, kv_head * HD, 1
    )
    value_part = lax.dynamic_update_slice_in_dim(
        jnp.zeros((width, kv_width), jnp.float32), value_head_part, kv_head * HD, 1
    )
    _, first_back = jax.vjp(rms_norm, tokens_f, gain_attn)
    input_norm_grad, attn_gain_part = first_back(attn_in_grad)
    in_grad = residual_grad + input_norm_grad
    query_proj_grad, output_proj_grad = (
        lax.psum_scatter(
            query_part.astype(jnp.bfloat16), "fsdp", scatter_dimension=0, tiled=True
        ).astype(jnp.float32),
        lax.psum_scatter(
            output_part.astype(jnp.bfloat16), "fsdp", scatter_dimension=1, tiled=True
        ).astype(jnp.float32),
    )
    (
        key_proj_grad,
        value_proj_grad,
        attn_gain_grad,
        query_gain_grad,
        key_gain_grad,
        ffn_gain_grad,
    ) = (
        lax.psum_scatter(key_part, ("fsdp", "tp"), scatter_dimension=0, tiled=True),
        lax.psum_scatter(value_part, ("fsdp", "tp"), scatter_dimension=0, tiled=True),
        lax.psum_scatter(attn_gain_part, ("fsdp", "tp"), scatter_dimension=0, tiled=True),
        lax.psum_scatter(query_gain_part, ("fsdp", "tp"), scatter_dimension=0, tiled=True),
        lax.psum_scatter(key_gain_part, ("fsdp", "tp"), scatter_dimension=0, tiled=True),
        lax.psum_scatter(ffn_gain_part, ("fsdp", "tp"), scatter_dimension=0, tiled=True),
    )
    return (
        layer_out,
        in_grad,
        query_proj_grad,
        key_proj_grad,
        value_proj_grad,
        output_proj_grad,
        attn_gain_grad,
        query_gain_grad,
        key_gain_grad,
        ffn_gain_grad,
        gate_grad,
        up_grad,
        down_grad,
    )


def solution(mesh):
    in_specs = (
        P(("fsdp", "tp"), None),
        P("fsdp", "tp"),
        P(("fsdp", "tp"), None),
        P(("fsdp", "tp"), None),
        P("tp", "fsdp"),
        P(("fsdp", "tp")),
        P(("fsdp", "tp")),
        P(("fsdp", "tp")),
        P(("fsdp", "tp")),
        P("fsdp", None, "tp"),
        P("fsdp", None, "tp"),
        P("fsdp", "tp", None),
        P("fsdp", None),
        P("fsdp", None),
        P("fsdp"),
        P(("fsdp", "tp"), None),
    )
    out_specs = (
        P(("fsdp", "tp"), None),
        P(("fsdp", "tp"), None),
        P("fsdp", "tp"),
        P(("fsdp", "tp"), None),
        P(("fsdp", "tp"), None),
        P("tp", "fsdp"),
        P(("fsdp", "tp")),
        P(("fsdp", "tp")),
        P(("fsdp", "tp")),
        P(("fsdp", "tp")),
        P("fsdp", None, "tp"),
        P("fsdp", None, "tp"),
        P("fsdp", "tp", None),
    )
    return jax.shard_map(body, mesh=mesh, in_specs=in_specs, out_specs=out_specs, check_vma=False)
```

profile of v0, /device:TPU:0, one launch (start us, length us, event | category | flops | bytes accessed | tf_op | source)
XLA Modules:
  0.0 2757.8 jit_solution(2057339473192245555)
XLA Ops:
  11.4 42.3 %all-reduce.15 = (bf16[2048]{0:T(1024)(128)(2,1)S(1)}, bf16[128]{0:T(256)(128)(2,1)S(1)}, bf16[128]{0:T(256)(128)(2,1)S(1)}, bf16[2048]{0:T(1024)(128)(2,1)S(1)}) all-reduce(bf16[2048]{0:T(1024)(128)(2,1)S(1)} %dynamic-update-slice, bf16[128]{0:T(256)(128)(2,1)S(1)} %dynamic-update-slice.2, ...), channel_id=1, replica_groups=mesh['fsdp'=8,'tp'=4] {'fsdp','tp'}, use_global_device_ids=true, to_apply=%add.6 | all-reduce | flops 4352 | bytes 17408
  70.1 81.8 %all-gather.12.cloned.1.call-done = bf16[1024,2048]{1,0:T(8,128)(2,1)} async-done(((bf16[256,2048]{1,0:T(8,128)(2,1)}), bf16[1024,2048]{1,0:T(8,128)(2,1)}) %all-gather.12.cloned.1.call-update) | async-done | bytes 4194320 | tf_op jit(solution)/shard_map/all_gather | solution.py:96
  158.5 51.2 %all-gather.14.cloned.1.call-done = bf16[2048,512]{1,0:T(8,128)(2,1)} async-done(((bf16[64,512]{1,0:T(8,128)(2,1)}), bf16[2048,512]{1,0:T(8,128)(2,1)}) %all-gather.14.cloned.1.call-update) | async-done | bytes 2097168 | tf_op jit(solution)/shard_map/all_gather | solution.py:73
  322.1 76.2 %reduce-scatter.9.cloned.1.call-done = bf16[256,2048]{1,0:T(8,128)(2,1)} async-done(((bf16[1024,2048]{1,0:T(8,128)(2,1)}), bf16[256,2048]{1,0:T(8,128)(2,1)}) %reduce-scatter.9.cloned.1.call-update) | async-done | bytes 1048592 | tf_op jit(solution)/shard_map/reduce_scatter | solution.py:132
  590.0 149.1 %all-gather.24.cloned.1.call-done = bf16[16,2048,192]{1,2,0:T(8,128)(2,1)} async-done(((bf16[2,2048,192]{1,2,0:T(8,128)(2,1)}), bf16[16,2048,192]{1,2,0:T(8,128)(2,1)}) %all-gather.24.cloned.1.call-update) | async-done | bytes 12582928 | tf_op jit(solution)/shard_map/all_gather | solution.py:86
  739.0 117.9 %all-gather.26.cloned.1.call-done = bf16[16,2048,192]{1,2,0:T(8,128)(2,1)} async-done(((bf16[2,2048,192]{1,2,0:T(8,128)(2,1)}), bf16[16,2048,192]{1,2,0:T(8,128)(2,1)}) %all-gather.26.cloned.1.call-update) | async-done | bytes 12582928 | tf_op jit(solution)/shard_map/all_gather | solution.py:87
  857.0 70.6 %all-gather.28.cloned.1.call-done = bf16[16,192,2048]{2,1,0:T(8,128)(2,1)} async-done(((bf16[2,192,2048]{2,1,0:T(8,128)(2,1)}), bf16[16,192,2048]{2,1,0:T(8,128)(2,1)}) %all-gather.28.cloned.1.call-update) | async-done | bytes 12582928 | tf_op jit(solution)/shard_map/all_gather | solution.py:88
  934.5 394.3 %while.6 = (s32[]{:T(128)}, f32[1025,2048]{1,0:T(8,128)}, f32[4,4,576,192]{2,3,1,0:T(8,128)}, f32[4,4,576,192]{2,3,1,0:T(8,128)}, bf16[4,4,576,192]{2,3,1,0:T(8,...) while((s32[]{:T(128)}, f32[1025,2048]{1,0:T(8,128)}, ...), condition=%wide.region_14.15_spmd, body=%wide.region_12.14_spmd.sunk | while | flops 5447926272 | bytes 136991472 | solution.py:193
  988.4 40.1 %scatter_fusion = f32[1025,2048]{1,0:T(8,128)} fusion(f32[1025,2048]{1,0:T(8,128)} %get-tuple-element.511, s32[2304]{0:T(1024)S(1)} %fusion.177, f32[2304,2048]{1,0:T(8,128)} %bitcast.249), kind=kCustom, calls=%fused_computation.6.clone.1 | custom fusion | flops 4718592 | bytes 56632320 | tf_op jit(solution)/shard_map/while/body/eval_jaxpr/scatter-add | solution.py:190
  1083.6 40.1 %scatter_fusion = f32[1025,2048]{1,0:T(8,128)} fusion(f32[1025,2048]{1,0:T(8,128)} %get-tuple-element.511, s32[2304]{0:T(1024)S(1)} %fusion.177, f32[2304,2048]{1,0:T(8,128)} %bitcast.249), kind=kCustom, calls=%fused_computation.6.clone.1 | custom fusion | flops 4718592 | bytes 56632320 | tf_op jit(solution)/shard_map/while/body/eval_jaxpr/scatter-add | solution.py:190
  1178.9 40.1 %scatter_fusion = f32[1025,2048]{1,0:T(8,128)} fusion(f32[1025,2048]{1,0:T(8,128)} %get-tuple-element.511, s32[2304]{0:T(1024)S(1)} %fusion.177, f32[2304,2048]{1,0:T(8,128)} %bitcast.249), kind=kCustom, calls=%fused_computation.6.clone.1 | custom fusion | flops 4718592 | bytes 56632320 | tf_op jit(solution)/shard_map/while/body/eval_jaxpr/scatter-add | solution.py:190
  1274.1 40.1 %scatter_fusion = f32[1025,2048]{1,0:T(8,128)} fusion(f32[1025,2048]{1,0:T(8,128)} %get-tuple-element.511, s32[2304]{0:T(1024)S(1)} %fusion.177, f32[2304,2048]{1,0:T(8,128)} %bitcast.249), kind=kCustom, calls=%fused_computation.6.clone.1 | custom fusion | flops 4718592 | bytes 56632320 | tf_op jit(solution)/shard_map/while/body/eval_jaxpr/scatter-add | solution.py:190
  1337.9 412.3 %while.7 = (s32[]{:T(128)}, f32[1025,2048]{1,0:T(8,128)}, bf16[4,4,576,192]{2,3,1,0:T(8,128)(2,1)}, bf16[4,4,576,192]{2,3,1,0:T(8,128)(2,1)}, s32[4]{0:T(128)S(1...) while((s32[]{:T(128)}, f32[1025,2048]{1,0:T(8,128)}, ...), condition=%wide.region_18.19_spmd, body=%wide.region_16.18_spmd.sunk | while | flops 5465178624 | bytes 160583440 | solution.py:240
  1400.9 40.0 %scatter_fusion.1 = f32[1025,2048]{1,0:T(8,128)} fusion(f32[1025,2048]{1,0:T(8,128)} %get-tuple-element.560, s32[2304]{0:T(1024)S(1)} %fusion.182, f32[2304,2048]{1,0:T(8,128)} %bitcast.248), kind=kCustom, calls=%fused_computation.7.clone.1 | custom fusion | flops 4718592 | bytes 56632320 | tf_op jit(solution)/shard_map/while/body/eval_jaxpr/scatter-add | solution.py:237
  1503.8 40.0 %scatter_fusion.1 = f32[1025,2048]{1,0:T(8,128)} fusion(f32[1025,2048]{1,0:T(8,128)} %get-tuple-element.560, s32[2304]{0:T(1024)S(1)} %fusion.182, f32[2304,2048]{1,0:T(8,128)} %bitcast.248), kind=kCustom, calls=%fused_computation.7.clone.1 | custom fusion | flops 4718592 | bytes 56632320 | tf_op jit(solution)/shard_map/while/body/eval_jaxpr/scatter-add | solution.py:237
  1606.8 40.0 %scatter_fusion.1 = f32[1025,2048]{1,0:T(8,128)} fusion(f32[1025,2048]{1,0:T(8,128)} %get-tuple-element.560, s32[2304]{0:T(1024)S(1)} %fusion.182, f32[2304,2048]{1,0:T(8,128)} %bitcast.248), kind=kCustom, calls=%fused_computation.7.clone.1 | custom fusion | flops 4718592 | bytes 56632320 | tf_op jit(solution)/shard_map/while/body/eval_jaxpr/scatter-add | solution.py:237
  1709.8 40.0 %scatter_fusion.1 = f32[1025,2048]{1,0:T(8,128)} fusion(f32[1025,2048]{1,0:T(8,128)} %get-tuple-element.560, s32[2304]{0:T(1024)S(1)} %fusion.182, f32[2304,2048]{1,0:T(8,128)} %bitcast.248), kind=kCustom, calls=%fused_computation.7.clone.1 | custom fusion | flops 4718592 | bytes 56632320 | tf_op jit(solution)/shard_map/while/body/eval_jaxpr/scatter-add | solution.py:237
  1781.0 52.2 %reduce-scatter.13.cloned.1.call-done = bf16[256,2048]{1,0:T(8,128)(2,1)} async-done(((bf16[1024,2048]{1,0:T(8,128)(2,1)}), bf16[256,2048]{1,0:T(8,128)(2,1)}) %reduce-scatter.13.cloned.1.call-update) | async-done | bytes 1048592 | tf_op jit(solution)/shard_map/reduce_scatter | solution.py:286
  1846.6 74.5 %all-gather.32.cloned.1.call-done = bf16[1024,2048]{1,0:T(8,128)(2,1)} async-done(((bf16[256,2048]{1,0:T(8,128)(2,1)}), bf16[1024,2048]{1,0:T(8,128)(2,1)}) %all-gather.32.cloned.1.call-update) | async-done | bytes 4194320 | tf_op jit(solution)/shard_map/all_gather | solution.py:292
  1937.3 66.8 %all-to-all-done.7 = bf16[8,576,2048]{2,1,0:T(8,128)(2,1)} async-done(((bf16[8,576,2048]{2,1,0:T(8,128)(2,1)}), bf16[8,576,2048]{2,1,0:T(8,128)(2,1)}, u32[]{:S(2)}, u32[]{:S(2)}) %all-to-all-start.7) | async-done | bytes 18874400 | tf_op jit(solution)/shard_map/all_to_all | solution.py:265
  2223.7 38.0 %gather_fusion.2 = bf16[4608,2048]{1,0:T(8,128)(2,1)} fusion(bf16[1025,2048]{1,0:T(8,128)(2,1)} %get-tuple-element.612, s32[5120]{0:T(1024)S(1)} %copy-done.41), kind=kCustom, calls=%fused_computation.2 | custom fusion | bytes 37767168 | tf_op jit(solution)/shard_map/gather | solution.py:259
  2261.7 113.7 %all-to-all-done.2 = bf16[8,576,2048]{2,1,0:T(8,128)(2,1)} async-done(((bf16[8,576,2048]{2,1,0:T(8,128)(2,1)}), bf16[8,576,2048]{2,1,0:T(8,128)(2,1)}, u32[]{:S(2)}, u32[]{:S(2)}) %all-to-all-start.2) | async-done | bytes 18874400 | tf_op jit(solution)/shard_map/all_to_all | solution.py:264
  2425.6 194.7 %all-to-all-done = bf16[8,576,2048]{2,1,0:T(8,128)(2,1)} async-done(((bf16[8,576,2048]{2,1,0:T(8,128)(2,1)}), bf16[8,576,2048]{2,1,0:T(8,128)(2,1)}, u32[]{:S(2)}, u32[]{:S(2)}) %all-to-all-start) | async-done | bytes 18874400 | tf_op jit(solution)/shard_map/all_to_all | solution.py:264
  2704.2 39.4 %all-reduce.14 = (f32[2048]{0:T(1024)S(1)}, f32[128]{0:T(128)S(1)}, f32[128]{0:T(128)S(1)}, f32[2048]{0:T(1024)S(1)}) all-reduce(f32[2048]{0:T(1024)S(1)} %get-tuple-element.209, f32[128]{0:T(128)S(1)} %copy-done.78, f32[128]{0:T(128)S(1)} %copy-done.75, f32[2048]{0:T(1024)S(1)} %copy-done.58), channel_id=10, replica_groups=mesh['fsdp'=8,'tp'=4] {'fsdp','tp'}, use_global_device_ids=true, to_apply=%region_31.32.clone | all-reduce | flops 4352 | bytes 34816
  (455 shorter events, 1226.0 us)
Async XLA Ops:
  7.2 62.9 %all-gather.16.cloned.1.call-start = ((), (), s32[]{:S(2)}) async-start(), calls=%async_computation.20 | async-start | bytes 2162688 | tf_op jit(solution)/shard_map/all_gather | solution.py:72
  7.9 144.0 %all-gather.12.cloned.1.call-start = ((), (), s32[]{:S(2)}) async-start(), calls=%async_computation.18 | async-start | bytes 5242880 | tf_op jit(solution)/shard_map/all_gather | solution.py:96
  58.9 150.8 %all-gather.14.cloned.1.call-start = ((), (), s32[]{:S(2)}) async-start(), calls=%async_computation.19 | async-start | bytes 2162688 | tf_op jit(solution)/shard_map/all_gather | solution.py:73
  59.6 187.3 %all-gather.18.cloned.1.call-start = ((), (), s32[]{:S(2)}) async-start(), calls=%async_computation.21 | async-start | bytes 4718592 | tf_op jit(solution)/shard_map/all_gather | solution.py:84
  60.2 251.5 %all-gather.20.cloned.1.call-start = ((), (), s32[]{:S(2)}) async-start(), calls=%async_computation.22 | async-start | bytes 4718592 | tf_op jit(solution)/shard_map/all_gather | solution.py:85
  60.8 337.5 %reduce-scatter.9.cloned.1.call-start = ((), (), s32[]{:S(2)}) async-start(), calls=%async_computation.23 | async-start | bytes 5242880 | tf_op jit(solution)/shard_map/reduce_scatter | solution.py:132
  321.2 159.9 %all-gather.30.cloned.1.call-start = ((), (), s32[]{:S(2)}) async-start(), calls=%async_computation.29 | async-start | bytes 5242880 | tf_op jit(solution)/shard_map/all_gather | solution.py:201
  322.0 263.2 %all-gather.22.cloned.1.call-start = ((), (), s32[]{:S(2)}) async-start(), calls=%async_computation.24 | async-start | bytes 5242880 | tf_op jit(solution)/shard_map/all_gather | solution.py:140
  403.1 336.0 %all-gather.24.cloned.1.call-start = ((), (), s32[]{:S(2)}) async-start(), calls=%async_computation.25 | async-start | bytes 14155776 | tf_op jit(solution)/shard_map/all_gather | solution.py:86
  403.8 453.2 %all-gather.26.cloned.1.call-start = ((), (), s32[]{:S(2)}) async-start(), calls=%async_computation.26 | async-start | bytes 14155776 | tf_op jit(solution)/shard_map/all_gather | solution.py:87
  404.4 523.2 %all-gather.28.cloned.1.call-start = ((), (), s32[]{:S(2)}) async-start(), calls=%async_computation.27 | async-start | bytes 14155776 | tf_op jit(solution)/shard_map/all_gather | solution.py:88
  541.4 1233.3 %all-to-all-start.9 = ((bf16[8,576,2048]{2,1,0:T(8,128)(2,1)}), bf16[8,576,2048]{2,1,0:T(8,128)(2,1)}, u32[]{:S(2)}, u32[]{:S(2)}) async-start(bf16[8,576,2048]{2,1,0:T(8,128)(2,1)} %fusion.30), calls=%async_computation.17 | async-start | bytes 37748736 | tf_op jit(solution)/shard_map/all_to_all | solution.py:265
  547.3 1285.9 %reduce-scatter.13.cloned.1.call-start = ((), (), s32[]{:S(2)}) async-start(), calls=%async_computation.30 | async-start | bytes 5242880 | tf_op jit(solution)/shard_map/reduce_scatter | solution.py:286
  1774.7 229.5 %all-to-all-start.7 = ((bf16[8,576,2048]{2,1,0:T(8,128)(2,1)}), bf16[8,576,2048]{2,1,0:T(8,128)(2,1)}, u32[]{:S(2)}, u32[]{:S(2)}) async-start(bf16[8,576,2048]{2,1,0:T(8,128)(2,1)} %fusion.31), calls=%async_computation.15 | async-start | bytes 37748736 | tf_op jit(solution)/shard_map/all_to_all | solution.py:265
  1780.9 140.1 %all-gather.32.cloned.1.call-start = ((), (), s32[]{:S(2)}) async-start(), calls=%async_computation.31 | async-start | bytes 5242880 | tf_op jit(solution)/shard_map/all_gather | solution.py:292
  1839.7 857.8 %reduce-scatter.23.cloned.1.call-start = ((), (), s32[]{:S(2)}) async-start(), calls=%async_computation.36 | async-start | bytes 4718592 | tf_op jit(solution)/shard_map/reduce_scatter | solution.py:367
  2096.8 62.5 %all-to-all-start.4 = ((bf16[8,576,192]{1,2,0:T(8,128)(2,1)}), bf16[8,576,192]{1,2,0:T(8,128)(2,1)}, u32[]{:S(2)}, u32[]{:S(2)}) async-start(bf16[8,576,192]{1,2,0:T(8,128)(2,1)} %get-tuple-element.294), calls=%async_computation.12 | async-start | bytes 3932160 | tf_op jit(solution)/shard_map/all_to_all | solution.py:269
  2101.2 598.5 %reduce-scatter.17.cloned.1.call-start = ((), (), s32[]{:S(2)}) async-start(), calls=%async_computation.33 | async-start | bytes 4718592 | tf_op jit(solution)/shard_map/reduce_scatter | solution.py:364
  2159.3 216.1 %all-to-all-start.2 = ((bf16[8,576,2048]{2,1,0:T(8,128)(2,1)}), bf16[8,576,2048]{2,1,0:T(8,128)(2,1)}, u32[]{:S(2)}, u32[]{:S(2)}) async-start(bf16[8,576,2048]{2,1,0:T(8,128)(2,1)} %bitcast.254), calls=%async_computation.10 | async-start | bytes 37748736 | tf_op jit(solution)/shard_map/all_to_all | solution.py:264
  2165.5 536.4 %reduce-scatter.15.cloned.1.call-start = ((), (), s32[]{:S(2)}) async-start(), calls=%async_computation.32 | async-start | bytes 5242880 | tf_op jit(solution)/shard_map/reduce_scatter | solution.py:339
  2216.9 529.0 %reduce-scatter.11.cloned.1.call-start = ((), (), s32[]{:S(2)}) async-start(), calls=%async_computation.28 | async-start | bytes 5242880 | tf_op jit(solution)/shard_map/reduce_scatter | solution.py:196
  2375.4 244.9 %all-to-all-start = ((bf16[8,576,2048]{2,1,0:T(8,128)(2,1)}), bf16[8,576,2048]{2,1,0:T(8,128)(2,1)}, u32[]{:S(2)}, u32[]{:S(2)}) async-start(bf16[8,576,2048]{2,1,0:T(8,128)(2,1)} %bitcast.255), calls=%async_computation.8 | async-start | bytes 37748736 | tf_op jit(solution)/shard_map/all_to_all | solution.py:264
  2381.3 369.7 %reduce-scatter.21.cloned.1.call-start = ((), (), s32[]{:S(2)}) async-start(), calls=%async_computation.35 | async-start | bytes 4325376 | tf_op jit(solution)/shard_map/reduce_scatter | solution.py:380
  2387.5 363.6 %reduce-scatter.19.cloned.1.call-start = ((), (), s32[]{:S(2)}) async-start(), calls=%async_computation.34 | async-start | bytes 4325376 | tf_op jit(solution)/shard_map/reduce_scatter | solution.py:379
  (86 other events, 2838.9 us)
Sparse Core Ops, SparseCore 0:
  10.9 59.1 all-gather.15
  72.2 79.5 all-gather.11
  154.8 54.8 all-gather.13
  211.4 35.4 all-gather.17
  248.6 37.3 all-gather.19
  321.4 76.8 reduce-scatter.8
  399.8 81.2 all-gather.29
  483.3 79.2 all-gather.21
  564.4 174.5 all-gather.23
  740.8 116.1 all-gather.25
  858.9 68.6 all-gather.27
  1756.3 76.7 reduce-scatter.12
  1839.8 81.2 all-gather.31
  1929.4 67.5 reduce-scatter.22
  2120.9 55.9 reduce-scatter.16
  2217.0 89.6 reduce-scatter.14
  2308.9 77.2 reduce-scatter.10
  2388.9 150.8 reduce-scatter.20
  2542.7 147.8 reduce-scatter.18
where the time goes:
time: 2760 us
  waiting for transfers between devices  1140 us (41%)
  matrix products  506 us (18%)
  local copies, waits for them, and re-layouts  472 us (17%)
  other arithmetic  462 us (17%)
  blocking collectives  81.7 us (3%)
  starting transfers between devices  50.1 us (2%)
    all_to_all x2, waiting for transfers between devices, body(): lax.all_to_all(inputs, 'fsdp', split_axis=0, concat_axis=1, tiled=True)  308 us
    scatter-add x4, other arithmetic, ffn_block(): accum = accum.at[slot_rows.reshape(-1)].add(expert_out.reshape(-1, width))  160 us
    scatter-add x4, other arithmetic, ffn_back(): accum = accum.at[slot_rows.reshape(-1)].add(input_grad.reshape(-1, width))  160 us
    all_gather x1, waiting for transfers between devices, body(): lax.all_gather(expert_gate, 'fsdp', axis=0, tiled=True)  149 us
    all_gather x1, waiting for transfers between devices, body(): lax.all_gather(expert_up, 'fsdp', axis=0, tiled=True)  118 us
    gather x4, local copies, waits for them, and re-layouts, ffn_block(): inputs = padded[slot_rows]  84.2 us
    gather x4, local copies, waits for them, and re-layouts, ffn_back(): grad_pad[slot_rows].astype(jnp.float32) * slot_share[..., None]  84.1 us
    all_gather x1, waiting for transfers between devices, body(): attn_rows = lax.all_gather(attn_in, 'tp', axis=0, tiled=True)  81.8 us
  transfers between devices with their start and end apart: 29, of which 18 were waited for; matrix products, arithmetic and copies ran while one was open for 52% of the time, Pallas kernels for 0%

commit v1 on v0

--- a/solution.py
+++ b/solution.py
@@ -68,14 +68,24 @@
     group_rows = tok_rows * lax.axis_size("tp")
     seq_count = group_rows // SEQ
     factor = 1.0 / math.sqrt(HD)
-    key_all, value_all, gain_attn, gain_query, gain_key, gain_ffn = (
-        lax.all_gather(key_proj, ("fsdp", "tp"), axis=0, tiled=True),
-        lax.all_gather(value_proj, ("fsdp", "tp"), axis=0, tiled=True),
-        lax.all_gather(attn_gain, ("fsdp", "tp"), axis=0, tiled=True),
-        lax.all_gather(query_gain, ("fsdp", "tp"), axis=0, tiled=True),
-        lax.all_gather(key_gain, ("fsdp", "tp"), axis=0, tiled=True),
-        lax.all_gather(ffn_gain, ("fsdp", "tp"), axis=0, tiled=True),
-    )
+    gain_sizes = (attn_gain.shape[0], query_gain.shape[0], key_gain.shape[0], ffn_gain.shape[0])
+    kv_rows, kv_width = key_proj.shape
+    gain_row = jnp.concatenate([attn_gain, query_gain, key_gain, ffn_gain])
+    gain_block = jnp.zeros((8, 2 * kv_width), jnp.bfloat16).at[0, : gain_row.shape[0]].set(gain_row)
+    packed = jnp.concatenate(
+        [jnp.concatenate([key_proj, value_proj], axis=1), gain_block], axis=0
+    )
+    packed_all = lax.all_gather(packed, ("fsdp", "tp"), axis=0, tiled=False)
+    kv_all = packed_all[:, :kv_rows].reshape(-1, 2 * kv_width)
+    key_all = kv_all[:, :kv_width]
+    value_all = kv_all[:, kv_width:]
+    gain_all = packed_all[:, kv_rows]
+    gains = []
+    offset = 0
+    for size in gain_sizes:
+        gains.append(gain_all[:, offset : offset + size].reshape(-1))
+        offset += size
+    gain_attn, gain_query, gain_key, gain_ffn = gains
     gain_attn = gain_attn.astype(jnp.float32)
     gain_query = gain_query.astype(jnp.float32)
     gain_key = gain_key.astype(jnp.float32)
@@ -138,153 +148,48 @@
     residual = tokens_f + attn_out
     ffn_in = rms_norm(residual, gain_ffn).astype(jnp.bfloat16)
     ffn_rows = lax.all_gather(ffn_in, "tp", axis=0, tiled=True)
-    padded = jnp.concatenate([ffn_rows, jnp.zeros((1, width), jnp.bfloat16)], axis=0)
     expert_count = gate_w.shape[0]
-    capacity = 9 * TOP * group_rows // (8 * expert_count)
-    route_flat = routes.reshape(-1)
-    one_hot = (route_flat[:, None] == lax.iota(jnp.int32, expert_count)[None, :]).astype(jnp.int32)
-    slot_rank = jnp.sum((jnp.cumsum(one_hot, axis=0) - one_hot) * one_hot, axis=1)
-    slot_index = route_flat * capacity + slot_rank
-    token_of = (
-        jnp.full((expert_count * capacity,), group_rows, jnp.int32)
-        .at[slot_index]
-        .set(lax.iota(jnp.int32, route_flat.shape[0]) // TOP)
-        .reshape(expert_count, capacity)
-    )
-    share_of = (
-        jnp.zeros((expert_count * capacity,), jnp.float32)
-        .at[slot_index]
-        .set(route_weights.reshape(-1))
-        .reshape(expert_count, capacity)
-    )
-    block_size = math.gcd(expert_count, 4)
-    block_count = expert_count // block_size
-
-    def ffn_block(accum, block_id):
-        first_exp = block_id * block_size
-        slot_rows = lax.dynamic_slice_in_dim(token_of, first_exp, block_size, 0)
-        slot_share = lax.dynamic_slice_in_dim(share_of, first_exp, block_size, 0)
-        inputs = padded[slot_rows]
-        gate_val = jnp.einsum(
-            "ecd,edf->ecf",
-            inputs,
-            lax.dynamic_slice_in_dim(gate_w, first_exp, block_size, 0),
-            preferred_element_type=jnp.float32,
-        )
-        up_val = jnp.einsum(
-            "ecd,edf->ecf",
-            inputs,
-            lax.dynamic_slice_in_dim(up_w, first_exp, block_size, 0),
-            preferred_element_type=jnp.float32,
-        )
-        hidden = (jax.nn.silu(gate_val) * up_val).astype(jnp.bfloat16)
-        expert_out = (
-            jnp.einsum(
-                "ecf,efd->ecd",
-                hidden,
-                lax.dynamic_slice_in_dim(down_w, first_exp, block_size, 0),
-                preferred_element_type=jnp.float32,
-            )
-            * slot_share[..., None]
-        )
-        accum = accum.at[slot_rows.reshape(-1)].add(expert_out.reshape(-1, width))
-        return (accum, (gate_val, up_val, hidden))
-
-    mixture, (gate_all, up_all, hidden_all) = lax.scan(
-        ffn_block, jnp.zeros((group_rows + 1, width), jnp.float32), lax.iota(jnp.int32, block_count)
+    chosen = routes[:, :, None] == lax.iota(jnp.int32, expert_count)[None, None, :]
+    share = jnp.sum(jnp.where(chosen, route_weights[:, :, None], 0.0), axis=1)
+    gate_val = jnp.einsum("td,edf->tef", ffn_rows, gate_w, preferred_element_type=jnp.float32)
+    up_val = jnp.einsum("td,edf->tef", ffn_rows, up_w, preferred_element_type=jnp.float32)
+    sigma = jax.nn.sigmoid(gate_val)
+    active = gate_val * sigma
+    hidden = (active * up_val).astype(jnp.bfloat16)
+    hidden_share = (hidden.astype(jnp.float32) * share[:, :, None]).astype(jnp.bfloat16)
+    mixture = jnp.einsum(
+        "tef,efd->td", hidden_share, down_w, preferred_element_type=jnp.float32
     )
     mixture_own = lax.psum_scatter(
-        mixture[:group_rows].astype(jnp.bfloat16), "tp", scatter_dimension=0, tiled=True
+        mixture.astype(jnp.bfloat16), "tp", scatter_dimension=0, tiled=True
     ).astype(jnp.float32)
     layer_out = (residual + mixture_own).astype(jnp.bfloat16)
     grad_out = out_grad.astype(jnp.float32)
     grad_rows = lax.all_gather(out_grad, "tp", axis=0, tiled=True)
-    grad_pad = jnp.concatenate([grad_rows, jnp.zeros((1, width), jnp.bfloat16)], axis=0)
-
-    def ffn_back(accum, block_id):
-        first_exp = block_id * block_size
-        slot_rows = lax.dynamic_slice_in_dim(token_of, first_exp, block_size, 0)
-        slot_share = lax.dynamic_slice_in_dim(share_of, first_exp, block_size, 0)
-        gate_val = gate_all[block_id]
-        up_val = up_all[block_id]
-        sigma = jax.nn.sigmoid(gate_val)
-        active = gate_val * sigma
-        slot_grad = (grad_pad[slot_rows].astype(jnp.float32) * slot_share[..., None]).astype(
-            jnp.bfloat16
-        )
-        hidden_grad = jnp.einsum(
-            "ecd,efd->ecf",
-            slot_grad,
-            lax.dynamic_slice_in_dim(down_w, first_exp, block_size, 0),
-            preferred_element_type=jnp.float32,
-        )
-        gate_back = (hidden_grad * up_val * sigma * (1.0 + gate_val * (1.0 - sigma))).astype(
-            jnp.bfloat16
-        )
-        up_back = (hidden_grad * active).astype(jnp.bfloat16)
-        input_grad = jnp.einsum(
-            "ecf,edf->ecd",
-            gate_back,
-            lax.dynamic_slice_in_dim(gate_w, first_exp, block_size, 0),
-            preferred_element_type=jnp.float32,
-        )
-        input_grad = input_grad + jnp.einsum(
-            "ecf,edf->ecd",
-            up_back,
-            lax.dynamic_slice_in_dim(up_w, first_exp, block_size, 0),
-            preferred_element_type=jnp.float32,
-        )
-        accum = accum.at[slot_rows.reshape(-1)].add(input_grad.reshape(-1, width))
-        return (accum, (gate_back, up_back))
-
-    ffn_in_grad, (gate_back_all, up_back_all) = lax.scan(
-        ffn_back, jnp.zeros((group_rows + 1, width), jnp.float32), lax.iota(jnp.int32, block_count)
-    )
-    hidden_width = gate_w.shape[2]
-    gate_back_all = gate_back_all.reshape(expert_count, capacity, hidden_width)
-    up_back_all = up_back_all.reshape(expert_count, capacity, hidden_width)
-    hidden_all = hidden_all.reshape(expert_count, capacity, hidden_width)
-    owners = lax.axis_size("fsdp")
-    local_count = expert_count // owners
-    rows_split = token_of.reshape(owners, local_count, capacity)
-    share_split = share_of.reshape(owners, local_count, capacity)
-    gate_split = gate_back_all.reshape(owners, local_count, capacity, hidden_width)
-    up_split = up_back_all.reshape(owners, local_count, capacity, hidden_width)
-    hidden_split = hidden_all.reshape(owners, local_count, capacity, hidden_width)
-    gate_list = []
-    up_list = []
-    down_list = []
-    for local_id in range(local_count):
-        slot_rows = rows_split[:, local_id]
-        inputs = padded[slot_rows]
-        slot_grad = (
-            grad_pad[slot_rows].astype(jnp.float32) * share_split[:, local_id][..., None]
-        ).astype(jnp.bfloat16)
-        got_in, got_grad, got_gate, got_up, got_hidden = (
-            lax.all_to_all(inputs, "fsdp", split_axis=0, concat_axis=1, tiled=True),
-            lax.all_to_all(slot_grad, "fsdp", split_axis=0, concat_axis=1, tiled=True),
-            lax.all_to_all(
-                gate_split[:, local_id], "fsdp", split_axis=0, concat_axis=1, tiled=True
-            ),
-            lax.all_to_all(up_split[:, local_id], "fsdp", split_axis=0, concat_axis=1, tiled=True),
-            lax.all_to_all(
-                hidden_split[:, local_id], "fsdp", split_axis=0, concat_axis=1, tiled=True
-            ),
-        )
-        gate_list.append(
-            jnp.einsum("ecd,ecf->edf", got_in, got_gate, preferred_element_type=jnp.float32)[0]
-        )
-        up_list.append(
-            jnp.einsum("ecd,ecf->edf", got_in, got_up, preferred_element_type=jnp.float32)[0]
-        )
-        down_list.append(
-            jnp.einsum("ecf,ecd->efd", got_hidden, got_grad, preferred_element_type=jnp.float32)[0]
-        )
-    gate_grad = jnp.stack(gate_list, axis=0)
-    up_grad = jnp.stack(up_list, axis=0)
-    down_grad = jnp.stack(down_list, axis=0)
+    hidden_grad = (
+        jnp.einsum("td,efd->tef", grad_rows, down_w, preferred_element_type=jnp.float32)
+        * share[:, :, None]
+    )
+    gate_back = (hidden_grad * up_val * sigma * (1.0 + gate_val * (1.0 - sigma))).astype(
+        jnp.bfloat16
+    )
+    up_back = (hidden_grad * active).astype(jnp.bfloat16)
+    ffn_in_grad = jnp.einsum(
+        "tef,edf->td", gate_back, gate_w, preferred_element_type=jnp.float32
+    ) + jnp.einsum("tef,edf->td", up_back, up_w, preferred_element_type=jnp.float32)
+    gate_part = jnp.einsum("td,tef->edf", ffn_rows, gate_back, preferred_element_type=jnp.float32)
+    up_part = jnp.einsum("td,tef->edf", ffn_rows, up_back, preferred_element_type=jnp.float32)
+    down_part = jnp.einsum(
+        "tef,td->efd", hidden_share, grad_rows, preferred_element_type=jnp.float32
+    )
+    gate_grad, up_grad, down_grad = (
+        lax.psum_scatter(
+            part.astype(jnp.bfloat16), "fsdp", scatter_dimension=0, tiled=True
+        ).astype(jnp.float32)
+        for part in (gate_part, up_part, down_part)
+    )
     ffn_in_own = lax.psum_scatter(
-        ffn_in_grad[:group_rows].astype(jnp.bfloat16), "tp", scatter_dimension=0, tiled=True
+        ffn_in_grad.astype(jnp.bfloat16), "tp", scatter_dimension=0, tiled=True
     ).astype(jnp.float32)
     _, second_back = jax.vjp(rms_norm, residual, gain_ffn)
     residual_norm_grad, ffn_gain_part = second_back(ffn_in_own)
@@ -346,17 +251,28 @@
         tiled=True,
     ).astype(jnp.float32)
     query_part = jnp.einsum("gd,gq->dq", attn_rows, query_back, preferred_element_type=jnp.float32)
-    kv_width = key_all.shape[1]
     key_head_part = jnp.einsum("gd,gk->dk", attn_rows, key_back, preferred_element_type=jnp.float32)
     value_head_part = jnp.einsum(
         "gd,gk->dk", attn_rows, value_back, preferred_element_type=jnp.float32
     )
-    key_part = lax.dynamic_update_slice_in_dim(
-        jnp.zeros((width, kv_width), jnp.float32), key_head_part, kv_head * HD, 1
-    )
-    value_part = lax.dynamic_update_slice_in_dim(
-        jnp.zeros((width, kv_width), jnp.float32), value_head_part, kv_head * HD, 1
-    )
+    kv_part = lax.psum_scatter(
+        jnp.concatenate([key_head_part, value_head_part], axis=1),
+        "fsdp",
+        scatter_dimension=0,
+        tiled=True,
+    )
+    tp_size = lax.axis_size("tp")
+    kv_got = lax.all_to_all(
+        kv_part.reshape(tp_size, kv_part.shape[0] // tp_size, 2 * HD),
+        "tp",
+        split_axis=0,
+        concat_axis=0,
+        tiled=True,
+    )
+    sub_rows = kv_part.shape[0] // tp_size
+    kv_got = jnp.sum(kv_got.reshape(HK, tp_size // HK, sub_rows, 2 * HD), axis=1)
+    key_proj_grad = kv_got[:, :, :HD].transpose(1, 0, 2).reshape(sub_rows, HK * HD)
+    value_proj_grad = kv_got[:, :, HD:].transpose(1, 0, 2).reshape(sub_rows, HK * HD)
     _, first_back = jax.vjp(rms_norm, tokens_f, gain_attn)
     input_norm_grad, attn_gain_part = first_back(attn_in_grad)
     in_grad = residual_grad + input_norm_grad
@@ -368,16 +284,7 @@
             output_part.astype(jnp.bfloat16), "fsdp", scatter_dimension=1, tiled=True
         ).astype(jnp.float32),
     )
-    (
-        key_proj_grad,
-        value_proj_grad,
-        attn_gain_grad,
-        query_gain_grad,
-        key_gain_grad,
-        ffn_gain_grad,
-    ) = (
-        lax.psum_scatter(key_part, ("fsdp", "tp"), scatter_dimension=0, tiled=True),
-        lax.psum_scatter(value_part, ("fsdp", "tp"), scatter_dimension=0, tiled=True),
+    attn_gain_grad, query_gain_grad, key_gain_grad, ffn_gain_grad = (
         lax.psum_scatter(attn_gain_part, ("fsdp", "tp"), scatter_dimension=0, tiled=True),
         lax.psum_scatter(query_gain_part, ("fsdp", "tp"), scatter_dimension=0, tiled=True),
         lax.psum_scatter(key_gain_part, ("fsdp", "tp"), scatter_dimension=0, tiled=True),

time: 2760 us -> 1680 us (0.61)
  local copies, waits for them, and re-layouts: 472 us -> 26.3 us
  other arithmetic: 462 us -> 105 us
  matrix products: 506 us -> 345 us
  starting transfers between devices: 50.1 us -> 4.97 us
  blocking collectives: 81.7 us -> 45.9 us
    all_to_all x10 -> x1, waiting for transfers between devices: 417 us -> 9.5 us  [body(): lax.all_to_all(kv_part.reshape(tp_size, kv_part.shape[0] // tp_size, 2 *...]
    scatter-add x8 -> x0, other arithmetic: 320 us -> none  [the longest x4 160 us: ffn_block(): accum = accum.at[slot_rows.reshape(-1)].add(expert_out.reshape(-1, width))]
    gather x12 -> x0, local copies, waits for them, and re-layouts: 320 us -> none  [the longest x4 84.2 us: ffn_block(): inputs = padded[slot_rows]]
    reduce_scatter x4 -> x6, waiting for transfers between devices: 52.2 us -> 269 us  [the longest x3 163 us: body(): lax.psum_scatter(part.astype(jnp.bfloat16), 'fsdp', scatter_dimension=0,...]
    dot_general x30 -> x7, matrix products: 332 us -> 145 us  [the longest x1 27.8 us: body(): jnp.einsum('td,efd->tef', grad_rows, down_w, preferred_element_type=jnp.f...]
    all_gather x1, waiting for transfers between devices: 149 us -> 53.4 us  [body(): lax.all_gather(expert_gate, 'fsdp', axis=0, tiled=True)]
    all_gather x1, waiting for transfers between devices: 0.01 us -> 82.9 us  [body(): ffn_rows = lax.all_gather(ffn_in, 'tp', axis=0, tiled=True)]
    reduce_scatter x1, waiting for transfers between devices: 0.01 us -> 77 us  [body(): lax.psum_scatter((result + jnp.einsum('gk,dk->gd', value_back, value_w, p...]
  transfers between devices with their start and end apart: 29 -> 21, of which waited for: 18 -> 18; matrix products, arithmetic and copies ran while one was open for 52% -> 17% of each run, Pallas kernels for 0% -> 0%
where the time goes in v1:
time: 1680 us; the launch traced here: 1670 us
  waiting for transfers between devices  1130 us (67%)
  matrix products  345 us (21%)
  other arithmetic  105 us (6%)
  blocking collectives  45.9 us (3%)
  local copies, waits for them, and re-layouts  26.3 us (2%)
    reduce_scatter x3, waiting for transfers between devices, body(): lax.psum_scatter(part.astype(jnp.bfloat16), 'fsdp', scatter_dimension=0,...  163 us
    all_gather x1, waiting for transfers between devices, body(): ffn_rows = lax.all_gather(ffn_in, 'tp', axis=0, tiled=True)  82.9 us
    all_gather x1, waiting for transfers between devices, body(): lax.all_gather(residual_grad.astype(jnp.bfloat16), 'tp', axis=0, tiled=True)  81.1 us
    reduce_scatter x1, waiting for transfers between devices, body(): lax.psum_scatter((result + jnp.einsum('gk,dk->gd', value_back, value_w, p...  77 us
    reduce_scatter x1, waiting for transfers between devices, body(): lax.psum_scatter(ffn_in_grad.astype(jnp.bfloat16), 'tp', scatter_dimensio...  76.9 us
    reduce_scatter x1, waiting for transfers between devices, body(): lax.psum_scatter(jnp.dot(context_b, out_w, preferred_element_type=jnp.flo...  76.3 us
    all_gather x1, waiting for transfers between devices, body(): lax.all_gather(expert_down, 'fsdp', axis=0, tiled=True)  72.3 us
    all_gather x1, waiting for transfers between devices, body(): attn_rows = lax.all_gather(attn_in, 'tp', axis=0, tiled=True)  72.1 us
  transfers between devices with their start and end apart: 21, of which 18 were waited for; matrix products, arithmetic and copies ran while one was open for 17% of the time, Pallas kernels for 0%

profile of v1, /device:TPU:0, one launch (start us, length us, event | category | flops | bytes accessed | tf_op | source)
XLA Modules:
  0.0 1671.0 jit_solution(10220839119883781289)
XLA Ops:
  11.7 66.0 %all-gather.30.cloned.1.call-done = bf16[2304,1024]{1,0:T(8,128)(2,1)} async-done(((bf16[72,1024]{1,0:T(8,128)(2,1)}), bf16[2304,1024]{1,0:T(8,128)(2,1)}) %all-gather.30.cloned.1.call-update) | async-done | bytes 4718608 | tf_op jit(solution)/shard_map/all_gather | solution.py:78
  88.6 72.1 %all-gather.12.cloned.1.call-done = bf16[1024,2048]{1,0:T(8,128)(2,1)} async-done(((bf16[256,2048]{1,0:T(8,128)(2,1)}), bf16[1024,2048]{1,0:T(8,128)(2,1)}) %all-gather.12.cloned.1.call-update) | async-done | bytes 4194320 | tf_op jit(solution)/shard_map/all_gather | solution.py:106
  167.5 30.2 %all-gather.14.cloned.1.call-done = bf16[2048,1024]{1,0:T(8,128)(2,1)} async-done(((bf16[256,1024]{1,0:T(8,128)(2,1)}), bf16[2048,1024]{1,0:T(8,128)(2,1)}) %all-gather.14.cloned.1.call-update) | async-done | bytes 4194320 | tf_op jit(solution)/shard_map/all_gather | solution.py:94
  274.3 76.3 %reduce-scatter.11.cloned.1.call-done = bf16[256,2048]{1,0:T(8,128)(2,1)} async-done(((bf16[1024,2048]{1,0:T(8,128)(2,1)}), bf16[256,2048]{1,0:T(8,128)(2,1)}) %reduce-scatter.11.cloned.1.call-update) | async-done | bytes 1048592 | tf_op jit(solution)/shard_map/reduce_scatter | solution.py:142
  357.1 67.8 %all-gather.22.cloned.1.call-done = bf16[16,2048,192]{1,2,0:T(8,128)(2,1)} async-done(((bf16[2,2048,192]{1,2,0:T(8,128)(2,1)}), bf16[16,2048,192]{1,2,0:T(8,128)(2,1)}) %all-gather.22.cloned.1.call-update) | async-done | bytes 12582928 | tf_op jit(solution)/shard_map/all_gather | solution.py:97
  424.8 82.9 %all-gather.18.cloned.1.call-done = bf16[1024,2048]{1,0:T(8,128)(2,1)} async-done(((bf16[256,2048]{1,0:T(8,128)(2,1)}), bf16[1024,2048]{1,0:T(8,128)(2,1)}) %all-gather.18.cloned.1.call-update) | async-done | bytes 4194320 | tf_op jit(solution)/shard_map/all_gather | solution.py:150
  526.8 53.4 %all-gather.20.cloned.1.call-done = bf16[16,2048,192]{1,2,0:T(8,128)(2,1)} async-done(((bf16[2,2048,192]{1,2,0:T(8,128)(2,1)}), bf16[16,2048,192]{1,2,0:T(8,128)(2,1)}) %all-gather.20.cloned.1.call-update) | async-done | bytes 12582928 | tf_op jit(solution)/shard_map/all_gather | solution.py:96
  599.3 63.2 %all-gather.26.cloned.1.call-done = bf16[1024,2048]{1,0:T(8,128)(2,1)} async-done(((bf16[256,2048]{1,0:T(8,128)(2,1)}), bf16[1024,2048]{1,0:T(8,128)(2,1)}) %all-gather.26.cloned.1.call-update) | async-done | bytes 4194320 | tf_op jit(solution)/shard_map/all_gather | solution.py:168
  662.5 72.3 %all-gather.24.cloned.1.call-done = bf16[16,192,2048]{2,1,0:T(8,128)(2,1)} async-done(((bf16[2,192,2048]{2,1,0:T(8,128)(2,1)}), bf16[16,192,2048]{2,1,0:T(8,128)(2,1)}) %all-gather.24.cloned.1.call-update) | async-done | bytes 12582928 | tf_op jit(solution)/shard_map/all_gather | solution.py:98
  734.8 27.8 %multiply_convert_fusion = (bf16[1024,16,192]{0,2,1:T(8,128)(2,1)}, bf16[1024,16,192]{0,2,1:T(8,128)(2,1)}, bf16[1024,16,192]{0,2,1:T(8,128)(2,1)}) fusion(f32[1024,16]{0,1:T(8,128)S(1)} %select_reduce_fusion, f32[1024,16,192]{0,2,1:T(8,128)} %bitcast.141, f32[1024,16,192]{0,2,1:T(8,128)} %bitcast.140, ...), kind=kOutput, calls=%fused_computation.16 | convolution fusion | flops 12944670720 | bytes 60882944 | tf_op jit(solution)/shard_map/td,efd->tef/dot_general | solution.py:170
  780.1 20.3 %fusion.10 = bf16[1024,2048]{1,0:T(8,128)(2,1)} fusion(f32[1024,2048,1]{1,0,2:T(8,128)S(1)} %fusion.82, bf16[1024,16,192]{0,2,1:T(8,128)(2,1)} %get-tuple-element.88, bf16[16,2048,192]{1,2,0:T(8,128)(2,1)} %all-gather.22.cloned.1.call-done), kind=kOutput, calls=%fused_computation.23 | convolution fusion | flops 12889096192 | bytes 31457280 | tf_op jit(solution)/shard_map/tef,edf->td/dot_general | solution.py:179
  800.5 76.9 %reduce-scatter.15.cloned.1.call-done = bf16[256,2048]{1,0:T(8,128)(2,1)} async-done(((bf16[1024,2048]{1,0:T(8,128)(2,1)}), bf16[256,2048]{1,0:T(8,128)(2,1)}) %reduce-scatter.15.cloned.1.call-update) | async-done | bytes 1048592 | tf_op jit(solution)/shard_map/reduce_scatter | solution.py:191
  884.2 81.1 %all-gather.28.cloned.1.call-done = bf16[1024,2048]{1,0:T(8,128)(2,1)} async-done(((bf16[256,2048]{1,0:T(8,128)(2,1)}), bf16[1024,2048]{1,0:T(8,128)(2,1)}) %all-gather.28.cloned.1.call-update) | async-done | bytes 4194320 | tf_op jit(solution)/shard_map/all_gather | solution.py:197
  988.5 25.3 %fusion = (f32[8,1024]{1,0:T(8,128)S(1)}, f32[1024,1024,8]{1,0,2:T(8,128)}) fusion(f32[8,1024,1024]{1,2,0:T(8,128)} %get-tuple-element.116, f32[8,1024]{1,0:T(8,128)S(1)} %log_add_fusion, bf16[1024,128,1]{1,0,2:T(8,128)(2,1)S(1)} %copy-done.29, bf16[1024,8,128]{0,2,1:T(8,128)(2,1)S(1)} %bitcast.130), kind=kOutput, calls=%fused_computation.2 | convolution fusion | flops 2172641280 | bytes 69533696 | tf_op jit(solution)/shard_map/while/body/eval_jaxpr/qhd,kd->hqk/dot_general | solution.py:217
  1013.7 28.3 %fusion.2 = bf16[8,1024,1024]{1,2,0:T(8,128)(2,1)} fusion(f32[1024,1024,8]{1,0,2:T(8,128)} %get-tuple-element.118, f32[8,1024,1024]{1,2,0:T(8,128)} %get-tuple-element.116, f32[8,1024]{1,0:T(8,128)S(1)} %get-tuple-element.117, f32[8,1024]{1,0:T(8,128)S(1)} %log_add_fusion), kind=kLoop, calls=%fused_computation.4 | loop fusion | flops 33554432 | bytes 83951616 | tf_op jit(solution)/shard_map/while/body/eval_jaxpr/convert_element_type | solution.py:222
  1102.9 20.8 %convolution_convert_fusion = bf16[16,192,2048]{2,1,0:T(8,128)(2,1)} fusion(bf16[1024,16,192]{0,2,1:T(8,128)(2,1)} %get-tuple-element.90, bf16[1024,2048]{1,0:T(8,128)(2,1)} %all-gather.26.cloned.1.call-done), kind=kOutput, calls=%fused_computation.26 | convolution fusion | flops 12891193344 | bytes 23068672 | tf_op jit(solution)/shard_map/tef,td->efd/dot_general | solution.py:182
  1185.7 19.7 %bitcast_convert_fusion = bf16[1024,2048]{1,0:T(8,128)(2,1)} fusion(bf16[1024,16,192]{0,2,1:T(8,128)(2,1)} %get-tuple-element.90, bf16[16,192,2048]{2,1,0:T(8,128)(2,1)} %all-gather.24.cloned.1.call-done), kind=kOutput, calls=%fused_computation.24 | convolution fusion | flops 12886999040 | bytes 23068672 | tf_op jit(solution)/shard_map/tef,efd->td/dot_general | solution.py:160
  1224.5 70.4 %reduce-scatter.25.cloned.1.call-done = bf16[2,2048,192]{1,2,0:T(8,128)(2,1)} async-done(((bf16[16,2048,192]{1,2,0:T(8,128)(2,1)}), bf16[2,2048,192]{1,2,0:T(8,128)(2,1)}) %reduce-scatter.25.cloned.1.call-update) | async-done | bytes 1572880 | tf_op jit(solution)/shard_map/reduce_scatter | solution.py:186
  1298.4 92.1 %reduce-scatter.29.cloned.1.call-done = bf16[2,192,2048]{2,1,0:T(8,128)(2,1)} async-done(((bf16[16,192,2048]{2,1,0:T(8,128)(2,1)}), bf16[2,192,2048]{2,1,0:T(8,128)(2,1)}) %reduce-scatter.29.cloned.1.call-update) | async-done | bytes 1572880 | tf_op jit(solution)/shard_map/reduce_scatter | solution.py:186
  1393.9 50.9 %reduce-scatter.23.cloned.1.call-done = bf16[1024,256]{1,0:T(8,128)(2,1)} async-done(((bf16[1024,2048]{1,0:T(8,128)(2,1)}), bf16[1024,256]{1,0:T(8,128)(2,1)}) %reduce-scatter.23.cloned.1.call-update) | async-done | bytes 524304 | tf_op jit(solution)/shard_map/reduce_scatter | solution.py:283
  1446.9 52.3 %reduce-scatter.19.cloned.1.call-done = bf16[256,1024]{1,0:T(8,128)(2,1)} async-done(((bf16[2048,1024]{1,0:T(8,128)(2,1)}), bf16[256,1024]{1,0:T(8,128)(2,1)}) %reduce-scatter.19.cloned.1.call-update) | async-done | bytes 524304 | tf_op jit(solution)/shard_map/reduce_scatter | solution.py:280
  1501.3 77.0 %reduce-scatter.17.cloned.1.call-done = bf16[256,2048]{1,0:T(8,128)(2,1)} async-done(((bf16[1024,2048]{1,0:T(8,128)(2,1)}), bf16[256,2048]{1,0:T(8,128)(2,1)}) %reduce-scatter.17.cloned.1.call-update) | async-done | bytes 1048592 | tf_op jit(solution)/shard_map/reduce_scatter | solution.py:244
  1580.6 45.9 %all-reduce.9 = (f32[2048]{0:T(1024)S(1)}, f32[128]{0:T(128)S(1)}, f32[128]{0:T(128)S(1)}, f32[2048]{0:T(1024)S(1)}) all-reduce(f32[2048]{0:T(1024)S(1)} %get-tuple-element.80, f32[128]{0:T(128)S(1)} %get-tuple-element.76, f32[128]{0:T(128)S(1)} %copy-done.57, ...), channel_id=10, replica_groups=mesh['fsdp'=8,'tp'=4] {'fsdp','tp'}, use_global_device_ids=true, to_apply=%region_20.21.clone | all-reduce | flops 4352 | bytes 34816
  1628.8 30.0 %reduce-scatter.13.cloned.1.call-done = bf16[256,2048]{1,0:T(8,128)(2,1)} async-done(((bf16[1024,2048]{1,0:T(8,128)(2,1)}), bf16[256,2048]{1,0:T(8,128)(2,1)}) %reduce-scatter.13.cloned.1.call-update) | async-done | bytes 1048592 | tf_op jit(solution)/shard_map/reduce_scatter | solution.py:163
  (256 shorter events, 351.9 us)
Async XLA Ops:
  7.2 70.5 %all-gather.30.cloned.1.call-start = ((), (), s32[]{:S(2)}) async-start(), calls=%async_computation.30 | async-start | bytes 4866048 | tf_op jit(solution)/shard_map/all_gather | solution.py:78
  9.6 151.2 %all-gather.12.cloned.1.call-start = ((), (), s32[]{:S(2)}) async-start(), calls=%async_computation.11 | async-start | bytes 5242880 | tf_op jit(solution)/shard_map/all_gather | solution.py:106
  81.5 116.2 %all-gather.14.cloned.1.call-start = ((), (), s32[]{:S(2)}) async-start(), calls=%async_computation.12 | async-start | bytes 4718592 | tf_op jit(solution)/shard_map/all_gather | solution.py:94
  82.3 181.6 %all-gather.16.cloned.1.call-start = ((), (), s32[]{:S(2)}) async-start(), calls=%async_computation.13 | async-start | bytes 4718592 | tf_op jit(solution)/shard_map/all_gather | solution.py:95
  82.8 267.7 %reduce-scatter.11.cloned.1.call-start = ((), (), s32[]{:S(2)}) async-start(), calls=%async_computation.14 | async-start | bytes 5242880 | tf_op jit(solution)/shard_map/reduce_scatter | solution.py:142
  273.6 151.2 %all-gather.22.cloned.1.call-start = ((), (), s32[]{:S(2)}) async-start(), calls=%async_computation.17 | async-start | bytes 14155776 | tf_op jit(solution)/shard_map/all_gather | solution.py:97
  274.2 233.6 %all-gather.18.cloned.1.call-start = ((), (), s32[]{:S(2)}) async-start(), calls=%async_computation.15 | async-start | bytes 5242880 | tf_op jit(solution)/shard_map/all_gather | solution.py:150
  274.3 605.9 %copy-start.30 = (f32[2048]{0:T(1024)}, f32[2048]{0:T(1024)S(1)}, u32[]{:S(2)}) copy-start(f32[2048]{0:T(1024)S(1)} %reshape.326) | copy-start | bytes 24580
  352.2 528.0 %copy-start.45 = (f32[256]{0:T(256)}, f32[256]{0:T(256)S(1)}, u32[]{:S(2)}) copy-start(f32[256]{0:T(256)S(1)} %fusion.69) | copy-start | bytes 3076
  354.9 225.3 %all-gather.20.cloned.1.call-start = ((), (), s32[]{:S(2)}) async-start(), calls=%async_computation.16 | async-start | bytes 14155776 | tf_op jit(solution)/shard_map/all_gather | solution.py:96
  355.6 306.9 %all-gather.26.cloned.1.call-start = ((), (), s32[]{:S(2)}) async-start(), calls=%async_computation.20 | async-start | bytes 5242880 | tf_op jit(solution)/shard_map/all_gather | solution.py:168
  356.4 378.4 %all-gather.24.cloned.1.call-start = ((), (), s32[]{:S(2)}) async-start(), calls=%async_computation.18 | async-start | bytes 14155776 | tf_op jit(solution)/shard_map/all_gather | solution.py:98
  356.9 520.5 %reduce-scatter.15.cloned.1.call-start = ((), (), s32[]{:S(2)}) async-start(), calls=%async_computation.21 | async-start | bytes 5242880 | tf_op jit(solution)/shard_map/reduce_scatter | solution.py:191
  800.5 164.9 %all-gather.28.cloned.1.call-start = ((), (), s32[]{:S(2)}) async-start(), calls=%async_computation.22 | async-start | bytes 5242880 | tf_op jit(solution)/shard_map/all_gather | solution.py:197
  884.0 321.5 %reduce-scatter.21.cloned.1.call-start = ((), (), s32[]{:S(2)}) async-start(), calls=%async_computation.25 | async-start | bytes 2359296 | tf_op jit(solution)/shard_map/reduce_scatter | solution.py:258
  1063.7 157.2 %reduce-scatter.27.cloned.1.call-start = ((), (), s32[]{:S(2)}) async-start(), calls=%async_computation.28 | async-start | bytes 14155776 | tf_op jit(solution)/shard_map/reduce_scatter | solution.py:186
  1083.4 211.4 %reduce-scatter.25.cloned.1.call-start = ((), (), s32[]{:S(2)}) async-start(), calls=%async_computation.27 | async-start | bytes 14155776 | tf_op jit(solution)/shard_map/reduce_scatter | solution.py:186
  1102.8 287.7 %reduce-scatter.29.cloned.1.call-start = ((), (), s32[]{:S(2)}) async-start(), calls=%async_computation.29 | async-start | bytes 14155776 | tf_op jit(solution)/shard_map/reduce_scatter | solution.py:186
  1123.7 321.2 %reduce-scatter.23.cloned.1.call-start = ((), (), s32[]{:S(2)}) async-start(), calls=%async_computation.26 | async-start | bytes 4718592 | tf_op jit(solution)/shard_map/reduce_scatter | solution.py:283
  1134.2 365.0 %reduce-scatter.19.cloned.1.call-start = ((), (), s32[]{:S(2)}) async-start(), calls=%async_computation.24 | async-start | bytes 4718592 | tf_op jit(solution)/shard_map/reduce_scatter | solution.py:280
  1173.4 404.9 %reduce-scatter.17.cloned.1.call-start = ((), (), s32[]{:S(2)}) async-start(), calls=%async_computation.23 | async-start | bytes 5242880 | tf_op jit(solution)/shard_map/reduce_scatter | solution.py:244
  1185.4 473.4 %reduce-scatter.13.cloned.1.call-start = ((), (), s32[]{:S(2)}) async-start(), calls=%async_computation.19 | async-start | bytes 5242880 | tf_op jit(solution)/shard_map/reduce_scatter | solution.py:163
  1207.2 12.9 all-to-all-start
  1298.3 360.5 %copy-start.6 = (bf16[256,2048]{1,0:T(8,128)(2,1)S(1)}, bf16[256,2048]{1,0:T(8,128)(2,1)}, u32[]{:S(2)}) copy-start(bf16[256,2048]{1,0:T(8,128)(2,1)} %reduce-scatter.11.cloned.1.call-done) | copy-start | bytes 3145732
  (60 other events, 4539.4 us)
Sparse Core Ops, SparseCore 0:
  11.4 66.2 all-gather.29
  81.7 79.0 all-gather.11
  162.6 35.0 all-gather.13
  199.5 37.3 all-gather.15
  273.7 76.7 reduce-scatter.10
  352.3 72.4 all-gather.21
  427.0 80.7 all-gather.17
  509.6 70.4 all-gather.19
  581.7 80.7 all-gather.25
  664.2 70.4 all-gather.23
  800.6 76.7 reduce-scatter.14
  884.1 81.2 all-gather.27
  1063.9 39.6 reduce-scatter.20
  1106.9 92.2 reduce-scatter.26
  1202.5 92.2 reduce-scatter.24
  1298.2 92.2 reduce-scatter.28
  1393.7 51.0 reduce-scatter.22
  1448.0 51.1 reduce-scatter.18
  1501.5 76.7 reduce-scatter.16
  1580.4 78.3 reduce-scatter.12

commit v2 on v1

--- a/solution.py
+++ b/solution.py
@@ -43,6 +43,53 @@
     position = lax.iota(jnp.int32, queries.shape[0])
     allowed = (position[None, :] <= position[:, None]) | (position[None, :] < prefix_end)
     return jnp.where(allowed[None], scores, -1e30)
+
+
+def tp_gather(block, count):
+    place = lax.axis_index("tp")
+    from_left = []
+    from_right = []
+    going_right = block
+    going_left = block
+    for step in range(1, count):
+        going_right = lax.ppermute(
+            going_right, "tp", [(i, i + 1) for i in range(step - 1, count - 1)]
+        )
+        going_left = lax.ppermute(going_left, "tp", [(i + 1, i) for i in range(0, count - step)])
+        from_left.append(going_right)
+        from_right.append(going_left)
+    stacked = jnp.stack(from_left[::-1] + [block] + from_right, axis=0)
+    picked = lax.dynamic_slice_in_dim(stacked, count - 1 - place, count, 0)
+    return picked.reshape((count * block.shape[0],) + block.shape[1:])
+
+
+def tp_scatter_sum(partial, count, send_type):
+    place = lax.axis_index("tp")
+    rows = partial.shape[0] // count
+    pieces = partial.reshape((count, rows) + partial.shape[1:])
+
+    def piece(target):
+        return lax.dynamic_index_in_dim(pieces, jnp.clip(target, 0, count - 1), 0, keepdims=False)
+
+    left_sum = None
+    right_sum = None
+    for step in range(1, count):
+        outgoing = piece(place + count - step)
+        if left_sum is not None:
+            outgoing = outgoing + left_sum.astype(outgoing.dtype)
+        left_sum = lax.ppermute(
+            outgoing.astype(send_type), "tp", [(i, i + 1) for i in range(step)]
+        )
+        outgoing = piece(place - count + step)
+        if right_sum is not None:
+            outgoing = outgoing + right_sum.astype(outgoing.dtype)
+        right_sum = lax.ppermute(
+            outgoing.astype(send_type), "tp", [(i, i - 1) for i in range(count - step, count)]
+        )
+    own = piece(place)
+    if left_sum is not None:
+        own = own + left_sum.astype(own.dtype) + right_sum.astype(own.dtype)
+    return own
 
 
 def body(
@@ -102,8 +149,9 @@
     key_w = lax.dynamic_slice_in_dim(key_all, kv_head * HD, HD, 1)
     value_w = lax.dynamic_slice_in_dim(value_all, kv_head * HD, HD, 1)
     tokens_f = layer_in.astype(jnp.float32)
-    attn_in = rms_norm(tokens_f, gain_attn).astype(jnp.bfloat16)
-    attn_rows = lax.all_gather(attn_in, "tp", axis=0, tiled=True)
+    tp_size = lax.axis_size("tp")
+    layer_rows = tp_gather(layer_in, tp_size)
+    attn_rows = rms_norm(layer_rows.astype(jnp.float32), gain_attn).astype(jnp.bfloat16)
     query_raw = jnp.dot(attn_rows, query_w, preferred_element_type=jnp.float32)
     key_raw = jnp.dot(attn_rows, key_w, preferred_element_type=jnp.float32)
     value_rows = jnp.dot(attn_rows, value_w, preferred_element_type=jnp.float32).astype(
@@ -139,15 +187,12 @@
 
     context_all, log_sums = lax.map(attend, (query_seq, key_seq, value_seq, prefix_len))
     context_b = context_all.reshape(group_rows, per_dev * HD).astype(jnp.bfloat16)
-    attn_out = lax.psum_scatter(
-        jnp.dot(context_b, out_w, preferred_element_type=jnp.float32).astype(jnp.bfloat16),
-        "tp",
-        scatter_dimension=0,
-        tiled=True,
-    ).astype(jnp.float32)
+    attn_out = tp_scatter_sum(
+        jnp.dot(context_b, out_w, preferred_element_type=jnp.float32), tp_size, jnp.bfloat16
+    )
     residual = tokens_f + attn_out
     ffn_in = rms_norm(residual, gain_ffn).astype(jnp.bfloat16)
-    ffn_rows = lax.all_gather(ffn_in, "tp", axis=0, tiled=True)
+    ffn_rows = tp_gather(ffn_in, tp_size)
     expert_count = gate_w.shape[0]
     chosen = routes[:, :, None] == lax.iota(jnp.int32, expert_count)[None, None, :]
     share = jnp.sum(jnp.where(chosen, route_weights[:, :, None], 0.0), axis=1)
@@ -160,12 +205,10 @@
     mixture = jnp.einsum(
         "tef,efd->td", hidden_share, down_w, preferred_element_type=jnp.float32
     )
-    mixture_own = lax.psum_scatter(
-        mixture.astype(jnp.bfloat16), "tp", scatter_dimension=0, tiled=True
-    ).astype(jnp.float32)
+    mixture_own = tp_scatter_sum(mixture, tp_size, jnp.bfloat16)
     layer_out = (residual + mixture_own).astype(jnp.bfloat16)
     grad_out = out_grad.astype(jnp.float32)
-    grad_rows = lax.all_gather(out_grad, "tp", axis=0, tiled=True)
+    grad_rows = tp_gather(out_grad, tp_size)
     hidden_grad = (
         jnp.einsum("td,efd->tef", grad_rows, down_w, preferred_element_type=jnp.float32)
         * share[:, :, None]
@@ -188,13 +231,11 @@
         ).astype(jnp.float32)
         for part in (gate_part, up_part, down_part)
     )
-    ffn_in_own = lax.psum_scatter(
-        ffn_in_grad.astype(jnp.bfloat16), "tp", scatter_dimension=0, tiled=True
-    ).astype(jnp.float32)
+    ffn_in_own = tp_scatter_sum(ffn_in_grad, tp_size, jnp.bfloat16)
     _, second_back = jax.vjp(rms_norm, residual, gain_ffn)
     residual_norm_grad, ffn_gain_part = second_back(ffn_in_own)
     residual_grad = grad_out + residual_norm_grad
-    attn_out_grad = lax.all_gather(residual_grad.astype(jnp.bfloat16), "tp", axis=0, tiled=True)
+    attn_out_grad = tp_gather(residual_grad.astype(jnp.bfloat16), tp_size)
     output_part = jnp.einsum(
         "gq,gd->qd", context_b, attn_out_grad, preferred_element_type=jnp.float32
     )
@@ -241,15 +282,10 @@
     value_back = value_grad.reshape(group_rows, HD).astype(jnp.bfloat16)
     result = jnp.einsum("gq,dq->gd", query_back, query_w, preferred_element_type=jnp.float32)
     result = result + jnp.einsum("gk,dk->gd", key_back, key_w, preferred_element_type=jnp.float32)
-    attn_in_grad = lax.psum_scatter(
-        (
-            result
-            + jnp.einsum("gk,dk->gd", value_back, value_w, preferred_element_type=jnp.float32)
-        ).astype(jnp.bfloat16),
-        "tp",
-        scatter_dimension=0,
-        tiled=True,
-    ).astype(jnp.float32)
+    attn_in_part = result + jnp.einsum(
+        "gk,dk->gd", value_back, value_w, preferred_element_type=jnp.float32
+    )
+    attn_in_grad = tp_scatter_sum(attn_in_part, tp_size, jnp.bfloat16)
     query_part = jnp.einsum("gd,gq->dq", attn_rows, query_back, preferred_element_type=jnp.float32)
     key_head_part = jnp.einsum("gd,gk->dk", attn_rows, key_back, preferred_element_type=jnp.float32)
     value_head_part = jnp.einsum(
@@ -261,7 +297,6 @@
         scatter_dimension=0,
         tiled=True,
     )
-    tp_size = lax.axis_size("tp")
     kv_got = lax.all_to_all(
         kv_part.reshape(tp_size, kv_part.shape[0] // tp_size, 2 * HD),
         "tp",
@@ -274,7 +309,11 @@
     key_proj_grad = kv_got[:, :, :HD].transpose(1, 0, 2).reshape(sub_rows, HK * HD)
     value_proj_grad = kv_got[:, :, HD:].transpose(1, 0, 2).reshape(sub_rows, HK * HD)
     _, first_back = jax.vjp(rms_norm, tokens_f, gain_attn)
-    input_norm_grad, attn_gain_part = first_back(attn_in_grad)
+    input_norm_grad, _ = first_back(attn_in_grad)
+    _, rows_back = jax.vjp(
+        lambda weight: rms_norm(layer_rows.astype(jnp.float32), weight), gain_attn
+    )
+    (attn_gain_part,) = rows_back(attn_in_part)
     in_grad = residual_grad + input_norm_grad
     query_proj_grad, output_proj_grad = (
         lax.psum_scatter(

time: 1680 us -> 1230 us (0.73)
  waiting for transfers between devices: 1130 us -> 556 us
  starting transfers between devices: 4.97 us -> 118 us
  local copies, waits for them, and re-layouts: 26.3 us -> 56.2 us
  matrix products: 345 us -> 323 us
    ppermute x0 -> x48, waiting for transfers between devices: none -> 403 us  [the longest x12 179 us: tp_gather(): lax.ppermute(going_left, 'tp', [(i + 1, i) for i in range(0, count - step)])]
    all_gather x4 -> x0, waiting for transfers between devices: 299 us -> none  [the longest x1 82.9 us: body(): ffn_rows = lax.all_gather(ffn_in, 'tp', axis=0, tiled=True)]
    reduce_scatter x4 -> x0, waiting for transfers between devices: 260 us -> none  [the longest x1 77 us: body(): lax.psum_scatter((result + jnp.einsum('gk,dk->gd', value_back, value_w, p...]
    ppermute x0 -> x48, starting transfers between devices: none -> 113 us  [the longest x12 48.4 us: tp_scatter_sum(): lax.ppermute(outgoing.astype(send_type), 'tp', [(i, i + 1) for i in range...]
    all_gather x1, waiting for transfers between devices: 72.3 us -> 0.01 us  [body(): lax.all_gather(expert_down, 'fsdp', axis=0, tiled=True)]
    all_gather x1, waiting for transfers between devices: 67.8 us -> 0.01 us  [body(): lax.all_gather(expert_up, 'fsdp', axis=0, tiled=True)]
    all_gather x1, waiting for transfers between devices: 66 us -> 0.01 us  [body(): packed_all = lax.all_gather(packed, ('fsdp', 'tp'), axis=0, tiled=False)]
    all_gather x1, waiting for transfers between devices: 53.4 us -> 0.01 us  [body(): lax.all_gather(expert_gate, 'fsdp', axis=0, tiled=True)]
  transfers between devices with their start and end apart: 21 -> 61, of which waited for: 18 -> 29; matrix products, arithmetic and copies ran while one was open for 17% -> 26% of each run, Pallas kernels for 0% -> 0%
where the time goes in v2:
time: 1230 us
  waiting for transfers between devices  556 us (45%)
  matrix products  323 us (26%)
  starting transfers between devices  118 us (10%)
  other arithmetic  113 us (9%)
  local copies, waits for them, and re-layouts  56.2 us (5%)
  blocking collectives  43.7 us (4%)
  between operations  17.1 us (1%)
    ppermute x12, waiting for transfers between devices, tp_gather(): lax.ppermute(going_left, 'tp', [(i + 1, i) for i in range(0, count - step)])  179 us
    reduce_scatter x3, waiting for transfers between devices, body(): lax.psum_scatter(part.astype(jnp.bfloat16), 'fsdp', scatter_dimension=0,...  150 us
    ppermute x12, waiting for transfers between devices, tp_scatter_sum(): lax.ppermute(outgoing.astype(send_type), 'tp', [(i, i + 1) for i in range...  135 us
    ppermute x12, starting transfers between devices, tp_scatter_sum(): lax.ppermute(outgoing.astype(send_type), 'tp', [(i, i + 1) for i in range...  48.4 us
    ppermute x12, waiting for transfers between devices, tp_scatter_sum(): lax.ppermute(outgoing.astype(send_type), 'tp', [(i, i - 1) for i in range...  47 us
    unnamed x1, blocking collectives  43.7 us
    ppermute x12, waiting for transfers between devices, tp_gather(): lax.ppermute(going_right, 'tp', [(i, i + 1) for i in range(step - 1, coun...  42.5 us
    unnamed x2, matrix products  38.2 us
  transfers between devices with their start and end apart: 61, of which 29 were waited for; matrix products, arithmetic and copies ran while one was open for 26% of the time, Pallas kernels for 0%

profile of v2, /device:TPU:0, one launch (start us, length us, event | category | flops | bytes accessed | tf_op | source)
XLA Modules:
  0.0 1227.5 jit_solution(179499071037342525)
XLA Ops:
  18.6 21.0 %collective-permute-done = bf16[256,2048]{1,0:T(8,128)(2,1)S(1)} collective-permute-done((bf16[256,2048]{1,0:T(8,128)(2,1)S(1)}, bf16[256,2048]{1,0:T(8,128)(2,1)S(1)}, u32[]{:S(2)}, u32[]{:S(2)}) %collective-permute-start) | collective-permute-done | bytes 1048608 | tf_op jit(solution)/shard_map/ppermute | solution.py:55
  49.0 24.9 %collective-permute-done.4 = bf16[256,2048]{1,0:T(8,128)(2,1)} collective-permute-done((bf16[256,2048]{1,0:T(8,128)(2,1)S(1)}, bf16[256,2048]{1,0:T(8,128)(2,1)}, u32[]{:S(2)}, u32[]{:S(2)}) %collective-permute-start.4) | collective-permute-done | bytes 1048608 | tf_op jit(solution)/shard_map/ppermute | solution.py:58
  79.4 38.1 %collective-permute-done.5 = bf16[256,2048]{1,0:T(8,128)(2,1)S(1)} collective-permute-done((bf16[256,2048]{1,0:T(8,128)(2,1)}, bf16[256,2048]{1,0:T(8,128)(2,1)S(1)}, u32[]{:S(2)}, u32[]{:S(2)}) %collective-permute-start.5) | collective-permute-done | bytes 1048608 | tf_op jit(solution)/shard_map/ppermute | solution.py:58
  238.0 20.6 %collective-permute-done.7 = bf16[256,2048]{1,0:T(8,128)(2,1)} collective-permute-done((bf16[256,2048]{1,0:T(8,128)(2,1)}, bf16[256,2048]{1,0:T(8,128)(2,1)}, u32[]{:S(2)}, u32[]{:S(2)}) %collective-permute-start.7) | collective-permute-done | bytes 1048608 | tf_op jit(solution)/shard_map/ppermute | solution.py:80
  293.0 22.3 %collective-permute-done.11 = bf16[256,2048]{1,0:T(8,128)(2,1)} collective-permute-done((bf16[256,2048]{1,0:T(8,128)(2,1)}, bf16[256,2048]{1,0:T(8,128)(2,1)}, u32[]{:S(2)}, u32[]{:S(2)}) %collective-permute-start.11) | collective-permute-done | bytes 1048608 | tf_op jit(solution)/shard_map/ppermute | solution.py:86
  349.4 40.9 %collective-permute-done.15 = bf16[256,2048]{1,0:T(8,128)(2,1)S(1)} collective-permute-done((bf16[256,2048]{1,0:T(8,128)(2,1)S(1)}, bf16[256,2048]{1,0:T(8,128)(2,1)S(1)}, u32[]{:S(2)}, u32[]{:S(2)}) %collective-permute-start.15) | collective-permute-done | bytes 1048608 | tf_op jit(solution)/shard_map/ppermute | solution.py:58
  428.5 19.1 %fusion.105 = f32[1024,3072]{0,1} fusion(bf16[1024,2048]{1,0:T(8,128)(2,1)} %bitcast.338, bf16[2048,3072]{0,1:T(8,128)(2,1)} %bitcast.356), kind=kOutput, calls=%fused_computation.243 | convolution fusion | flops 12884901888 | bytes 29360128
  447.5 19.2 %fusion.104 = f32[1024,3072]{0,1} fusion(bf16[1024,2048]{1,0:T(8,128)(2,1)} %bitcast.339, bf16[2048,3072]{0,1:T(8,128)(2,1)} %bitcast.357), kind=kOutput, calls=%fused_computation.242 | convolution fusion | flops 12884901888 | bytes 29360128
  466.7 28.1 %multiply_convert_fusion = (bf16[1024,16,192]{0,2,1:T(8,128)(2,1)}, bf16[1024,16,192]{0,2,1:T(8,128)(2,1)}, bf16[1024,16,192]{0,2,1:T(8,128)(2,1)}) fusion(f32[1024,16]{0,1:T(8,128)S(1)} %select_reduce_fusion, f32[1024,16,192]{0,2,1:T(8,128)} %bitcast.359, f32[1024,16,192]{0,2,1:T(8,128)} %bitcast.358, bf16[1024,2048,1]{1,0,2:T(8,128)(2,1)} %bitcast.336, ...), kind=kOutput, calls=%fused_computation.16 | convolution fusion | flops 12944670720 | bytes 60882944 | tf_op jit(solution)/shard_map/td,efd->tef/dot_general | solution.py:213
  494.8 19.0 %fusion.107 = f32[1024,2048,1]{1,0,2:T(8,128)} fusion(bf16[1024,16,192]{0,2,1:T(8,128)(2,1)} %get-tuple-element.92, bf16[16,2048,192]{1,2,0:T(8,128)(2,1)} %all-gather.12.cloned.1.call-done), kind=kOutput, calls=%fused_computation.245 | convolution fusion | flops 12884901888 | bytes 27262976 | tf_op jit(solution)/shard_map/tef,edf->td/dot_general | solution.py:220
  513.8 18.3 %bitcast_add_fusion = f32[1024,2048]{1,0:T(8,128)S(1)} fusion(f32[1024,2048,1]{1,0,2:T(8,128)} %fusion.107, bf16[1024,16,192]{0,2,1:T(8,128)(2,1)} %get-tuple-element.91, bf16[16,2048,192]{1,2,0:T(8,128)(2,1)} %all-gather.14.cloned.1.call-done), kind=kOutput, calls=%fused_computation.22 | convolution fusion | flops 12886999040 | bytes 35651584 | tf_op jit(solution)/shard_map/tef,edf->td/dot_general | solution.py:222
  577.6 20.7 %collective-permute-done.32 = bf16[256,2048]{1,0:T(8,128)(2,1)S(1)} collective-permute-done((bf16[256,2048]{1,0:T(8,128)(2,1)S(1)}, bf16[256,2048]{1,0:T(8,128)(2,1)S(1)}, u32[]{:S(2)}, u32[]{:S(2)}) %collective-permute-start.32) | collective-permute-done | bytes 1048608 | tf_op jit(solution)/shard_map/ppermute | solution.py:80
  598.3 24.7 %collective-permute-done.35 = bf16[256,2048]{1,0:T(8,128)(2,1)S(1)} collective-permute-done((bf16[256,2048]{1,0:T(8,128)(2,1)S(1)}, bf16[256,2048]{1,0:T(8,128)(2,1)S(1)}, u32[]{:S(2)}, u32[]{:S(2)}) %collective-permute-start.35) | collective-permute-done | bytes 1048608 | tf_op jit(solution)/shard_map/ppermute | solution.py:86
  708.5 25.2 %fusion = (f32[8,1024]{1,0:T(8,128)S(1)}, f32[1024,1024,8]{1,0,2:T(8,128)}) fusion(f32[8,1024,1024]{1,2,0:T(8,128)} %get-tuple-element.139, f32[8,1024]{1,0:T(8,128)S(1)} %log_add_fusion, bf16[1024,128,1]{1,0,2:T(8,128)(2,1)S(1)} %copy-done.50, bf16[1024,8,128]{0,2,1:T(8,128)(2,1)S(1)} %bitcast.334), kind=kOutput, calls=%fused_computation.2 | convolution fusion | flops 2172641280 | bytes 69533696 | tf_op jit(solution)/shard_map/while/body/eval_jaxpr/qhd,kd->hqk/dot_general | solution.py:258
  733.7 28.9 %fusion.2 = bf16[8,1024,1024]{1,2,0:T(8,128)(2,1)} fusion(f32[1024,1024,8]{1,0,2:T(8,128)} %get-tuple-element.141, f32[8,1024,1024]{1,2,0:T(8,128)} %get-tuple-element.139, f32[8,1024]{1,0:T(8,128)S(1)} %get-tuple-element.140, f32[8,1024]{1,0:T(8,128)S(1)} %log_add_fusion), kind=kLoop, calls=%fused_computation.4 | loop fusion | flops 33554432 | bytes 83951616 | tf_op jit(solution)/shard_map/while/body/eval_jaxpr/convert_element_type | solution.py:263
  812.4 19.5 %convert_bitcast_fusion = bf16[16,2048,192]{1,2,0:T(8,128)(2,1)} fusion(bf16[1024,16,192]{0,2,1:T(8,128)(2,1)} %get-tuple-element.91, bf16[1024,2048,1]{1,0,2:T(8,128)(2,1)} %bitcast.340), kind=kOutput, calls=%fused_computation.14 | convolution fusion | flops 12891193344 | bytes 23068672 | tf_op jit(solution)/shard_map/td,tef->edf/dot_general | solution.py:224
  832.0 19.9 %convert_bitcast_fusion.1 = bf16[16,2048,192]{1,2,0:T(8,128)(2,1)} fusion(bf16[1024,16,192]{0,2,1:T(8,128)(2,1)} %get-tuple-element.92, bf16[1024,2048,1]{1,0,2:T(8,128)(2,1)} %bitcast.341), kind=kOutput, calls=%fused_computation.15 | convolution fusion | flops 12891193344 | bytes 23068672 | tf_op jit(solution)/shard_map/td,tef->edf/dot_general | solution.py:223
  852.2 19.3 %convolution_convert_fusion = bf16[16,192,2048]{2,1,0:T(8,128)(2,1)} fusion(bf16[1024,16,192]{0,2,1:T(8,128)(2,1)} %get-tuple-element.93, bf16[1024,2048,1]{1,0,2:T(8,128)(2,1)} %bitcast.337), kind=kOutput, calls=%fused_computation.29 | convolution fusion | flops 12891193344 | bytes 23068672 | tf_op jit(solution)/shard_map/tef,td->efd/dot_general | solution.py:225
  890.0 18.8 %fusion.106 = f32[1024,2048,1]{1,0,2:T(8,128)S(1)} fusion(bf16[1024,16,192]{0,2,1:T(8,128)(2,1)} %get-tuple-element.93, bf16[16,192,2048]{2,1,0:T(8,128)(2,1)} %all-gather.16.cloned.1.call-done), kind=kOutput, calls=%fused_computation.244 | convolution fusion | flops 12884901888 | bytes 27262976 | tf_op jit(solution)/shard_map/tef,efd->td/dot_general | solution.py:205
  932.4 17.6 %collective-permute-done.43 = bf16[256,2048]{1,0:T(8,128)(2,1)S(1)} collective-permute-done((bf16[256,2048]{1,0:T(8,128)(2,1)S(1)}, bf16[256,2048]{1,0:T(8,128)(2,1)S(1)}, u32[]{:S(2)}, u32[]{:S(2)}) %collective-permute-start.43) | collective-permute-done | bytes 1048608 | tf_op jit(solution)/shard_map/ppermute | solution.py:80
  952.4 20.1 %collective-permute-done.19 = bf16[256,2048]{1,0:T(8,128)(2,1)S(1)} collective-permute-done((bf16[256,2048]{1,0:T(8,128)(2,1)S(1)}, bf16[256,2048]{1,0:T(8,128)(2,1)S(1)}, u32[]{:S(2)}, u32[]{:S(2)}) %collective-permute-start.19) | collective-permute-done | bytes 1048608 | tf_op jit(solution)/shard_map/ppermute | solution.py:80
  998.8 43.7 %all-reduce.9 = (f32[2048]{0:T(1024)S(1)}, f32[128]{0:T(128)S(1)}, f32[128]{0:T(128)S(1)}, f32[2048]{0:T(1024)S(1)}) all-reduce(f32[2048]{0:T(1024)S(1)} %get-tuple-element.142, f32[128]{0:T(128)S(1)} %copy-done.81, f32[128]{0:T(128)S(1)} %copy-done.78, f32[2048]{0:T(1024)S(1)} %copy-done.69), channel_id=6, replica_groups=mesh['fsdp'=8,'tp'=4] {'fsdp','tp'}, use_global_device_ids=true, to_apply=%region_17.18.clone | all-reduce | flops 4352 | bytes 34816
  1063.5 57.9 %reduce-scatter.13.cloned.1.call-done = bf16[2,2048,192]{1,2,0:T(8,128)(2,1)} async-done(((bf16[16,2048,192]{1,2,0:T(8,128)(2,1)}), bf16[2,2048,192]{1,2,0:T(8,128)(2,1)}) %reduce-scatter.13.cloned.1.call-update) | async-done | bytes 1572880 | tf_op jit(solution)/shard_map/reduce_scatter | solution.py:229
  1124.8 92.2 %reduce-scatter.17.cloned.1.call-done = bf16[2,192,2048]{2,1,0:T(8,128)(2,1)} async-done(((bf16[16,192,2048]{2,1,0:T(8,128)(2,1)}), bf16[2,192,2048]{2,1,0:T(8,128)(2,1)}) %reduce-scatter.17.cloned.1.call-update) | async-done | bytes 1572880 | tf_op jit(solution)/shard_map/reduce_scatter | solution.py:229
  (425 shorter events, 530.4 us)
Async XLA Ops:
  7.2 114.4 %all-gather.8.cloned.1.call-start = ((), (), s32[]{:S(2)}) async-start(), calls=%async_computation.7 | async-start | bytes 4718592 | tf_op jit(solution)/shard_map/all_gather | solution.py:141
  7.9 120.4 %all-gather.18.cloned.1.call-start = ((), (), s32[]{:S(2)}) async-start(), calls=%async_computation.18 | async-start | bytes 4866048 | tf_op jit(solution)/shard_map/all_gather | solution.py:125
  10.3 188.0 %all-gather.10.cloned.1.call-start = ((), (), s32[]{:S(2)}) async-start(), calls=%async_computation.8 | async-start | bytes 4718592 | tf_op jit(solution)/shard_map/all_gather | solution.py:142
  11.1 417.4 %all-gather.14.cloned.1.call-start = ((), (), s32[]{:S(2)}) async-start(), calls=%async_computation.10 | async-start | bytes 14155776 | tf_op jit(solution)/shard_map/all_gather | solution.py:144
  11.6 435.9 %all-gather.12.cloned.1.call-start = ((), (), s32[]{:S(2)}) async-start(), calls=%async_computation.9 | async-start | bytes 14155776 | tf_op jit(solution)/shard_map/all_gather | solution.py:143
  12.2 454.4 %all-gather.16.cloned.1.call-start = ((), (), s32[]{:S(2)}) async-start(), calls=%async_computation.11 | async-start | bytes 14155776 | tf_op jit(solution)/shard_map/all_gather | solution.py:145
  46.9 942.4 %reduce-scatter.9.cloned.1.call-start = ((), (), s32[]{:S(2)}) async-start(), calls=%async_computation.13 | async-start | bytes 2359296 | tf_op jit(solution)/shard_map/reduce_scatter | solution.py:294
  287.9 50.0 %collective-permute-start.28 = (bf16[256,2048]{1,0:T(8,128)(2,1)}, bf16[256,2048]{1,0:T(8,128)(2,1)}, u32[]{:S(2)}, u32[]{:S(2)}) collective-permute-start(bf16[256,2048]{1,0:T(8,128)(2,1)} %collective-permute-done.27), channel_id=1, source_target_pairs={{1,0},{2,1},{5,4},{6,5},{9,8},{10,9},{13,12},{14,13},{17,16},{18,1... | collective-permute-start | bytes 3145736 | tf_op jit(solution)/shard_map/ppermute | solution.py:58
  289.2 50.0 %collective-permute-start.26 = (bf16[256,2048]{1,0:T(8,128)(2,1)}, bf16[256,2048]{1,0:T(8,128)(2,1)}, u32[]{:S(2)}, u32[]{:S(2)}) collective-permute-start(bf16[256,2048]{1,0:T(8,128)(2,1)} %collective-permute-done.25), channel_id=1, source_target_pairs={{2,3},{6,7},{10,11},{14,15},{18,19},{22,23},{26,27},{30,31}} | collective-permute-start | bytes 3145736 | tf_op jit(solution)/shard_map/ppermute | solution.py:55
  337.9 55.7 %collective-permute-start.29 = (bf16[256,2048]{1,0:T(8,128)(2,1)}, bf16[256,2048]{1,0:T(8,128)(2,1)S(1)}, u32[]{:S(2)}, u32[]{:S(2)}) collective-permute-start(bf16[256,2048]{1,0:T(8,128)(2,1)} %collective-permute-done.28), channel_id=1, source_target_pairs={{1,0},{5,4},{9,8},{13,12},{17,16},{21,20},{25,24},{29,28}} | collective-permute-start | bytes 3145736 | tf_op jit(solution)/shard_map/ppermute | solution.py:58
  342.1 48.1 %collective-permute-start.15 = (bf16[256,2048]{1,0:T(8,128)(2,1)S(1)}, bf16[256,2048]{1,0:T(8,128)(2,1)S(1)}, u32[]{:S(2)}, u32[]{:S(2)}) collective-permute-start(bf16[256,2048]{1,0:T(8,128)(2,1)S(1)} %multiply_convert_fusion.6), channel_id=1, source_target_pairs={{1,0},{2,1},{3,2},{5,4},{6,5},{7,6},{9,8},{10,9},{11,10},{13,12},{... | collective-permute-start | bytes 3145736 | tf_op jit(solution)/shard_map/ppermute | solution.py:58
  345.9 45.6 %collective-permute-start.13 = (bf16[256,2048]{1,0:T(8,128)(2,1)S(1)}, bf16[256,2048]{1,0:T(8,128)(2,1)S(1)}, u32[]{:S(2)}, u32[]{:S(2)}) collective-permute-start(bf16[256,2048]{1,0:T(8,128)(2,1)S(1)} %collective-permute-done.12), channel_id=1, source_target_pairs={{1,2},{2,3},{5,6},{6,7},{9,10},{10,11},{13,14},{14,15},{17,18},{18... | collective-permute-start | bytes 3145736 | tf_op jit(solution)/shard_map/ppermute | solution.py:55
  576.3 46.8 %collective-permute-start.35 = (bf16[256,2048]{1,0:T(8,128)(2,1)S(1)}, bf16[256,2048]{1,0:T(8,128)(2,1)S(1)}, u32[]{:S(2)}, u32[]{:S(2)}) collective-permute-start(bf16[256,2048]{1,0:T(8,128)(2,1)S(1)} %fusion.25), channel_id=1, source_target_pairs={{1,0},{2,1},{3,2},{5,4},{6,5},{7,6},{9,8},{10,9},{11,10},{13,12},{... | collective-permute-start | bytes 3145736 | tf_op jit(solution)/shard_map/ppermute | solution.py:86
  780.2 275.5 %reduce-scatter.11.cloned.1.call-start = ((), (), s32[]{:S(2)}) async-start(), calls=%async_computation.14 | async-start | bytes 4718592 | tf_op jit(solution)/shard_map/reduce_scatter | solution.py:322
  789.2 268.6 %reduce-scatter.7.cloned.1.call-start = ((), (), s32[]{:S(2)}) async-start(), calls=%async_computation.12 | async-start | bytes 4718592 | tf_op jit(solution)/shard_map/reduce_scatter | solution.py:319
  812.2 247.9 %reduce-scatter.15.cloned.1.call-start = ((), (), s32[]{:S(2)}) async-start(), calls=%async_computation.16 | async-start | bytes 14155776 | tf_op jit(solution)/shard_map/reduce_scatter | solution.py:229
  831.9 289.4 %reduce-scatter.13.cloned.1.call-start = ((), (), s32[]{:S(2)}) async-start(), calls=%async_computation.15 | async-start | bytes 14155776 | tf_op jit(solution)/shard_map/reduce_scatter | solution.py:229
  851.9 365.1 %reduce-scatter.17.cloned.1.call-start = ((), (), s32[]{:S(2)}) async-start(), calls=%async_computation.17 | async-start | bytes 14155776 | tf_op jit(solution)/shard_map/reduce_scatter | solution.py:229
  927.9 44.6 %collective-permute-start.19 = (bf16[256,2048]{1,0:T(8,128)(2,1)S(1)}, bf16[256,2048]{1,0:T(8,128)(2,1)S(1)}, u32[]{:S(2)}, u32[]{:S(2)}) collective-permute-start(bf16[256,2048]{1,0:T(8,128)(2,1)S(1)} %fusion.31), channel_id=1, source_target_pairs={{0,1},{1,2},{4,5},{5,6},{8,9},{9,10},{12,13},{13,14},{16,17},{17,1... | collective-permute-start | bytes 3145736 | tf_op jit(solution)/shard_map/ppermute | solution.py:80
  974.9 70.6 %collective-permute-start.44 = (bf16[256,2048]{1,0:T(8,128)(2,1)}, bf16[256,2048]{1,0:T(8,128)(2,1)}, u32[]{:S(2)}, u32[]{:S(2)}) collective-permute-start(bf16[256,2048]{1,0:T(8,128)(2,1)} %get-tuple-element.94), channel_id=1, source_target_pairs={{0,1},{1,2},{2,3},{4,5},{5,6},{6,7},{8,9},{9,10},{10,11},{12,13},{... | collective-permute-start | bytes 3145736 | tf_op jit(solution)/shard_map/ppermute | solution.py:80
  982.3 63.3 %collective-permute-start.47 = (bf16[256,2048]{1,0:T(8,128)(2,1)}, bf16[256,2048]{1,0:T(8,128)(2,1)}, u32[]{:S(2)}, u32[]{:S(2)}) collective-permute-start(bf16[256,2048]{1,0:T(8,128)(2,1)} %fusion.19), channel_id=1, source_target_pairs={{1,0},{2,1},{3,2},{5,4},{6,5},{7,6},{9,8},{10,9},{11,10},{13,12},{... | collective-permute-start | bytes 3145736 | tf_op jit(solution)/shard_map/ppermute | solution.py:86
  983.7 66.3 %collective-permute-start.20 = (bf16[256,2048]{1,0:T(8,128)(2,1)}, bf16[256,2048]{1,0:T(8,128)(2,1)}, u32[]{:S(2)}, u32[]{:S(2)}) collective-permute-start(bf16[256,2048]{1,0:T(8,128)(2,1)} %get-tuple-element.102), channel_id=1, source_target_pairs={{0,1},{1,2},{2,3},{4,5},{5,6},{6,7},{8,9},{9,10},{10,11},{12,13},{... | collective-permute-start | bytes 3145736 | tf_op jit(solution)/shard_map/ppermute | solution.py:80
  991.0 53.8 %all-to-all-start = ((f32[4,64,256]{2,1,0:T(8,128)}), f32[4,64,256]{2,1,0:T(8,128)S(1)}, u32[]{:S(2)}, u32[]{:S(2)}) async-start(f32[4,64,256]{2,1,0:T(8,128)} %bitcast.351), calls=%async_computation.2 | async-start | bytes 524288 | tf_op jit(solution)/shard_map/all_to_all | solution.py:300
  997.4 52.6 %collective-permute-start.23 = (bf16[256,2048]{1,0:T(8,128)(2,1)}, bf16[256,2048]{1,0:T(8,128)(2,1)}, u32[]{:S(2)}, u32[]{:S(2)}) collective-permute-start(bf16[256,2048]{1,0:T(8,128)(2,1)} %fusion.30), channel_id=1, source_target_pairs={{1,0},{2,1},{3,2},{5,4},{6,5},{7,6},{9,8},{10,9},{11,10},{13,12},{... | collective-permute-start | bytes 3145736 | tf_op jit(solution)/shard_map/ppermute | solution.py:86
  (124 other events, 3417.0 us)
Sparse Core Ops, SparseCore 0:
  9.9 39.2 all-gather.7
  52.6 65.2 all-gather.17
  119.8 36.0 all-gather.9
  157.7 71.9 all-gather.13
  231.4 71.9 all-gather.11
  305.2 71.9 all-gather.15
  780.3 39.8 reduce-scatter.8
  823.5 51.0 reduce-scatter.10
  878.0 51.1 reduce-scatter.6
  932.6 92.9 reduce-scatter.14
  1029.1 92.2 reduce-scatter.12
  1124.7 92.2 reduce-scatter.16

commit v3 on v2

--- a/solution.py
+++ b/solution.py
@@ -137,6 +137,7 @@
     gain_query = gain_query.astype(jnp.float32)
     gain_key = gain_key.astype(jnp.float32)
     gain_ffn = gain_ffn.astype(jnp.float32)
+    packed_all, query_proj = lax.optimization_barrier((packed_all, query_proj))
     query_w, out_w, gate_w, up_w, down_w = (
         lax.all_gather(query_proj, "fsdp", axis=0, tiled=True),
         lax.all_gather(output_proj, "fsdp", axis=1, tiled=True),
@@ -152,6 +153,8 @@
     tp_size = lax.axis_size("tp")
     layer_rows = tp_gather(layer_in, tp_size)
     attn_rows = rms_norm(layer_rows.astype(jnp.float32), gain_attn).astype(jnp.bfloat16)
+    out_grad, attn_rows = lax.optimization_barrier((out_grad, attn_rows))
+    grad_rows = tp_gather(out_grad, tp_size)
     query_raw = jnp.dot(attn_rows, query_w, preferred_element_type=jnp.float32)
     key_raw = jnp.dot(attn_rows, key_w, preferred_element_type=jnp.float32)
     value_rows = jnp.dot(attn_rows, value_w, preferred_element_type=jnp.float32).astype(
@@ -187,6 +190,7 @@
 
     context_all, log_sums = lax.map(attend, (query_seq, key_seq, value_seq, prefix_len))
     context_b = context_all.reshape(group_rows, per_dev * HD).astype(jnp.bfloat16)
+    context_b, grad_rows = lax.optimization_barrier((context_b, grad_rows))
     attn_out = tp_scatter_sum(
         jnp.dot(context_b, out_w, preferred_element_type=jnp.float32), tp_size, jnp.bfloat16
     )
@@ -206,9 +210,7 @@
         "tef,efd->td", hidden_share, down_w, preferred_element_type=jnp.float32
     )
     mixture_own = tp_scatter_sum(mixture, tp_size, jnp.bfloat16)
-    layer_out = (residual + mixture_own).astype(jnp.bfloat16)
     grad_out = out_grad.astype(jnp.float32)
-    grad_rows = tp_gather(out_grad, tp_size)
     hidden_grad = (
         jnp.einsum("td,efd->tef", grad_rows, down_w, preferred_element_type=jnp.float32)
         * share[:, :, None]
@@ -225,16 +227,20 @@
     down_part = jnp.einsum(
         "tef,td->efd", hidden_share, grad_rows, preferred_element_type=jnp.float32
     )
+    ffn_in_own = tp_scatter_sum(ffn_in_grad, tp_size, jnp.bfloat16)
+    _, second_back = jax.vjp(rms_norm, residual, gain_ffn)
+    residual_norm_grad, ffn_gain_part = second_back(ffn_in_own)
+    residual_grad = grad_out + residual_norm_grad
+    residual_grad, mixture_own, gate_part, up_part, down_part = lax.optimization_barrier(
+        (residual_grad, mixture_own, gate_part, up_part, down_part)
+    )
     gate_grad, up_grad, down_grad = (
         lax.psum_scatter(
             part.astype(jnp.bfloat16), "fsdp", scatter_dimension=0, tiled=True
         ).astype(jnp.float32)
         for part in (gate_part, up_part, down_part)
     )
-    ffn_in_own = tp_scatter_sum(ffn_in_grad, tp_size, jnp.bfloat16)
-    _, second_back = jax.vjp(rms_norm, residual, gain_ffn)
-    residual_norm_grad, ffn_gain_part = second_back(ffn_in_own)
-    residual_grad = grad_out + residual_norm_grad
+    layer_out = (residual + mixture_own).astype(jnp.bfloat16)
     attn_out_grad = tp_gather(residual_grad.astype(jnp.bfloat16), tp_size)
     output_part = jnp.einsum(
         "gq,gd->qd", context_b, attn_out_grad, preferred_element_type=jnp.float32
@@ -291,23 +297,6 @@
     value_head_part = jnp.einsum(
         "gd,gk->dk", attn_rows, value_back, preferred_element_type=jnp.float32
     )
-    kv_part = lax.psum_scatter(
-        jnp.concatenate([key_head_part, value_head_part], axis=1),
-        "fsdp",
-        scatter_dimension=0,
-        tiled=True,
-    )
-    kv_got = lax.all_to_all(
-        kv_part.reshape(tp_size, kv_part.shape[0] // tp_size, 2 * HD),
-        "tp",
-        split_axis=0,
-        concat_axis=0,
-        tiled=True,
-    )
-    sub_rows = kv_part.shape[0] // tp_size
-    kv_got = jnp.sum(kv_got.reshape(HK, tp_size // HK, sub_rows, 2 * HD), axis=1)
-    key_proj_grad = kv_got[:, :, :HD].transpose(1, 0, 2).reshape(sub_rows, HK * HD)
-    value_proj_grad = kv_got[:, :, HD:].transpose(1, 0, 2).reshape(sub_rows, HK * HD)
     _, first_back = jax.vjp(rms_norm, tokens_f, gain_attn)
     input_norm_grad, _ = first_back(attn_in_grad)
     _, rows_back = jax.vjp(
@@ -323,12 +312,52 @@
             output_part.astype(jnp.bfloat16), "fsdp", scatter_dimension=1, tiled=True
         ).astype(jnp.float32),
     )
-    attn_gain_grad, query_gain_grad, key_gain_grad, ffn_gain_grad = (
-        lax.psum_scatter(attn_gain_part, ("fsdp", "tp"), scatter_dimension=0, tiled=True),
-        lax.psum_scatter(query_gain_part, ("fsdp", "tp"), scatter_dimension=0, tiled=True),
-        lax.psum_scatter(key_gain_part, ("fsdp", "tp"), scatter_dimension=0, tiled=True),
-        lax.psum_scatter(ffn_gain_part, ("fsdp", "tp"), scatter_dimension=0, tiled=True),
-    )
+    fsdp_size = lax.axis_size("fsdp")
+    device_count = fsdp_size * tp_size
+    gain_parts = (attn_gain_part, query_gain_part, key_gain_part, ffn_gain_part)
+    gain_table = jnp.concatenate(
+        [part.reshape(device_count, -1) for part in gain_parts], axis=1
+    )
+    gain_width = gain_table.shape[1]
+    kv_full = jnp.concatenate([key_head_part, value_head_part], axis=1)
+    block_rows = kv_full.shape[0] // fsdp_size
+    sub_rows = block_rows // tp_size
+    gain_rows = -(-(tp_size * gain_width) // (8 * 2 * HD)) * 8
+    gain_block = jnp.pad(
+        gain_table.reshape(fsdp_size, tp_size * gain_width),
+        ((0, 0), (0, gain_rows * 2 * HD - tp_size * gain_width)),
+    ).reshape(fsdp_size, gain_rows, 2 * HD)
+    combined = jnp.concatenate(
+        [kv_full.reshape(fsdp_size, block_rows, 2 * HD), gain_block], axis=1
+    ).reshape(fsdp_size * (block_rows + gain_rows), 2 * HD)
+    summed = lax.psum_scatter(combined, "fsdp", scatter_dimension=0, tiled=True)
+    summed = jnp.concatenate(
+        [
+            summed[:block_rows].reshape(-1),
+            summed[block_rows:].reshape(-1)[: tp_size * gain_width],
+        ]
+    )
+    kv_local = summed[: block_rows * 2 * HD].reshape(tp_size, sub_rows * 2 * HD)
+    gain_local = summed[block_rows * 2 * HD :].reshape(tp_size, gain_width)
+    got = lax.all_to_all(
+        jnp.concatenate([kv_local, gain_local], axis=1),
+        "tp",
+        split_axis=0,
+        concat_axis=0,
+        tiled=True,
+    )
+    kv_got = got[:, : sub_rows * 2 * HD].reshape(tp_size, sub_rows, 2 * HD)
+    kv_got = jnp.sum(kv_got.reshape(HK, tp_size // HK, sub_rows, 2 * HD), axis=1)
+    key_proj_grad = kv_got[:, :, :HD].transpose(1, 0, 2).reshape(sub_rows, HK * HD)
+    value_proj_grad = kv_got[:, :, HD:].transpose(1, 0, 2).reshape(sub_rows, HK * HD)
+    gain_sum = jnp.sum(got[:, sub_rows * 2 * HD :], axis=0)
+    gain_grads = []
+    offset = 0
+    for part in gain_parts:
+        size = part.shape[0] // device_count
+        gain_grads.append(gain_sum[offset : offset + size])
+        offset += size
+    attn_gain_grad, query_gain_grad, key_gain_grad, ffn_gain_grad = gain_grads
     return (
         layer_out,
         in_grad,

time: 1230 us -> 1460 us (1.19)
  waiting for transfers between devices: 556 us -> 727 us
  other arithmetic: 113 us -> 173 us
  blocking collectives: 43.7 us -> 0 us
  starting transfers between devices: 118 us -> 137 us
  local copies, waits for them, and re-layouts: 56.2 us -> 72.9 us
    reduce_scatter x3, waiting for transfers between devices: 150 us -> 278 us  [body(): lax.psum_scatter(part.astype(jnp.bfloat16), 'fsdp', scatter_dimension=0,...]
    all_gather x1, waiting for transfers between devices: 0.01 us -> 68 us  [body(): packed_all = lax.all_gather(packed, ('fsdp', 'tp'), axis=0, tiled=False)]
    unnamed x1 -> x0, blocking collectives: 43.7 us -> none
    ppermute x12, waiting for transfers between devices: 135 us -> 103 us  [tp_scatter_sum(): lax.ppermute(outgoing.astype(send_type), 'tp', [(i, i + 1) for i in range...]
    ppermute x12, waiting for transfers between devices: 179 us -> 153 us  [tp_gather(): lax.ppermute(going_left, 'tp', [(i + 1, i) for i in range(0, count - step)])]
    convert_element_type x0 -> x2, other arithmetic: none -> 23.1 us  [the longest x1 20.2 us: body(): (hidden.astype(jnp.float32) * share[:, :, None]).astype(jnp.bfloat16)]
    reduce_scatter x1, waiting for transfers between devices: 0.01 us -> 22.5 us  [body(): lax.psum_scatter(query_part.astype(jnp.bfloat16), 'fsdp', scatter_dimensi...]
    ppermute x12, waiting for transfers between devices: 42.5 us -> 61.9 us  [tp_gather(): lax.ppermute(going_right, 'tp', [(i, i + 1) for i in range(step - 1, coun...]
  transfers between devices with their start and end apart: 61 -> 61, of which waited for: 29 -> 29; matrix products, arithmetic and copies ran while one was open for 26% -> 22% of each run, Pallas kernels for 0% -> 0%
where the time goes in v3:
time: 1460 us
  waiting for transfers between devices  727 us (50%)
  matrix products  329 us (23%)
  other arithmetic  173 us (12%)
  starting transfers between devices  137 us (9%)
  local copies, waits for them, and re-layouts  72.9 us (5%)
  between operations  16.9 us (1%)
    reduce_scatter x3, waiting for transfers between devices, body(): lax.psum_scatter(part.astype(jnp.bfloat16), 'fsdp', scatter_dimension=0,...  278 us
    ppermute x12, waiting for transfers between devices, tp_gather(): lax.ppermute(going_left, 'tp', [(i + 1, i) for i in range(0, count - step)])  153 us
    ppermute x12, waiting for transfers between devices, tp_scatter_sum(): lax.ppermute(outgoing.astype(send_type), 'tp', [(i, i + 1) for i in range...  103 us
    all_gather x1, waiting for transfers between devices, body(): packed_all = lax.all_gather(packed, ('fsdp', 'tp'), axis=0, tiled=False)  68 us
    ppermute x12, waiting for transfers between devices, tp_gather(): lax.ppermute(going_right, 'tp', [(i, i + 1) for i in range(step - 1, coun...  61.9 us
    ppermute x12, starting transfers between devices, tp_scatter_sum(): lax.ppermute(outgoing.astype(send_type), 'tp', [(i, i + 1) for i in range...  46.1 us
    ppermute x12, starting transfers between devices, tp_gather(): lax.ppermute(going_right, 'tp', [(i, i + 1) for i in range(step - 1, coun...  41.5 us
    unnamed x2, matrix products  38.4 us
  transfers between devices with their start and end apart: 61, of which 29 were waited for; matrix products, arithmetic and copies ran while one was open for 22% of the time, Pallas kernels for 0%

profile of v3, /device:TPU:0, one launch (start us, length us, event | category | flops | bytes accessed | tf_op | source)
XLA Modules:
  0.0 1455.4 jit_solution(1170301718475687400)
XLA Ops:
  9.7 68.0 %all-gather.18.cloned.1.call-done = bf16[2304,1024]{1,0:T(8,128)(2,1)} async-done(((bf16[72,1024]{1,0:T(8,128)(2,1)}), bf16[2304,1024]{1,0:T(8,128)(2,1)}) %all-gather.18.cloned.1.call-update) | async-done | bytes 4718608 | tf_op jit(solution)/shard_map/all_gather | solution.py:125
  84.4 21.4 %collective-permute-done = bf16[256,2048]{1,0:T(8,128)(2,1)S(1)} collective-permute-done((bf16[256,2048]{1,0:T(8,128)(2,1)S(1)}, bf16[256,2048]{1,0:T(8,128)(2,1)S(1)}, u32[]{:S(2)}, u32[]{:S(2)}) %collective-permute-start) | collective-permute-done | bytes 1048608 | tf_op jit(solution)/shard_map/ppermute | solution.py:55
  112.9 23.6 %collective-permute-done.4 = bf16[256,2048]{1,0:T(8,128)(2,1)} collective-permute-done((bf16[256,2048]{1,0:T(8,128)(2,1)S(1)}, bf16[256,2048]{1,0:T(8,128)(2,1)}, u32[]{:S(2)}, u32[]{:S(2)}) %collective-permute-start.4) | collective-permute-done | bytes 1048608 | tf_op jit(solution)/shard_map/ppermute | solution.py:58
  142.2 20.2 %collective-permute-done.5 = bf16[256,2048]{1,0:T(8,128)(2,1)S(1)} collective-permute-done((bf16[256,2048]{1,0:T(8,128)(2,1)}, bf16[256,2048]{1,0:T(8,128)(2,1)S(1)}, u32[]{:S(2)}, u32[]{:S(2)}) %collective-permute-start.5) | collective-permute-done | bytes 1048608 | tf_op jit(solution)/shard_map/ppermute | solution.py:58
  409.0 21.4 %collective-permute-done.17 = bf16[256,2048]{1,0:T(8,128)(2,1)} collective-permute-done((bf16[256,2048]{1,0:T(8,128)(2,1)S(1)}, bf16[256,2048]{1,0:T(8,128)(2,1)}, u32[]{:S(2)}, u32[]{:S(2)}) %collective-permute-start.17) | collective-permute-done | bytes 1048608 | tf_op jit(solution)/shard_map/ppermute | solution.py:86
  463.6 19.1 %fusion.13 = f32[1024,16,192]{0,2,1:T(8,128)} fusion(bf16[16,192,2048]{2,1,0:T(8,128)(2,1)} %all-gather.12.cloned.1.call-done, bf16[1024,2048]{1,0:T(8,128)(2,1)} %bitcast.354), kind=kOutput, calls=%fused_computation.32 | convolution fusion | flops 12884901888 | bytes 29360128 | tf_op jit(solution)/shard_map/td,efd->tef/dot_general | solution.py:215
  488.9 22.2 %collective-permute-done.23 = bf16[256,2048]{1,0:T(8,128)(2,1)S(1)} collective-permute-done((bf16[256,2048]{1,0:T(8,128)(2,1)}, bf16[256,2048]{1,0:T(8,128)(2,1)S(1)}, u32[]{:S(2)}, u32[]{:S(2)}) %collective-permute-start.23) | collective-permute-done | bytes 1048608 | tf_op jit(solution)/shard_map/ppermute | solution.py:58
  513.6 19.1 %fusion.103 = f32[1024,3072]{0,1} fusion(bf16[1024,2048]{1,0:T(8,128)(2,1)} %bitcast.356, bf16[2048,3072]{0,1:T(8,128)(2,1)} %bitcast.378), kind=kOutput, calls=%fused_computation.249 | convolution fusion | flops 12884901888 | bytes 29360128
  532.6 19.4 %fusion.102 = f32[1024,3072]{0,1} fusion(bf16[1024,2048]{1,0:T(8,128)(2,1)} %bitcast.357, bf16[2048,3072]{0,1:T(8,128)(2,1)} %bitcast.379), kind=kOutput, calls=%fused_computation.248 | convolution fusion | flops 12884901888 | bytes 29360128
  552.0 20.2 %multiply_convert_fusion = (bf16[1024,16,192]{0,2,1:T(8,128)(2,1)}, bf16[1024,16,192]{0,2,1:T(8,128)(2,1)}, bf16[1024,16,192]{0,2,1:T(8,128)(2,1)}) fusion(f32[1024,16,192]{0,2,1:T(8,128)} %bitcast.345, f32[1024,16]{0,1:T(8,128)S(1)} %select_reduce_fusion, f32[1024,16,192]{0,2,1:T(8,128)} %bitcast.344, f32[1024,16,192]{0,2,1:T(8,128)S(1)} %bitcast.343), kind=kLoop, calls=%fused_computation.14 | loop fusion | flops 59768832 | bytes 56688640 | tf_op jit(solution)/shard_map/convert_element_type | solution.py:208
  572.2 19.3 %fusion.104 = f32[1024,2048,1]{1,0,2:T(8,128)} fusion(bf16[1024,16,192]{0,2,1:T(8,128)(2,1)} %get-tuple-element.108, bf16[16,2048,192]{1,2,0:T(8,128)(2,1)} %all-gather.16.cloned.1.call-done), kind=kOutput, calls=%fused_computation.250 | convolution fusion | flops 12884901888 | bytes 27262976 | tf_op jit(solution)/shard_map/tef,edf->td/dot_general | solution.py:222
  610.8 17.6 %fusion.105 = f32[1024,2048,1]{1,0,2:T(8,128)S(1)} fusion(bf16[1024,16,192]{0,2,1:T(8,128)(2,1)} %get-tuple-element.107, bf16[16,192,2048]{2,1,0:T(8,128)(2,1)} %all-gather.12.cloned.1.call-done), kind=kOutput, calls=%fused_computation.251 | convolution fusion | flops 12884901888 | bytes 27262976 | tf_op jit(solution)/shard_map/tef,efd->td/dot_general | solution.py:209
  636.0 18.0 %fusion.11 = bf16[16,192,2048]{2,1,0:T(8,128)(2,1)} fusion(bf16[1024,16,192]{0,2,1:T(8,128)(2,1)S(1)} %bitcast.353, bf16[1024,2048]{1,0:T(8,128)(2,1)} %bitcast.355), kind=kOutput, calls=%fused_computation.30 | convolution fusion | flops 12884901888 | bytes 23068672 | tf_op jit(solution)/shard_map/tef,td->efd/dot_general | solution.py:227
  715.6 18.3 %convolution_bitcast_fusion = bf16[16,2048,192]{1,2,0:T(8,128)(2,1)} fusion(bf16[1024,16,192]{0,2,1:T(8,128)(2,1)} %get-tuple-element.109, bf16[1024,2048,1]{1,0,2:T(8,128)(2,1)S(1)} %bitcast.359), kind=kOutput, calls=%fused_computation.20 | convolution fusion | flops 12884901888 | bytes 23068672 | tf_op jit(solution)/shard_map/td,tef->edf/dot_general | solution.py:226
  761.5 18.1 %collective-permute-start.36 = (bf16[256,2048]{1,0:T(8,128)(2,1)S(1)}, bf16[256,2048]{1,0:T(8,128)(2,1)S(1)}, u32[]{:S(2)}, u32[]{:S(2)}) collective-permute-start(bf16[256,2048]{1,0:T(8,128)(2,1)S(1)} %convert_element_type.430), channel_id=1, source_target_pairs={{0,1},{1,2},{2,3},{4,5},{5,6},{6,7},{8,9},{9,10},{10,11},{12,13},{... | collective-permute-start | bytes 3145736 | tf_op jit(solution)/shard_map/ppermute | solution.py:55
  808.3 23.1 %collective-permute-done.40 = bf16[256,2048]{1,0:T(8,128)(2,1)} collective-permute-done((bf16[256,2048]{1,0:T(8,128)(2,1)S(1)}, bf16[256,2048]{1,0:T(8,128)(2,1)}, u32[]{:S(2)}, u32[]{:S(2)}) %collective-permute-start.40) | collective-permute-done | bytes 1048608 | tf_op jit(solution)/shard_map/ppermute | solution.py:58
  872.0 25.1 %fusion = (f32[8,1024]{1,0:T(8,128)S(1)}, f32[1024,1024,8]{1,0,2:T(8,128)}) fusion(f32[8,1024,1024]{1,2,0:T(8,128)} %get-tuple-element.155, f32[8,1024]{1,0:T(8,128)S(1)} %log_add_fusion, bf16[1024,128,1]{1,0,2:T(8,128)(2,1)S(1)} %copy-done.47, bf16[1024,8,128]{0,2,1:T(8,128)(2,1)S(1)} %bitcast.347), kind=kOutput, calls=%fused_computation.2 | convolution fusion | flops 2172641280 | bytes 69533696 | tf_op jit(solution)/shard_map/while/body/eval_jaxpr/qhd,kd->hqk/dot_general | solution.py:264
  897.1 28.6 %fusion.2 = bf16[8,1024,1024]{1,2,0:T(8,128)(2,1)} fusion(f32[1024,1024,8]{1,0,2:T(8,128)} %get-tuple-element.157, f32[8,1024,1024]{1,2,0:T(8,128)} %get-tuple-element.155, f32[8,1024]{1,0:T(8,128)S(1)} %get-tuple-element.156, f32[8,1024]{1,0:T(8,128)S(1)} %log_add_fusion), kind=kLoop, calls=%fused_computation.4 | loop fusion | flops 33554432 | bytes 83951616 | tf_op jit(solution)/shard_map/while/body/eval_jaxpr/convert_element_type | solution.py:269
  1027.1 20.3 %collective-permute-done.42 = bf16[256,2048]{1,0:T(8,128)(2,1)S(1)} collective-permute-done((bf16[256,2048]{1,0:T(8,128)(2,1)S(1)}, bf16[256,2048]{1,0:T(8,128)(2,1)S(1)}, u32[]{:S(2)}, u32[]{:S(2)}) %collective-permute-start.42) | collective-permute-done | bytes 1048608 | tf_op jit(solution)/shard_map/ppermute | solution.py:80
  1053.8 22.7 %collective-permute-done.43 = bf16[256,2048]{1,0:T(8,128)(2,1)S(1)} collective-permute-done((bf16[256,2048]{1,0:T(8,128)(2,1)S(1)}, bf16[256,2048]{1,0:T(8,128)(2,1)S(1)}, u32[]{:S(2)}, u32[]{:S(2)}) %collective-permute-start.43) | collective-permute-done | bytes 1048608 | tf_op jit(solution)/shard_map/ppermute | solution.py:80
  1135.2 22.5 %reduce-scatter.7.cloned.1.call-done = bf16[256,1024]{1,0:T(8,128)(2,1)} async-done(((bf16[2048,1024]{1,0:T(8,128)(2,1)}), bf16[256,1024]{1,0:T(8,128)(2,1)}) %reduce-scatter.7.cloned.1.call-update) | async-done | bytes 524304 | tf_op jit(solution)/shard_map/reduce_scatter | solution.py:308
  1159.9 93.5 %reduce-scatter.17.cloned.1.call-done = bf16[2,192,2048]{2,1,0:T(8,128)(2,1)} async-done(((bf16[16,192,2048]{2,1,0:T(8,128)(2,1)}), bf16[2,192,2048]{2,1,0:T(8,128)(2,1)}) %reduce-scatter.17.cloned.1.call-update) | async-done | bytes 1572880 | tf_op jit(solution)/shard_map/reduce_scatter | solution.py:238
  1256.8 92.4 %reduce-scatter.15.cloned.1.call-done = bf16[2,2048,192]{1,2,0:T(8,128)(2,1)} async-done(((bf16[16,2048,192]{1,2,0:T(8,128)(2,1)}), bf16[2,2048,192]{1,2,0:T(8,128)(2,1)}) %reduce-scatter.15.cloned.1.call-update) | async-done | bytes 1572880 | tf_op jit(solution)/shard_map/reduce_scatter | solution.py:238
  1352.7 92.2 %reduce-scatter.13.cloned.1.call-done = bf16[2,2048,192]{1,2,0:T(8,128)(2,1)} async-done(((bf16[16,2048,192]{1,2,0:T(8,128)(2,1)}), bf16[2,2048,192]{1,2,0:T(8,128)(2,1)}) %reduce-scatter.13.cloned.1.call-update) | async-done | bytes 1572880 | tf_op jit(solution)/shard_map/reduce_scatter | solution.py:238
  (450 shorter events, 672.1 us)
Async XLA Ops:
  7.2 70.5 %all-gather.18.cloned.1.call-start = ((), (), s32[]{:S(2)}) async-start(), calls=%async_computation.18 | async-start | bytes 4866048 | tf_op jit(solution)/shard_map/all_gather | solution.py:125
  9.7 251.7 %all-gather.8.cloned.1.call-start = ((), (), s32[]{:S(2)}) async-start(), calls=%async_computation.7 | async-start | bytes 4718592 | tf_op jit(solution)/shard_map/all_gather | solution.py:142
  77.7 249.8 %all-gather.10.cloned.1.call-start = ((), (), s32[]{:S(2)}) async-start(), calls=%async_computation.8 | async-start | bytes 4718592 | tf_op jit(solution)/shard_map/all_gather | solution.py:143
  78.5 385.1 %all-gather.12.cloned.1.call-start = ((), (), s32[]{:S(2)}) async-start(), calls=%async_computation.9 | async-start | bytes 14155776 | tf_op jit(solution)/shard_map/all_gather | solution.py:146
  79.0 434.5 %all-gather.16.cloned.1.call-start = ((), (), s32[]{:S(2)}) async-start(), calls=%async_computation.11 | async-start | bytes 14155776 | tf_op jit(solution)/shard_map/all_gather | solution.py:144
  79.6 453.0 %all-gather.14.cloned.1.call-start = ((), (), s32[]{:S(2)}) async-start(), calls=%async_computation.10 | async-start | bytes 14155776 | tf_op jit(solution)/shard_map/all_gather | solution.py:145
  176.0 915.4 %reduce-scatter.9.cloned.1.call-start = ((), (), s32[]{:S(2)}) async-start(), calls=%async_computation.13 | async-start | bytes 2433024 | tf_op jit(solution)/shard_map/reduce_scatter | solution.py:333
  177.1 30.6 %collective-permute-start.9 = (bf16[256,2048]{1,0:T(8,128)(2,1)S(1)}, bf16[256,2048]{1,0:T(8,128)(2,1)}, u32[]{:S(2)}, u32[]{:S(2)}) collective-permute-start(bf16[256,2048]{1,0:T(8,128)(2,1)S(1)} %copy-done.26), channel_id=1, source_target_pairs={{1,0},{2,1},{3,2},{5,4},{6,5},{7,6},{9,8},{10,9},{11,10},{13,12},{... | collective-permute-start | bytes 3145736 | tf_op jit(solution)/shard_map/ppermute | solution.py:58
  396.5 33.9 %collective-permute-start.17 = (bf16[256,2048]{1,0:T(8,128)(2,1)S(1)}, bf16[256,2048]{1,0:T(8,128)(2,1)}, u32[]{:S(2)}, u32[]{:S(2)}) collective-permute-start(bf16[256,2048]{1,0:T(8,128)(2,1)S(1)} %fusion.37), channel_id=1, source_target_pairs={{1,0},{2,1},{3,2},{5,4},{6,5},{7,6},{9,8},{10,9},{11,10},{13,12},{... | collective-permute-start | bytes 3145736 | tf_op jit(solution)/shard_map/ppermute | solution.py:86
  610.0 54.2 %collective-permute-start.27 = (bf16[256,2048]{1,0:T(8,128)(2,1)S(1)}, bf16[256,2048]{1,0:T(8,128)(2,1)S(1)}, u32[]{:S(2)}, u32[]{:S(2)}) collective-permute-start(bf16[256,2048]{1,0:T(8,128)(2,1)S(1)} %get-tuple-element.121), channel_id=1, source_target_pairs={{3,2},{7,6},{11,10},{15,14},{19,18},{23,22},{27,26},{31,30}} | collective-permute-start | bytes 3145736 | tf_op jit(solution)/shard_map/ppermute | solution.py:86
  633.7 44.0 %collective-permute-start.25 = (bf16[256,2048]{1,0:T(8,128)(2,1)}, bf16[256,2048]{1,0:T(8,128)(2,1)}, u32[]{:S(2)}, u32[]{:S(2)}) collective-permute-start(bf16[256,2048]{1,0:T(8,128)(2,1)} %fusion.33), channel_id=1, source_target_pairs={{0,1},{1,2},{4,5},{5,6},{8,9},{9,10},{12,13},{13,14},{16,17},{17,1... | collective-permute-start | bytes 3145736 | tf_op jit(solution)/shard_map/ppermute | solution.py:80
  654.0 50.5 %collective-permute-start.33 = (bf16[256,2048]{1,0:T(8,128)(2,1)S(1)}, bf16[256,2048]{1,0:T(8,128)(2,1)}, u32[]{:S(2)}, u32[]{:S(2)}) collective-permute-start(bf16[256,2048]{1,0:T(8,128)(2,1)S(1)} %get-tuple-element.117), channel_id=1, source_target_pairs={{3,2},{7,6},{11,10},{15,14},{19,18},{23,22},{27,26},{31,30}} | collective-permute-start | bytes 3145736 | tf_op jit(solution)/shard_map/ppermute | solution.py:86
  658.9 45.6 %collective-permute-start.31 = (bf16[256,2048]{1,0:T(8,128)(2,1)}, bf16[256,2048]{1,0:T(8,128)(2,1)}, u32[]{:S(2)}, u32[]{:S(2)}) collective-permute-start(bf16[256,2048]{1,0:T(8,128)(2,1)} %fusion.28), channel_id=1, source_target_pairs={{0,1},{1,2},{4,5},{5,6},{8,9},{9,10},{12,13},{13,14},{16,17},{17,1... | collective-permute-start | bytes 3145736 | tf_op jit(solution)/shard_map/ppermute | solution.py:80
  682.2 28.9 %collective-permute-start.28 = (bf16[256,2048]{1,0:T(8,128)(2,1)}, bf16[256,2048]{1,0:T(8,128)(2,1)}, u32[]{:S(2)}, u32[]{:S(2)}) collective-permute-start(bf16[256,2048]{1,0:T(8,128)(2,1)} %get-tuple-element.119), channel_id=1, source_target_pairs={{2,1},{3,2},{6,5},{7,6},{10,9},{11,10},{14,13},{15,14},{18,17},{19... | collective-permute-start | bytes 3145736 | tf_op jit(solution)/shard_map/ppermute | solution.py:86
  699.5 43.1 %collective-permute-start.26 = (bf16[256,2048]{1,0:T(8,128)(2,1)S(1)}, bf16[256,2048]{1,0:T(8,128)(2,1)}, u32[]{:S(2)}, u32[]{:S(2)}) collective-permute-start(bf16[256,2048]{1,0:T(8,128)(2,1)S(1)} %get-tuple-element.118), channel_id=1, source_target_pairs={{0,1},{1,2},{2,3},{4,5},{5,6},{6,7},{8,9},{9,10},{10,11},{12,13},{... | collective-permute-start | bytes 3145736 | tf_op jit(solution)/shard_map/ppermute | solution.py:80
  709.4 29.3 %collective-permute-start.34 = (bf16[256,2048]{1,0:T(8,128)(2,1)}, bf16[256,2048]{1,0:T(8,128)(2,1)}, u32[]{:S(2)}, u32[]{:S(2)}) collective-permute-start(bf16[256,2048]{1,0:T(8,128)(2,1)} %get-tuple-element.115), channel_id=1, source_target_pairs={{2,1},{3,2},{6,5},{7,6},{10,9},{11,10},{14,13},{15,14},{18,17},{19... | collective-permute-start | bytes 3145736 | tf_op jit(solution)/shard_map/ppermute | solution.py:86
  761.5 30.3 %collective-permute-start.36 = (bf16[256,2048]{1,0:T(8,128)(2,1)S(1)}, bf16[256,2048]{1,0:T(8,128)(2,1)S(1)}, u32[]{:S(2)}, u32[]{:S(2)}) collective-permute-start(bf16[256,2048]{1,0:T(8,128)(2,1)S(1)} %convert_element_type.430), channel_id=1, source_target_pairs={{0,1},{1,2},{2,3},{4,5},{5,6},{6,7},{8,9},{9,10},{10,11},{12,13},{... | collective-permute-start | bytes 3145736 | tf_op jit(solution)/shard_map/ppermute | solution.py:55
  1001.6 131.5 %reduce-scatter.11.cloned.1.call-start = ((), (), s32[]{:S(2)}) async-start(), calls=%async_computation.14 | async-start | bytes 4718592 | tf_op jit(solution)/shard_map/reduce_scatter | solution.py:311
  1010.0 147.7 %reduce-scatter.7.cloned.1.call-start = ((), (), s32[]{:S(2)}) async-start(), calls=%async_computation.12 | async-start | bytes 4718592 | tf_op jit(solution)/shard_map/reduce_scatter | solution.py:308
  1020.2 233.2 %reduce-scatter.17.cloned.1.call-start = ((), (), s32[]{:S(2)}) async-start(), calls=%async_computation.17 | async-start | bytes 14155776 | tf_op jit(solution)/shard_map/reduce_scatter | solution.py:238
  1020.8 328.4 %reduce-scatter.15.cloned.1.call-start = ((), (), s32[]{:S(2)}) async-start(), calls=%async_computation.16 | async-start | bytes 14155776 | tf_op jit(solution)/shard_map/reduce_scatter | solution.py:238
  1021.5 423.4 %reduce-scatter.13.cloned.1.call-start = ((), (), s32[]{:S(2)}) async-start(), calls=%async_computation.15 | async-start | bytes 14155776 | tf_op jit(solution)/shard_map/reduce_scatter | solution.py:238
  1081.3 43.7 %collective-permute-start.44 = (bf16[256,2048]{1,0:T(8,128)(2,1)}, bf16[256,2048]{1,0:T(8,128)(2,1)}, u32[]{:S(2)}, u32[]{:S(2)}) collective-permute-start(bf16[256,2048]{1,0:T(8,128)(2,1)} %get-tuple-element.110), channel_id=1, source_target_pairs={{0,1},{1,2},{2,3},{4,5},{5,6},{6,7},{8,9},{9,10},{10,11},{12,13},{... | collective-permute-start | bytes 3145736 | tf_op jit(solution)/shard_map/ppermute | solution.py:80
  1090.1 34.9 %collective-permute-start.47 = (bf16[256,2048]{1,0:T(8,128)(2,1)}, bf16[256,2048]{1,0:T(8,128)(2,1)}, u32[]{:S(2)}, u32[]{:S(2)}) collective-permute-start(bf16[256,2048]{1,0:T(8,128)(2,1)} %fusion.21), channel_id=1, source_target_pairs={{1,0},{2,1},{3,2},{5,4},{6,5},{7,6},{9,8},{10,9},{11,10},{13,12},{... | collective-permute-start | bytes 3145736 | tf_op jit(solution)/shard_map/ppermute | solution.py:86
  (124 other events, 2641.5 us)
Sparse Core Ops, SparseCore 0:
  11.4 66.2 all-gather.17
  79.6 34.8 all-gather.7
  116.4 37.3 all-gather.9
  155.5 71.9 all-gather.11
  229.3 71.9 all-gather.15
  303.1 71.9 all-gather.13
  1001.7 46.9 reduce-scatter.8
  1052.1 51.0 reduce-scatter.10
  1106.6 51.0 reduce-scatter.6
  1161.1 92.2 reduce-scatter.16
  1256.9 92.2 reduce-scatter.14
  1352.6 92.2 reduce-scatter.12

commit v4 on v3

--- a/solution.py
+++ b/solution.py
@@ -137,7 +137,6 @@
     gain_query = gain_query.astype(jnp.float32)
     gain_key = gain_key.astype(jnp.float32)
     gain_ffn = gain_ffn.astype(jnp.float32)
-    packed_all, query_proj = lax.optimization_barrier((packed_all, query_proj))
     query_w, out_w, gate_w, up_w, down_w = (
         lax.all_gather(query_proj, "fsdp", axis=0, tiled=True),
         lax.all_gather(output_proj, "fsdp", axis=1, tiled=True),
@@ -153,7 +152,6 @@
     tp_size = lax.axis_size("tp")
     layer_rows = tp_gather(layer_in, tp_size)
     attn_rows = rms_norm(layer_rows.astype(jnp.float32), gain_attn).astype(jnp.bfloat16)
-    out_grad, attn_rows = lax.optimization_barrier((out_grad, attn_rows))
     grad_rows = tp_gather(out_grad, tp_size)
     query_raw = jnp.dot(attn_rows, query_w, preferred_element_type=jnp.float32)
     key_raw = jnp.dot(attn_rows, key_w, preferred_element_type=jnp.float32)
@@ -190,7 +188,6 @@
 
     context_all, log_sums = lax.map(attend, (query_seq, key_seq, value_seq, prefix_len))
     context_b = context_all.reshape(group_rows, per_dev * HD).astype(jnp.bfloat16)
-    context_b, grad_rows = lax.optimization_barrier((context_b, grad_rows))
     attn_out = tp_scatter_sum(
         jnp.dot(context_b, out_w, preferred_element_type=jnp.float32), tp_size, jnp.bfloat16
     )
@@ -291,6 +288,9 @@
     attn_in_part = result + jnp.einsum(
         "gk,dk->gd", value_back, value_w, preferred_element_type=jnp.float32
     )
+    attn_in_part, down_grad, gate_grad, up_grad = lax.optimization_barrier(
+        (attn_in_part, down_grad, gate_grad, up_grad)
+    )
     attn_in_grad = tp_scatter_sum(attn_in_part, tp_size, jnp.bfloat16)
     query_part = jnp.einsum("gd,gq->dq", attn_rows, query_back, preferred_element_type=jnp.float32)
     key_head_part = jnp.einsum("gd,gk->dk", attn_rows, key_back, preferred_element_type=jnp.float32)
@@ -304,15 +304,29 @@
     )
     (attn_gain_part,) = rows_back(attn_in_part)
     in_grad = residual_grad + input_norm_grad
-    query_proj_grad, output_proj_grad = (
-        lax.psum_scatter(
-            query_part.astype(jnp.bfloat16), "fsdp", scatter_dimension=0, tiled=True
+    fsdp_size = lax.axis_size("fsdp")
+    query_proj_grad = jnp.sum(
+        lax.all_to_all(
+            query_part.astype(jnp.bfloat16).reshape(fsdp_size, -1, query_part.shape[1]),
+            "fsdp",
+            split_axis=0,
+            concat_axis=0,
+            tiled=True,
         ).astype(jnp.float32),
-        lax.psum_scatter(
-            output_part.astype(jnp.bfloat16), "fsdp", scatter_dimension=1, tiled=True
+        axis=0,
+    )
+    output_proj_grad = jnp.sum(
+        lax.all_to_all(
+            output_part.astype(jnp.bfloat16)
+            .reshape(output_part.shape[0], fsdp_size, -1)
+            .transpose(1, 0, 2),
+            "fsdp",
+            split_axis=0,
+            concat_axis=0,
+            tiled=True,
         ).astype(jnp.float32),
-    )
-    fsdp_size = lax.axis_size("fsdp")
+        axis=0,
+    )
     device_count = fsdp_size * tp_size
     gain_parts = (attn_gain_part, query_gain_part, key_gain_part, ffn_gain_part)
     gain_table = jnp.concatenate(

time: 1460 us -> 1170 us (0.80)
  waiting for transfers between devices: 727 us -> 442 us
  matrix products: 329 us -> 309 us
    reduce_scatter x3, waiting for transfers between devices: 278 us -> 77.4 us  [body(): lax.psum_scatter(part.astype(jnp.bfloat16), 'fsdp', scatter_dimension=0,...]
    all_gather x1, waiting for transfers between devices: 68 us -> 0.01 us  [body(): packed_all = lax.all_gather(packed, ('fsdp', 'tp'), axis=0, tiled=False)]
    ppermute x12, waiting for transfers between devices: 103 us -> 59.7 us  [tp_scatter_sum(): lax.ppermute(outgoing.astype(send_type), 'tp', [(i, i + 1) for i in range...]
    ppermute x12, waiting for transfers between devices: 153 us -> 183 us  [tp_gather(): lax.ppermute(going_left, 'tp', [(i + 1, i) for i in range(0, count - step)])]
    reduce_scatter x2 -> x0, waiting for transfers between devices: 22.5 us -> none  [the longest x1 22.5 us: body(): lax.psum_scatter(query_part.astype(jnp.bfloat16), 'fsdp', scatter_dimensi...]
    ppermute x12, waiting for transfers between devices: 61.9 us -> 42.3 us  [tp_gather(): lax.ppermute(going_right, 'tp', [(i, i + 1) for i in range(step - 1, coun...]
    ppermute x12, waiting for transfers between devices: 28 us -> 46.8 us  [tp_scatter_sum(): lax.ppermute(outgoing.astype(send_type), 'tp', [(i, i - 1) for i in range...]
    all_to_all x0 -> x2, waiting for transfers between devices: none -> 15.6 us  [the longest x1 15.6 us: body(): lax.all_to_all(query_part.astype(jnp.bfloat16).reshape(fsdp_size, -1, que...]
  transfers between devices with their start and end apart: 61 -> 61, of which waited for: 29 -> 29; matrix products, arithmetic and copies ran while one was open for 22% -> 39% of each run, Pallas kernels for 0% -> 0%
where the time goes in v4:
time: 1170 us; the launch traced here: 1160 us
  waiting for transfers between devices  442 us (38%)
  matrix products  309 us (26%)
  other arithmetic  178 us (15%)
  starting transfers between devices  146 us (12%)
  local copies, waits for them, and re-layouts  68.9 us (6%)
  between operations  17 us (1%)
    ppermute x12, waiting for transfers between devices, tp_gather(): lax.ppermute(going_left, 'tp', [(i + 1, i) for i in range(0, count - step)])  183 us
    reduce_scatter x3, waiting for transfers between devices, body(): lax.psum_scatter(part.astype(jnp.bfloat16), 'fsdp', scatter_dimension=0,...  77.4 us
    ppermute x12, waiting for transfers between devices, tp_scatter_sum(): lax.ppermute(outgoing.astype(send_type), 'tp', [(i, i + 1) for i in range...  59.7 us
    ppermute x12, starting transfers between devices, tp_scatter_sum(): lax.ppermute(outgoing.astype(send_type), 'tp', [(i, i + 1) for i in range...  50.8 us
    ppermute x12, starting transfers between devices, tp_gather(): lax.ppermute(going_right, 'tp', [(i, i + 1) for i in range(step - 1, coun...  49.7 us
    ppermute x12, waiting for transfers between devices, tp_scatter_sum(): lax.ppermute(outgoing.astype(send_type), 'tp', [(i, i - 1) for i in range...  46.8 us
    ppermute x12, waiting for transfers between devices, tp_gather(): lax.ppermute(going_right, 'tp', [(i, i + 1) for i in range(step - 1, coun...  42.3 us
    convert_element_type x12, other arithmetic, tp_scatter_sum(): outgoing.astype(send_type)  40.8 us
  transfers between devices with their start and end apart: 61, of which 29 were waited for; matrix products, arithmetic and copies ran while one was open for 39% of the time, Pallas kernels for 0%

profile of v4, /device:TPU:0, one launch (start us, length us, event | category | flops | bytes accessed | tf_op | source)
XLA Modules:
  0.0 1160.4 jit_solution(8714676482919092165)
XLA Ops:
  18.6 21.0 %collective-permute-done = bf16[256,2048]{1,0:T(8,128)(2,1)S(1)} collective-permute-done((bf16[256,2048]{1,0:T(8,128)(2,1)S(1)}, bf16[256,2048]{1,0:T(8,128)(2,1)S(1)}, u32[]{:S(2)}, u32[]{:S(2)}) %collective-permute-start) | collective-permute-done | bytes 1048608 | tf_op jit(solution)/shard_map/ppermute | solution.py:55
  48.9 25.0 %collective-permute-done.4 = bf16[256,2048]{1,0:T(8,128)(2,1)} collective-permute-done((bf16[256,2048]{1,0:T(8,128)(2,1)S(1)}, bf16[256,2048]{1,0:T(8,128)(2,1)}, u32[]{:S(2)}, u32[]{:S(2)}) %collective-permute-start.4) | collective-permute-done | bytes 1048608 | tf_op jit(solution)/shard_map/ppermute | solution.py:58
  79.4 38.1 %collective-permute-done.5 = bf16[256,2048]{1,0:T(8,128)(2,1)S(1)} collective-permute-done((bf16[256,2048]{1,0:T(8,128)(2,1)}, bf16[256,2048]{1,0:T(8,128)(2,1)S(1)}, u32[]{:S(2)}, u32[]{:S(2)}) %collective-permute-start.5) | collective-permute-done | bytes 1048608 | tf_op jit(solution)/shard_map/ppermute | solution.py:58
  152.5 15.6 %fusion.102 = (f32[8,1024]{1,0:T(8,128)S(1)}, f32[8,1024,1024]{1,2,0:T(8,128)}) fusion(bf16[1024,8,64]{0,2,1:T(8,128)(2,1)S(1)} %get-tuple-element.127, bf16[1024,8,64]{0,2,1:T(8,128)(2,1)S(1)} %get-tuple-element.126, bf16[1024,64]{0,1:T(8,128)(2,1)S(1)} %get-tuple-element.133, bf16[1024,64]{0,1:T(8,128)(2,1)S(1)} %get-tuple-element.132, ...), kind=kOutput, calls=%fused_computation.251 | convolution fusion | flops 2177359872 | bytes 36995072 | tf_op jit(solution)/shard_map/while/body/eval_jaxpr/qhd,kd->hqk/dot_general | solution.py:42
  237.9 20.6 %collective-permute-done.7 = bf16[256,2048]{1,0:T(8,128)(2,1)} collective-permute-done((bf16[256,2048]{1,0:T(8,128)(2,1)}, bf16[256,2048]{1,0:T(8,128)(2,1)}, u32[]{:S(2)}, u32[]{:S(2)}) %collective-permute-start.7) | collective-permute-done | bytes 1048608 | tf_op jit(solution)/shard_map/ppermute | solution.py:80
  292.9 22.2 %collective-permute-done.11 = bf16[256,2048]{1,0:T(8,128)(2,1)} collective-permute-done((bf16[256,2048]{1,0:T(8,128)(2,1)}, bf16[256,2048]{1,0:T(8,128)(2,1)}, u32[]{:S(2)}, u32[]{:S(2)}) %collective-permute-start.11) | collective-permute-done | bytes 1048608 | tf_op jit(solution)/shard_map/ppermute | solution.py:86
  348.9 41.0 %collective-permute-done.21 = bf16[256,2048]{1,0:T(8,128)(2,1)S(1)} collective-permute-done((bf16[256,2048]{1,0:T(8,128)(2,1)S(1)}, bf16[256,2048]{1,0:T(8,128)(2,1)S(1)}, u32[]{:S(2)}, u32[]{:S(2)}) %collective-permute-start.21) | collective-permute-done | bytes 1048608 | tf_op jit(solution)/shard_map/ppermute | solution.py:58
  428.1 19.0 %fusion.105 = f32[1024,3072]{0,1} fusion(bf16[1024,2048]{1,0:T(8,128)(2,1)} %bitcast.364, bf16[2048,3072]{0,1:T(8,128)(2,1)} %bitcast.392), kind=kOutput, calls=%fused_computation.254 | convolution fusion | flops 12884901888 | bytes 29360128
  447.1 19.1 %fusion.104 = f32[1024,3072]{0,1} fusion(bf16[1024,2048]{1,0:T(8,128)(2,1)} %bitcast.365, bf16[2048,3072]{0,1:T(8,128)(2,1)} %bitcast.393), kind=kOutput, calls=%fused_computation.253 | convolution fusion | flops 12884901888 | bytes 29360128
  466.2 19.2 %fusion.103 = f32[1024,16,192]{0,2,1:T(8,128)} fusion(bf16[1024,2048,1]{1,0,2:T(8,128)(2,1)} %bitcast.368, bf16[16,192,2048]{2,1,0:T(8,128)(2,1)} %all-gather.12.cloned.1.call-done), kind=kOutput, calls=%fused_computation.252 | convolution fusion | flops 12884901888 | bytes 29360128 | tf_op jit(solution)/shard_map/td,efd->tef/dot_general | solution.py:212
  485.4 20.3 %multiply_convert_fusion = (bf16[1024,16,192]{0,2,1:T(8,128)(2,1)}, bf16[1024,16,192]{0,2,1:T(8,128)(2,1)}, bf16[1024,16,192]{0,2,1:T(8,128)(2,1)}) fusion(f32[1024,16,192]{0,2,1:T(8,128)} %bitcast.354, f32[1024,16]{0,1:T(8,128)S(1)} %select_reduce_fusion, f32[1024,16,192]{0,2,1:T(8,128)S(1)} %bitcast.353, f32[1024,16,192]{0,2,1:T(8,128)} %fusion.103), kind=kLoop, calls=%fused_computation.14 | loop fusion | flops 59768832 | bytes 56688640 | tf_op jit(solution)/shard_map/convert_element_type | solution.py:205
  505.7 19.1 %fusion.106 = f32[1024,2048,1]{1,0,2:T(8,128)} fusion(bf16[1024,16,192]{0,2,1:T(8,128)(2,1)} %get-tuple-element.106, bf16[16,2048,192]{1,2,0:T(8,128)(2,1)} %all-gather.16.cloned.1.call-done), kind=kOutput, calls=%fused_computation.255 | convolution fusion | flops 12884901888 | bytes 27262976 | tf_op jit(solution)/shard_map/tef,edf->td/dot_general | solution.py:219
  524.8 16.5 %bitcast_add_fusion = f32[1024,2048]{1,0:T(8,128)S(1)} fusion(f32[1024,2048,1]{1,0,2:T(8,128)} %fusion.106, bf16[1024,16,192]{0,2,1:T(8,128)(2,1)S(1)} %copy-done.22, bf16[16,2048,192]{1,2,0:T(8,128)(2,1)} %all-gather.14.cloned.1.call-done), kind=kOutput, calls=%fused_computation.22 | convolution fusion | flops 12886999040 | bytes 35651584 | tf_op jit(solution)/shard_map/tef,edf->td/dot_general | solution.py:221
  543.9 18.3 %fusion.107 = f32[1024,2048,1]{1,0,2:T(8,128)S(1)} fusion(bf16[1024,16,192]{0,2,1:T(8,128)(2,1)} %get-tuple-element.105, bf16[16,192,2048]{2,1,0:T(8,128)(2,1)} %all-gather.12.cloned.1.call-done), kind=kOutput, calls=%fused_computation.256 | convolution fusion | flops 12884901888 | bytes 27262976 | tf_op jit(solution)/shard_map/tef,efd->td/dot_general | solution.py:206
  573.3 17.6 %fusion.108 = bf16[16,192,2048]{2,1,0:T(8,128)(2,1)} fusion(bf16[1024,16,192]{0,2,1:T(8,128)(2,1)S(1)} %bitcast.362, bf16[1024,2048,1]{1,0,2:T(8,128)(2,1)} %bitcast.369), kind=kOutput, calls=%fused_computation.257 | convolution fusion | flops 12884901888 | bytes 23068672 | tf_op jit(solution)/shard_map/tef,td->efd/dot_general | solution.py:224
  614.1 15.7 %convolution_bitcast_fusion.1 = bf16[16,2048,192]{1,2,0:T(8,128)(2,1)} fusion(bf16[1024,16,192]{0,2,1:T(8,128)(2,1)S(1)} %bitcast.360, bf16[1024,2048,1]{1,0,2:T(8,128)(2,1)S(1)} %bitcast.366), kind=kOutput, calls=%fused_computation.21 | convolution fusion | flops 12884901888 | bytes 23068672 | tf_op jit(solution)/shard_map/td,tef->edf/dot_general | solution.py:222
  646.1 18.4 %convolution_bitcast_fusion = bf16[16,2048,192]{1,2,0:T(8,128)(2,1)} fusion(bf16[1024,16,192]{0,2,1:T(8,128)(2,1)} %get-tuple-element.107, bf16[1024,2048,1]{1,0,2:T(8,128)(2,1)S(1)} %bitcast.367), kind=kOutput, calls=%fused_computation.20 | convolution fusion | flops 12884901888 | bytes 23068672 | tf_op jit(solution)/shard_map/td,tef->edf/dot_general | solution.py:223
  693.6 16.6 %collective-permute-start.36 = (bf16[256,2048]{1,0:T(8,128)(2,1)S(1)}, bf16[256,2048]{1,0:T(8,128)(2,1)S(1)}, u32[]{:S(2)}, u32[]{:S(2)}) collective-permute-start(bf16[256,2048]{1,0:T(8,128)(2,1)S(1)} %convert_element_type.449), channel_id=1, source_target_pairs={{0,1},{1,2},{2,3},{4,5},{5,6},{6,7},{8,9},{9,10},{10,11},{12,13},{... | collective-permute-start | bytes 3145736 | tf_op jit(solution)/shard_map/ppermute | solution.py:55
  737.8 21.9 %collective-permute-done.40 = bf16[256,2048]{1,0:T(8,128)(2,1)} collective-permute-done((bf16[256,2048]{1,0:T(8,128)(2,1)}, bf16[256,2048]{1,0:T(8,128)(2,1)}, u32[]{:S(2)}, u32[]{:S(2)}) %collective-permute-start.40) | collective-permute-done | bytes 1048608 | tf_op jit(solution)/shard_map/ppermute | solution.py:58
  799.1 25.0 %fusion = (f32[8,1024]{1,0:T(8,128)S(1)}, f32[1024,1024,8]{1,0,2:T(8,128)}) fusion(f32[8,1024,1024]{1,2,0:T(8,128)} %get-tuple-element.155, f32[8,1024]{1,0:T(8,128)S(1)} %log_add_fusion, bf16[1024,128,1]{1,0,2:T(8,128)(2,1)S(1)} %copy-done.52, bf16[1024,8,128]{0,2,1:T(8,128)(2,1)S(1)} %bitcast.355), kind=kOutput, calls=%fused_computation.2 | convolution fusion | flops 2172641280 | bytes 69533696 | tf_op jit(solution)/shard_map/while/body/eval_jaxpr/qhd,kd->hqk/dot_general | solution.py:261
  824.1 34.1 %fusion.2 = bf16[8,1024,1024]{1,2,0:T(8,128)(2,1)} fusion(f32[1024,1024,8]{1,0,2:T(8,128)} %get-tuple-element.157, f32[8,1024,1024]{1,2,0:T(8,128)} %get-tuple-element.155, f32[8,1024]{1,0:T(8,128)S(1)} %get-tuple-element.156, f32[8,1024]{1,0:T(8,128)S(1)} %log_add_fusion), kind=kLoop, calls=%fused_computation.4 | loop fusion | flops 33554432 | bytes 83951616 | tf_op jit(solution)/shard_map/while/body/eval_jaxpr/convert_element_type | solution.py:266
  931.5 77.4 %reduce-scatter.5.cloned.1.call-done = bf16[2,192,2048]{2,1,0:T(8,128)(2,1)} async-done(((bf16[16,192,2048]{2,1,0:T(8,128)(2,1)}), bf16[2,192,2048]{2,1,0:T(8,128)(2,1)}) %reduce-scatter.5.cloned.1.call-update) | async-done | bytes 1572880 | tf_op jit(solution)/shard_map/reduce_scatter | solution.py:235
  1098.1 15.6 %all-to-all-done = bf16[8,256,1024]{2,1,0:T(8,128)(2,1)} async-done(((bf16[8,256,1024]{2,1,0:T(8,128)(2,1)}), bf16[8,256,1024]{2,1,0:T(8,128)(2,1)}, u32[]{:S(2)}, u32[]{:S(2)}) %all-to-all-start) | async-done | bytes 4194336 | tf_op jit(solution)/shard_map/all_to_all | solution.py:309
  1127.7 18.1 %collective-permute-done.47 = bf16[256,2048]{1,0:T(8,128)(2,1)} collective-permute-done((bf16[256,2048]{1,0:T(8,128)(2,1)}, bf16[256,2048]{1,0:T(8,128)(2,1)}, u32[]{:S(2)}, u32[]{:S(2)}) %collective-permute-start.47) | collective-permute-done | bytes 1048608 | tf_op jit(solution)/shard_map/ppermute | solution.py:86
  (452 shorter events, 567.9 us)
Async XLA Ops:
  7.2 114.5 %all-gather.8.cloned.1.call-start = ((), (), s32[]{:S(2)}) async-start(), calls=%async_computation.7 | async-start | bytes 4718592 | tf_op jit(solution)/shard_map/all_gather | solution.py:141
  7.9 120.4 %all-gather.18.cloned.1.call-start = ((), (), s32[]{:S(2)}) async-start(), calls=%async_computation.16 | async-start | bytes 4866048 | tf_op jit(solution)/shard_map/all_gather | solution.py:125
  10.3 187.8 %all-gather.10.cloned.1.call-start = ((), (), s32[]{:S(2)}) async-start(), calls=%async_computation.8 | async-start | bytes 4718592 | tf_op jit(solution)/shard_map/all_gather | solution.py:142
  11.1 417.0 %all-gather.16.cloned.1.call-start = ((), (), s32[]{:S(2)}) async-start(), calls=%async_computation.11 | async-start | bytes 14155776 | tf_op jit(solution)/shard_map/all_gather | solution.py:143
  11.6 435.4 %all-gather.14.cloned.1.call-start = ((), (), s32[]{:S(2)}) async-start(), calls=%async_computation.10 | async-start | bytes 14155776 | tf_op jit(solution)/shard_map/all_gather | solution.py:144
  12.2 454.0 %all-gather.12.cloned.1.call-start = ((), (), s32[]{:S(2)}) async-start(), calls=%async_computation.9 | async-start | bytes 14155776 | tf_op jit(solution)/shard_map/all_gather | solution.py:145
  46.8 876.5 %reduce-scatter.9.cloned.1.call-start = ((), (), s32[]{:S(2)}) async-start(), calls=%async_computation.14 | async-start | bytes 14155776 | tf_op jit(solution)/shard_map/reduce_scatter | solution.py:235
  73.9 43.7 %collective-permute-start.5 = (bf16[256,2048]{1,0:T(8,128)(2,1)}, bf16[256,2048]{1,0:T(8,128)(2,1)S(1)}, u32[]{:S(2)}, u32[]{:S(2)}) collective-permute-start(bf16[256,2048]{1,0:T(8,128)(2,1)} %collective-permute-done.4), channel_id=1, source_target_pairs={{1,0},{5,4},{9,8},{13,12},{17,16},{21,20},{25,24},{29,28}} | collective-permute-start | bytes 3145736 | tf_op jit(solution)/shard_map/ppermute | solution.py:58
  288.1 49.2 %collective-permute-start.16 = (bf16[256,2048]{1,0:T(8,128)(2,1)}, bf16[256,2048]{1,0:T(8,128)(2,1)}, u32[]{:S(2)}, u32[]{:S(2)}) collective-permute-start(bf16[256,2048]{1,0:T(8,128)(2,1)} %collective-permute-done.15), channel_id=1, source_target_pairs={{1,0},{2,1},{5,4},{6,5},{9,8},{10,9},{13,12},{14,13},{17,16},{18,1... | collective-permute-start | bytes 3145736 | tf_op jit(solution)/shard_map/ppermute | solution.py:58
  289.4 49.2 %collective-permute-start.14 = (bf16[256,2048]{1,0:T(8,128)(2,1)}, bf16[256,2048]{1,0:T(8,128)(2,1)}, u32[]{:S(2)}, u32[]{:S(2)}) collective-permute-start(bf16[256,2048]{1,0:T(8,128)(2,1)} %collective-permute-done.13), channel_id=1, source_target_pairs={{2,3},{6,7},{10,11},{14,15},{18,19},{22,23},{26,27},{30,31}} | collective-permute-start | bytes 3145736 | tf_op jit(solution)/shard_map/ppermute | solution.py:55
  337.4 55.9 %collective-permute-start.17 = (bf16[256,2048]{1,0:T(8,128)(2,1)}, bf16[256,2048]{1,0:T(8,128)(2,1)S(1)}, u32[]{:S(2)}, u32[]{:S(2)}) collective-permute-start(bf16[256,2048]{1,0:T(8,128)(2,1)} %collective-permute-done.16), channel_id=1, source_target_pairs={{1,0},{5,4},{9,8},{13,12},{17,16},{21,20},{25,24},{29,28}} | collective-permute-start | bytes 3145736 | tf_op jit(solution)/shard_map/ppermute | solution.py:58
  341.9 48.0 %collective-permute-start.21 = (bf16[256,2048]{1,0:T(8,128)(2,1)S(1)}, bf16[256,2048]{1,0:T(8,128)(2,1)S(1)}, u32[]{:S(2)}, u32[]{:S(2)}) collective-permute-start(bf16[256,2048]{1,0:T(8,128)(2,1)S(1)} %multiply_convert_fusion.6), channel_id=1, source_target_pairs={{1,0},{2,1},{3,2},{5,4},{6,5},{7,6},{9,8},{10,9},{11,10},{13,12},{... | collective-permute-start | bytes 3145736 | tf_op jit(solution)/shard_map/ppermute | solution.py:58
  345.5 45.7 %collective-permute-start.19 = (bf16[256,2048]{1,0:T(8,128)(2,1)S(1)}, bf16[256,2048]{1,0:T(8,128)(2,1)S(1)}, u32[]{:S(2)}, u32[]{:S(2)}) collective-permute-start(bf16[256,2048]{1,0:T(8,128)(2,1)S(1)} %collective-permute-done.18), channel_id=1, source_target_pairs={{1,2},{2,3},{5,6},{6,7},{9,10},{10,11},{13,14},{14,15},{17,18},{18... | collective-permute-start | bytes 3145736 | tf_op jit(solution)/shard_map/ppermute | solution.py:55
  543.1 55.3 %collective-permute-start.27 = (bf16[256,2048]{1,0:T(8,128)(2,1)S(1)}, bf16[256,2048]{1,0:T(8,128)(2,1)S(1)}, u32[]{:S(2)}, u32[]{:S(2)}) collective-permute-start(bf16[256,2048]{1,0:T(8,128)(2,1)S(1)} %get-tuple-element.119), channel_id=1, source_target_pairs={{3,2},{7,6},{11,10},{15,14},{19,18},{23,22},{27,26},{31,30}} | collective-permute-start | bytes 3145736 | tf_op jit(solution)/shard_map/ppermute | solution.py:86
  567.9 40.0 %collective-permute-start.25 = (bf16[256,2048]{1,0:T(8,128)(2,1)}, bf16[256,2048]{1,0:T(8,128)(2,1)}, u32[]{:S(2)}, u32[]{:S(2)}) collective-permute-start(bf16[256,2048]{1,0:T(8,128)(2,1)} %fusion.31), channel_id=1, source_target_pairs={{0,1},{1,2},{4,5},{5,6},{8,9},{9,10},{12,13},{13,14},{16,17},{17,1... | collective-permute-start | bytes 3145736 | tf_op jit(solution)/shard_map/ppermute | solution.py:80
  590.9 44.1 %collective-permute-start.33 = (bf16[256,2048]{1,0:T(8,128)(2,1)S(1)}, bf16[256,2048]{1,0:T(8,128)(2,1)}, u32[]{:S(2)}, u32[]{:S(2)}) collective-permute-start(bf16[256,2048]{1,0:T(8,128)(2,1)S(1)} %get-tuple-element.115), channel_id=1, source_target_pairs={{3,2},{7,6},{11,10},{15,14},{19,18},{23,22},{27,26},{31,30}} | collective-permute-start | bytes 3145736 | tf_op jit(solution)/shard_map/ppermute | solution.py:86
  595.9 39.1 %collective-permute-start.31 = (bf16[256,2048]{1,0:T(8,128)(2,1)}, bf16[256,2048]{1,0:T(8,128)(2,1)}, u32[]{:S(2)}, u32[]{:S(2)}) collective-permute-start(bf16[256,2048]{1,0:T(8,128)(2,1)} %fusion.26), channel_id=1, source_target_pairs={{0,1},{1,2},{4,5},{5,6},{8,9},{9,10},{12,13},{13,14},{16,17},{17,1... | collective-permute-start | bytes 3145736 | tf_op jit(solution)/shard_map/ppermute | solution.py:80
  629.8 43.2 %collective-permute-start.26 = (bf16[256,2048]{1,0:T(8,128)(2,1)S(1)}, bf16[256,2048]{1,0:T(8,128)(2,1)}, u32[]{:S(2)}, u32[]{:S(2)}) collective-permute-start(bf16[256,2048]{1,0:T(8,128)(2,1)S(1)} %get-tuple-element.116), channel_id=1, source_target_pairs={{0,1},{1,2},{2,3},{4,5},{5,6},{6,7},{8,9},{9,10},{10,11},{12,13},{... | collective-permute-start | bytes 3145736 | tf_op jit(solution)/shard_map/ppermute | solution.py:80
  691.9 235.5 %reduce-scatter.7.cloned.1.call-start = ((), (), s32[]{:S(2)}) async-start(), calls=%async_computation.13 | async-start | bytes 14155776 | tf_op jit(solution)/shard_map/reduce_scatter | solution.py:235
  692.6 316.3 %reduce-scatter.5.cloned.1.call-start = ((), (), s32[]{:S(2)}) async-start(), calls=%async_computation.12 | async-start | bytes 14155776 | tf_op jit(solution)/shard_map/reduce_scatter | solution.py:235
  786.1 271.0 %all-to-all-start.2 = ((bf16[8,1024,256]{2,1,0:T(8,128)(2,1)}), bf16[8,1024,256]{2,1,0:T(8,128)(2,1)}, u32[]{:S(2)}, u32[]{:S(2)}) async-start(bf16[8,1024,256]{2,1,0:T(8,128)(2,1)} %bitcast.351), calls=%async_computation.6 | async-start | bytes 8388608 | tf_op jit(solution)/shard_map/all_to_all | solution.py:319
  790.7 304.5 %reduce-scatter.11.cloned.1.call-start = ((), (), s32[]{:S(2)}) async-start(), calls=%async_computation.15 | async-start | bytes 2433024 | tf_op jit(solution)/shard_map/reduce_scatter | solution.py:347
  1057.0 56.7 %all-to-all-start = ((bf16[8,256,1024]{2,1,0:T(8,128)(2,1)}), bf16[8,256,1024]{2,1,0:T(8,128)(2,1)}, u32[]{:S(2)}, u32[]{:S(2)}) async-start(bf16[8,256,1024]{2,1,0:T(8,128)(2,1)} %bitcast.370), calls=%async_computation.3 | async-start | bytes 8388608 | tf_op jit(solution)/shard_map/all_to_all | solution.py:309
  1075.7 52.1 %collective-permute-start.44 = (bf16[256,2048]{1,0:T(8,128)(2,1)}, bf16[256,2048]{1,0:T(8,128)(2,1)}, u32[]{:S(2)}, u32[]{:S(2)}) collective-permute-start(bf16[256,2048]{1,0:T(8,128)(2,1)} %get-tuple-element.108), channel_id=1, source_target_pairs={{0,1},{1,2},{2,3},{4,5},{5,6},{6,7},{8,9},{9,10},{10,11},{12,13},{... | collective-permute-start | bytes 3145736 | tf_op jit(solution)/shard_map/ppermute | solution.py:80
  (126 other events, 2428.3 us)
Sparse Core Ops, SparseCore 0:
  9.9 39.2 all-gather.7
  52.6 65.2 all-gather.17
  119.8 36.0 all-gather.9
  157.7 71.9 all-gather.15
  231.4 71.9 all-gather.13
  305.2 71.9 all-gather.11
  691.9 107.2 reduce-scatter.8
  802.7 110.2 reduce-scatter.6
  916.5 92.3 reduce-scatter.4
  1031.7 63.4 reduce-scatter.10

commit v5 on v4

--- a/solution.py
+++ b/solution.py
@@ -152,6 +152,7 @@
     tp_size = lax.axis_size("tp")
     layer_rows = tp_gather(layer_in, tp_size)
     attn_rows = rms_norm(layer_rows.astype(jnp.float32), gain_attn).astype(jnp.bfloat16)
+    out_grad, attn_rows = lax.optimization_barrier((out_grad, attn_rows))
     grad_rows = tp_gather(out_grad, tp_size)
     query_raw = jnp.dot(attn_rows, query_w, preferred_element_type=jnp.float32)
     key_raw = jnp.dot(attn_rows, key_w, preferred_element_type=jnp.float32)
@@ -188,6 +189,7 @@
 
     context_all, log_sums = lax.map(attend, (query_seq, key_seq, value_seq, prefix_len))
     context_b = context_all.reshape(group_rows, per_dev * HD).astype(jnp.bfloat16)
+    context_b, grad_rows = lax.optimization_barrier((context_b, grad_rows))
     attn_out = tp_scatter_sum(
         jnp.dot(context_b, out_w, preferred_element_type=jnp.float32), tp_size, jnp.bfloat16
     )
@@ -228,9 +230,7 @@
     _, second_back = jax.vjp(rms_norm, residual, gain_ffn)
     residual_norm_grad, ffn_gain_part = second_back(ffn_in_own)
     residual_grad = grad_out + residual_norm_grad
-    residual_grad, mixture_own, gate_part, up_part, down_part = lax.optimization_barrier(
-        (residual_grad, mixture_own, gate_part, up_part, down_part)
-    )
+    residual_grad, mixture_own = lax.optimization_barrier((residual_grad, mixture_own))
     gate_grad, up_grad, down_grad = (
         lax.psum_scatter(
             part.astype(jnp.bfloat16), "fsdp", scatter_dimension=0, tiled=True

time: 1170 us -> 1160 us (level)
  matrix products: 309 us -> 332 us
  other arithmetic: 178 us -> 164 us
    ppermute x12, waiting for transfers between devices: 59.7 us -> 140 us  [tp_scatter_sum(): lax.ppermute(outgoing.astype(send_type), 'tp', [(i, i + 1) for i in range...]
    reduce_scatter x3, waiting for transfers between devices: 77.4 us -> 0.02 us  [body(): lax.psum_scatter(part.astype(jnp.bfloat16), 'fsdp', scatter_dimension=0,...]
    ppermute x12, waiting for transfers between devices: 183 us -> 161 us  [tp_gather(): lax.ppermute(going_left, 'tp', [(i + 1, i) for i in range(0, count - step)])]
    convert_element_type x12, other arithmetic: 40.8 us -> 22.9 us  [tp_scatter_sum(): outgoing.astype(send_type)]
    ppermute x12, waiting for transfers between devices: 42.3 us -> 57.7 us  [tp_gather(): lax.ppermute(going_right, 'tp', [(i, i + 1) for i in range(step - 1, coun...]
    unnamed x208 -> x180, local copies, waits for them, and re-layouts: 32.6 us -> 25.1 us
  transfers between devices with their start and end apart: 61 -> 61, of which waited for: 29 -> 30; matrix products, arithmetic and copies ran while one was open for 39% -> 42% of each run, Pallas kernels for 0% -> 0%
where the time goes in v5:
time: 1160 us; the launch traced here: 1150 us
  waiting for transfers between devices  435 us (38%)
  matrix products  332 us (29%)
  other arithmetic  164 us (14%)
  starting transfers between devices  136 us (12%)
  local copies, waits for them, and re-layouts  64.7 us (6%)
  between operations  16.9 us (1%)
    ppermute x12, waiting for transfers between devices, tp_gather(): lax.ppermute(going_left, 'tp', [(i + 1, i) for i in range(0, count - step)])  161 us
    ppermute x12, waiting for transfers between devices, tp_scatter_sum(): lax.ppermute(outgoing.astype(send_type), 'tp', [(i, i + 1) for i in range...  140 us
    ppermute x12, waiting for transfers between devices, tp_gather(): lax.ppermute(going_right, 'tp', [(i, i + 1) for i in range(step - 1, coun...  57.7 us
    ppermute x12, starting transfers between devices, tp_gather(): lax.ppermute(going_right, 'tp', [(i, i + 1) for i in range(step - 1, coun...  47.3 us
    ppermute x12, starting transfers between devices, tp_scatter_sum(): lax.ppermute(outgoing.astype(send_type), 'tp', [(i, i + 1) for i in range...  46.4 us
    ppermute x12, waiting for transfers between devices, tp_scatter_sum(): lax.ppermute(outgoing.astype(send_type), 'tp', [(i, i - 1) for i in range...  45.7 us
    unnamed x2, matrix products  38.2 us
    convert_element_type x1, other arithmetic, attend_back(): scores_grad = (attn_probs * (probs_grad - jnp.sum(attn_probs * probs_grad...  28.4 us
  transfers between devices with their start and end apart: 61, of which 30 were waited for; matrix products, arithmetic and copies ran while one was open for 42% of the time, Pallas kernels for 0%

profile of v5, /device:TPU:0, one launch (start us, length us, event | category | flops | bytes accessed | tf_op | source)
XLA Modules:
  0.0 1148.3 jit_solution(14753220842190331673)
XLA Ops:
  18.7 27.4 %collective-permute-done = bf16[256,2048]{1,0:T(8,128)(2,1)S(1)} collective-permute-done((bf16[256,2048]{1,0:T(8,128)(2,1)S(1)}, bf16[256,2048]{1,0:T(8,128)(2,1)S(1)}, u32[]{:S(2)}, u32[]{:S(2)}) %collective-permute-start) | collective-permute-done | bytes 1048608 | tf_op jit(solution)/shard_map/ppermute | solution.py:55
  55.6 34.0 %collective-permute-done.4 = bf16[256,2048]{1,0:T(8,128)(2,1)} collective-permute-done((bf16[256,2048]{1,0:T(8,128)(2,1)S(1)}, bf16[256,2048]{1,0:T(8,128)(2,1)}, u32[]{:S(2)}, u32[]{:S(2)}) %collective-permute-start.4) | collective-permute-done | bytes 1048608 | tf_op jit(solution)/shard_map/ppermute | solution.py:58
  95.3 19.1 %collective-permute-done.5 = bf16[256,2048]{1,0:T(8,128)(2,1)S(1)} collective-permute-done((bf16[256,2048]{1,0:T(8,128)(2,1)}, bf16[256,2048]{1,0:T(8,128)(2,1)S(1)}, u32[]{:S(2)}, u32[]{:S(2)}) %collective-permute-start.5) | collective-permute-done | bytes 1048608 | tf_op jit(solution)/shard_map/ppermute | solution.py:58
  235.4 17.7 %collective-permute-done.11 = bf16[256,2048]{1,0:T(8,128)(2,1)S(1)} collective-permute-done((bf16[256,2048]{1,0:T(8,128)(2,1)S(1)}, bf16[256,2048]{1,0:T(8,128)(2,1)S(1)}, u32[]{:S(2)}, u32[]{:S(2)}) %collective-permute-start.11) | collective-permute-done | bytes 1048608 | tf_op jit(solution)/shard_map/ppermute | solution.py:58
  269.8 16.8 %collective-permute-done.12 = bf16[256,2048]{1,0:T(8,128)(2,1)} collective-permute-done((bf16[256,2048]{1,0:T(8,128)(2,1)}, bf16[256,2048]{1,0:T(8,128)(2,1)}, u32[]{:S(2)}, u32[]{:S(2)}) %collective-permute-start.12) | collective-permute-done | bytes 1048608 | tf_op jit(solution)/shard_map/ppermute | solution.py:80
  338.2 22.2 %collective-permute-done.17 = bf16[256,2048]{1,0:T(8,128)(2,1)} collective-permute-done((bf16[256,2048]{1,0:T(8,128)(2,1)S(1)}, bf16[256,2048]{1,0:T(8,128)(2,1)}, u32[]{:S(2)}, u32[]{:S(2)}) %collective-permute-start.17) | collective-permute-done | bytes 1048608 | tf_op jit(solution)/shard_map/ppermute | solution.py:86
  392.6 21.2 %collective-permute-done.22 = bf16[256,2048]{1,0:T(8,128)(2,1)S(1)} collective-permute-done((bf16[256,2048]{1,0:T(8,128)(2,1)S(1)}, bf16[256,2048]{1,0:T(8,128)(2,1)S(1)}, u32[]{:S(2)}, u32[]{:S(2)}) %collective-permute-start.22) | collective-permute-done | bytes 1048608 | tf_op jit(solution)/shard_map/ppermute | solution.py:58
  433.7 19.1 %fusion.102 = f32[1024,3072]{0,1} fusion(bf16[1024,2048]{1,0:T(8,128)(2,1)} %bitcast.357, bf16[2048,3072]{0,1:T(8,128)(2,1)} %bitcast.383), kind=kOutput, calls=%fused_computation.252 | convolution fusion | flops 12884901888 | bytes 29360128
  452.8 19.1 %fusion.101 = f32[1024,3072]{0,1} fusion(bf16[1024,2048]{1,0:T(8,128)(2,1)} %bitcast.358, bf16[2048,3072]{0,1:T(8,128)(2,1)} %bitcast.384), kind=kOutput, calls=%fused_computation.251 | convolution fusion | flops 12884901888 | bytes 29360128
  471.9 19.2 %fusion.12 = f32[1024,16,192]{0,2,1:T(8,128)} fusion(bf16[16,192,2048]{2,1,0:T(8,128)(2,1)} %all-gather.12.cloned.1.call-done, bf16[1024,2048]{1,0:T(8,128)(2,1)} %bitcast.361), kind=kOutput, calls=%fused_computation.35 | convolution fusion | flops 12884901888 | bytes 29360128 | tf_op jit(solution)/shard_map/td,efd->tef/dot_general | solution.py:214
  491.1 20.4 %multiply_convert_fusion = (bf16[1024,16,192]{0,2,1:T(8,128)(2,1)}, bf16[1024,16,192]{0,2,1:T(8,128)(2,1)}, bf16[1024,16,192]{0,2,1:T(8,128)(2,1)}) fusion(f32[1024,16,192]{0,2,1:T(8,128)} %bitcast.350, f32[1024,16]{0,1:T(8,128)S(1)} %select_reduce_fusion, f32[1024,16,192]{0,2,1:T(8,128)S(1)} %bitcast.349, f32[1024,16,192]{0,2,1:T(8,128)} %fusion.12), kind=kLoop, calls=%fused_computation.16 | loop fusion | flops 59768832 | bytes 56688640 | tf_op jit(solution)/shard_map/convert_element_type | solution.py:207
  511.5 19.2 %convolution_convert_fusion = bf16[16,192,2048]{2,1,0:T(8,128)(2,1)} fusion(bf16[1024,16,192]{0,2,1:T(8,128)(2,1)} %get-tuple-element.107, bf16[1024,2048]{1,0:T(8,128)(2,1)} %bitcast.362), kind=kOutput, calls=%fused_computation.30 | convolution fusion | flops 12891193344 | bytes 23068672 | tf_op jit(solution)/shard_map/tef,td->efd/dot_general | solution.py:226
  530.8 19.3 %convert_bitcast_fusion.1 = bf16[16,2048,192]{1,2,0:T(8,128)(2,1)} fusion(bf16[1024,16,192]{0,2,1:T(8,128)(2,1)} %get-tuple-element.108, bf16[1024,2048,1]{1,0,2:T(8,128)(2,1)} %bitcast.359), kind=kOutput, calls=%fused_computation.15 | convolution fusion | flops 12891193344 | bytes 23068672 | tf_op jit(solution)/shard_map/td,tef->edf/dot_general | solution.py:224
  550.2 17.7 %fusion.103 = f32[1024,2048,1]{1,0,2:T(8,128)S(1)} fusion(bf16[1024,16,192]{0,2,1:T(8,128)(2,1)} %get-tuple-element.108, bf16[16,2048,192]{1,2,0:T(8,128)(2,1)} %all-gather.16.cloned.1.call-done), kind=kOutput, calls=%fused_computation.253 | convolution fusion | flops 12884901888 | bytes 27262976 | tf_op jit(solution)/shard_map/tef,edf->td/dot_general | solution.py:221
  567.9 19.3 %bitcast_add_fusion = f32[1024,2048]{1,0:T(8,128)S(1)} fusion(f32[1024,2048,1]{1,0,2:T(8,128)S(1)} %fusion.103, bf16[1024,16,192]{0,2,1:T(8,128)(2,1)} %get-tuple-element.109, bf16[16,2048,192]{1,2,0:T(8,128)(2,1)} %all-gather.14.cloned.1.call-done), kind=kOutput, calls=%fused_computation.22 | convolution fusion | flops 12886999040 | bytes 35651584 | tf_op jit(solution)/shard_map/tef,edf->td/dot_general | solution.py:223
  589.8 17.8 %fusion.104 = f32[1024,2048,1]{1,0,2:T(8,128)S(1)} fusion(bf16[1024,16,192]{0,2,1:T(8,128)(2,1)} %get-tuple-element.107, bf16[16,192,2048]{2,1,0:T(8,128)(2,1)} %all-gather.12.cloned.1.call-done), kind=kOutput, calls=%fused_computation.254 | convolution fusion | flops 12884901888 | bytes 27262976 | tf_op jit(solution)/shard_map/tef,efd->td/dot_general | solution.py:208
  612.4 20.3 %collective-permute-done.30 = bf16[256,2048]{1,0:T(8,128)(2,1)S(1)} collective-permute-done((bf16[256,2048]{1,0:T(8,128)(2,1)S(1)}, bf16[256,2048]{1,0:T(8,128)(2,1)S(1)}, u32[]{:S(2)}, u32[]{:S(2)}) %collective-permute-start.30) | collective-permute-done | bytes 1048608 | tf_op jit(solution)/shard_map/ppermute | solution.py:80
  637.4 17.7 %collective-permute-done.25 = bf16[256,2048]{1,0:T(8,128)(2,1)S(1)} collective-permute-done((bf16[256,2048]{1,0:T(8,128)(2,1)S(1)}, bf16[256,2048]{1,0:T(8,128)(2,1)S(1)}, u32[]{:S(2)}, u32[]{:S(2)}) %collective-permute-start.25) | collective-permute-done | bytes 1048608 | tf_op jit(solution)/shard_map/ppermute | solution.py:80
  725.4 23.2 %collective-permute-start.36 = (bf16[256,2048]{1,0:T(8,128)(2,1)S(1)}, bf16[256,2048]{1,0:T(8,128)(2,1)S(1)}, u32[]{:S(2)}, u32[]{:S(2)}) collective-permute-start(bf16[256,2048]{1,0:T(8,128)(2,1)S(1)} %convert_element_type.436), channel_id=1, source_target_pairs={{0,1},{1,2},{2,3},{4,5},{5,6},{6,7},{8,9},{9,10},{10,11},{12,13},{... | collective-permute-start | bytes 3145736 | tf_op jit(solution)/shard_map/ppermute | solution.py:55
  774.6 17.9 %convert_bitcast_fusion = bf16[16,2048,192]{1,2,0:T(8,128)(2,1)} fusion(bf16[1024,16,192]{0,2,1:T(8,128)(2,1)S(1)} %bitcast.356, bf16[1024,2048,1]{1,0,2:T(8,128)(2,1)} %bitcast.360), kind=kOutput, calls=%fused_computation.14 | convolution fusion | flops 12891193344 | bytes 23068672 | tf_op jit(solution)/shard_map/td,tef->edf/dot_general | solution.py:225
  801.4 26.7 %collective-permute-done.41 = bf16[256,2048]{1,0:T(8,128)(2,1)S(1)} collective-permute-done((bf16[256,2048]{1,0:T(8,128)(2,1)}, bf16[256,2048]{1,0:T(8,128)(2,1)S(1)}, u32[]{:S(2)}, u32[]{:S(2)}) %collective-permute-start.41) | collective-permute-done | bytes 1048608 | tf_op jit(solution)/shard_map/ppermute | solution.py:58
  850.2 26.5 %fusion = (f32[8,1024]{1,0:T(8,128)S(1)}, f32[1024,1024,8]{1,0,2:T(8,128)}) fusion(f32[8,1024,1024]{1,2,0:T(8,128)} %get-tuple-element.155, f32[8,1024]{1,0:T(8,128)S(1)} %log_add_fusion, bf16[1024,128,1]{1,0,2:T(8,128)(2,1)S(1)} %copy-done.41, bf16[1024,8,128]{0,2,1:T(8,128)(2,1)S(1)} %bitcast.351), kind=kOutput, calls=%fused_computation.2 | convolution fusion | flops 2172641280 | bytes 69533696 | tf_op jit(solution)/shard_map/while/body/eval_jaxpr/qhd,kd->hqk/dot_general | solution.py:261
  876.7 28.4 %fusion.2 = bf16[8,1024,1024]{1,2,0:T(8,128)(2,1)} fusion(f32[1024,1024,8]{1,0,2:T(8,128)} %get-tuple-element.157, f32[8,1024,1024]{1,2,0:T(8,128)} %get-tuple-element.155, f32[8,1024]{1,0:T(8,128)S(1)} %get-tuple-element.156, f32[8,1024]{1,0:T(8,128)S(1)} %log_add_fusion), kind=kLoop, calls=%fused_computation.4 | loop fusion | flops 33554432 | bytes 83951616 | tf_op jit(solution)/shard_map/while/body/eval_jaxpr/convert_element_type | solution.py:266
  1115.7 18.1 %collective-permute-done.47 = bf16[256,2048]{1,0:T(8,128)(2,1)} collective-permute-done((bf16[256,2048]{1,0:T(8,128)(2,1)}, bf16[256,2048]{1,0:T(8,128)(2,1)}, u32[]{:S(2)}, u32[]{:S(2)}) %collective-permute-start.47) | collective-permute-done | bytes 1048608 | tf_op jit(solution)/shard_map/ppermute | solution.py:86
  (423 shorter events, 623.1 us)
Async XLA Ops:
  7.2 111.2 %all-gather.18.cloned.1.call-start = ((), (), s32[]{:S(2)}) async-start(), calls=%async_computation.16 | async-start | bytes 4866048 | tf_op jit(solution)/shard_map/all_gather | solution.py:125
  9.7 141.4 %all-gather.8.cloned.1.call-start = ((), (), s32[]{:S(2)}) async-start(), calls=%async_computation.7 | async-start | bytes 4718592 | tf_op jit(solution)/shard_map/all_gather | solution.py:141
  10.4 245.2 %all-gather.10.cloned.1.call-start = ((), (), s32[]{:S(2)}) async-start(), calls=%async_computation.8 | async-start | bytes 4718592 | tf_op jit(solution)/shard_map/all_gather | solution.py:142
  11.2 422.5 %all-gather.16.cloned.1.call-start = ((), (), s32[]{:S(2)}) async-start(), calls=%async_computation.11 | async-start | bytes 14155776 | tf_op jit(solution)/shard_map/all_gather | solution.py:143
  11.7 441.0 %all-gather.14.cloned.1.call-start = ((), (), s32[]{:S(2)}) async-start(), calls=%async_computation.10 | async-start | bytes 14155776 | tf_op jit(solution)/shard_map/all_gather | solution.py:144
  12.3 459.5 %all-gather.12.cloned.1.call-start = ((), (), s32[]{:S(2)}) async-start(), calls=%async_computation.9 | async-start | bytes 14155776 | tf_op jit(solution)/shard_map/all_gather | solution.py:145
  51.4 38.2 %collective-permute-start.4 = (bf16[256,2048]{1,0:T(8,128)(2,1)S(1)}, bf16[256,2048]{1,0:T(8,128)(2,1)}, u32[]{:S(2)}, u32[]{:S(2)}) collective-permute-start(bf16[256,2048]{1,0:T(8,128)(2,1)S(1)} %collective-permute-done.3), channel_id=1, source_target_pairs={{1,0},{2,1},{5,4},{6,5},{9,8},{10,9},{13,12},{14,13},{17,16},{18,1... | collective-permute-start | bytes 3145736 | tf_op jit(solution)/shard_map/ppermute | solution.py:58
  52.7 38.2 %collective-permute-start.2 = (bf16[256,2048]{1,0:T(8,128)(2,1)}, bf16[256,2048]{1,0:T(8,128)(2,1)}, u32[]{:S(2)}, u32[]{:S(2)}) collective-permute-start(bf16[256,2048]{1,0:T(8,128)(2,1)} %collective-permute-done.1), channel_id=1, source_target_pairs={{2,3},{6,7},{10,11},{14,15},{18,19},{22,23},{26,27},{30,31}} | collective-permute-start | bytes 3145736 | tf_op jit(solution)/shard_map/ppermute | solution.py:55
  54.5 935.6 %reduce-scatter.5.cloned.1.call-start = ((), (), s32[]{:S(2)}) async-start(), calls=%async_computation.12 | async-start | bytes 14155776 | tf_op jit(solution)/shard_map/reduce_scatter | solution.py:235
  130.2 71.8 %collective-permute-start.9 = (bf16[256,2048]{1,0:T(8,128)(2,1)}, bf16[256,2048]{1,0:T(8,128)(2,1)}, u32[]{:S(2)}, u32[]{:S(2)}) collective-permute-start(bf16[256,2048]{1,0:T(8,128)(2,1)} %param.33), channel_id=1, source_target_pairs={{1,0},{2,1},{3,2},{5,4},{6,5},{7,6},{9,8},{10,9},{11,10},{13,12},{... | collective-permute-start | bytes 3145736 | tf_op jit(solution)/shard_map/ppermute | solution.py:58
  131.5 55.0 %collective-permute-start.6 = (bf16[256,2048]{1,0:T(8,128)(2,1)}, bf16[256,2048]{1,0:T(8,128)(2,1)}, u32[]{:S(2)}, u32[]{:S(2)}) collective-permute-start(bf16[256,2048]{1,0:T(8,128)(2,1)} %param.33), channel_id=1, source_target_pairs={{0,1},{1,2},{2,3},{4,5},{5,6},{6,7},{8,9},{9,10},{10,11},{12,13},{... | collective-permute-start | bytes 3145736 | tf_op jit(solution)/shard_map/ppermute | solution.py:55
  530.7 462.8 %reduce-scatter.7.cloned.1.call-start = ((), (), s32[]{:S(2)}) async-start(), calls=%async_computation.13 | async-start | bytes 14155776 | tf_op jit(solution)/shard_map/reduce_scatter | solution.py:235
  550.1 446.9 %reduce-scatter.9.cloned.1.call-start = ((), (), s32[]{:S(2)}) async-start(), calls=%async_computation.14 | async-start | bytes 14155776 | tf_op jit(solution)/shard_map/reduce_scatter | solution.py:235
  610.3 44.8 %collective-permute-start.25 = (bf16[256,2048]{1,0:T(8,128)(2,1)S(1)}, bf16[256,2048]{1,0:T(8,128)(2,1)S(1)}, u32[]{:S(2)}, u32[]{:S(2)}) collective-permute-start(bf16[256,2048]{1,0:T(8,128)(2,1)S(1)} %fusion.32), channel_id=1, source_target_pairs={{0,1},{1,2},{4,5},{5,6},{8,9},{9,10},{12,13},{13,14},{16,17},{17,1... | collective-permute-start | bytes 3145736 | tf_op jit(solution)/shard_map/ppermute | solution.py:80
  611.7 45.0 %collective-permute-start.33 = (bf16[256,2048]{1,0:T(8,128)(2,1)S(1)}, bf16[256,2048]{1,0:T(8,128)(2,1)S(1)}, u32[]{:S(2)}, u32[]{:S(2)}) collective-permute-start(bf16[256,2048]{1,0:T(8,128)(2,1)S(1)} %get-tuple-element.117), channel_id=1, source_target_pairs={{3,2},{7,6},{11,10},{15,14},{19,18},{23,22},{27,26},{31,30}} | collective-permute-start | bytes 3145736 | tf_op jit(solution)/shard_map/ppermute | solution.py:86
  633.0 38.1 %collective-permute-start.31 = (bf16[256,2048]{1,0:T(8,128)(2,1)S(1)}, bf16[256,2048]{1,0:T(8,128)(2,1)S(1)}, u32[]{:S(2)}, u32[]{:S(2)}) collective-permute-start(bf16[256,2048]{1,0:T(8,128)(2,1)S(1)} %fusion.27), channel_id=1, source_target_pairs={{0,1},{1,2},{4,5},{5,6},{8,9},{9,10},{12,13},{13,14},{16,17},{17,1... | collective-permute-start | bytes 3145736 | tf_op jit(solution)/shard_map/ppermute | solution.py:80
  679.4 36.8 %collective-permute-start.32 = (bf16[256,2048]{1,0:T(8,128)(2,1)S(1)}, bf16[256,2048]{1,0:T(8,128)(2,1)S(1)}, u32[]{:S(2)}, u32[]{:S(2)}) collective-permute-start(bf16[256,2048]{1,0:T(8,128)(2,1)S(1)} %get-tuple-element.114), channel_id=1, source_target_pairs={{0,1},{1,2},{2,3},{4,5},{5,6},{6,7},{8,9},{9,10},{10,11},{12,13},{... | collective-permute-start | bytes 3145736 | tf_op jit(solution)/shard_map/ppermute | solution.py:80
  684.8 36.5 %collective-permute-start.35 = (bf16[256,2048]{1,0:T(8,128)(2,1)S(1)}, bf16[256,2048]{1,0:T(8,128)(2,1)S(1)}, u32[]{:S(2)}, u32[]{:S(2)}) collective-permute-start(bf16[256,2048]{1,0:T(8,128)(2,1)S(1)} %fusion.26), channel_id=1, source_target_pairs={{1,0},{2,1},{3,2},{5,4},{6,5},{7,6},{9,8},{10,9},{11,10},{13,12},{... | collective-permute-start | bytes 3145736 | tf_op jit(solution)/shard_map/ppermute | solution.py:86
  725.4 41.2 %collective-permute-start.36 = (bf16[256,2048]{1,0:T(8,128)(2,1)S(1)}, bf16[256,2048]{1,0:T(8,128)(2,1)S(1)}, u32[]{:S(2)}, u32[]{:S(2)}) collective-permute-start(bf16[256,2048]{1,0:T(8,128)(2,1)S(1)} %convert_element_type.436), channel_id=1, source_target_pairs={{0,1},{1,2},{2,3},{4,5},{5,6},{6,7},{8,9},{9,10},{10,11},{12,13},{... | collective-permute-start | bytes 3145736 | tf_op jit(solution)/shard_map/ppermute | solution.py:55
  837.4 207.6 %all-to-all-start.2 = ((bf16[8,1024,256]{2,1,0:T(8,128)(2,1)}), bf16[8,1024,256]{2,1,0:T(8,128)(2,1)}, u32[]{:S(2)}, u32[]{:S(2)}) async-start(bf16[8,1024,256]{2,1,0:T(8,128)(2,1)} %bitcast.347), calls=%async_computation.6 | async-start | bytes 8388608 | tf_op jit(solution)/shard_map/all_to_all | solution.py:319
  842.1 241.1 %reduce-scatter.11.cloned.1.call-start = ((), (), s32[]{:S(2)}) async-start(), calls=%async_computation.15 | async-start | bytes 2433024 | tf_op jit(solution)/shard_map/reduce_scatter | solution.py:347
  1018.5 37.8 %collective-permute-start.45 = (bf16[256,2048]{1,0:T(8,128)(2,1)S(1)}, bf16[256,2048]{1,0:T(8,128)(2,1)}, u32[]{:S(2)}, u32[]{:S(2)}) collective-permute-start(bf16[256,2048]{1,0:T(8,128)(2,1)S(1)} %get-tuple-element.113), channel_id=1, source_target_pairs={{3,2},{7,6},{11,10},{15,14},{19,18},{23,22},{27,26},{31,30}} | collective-permute-start | bytes 3145736 | tf_op jit(solution)/shard_map/ppermute | solution.py:86
  1045.0 56.7 %all-to-all-start = ((bf16[8,256,1024]{2,1,0:T(8,128)(2,1)}), bf16[8,256,1024]{2,1,0:T(8,128)(2,1)}, u32[]{:S(2)}, u32[]{:S(2)}) async-start(bf16[8,256,1024]{2,1,0:T(8,128)(2,1)} %bitcast.363), calls=%async_computation.3 | async-start | bytes 8388608 | tf_op jit(solution)/shard_map/all_to_all | solution.py:309
  1064.8 50.9 %collective-permute-start.44 = (bf16[256,2048]{1,0:T(8,128)(2,1)}, bf16[256,2048]{1,0:T(8,128)(2,1)}, u32[]{:S(2)}, u32[]{:S(2)}) collective-permute-start(bf16[256,2048]{1,0:T(8,128)(2,1)} %get-tuple-element.110), channel_id=1, source_target_pairs={{0,1},{1,2},{2,3},{4,5},{5,6},{6,7},{8,9},{9,10},{10,11},{12,13},{... | collective-permute-start | bytes 3145736 | tf_op jit(solution)/shard_map/ppermute | solution.py:80
  (112 other events, 2523.6 us)
Sparse Core Ops, SparseCore 0:
  11.4 73.0 all-gather.17
  86.4 35.6 all-gather.7
  123.9 37.3 all-gather.9
  163.0 72.0 all-gather.15
  236.9 71.9 all-gather.13
  310.7 71.9 all-gather.11
  530.8 90.9 reduce-scatter.4
  625.3 92.2 reduce-scatter.6
  792.7 153.3 reduce-scatter.8
  1018.6 64.5 reduce-scatter.10

commit v6 on v5

--- a/solution.py
+++ b/solution.py
@@ -208,7 +208,6 @@
     mixture = jnp.einsum(
         "tef,efd->td", hidden_share, down_w, preferred_element_type=jnp.float32
     )
-    mixture_own = tp_scatter_sum(mixture, tp_size, jnp.bfloat16)
     grad_out = out_grad.astype(jnp.float32)
     hidden_grad = (
         jnp.einsum("td,efd->tef", grad_rows, down_w, preferred_element_type=jnp.float32)
@@ -230,15 +229,15 @@
     _, second_back = jax.vjp(rms_norm, residual, gain_ffn)
     residual_norm_grad, ffn_gain_part = second_back(ffn_in_own)
     residual_grad = grad_out + residual_norm_grad
-    residual_grad, mixture_own = lax.optimization_barrier((residual_grad, mixture_own))
     gate_grad, up_grad, down_grad = (
         lax.psum_scatter(
             part.astype(jnp.bfloat16), "fsdp", scatter_dimension=0, tiled=True
         ).astype(jnp.float32)
         for part in (gate_part, up_part, down_part)
     )
-    layer_out = (residual + mixture_own).astype(jnp.bfloat16)
     attn_out_grad = tp_gather(residual_grad.astype(jnp.bfloat16), tp_size)
+    attn_out_grad, mixture = lax.optimization_barrier((attn_out_grad, mixture))
+    mixture_own = tp_scatter_sum(mixture, tp_size, jnp.bfloat16)
     output_part = jnp.einsum(
         "gq,gd->qd", context_b, attn_out_grad, preferred_element_type=jnp.float32
     )
@@ -288,9 +287,10 @@
     attn_in_part = result + jnp.einsum(
         "gk,dk->gd", value_back, value_w, preferred_element_type=jnp.float32
     )
-    attn_in_part, down_grad, gate_grad, up_grad = lax.optimization_barrier(
-        (attn_in_part, down_grad, gate_grad, up_grad)
-    )
+    attn_in_part, down_grad, gate_grad, up_grad, mixture_own = lax.optimization_barrier(
+        (attn_in_part, down_grad, gate_grad, up_grad, mixture_own)
+    )
+    layer_out = (residual + mixture_own).astype(jnp.bfloat16)
     attn_in_grad = tp_scatter_sum(attn_in_part, tp_size, jnp.bfloat16)
     query_part = jnp.einsum("gd,gq->dq", attn_rows, query_back, preferred_element_type=jnp.float32)
     key_head_part = jnp.einsum("gd,gk->dk", attn_rows, key_back, preferred_element_type=jnp.float32)

time: 1160 us -> 1160 us (level)
  starting transfers between devices: 136 us -> 124 us
    ppermute x12, waiting for transfers between devices: 45.7 us -> 79.5 us  [tp_scatter_sum(): lax.ppermute(outgoing.astype(send_type), 'tp', [(i, i - 1) for i in range...]
    ppermute x12, starting transfers between devices: 47.3 us -> 30.7 us  [tp_gather(): lax.ppermute(going_right, 'tp', [(i, i + 1) for i in range(step - 1, coun...]
    unnamed x180 -> x221, local copies, waits for them, and re-layouts: 25.1 us -> 23.3 us
  transfers between devices with their start and end apart: 61 -> 61, of which waited for: 30 -> 29; matrix products, arithmetic and copies ran while one was open for 42% -> 42% of each run, Pallas kernels for 0% -> 0%
where the time goes in v6:
time: 1160 us; the launch traced here: 1150 us
  waiting for transfers between devices  445 us (38%)
  matrix products  328 us (28%)
  other arithmetic  171 us (15%)
  starting transfers between devices  124 us (11%)
  local copies, waits for them, and re-layouts  68.6 us (6%)
  between operations  17.3 us (1%)
    ppermute x12, waiting for transfers between devices, tp_gather(): lax.ppermute(going_left, 'tp', [(i + 1, i) for i in range(0, count - step)])  152 us
    ppermute x12, waiting for transfers between devices, tp_scatter_sum(): lax.ppermute(outgoing.astype(send_type), 'tp', [(i, i + 1) for i in range...  129 us
    ppermute x12, waiting for transfers between devices, tp_scatter_sum(): lax.ppermute(outgoing.astype(send_type), 'tp', [(i, i - 1) for i in range...  79.5 us
    ppermute x12, waiting for transfers between devices, tp_gather(): lax.ppermute(going_right, 'tp', [(i, i + 1) for i in range(step - 1, coun...  51.1 us
    ppermute x12, starting transfers between devices, tp_scatter_sum(): lax.ppermute(outgoing.astype(send_type), 'tp', [(i, i + 1) for i in range...  48.6 us
    unnamed x2, matrix products  38.1 us
    convert_element_type x12, other arithmetic, tp_scatter_sum(): outgoing.astype(send_type)  30.8 us
    ppermute x12, starting transfers between devices, tp_gather(): lax.ppermute(going_right, 'tp', [(i, i + 1) for i in range(step - 1, coun...  30.7 us
  transfers between devices with their start and end apart: 61, of which 29 were waited for; matrix products, arithmetic and copies ran while one was open for 42% of the time, Pallas kernels for 0%

profile of v6, /device:TPU:0, one launch (start us, length us, event | category | flops | bytes accessed | tf_op | source)
XLA Modules:
  0.0 1153.5 jit_solution(6215665433846758460)
XLA Ops:
  18.7 27.4 %collective-permute-done = bf16[256,2048]{1,0:T(8,128)(2,1)S(1)} collective-permute-done((bf16[256,2048]{1,0:T(8,128)(2,1)S(1)}, bf16[256,2048]{1,0:T(8,128)(2,1)S(1)}, u32[]{:S(2)}, u32[]{:S(2)}) %collective-permute-start) | collective-permute-done | bytes 1048608 | tf_op jit(solution)/shard_map/ppermute | solution.py:55
  55.5 34.1 %collective-permute-done.4 = bf16[256,2048]{1,0:T(8,128)(2,1)} collective-permute-done((bf16[256,2048]{1,0:T(8,128)(2,1)S(1)}, bf16[256,2048]{1,0:T(8,128)(2,1)}, u32[]{:S(2)}, u32[]{:S(2)}) %collective-permute-start.4) | collective-permute-done | bytes 1048608 | tf_op jit(solution)/shard_map/ppermute | solution.py:58
  95.3 19.2 %collective-permute-done.5 = bf16[256,2048]{1,0:T(8,128)(2,1)S(1)} collective-permute-done((bf16[256,2048]{1,0:T(8,128)(2,1)}, bf16[256,2048]{1,0:T(8,128)(2,1)S(1)}, u32[]{:S(2)}, u32[]{:S(2)}) %collective-permute-start.5) | collective-permute-done | bytes 1048608 | tf_op jit(solution)/shard_map/ppermute | solution.py:58
  237.1 18.9 %collective-permute-done.11 = bf16[256,2048]{1,0:T(8,128)(2,1)S(1)} collective-permute-done((bf16[256,2048]{1,0:T(8,128)(2,1)S(1)}, bf16[256,2048]{1,0:T(8,128)(2,1)S(1)}, u32[]{:S(2)}, u32[]{:S(2)}) %collective-permute-start.11) | collective-permute-done | bytes 1048608 | tf_op jit(solution)/shard_map/ppermute | solution.py:58
  272.7 16.8 %collective-permute-done.12 = bf16[256,2048]{1,0:T(8,128)(2,1)} collective-permute-done((bf16[256,2048]{1,0:T(8,128)(2,1)}, bf16[256,2048]{1,0:T(8,128)(2,1)}, u32[]{:S(2)}, u32[]{:S(2)}) %collective-permute-start.12) | collective-permute-done | bytes 1048608 | tf_op jit(solution)/shard_map/ppermute | solution.py:80
  298.2 16.6 %collective-permute-done.13 = bf16[256,2048]{1,0:T(8,128)(2,1)} collective-permute-done((bf16[256,2048]{1,0:T(8,128)(2,1)}, bf16[256,2048]{1,0:T(8,128)(2,1)}, u32[]{:S(2)}, u32[]{:S(2)}) %collective-permute-start.13) | collective-permute-done | bytes 1048608 | tf_op jit(solution)/shard_map/ppermute | solution.py:80
  341.0 21.6 %collective-permute-done.17 = bf16[256,2048]{1,0:T(8,128)(2,1)} collective-permute-done((bf16[256,2048]{1,0:T(8,128)(2,1)S(1)}, bf16[256,2048]{1,0:T(8,128)(2,1)}, u32[]{:S(2)}, u32[]{:S(2)}) %collective-permute-start.17) | collective-permute-done | bytes 1048608 | tf_op jit(solution)/shard_map/ppermute | solution.py:86
  394.8 21.2 %collective-permute-done.22 = bf16[256,2048]{1,0:T(8,128)(2,1)S(1)} collective-permute-done((bf16[256,2048]{1,0:T(8,128)(2,1)S(1)}, bf16[256,2048]{1,0:T(8,128)(2,1)S(1)}, u32[]{:S(2)}, u32[]{:S(2)}) %collective-permute-start.22) | collective-permute-done | bytes 1048608 | tf_op jit(solution)/shard_map/ppermute | solution.py:58
  436.0 19.1 %fusion.103 = f32[1024,3072]{0,1} fusion(bf16[1024,2048]{1,0:T(8,128)(2,1)} %bitcast.361, bf16[2048,3072]{0,1:T(8,128)(2,1)} %bitcast.385), kind=kOutput, calls=%fused_computation.254 | convolution fusion | flops 12884901888 | bytes 29360128
  455.1 19.0 %fusion.102 = f32[1024,3072]{0,1} fusion(bf16[1024,2048]{1,0:T(8,128)(2,1)} %bitcast.362, bf16[2048,3072]{0,1:T(8,128)(2,1)} %bitcast.386), kind=kOutput, calls=%fused_computation.253 | convolution fusion | flops 12884901888 | bytes 29360128
  474.2 19.3 %fusion.12 = f32[1024,16,192]{0,2,1:T(8,128)} fusion(bf16[16,192,2048]{2,1,0:T(8,128)(2,1)} %all-gather.12.cloned.1.call-done, bf16[1024,2048]{1,0:T(8,128)(2,1)} %bitcast.359), kind=kOutput, calls=%fused_computation.36 | convolution fusion | flops 12884901888 | bytes 29360128 | tf_op jit(solution)/shard_map/td,efd->tef/dot_general | solution.py:213
  493.4 20.4 %multiply_convert_fusion = (bf16[1024,16,192]{0,2,1:T(8,128)(2,1)}, bf16[1024,16,192]{0,2,1:T(8,128)(2,1)}, bf16[1024,16,192]{0,2,1:T(8,128)(2,1)}) fusion(f32[1024,16,192]{0,2,1:T(8,128)} %bitcast.352, f32[1024,16]{0,1:T(8,128)S(1)} %select_reduce_fusion, f32[1024,16,192]{0,2,1:T(8,128)S(1)} %bitcast.351, f32[1024,16,192]{0,2,1:T(8,128)} %fusion.12), kind=kLoop, calls=%fused_computation.16 | loop fusion | flops 59768832 | bytes 56688640 | tf_op jit(solution)/shard_map/convert_element_type | solution.py:207
  513.8 19.2 %convolution_convert_fusion = bf16[16,192,2048]{2,1,0:T(8,128)(2,1)} fusion(bf16[1024,16,192]{0,2,1:T(8,128)(2,1)} %get-tuple-element.109, bf16[1024,2048]{1,0:T(8,128)(2,1)} %bitcast.360), kind=kOutput, calls=%fused_computation.30 | convolution fusion | flops 12891193344 | bytes 23068672 | tf_op jit(solution)/shard_map/tef,td->efd/dot_general | solution.py:225
  533.1 19.7 %convert_bitcast_fusion.1 = bf16[16,2048,192]{1,2,0:T(8,128)(2,1)} fusion(bf16[1024,16,192]{0,2,1:T(8,128)(2,1)} %get-tuple-element.110, bf16[1024,2048,1]{1,0,2:T(8,128)(2,1)} %bitcast.363), kind=kOutput, calls=%fused_computation.15 | convolution fusion | flops 12891193344 | bytes 23068672 | tf_op jit(solution)/shard_map/td,tef->edf/dot_general | solution.py:223
  552.9 17.7 %fusion.104 = f32[1024,2048,1]{1,0,2:T(8,128)S(1)} fusion(bf16[1024,16,192]{0,2,1:T(8,128)(2,1)} %get-tuple-element.110, bf16[16,2048,192]{1,2,0:T(8,128)(2,1)} %all-gather.16.cloned.1.call-done), kind=kOutput, calls=%fused_computation.255 | convolution fusion | flops 12884901888 | bytes 27262976 | tf_op jit(solution)/shard_map/tef,edf->td/dot_general | solution.py:220
  570.6 19.3 %bitcast_add_fusion = f32[1024,2048]{1,0:T(8,128)S(1)} fusion(f32[1024,2048,1]{1,0,2:T(8,128)S(1)} %fusion.104, bf16[1024,16,192]{0,2,1:T(8,128)(2,1)} %get-tuple-element.111, bf16[16,2048,192]{1,2,0:T(8,128)(2,1)} %all-gather.14.cloned.1.call-done), kind=kOutput, calls=%fused_computation.22 | convolution fusion | flops 12886999040 | bytes 35651584 | tf_op jit(solution)/shard_map/tef,edf->td/dot_general | solution.py:222
  592.3 17.8 %collective-permute-done.24 = bf16[256,2048]{1,0:T(8,128)(2,1)S(1)} collective-permute-done((bf16[256,2048]{1,0:T(8,128)(2,1)S(1)}, bf16[256,2048]{1,0:T(8,128)(2,1)S(1)}, u32[]{:S(2)}, u32[]{:S(2)}) %collective-permute-start.24) | collective-permute-done | bytes 1048608 | tf_op jit(solution)/shard_map/ppermute | solution.py:80
  615.2 16.3 %collective-permute-done.25 = bf16[256,2048]{1,0:T(8,128)(2,1)S(1)} collective-permute-done((bf16[256,2048]{1,0:T(8,128)(2,1)S(1)}, bf16[256,2048]{1,0:T(8,128)(2,1)S(1)}, u32[]{:S(2)}, u32[]{:S(2)}) %collective-permute-start.25) | collective-permute-done | bytes 1048608 | tf_op jit(solution)/shard_map/ppermute | solution.py:80
  651.5 25.7 %collective-permute-done.29 = bf16[256,2048]{1,0:T(8,128)(2,1)S(1)} collective-permute-done((bf16[256,2048]{1,0:T(8,128)(2,1)S(1)}, bf16[256,2048]{1,0:T(8,128)(2,1)S(1)}, u32[]{:S(2)}, u32[]{:S(2)}) %collective-permute-start.29) | collective-permute-done | bytes 1048608 | tf_op jit(solution)/shard_map/ppermute | solution.py:86
  717.8 19.0 %convolution_bitcast_fusion = f32[1024,2048]{1,0:T(8,128)} fusion(bf16[1024,16,192]{0,2,1:T(8,128)(2,1)} %get-tuple-element.109, bf16[16,192,2048]{2,1,0:T(8,128)(2,1)} %all-gather.12.cloned.1.call-done), kind=kOutput, calls=%fused_computation.32 | convolution fusion | flops 12884901888 | bytes 27262976 | tf_op jit(solution)/shard_map/tef,efd->td/dot_general | solution.py:208
  796.6 26.0 %fusion = (f32[8,1024]{1,0:T(8,128)S(1)}, f32[1024,1024,8]{1,0,2:T(8,128)}) fusion(f32[8,1024,1024]{1,2,0:T(8,128)} %get-tuple-element.159, f32[8,1024]{1,0:T(8,128)S(1)} %log_add_fusion, bf16[1024,128,1]{1,0,2:T(8,128)(2,1)S(1)} %copy-done.58, bf16[1024,8,128]{0,2,1:T(8,128)(2,1)S(1)} %bitcast.353), kind=kOutput, calls=%fused_computation.2 | convolution fusion | flops 2172641280 | bytes 69533696 | tf_op jit(solution)/shard_map/while/body/eval_jaxpr/qhd,kd->hqk/dot_general | solution.py:260
  822.6 29.3 %fusion.2 = bf16[8,1024,1024]{1,2,0:T(8,128)(2,1)} fusion(f32[1024,1024,8]{1,0,2:T(8,128)} %get-tuple-element.161, f32[8,1024,1024]{1,2,0:T(8,128)} %get-tuple-element.159, f32[8,1024]{1,0:T(8,128)S(1)} %get-tuple-element.160, f32[8,1024]{1,0:T(8,128)S(1)} %log_add_fusion), kind=kLoop, calls=%fused_computation.4 | loop fusion | flops 33554432 | bytes 83951616 | tf_op jit(solution)/shard_map/while/body/eval_jaxpr/convert_element_type | solution.py:265
  915.6 16.0 %collective-permute-done.37 = bf16[256,2048]{1,0:T(8,128)(2,1)S(1)} collective-permute-done((bf16[256,2048]{1,0:T(8,128)(2,1)S(1)}, bf16[256,2048]{1,0:T(8,128)(2,1)S(1)}, u32[]{:S(2)}, u32[]{:S(2)}) %collective-permute-start.37) | collective-permute-done | bytes 1048608 | tf_op jit(solution)/shard_map/ppermute | solution.py:80
  1119.8 18.0 %collective-permute-done.47 = bf16[256,2048]{1,0:T(8,128)(2,1)} collective-permute-done((bf16[256,2048]{1,0:T(8,128)(2,1)}, bf16[256,2048]{1,0:T(8,128)(2,1)}, u32[]{:S(2)}, u32[]{:S(2)}) %collective-permute-start.47) | collective-permute-done | bytes 1048608 | tf_op jit(solution)/shard_map/ppermute | solution.py:86
  (462 shorter events, 638.7 us)
Async XLA Ops:
  7.2 111.2 %all-gather.18.cloned.1.call-start = ((), (), s32[]{:S(2)}) async-start(), calls=%async_computation.16 | async-start | bytes 4866048 | tf_op jit(solution)/shard_map/all_gather | solution.py:125
  9.7 144.0 %all-gather.8.cloned.1.call-start = ((), (), s32[]{:S(2)}) async-start(), calls=%async_computation.7 | async-start | bytes 4718592 | tf_op jit(solution)/shard_map/all_gather | solution.py:141
  10.4 248.1 %all-gather.10.cloned.1.call-start = ((), (), s32[]{:S(2)}) async-start(), calls=%async_computation.8 | async-start | bytes 4718592 | tf_op jit(solution)/shard_map/all_gather | solution.py:142
  11.2 424.9 %all-gather.16.cloned.1.call-start = ((), (), s32[]{:S(2)}) async-start(), calls=%async_computation.11 | async-start | bytes 14155776 | tf_op jit(solution)/shard_map/all_gather | solution.py:143
  11.7 443.4 %all-gather.14.cloned.1.call-start = ((), (), s32[]{:S(2)}) async-start(), calls=%async_computation.10 | async-start | bytes 14155776 | tf_op jit(solution)/shard_map/all_gather | solution.py:144
  12.3 461.8 %all-gather.12.cloned.1.call-start = ((), (), s32[]{:S(2)}) async-start(), calls=%async_computation.9 | async-start | bytes 14155776 | tf_op jit(solution)/shard_map/all_gather | solution.py:145
  51.4 38.2 %collective-permute-start.4 = (bf16[256,2048]{1,0:T(8,128)(2,1)S(1)}, bf16[256,2048]{1,0:T(8,128)(2,1)}, u32[]{:S(2)}, u32[]{:S(2)}) collective-permute-start(bf16[256,2048]{1,0:T(8,128)(2,1)S(1)} %collective-permute-done.3), channel_id=1, source_target_pairs={{1,0},{2,1},{5,4},{6,5},{9,8},{10,9},{13,12},{14,13},{17,16},{18,1... | collective-permute-start | bytes 3145736 | tf_op jit(solution)/shard_map/ppermute | solution.py:58
  52.7 38.2 %collective-permute-start.2 = (bf16[256,2048]{1,0:T(8,128)(2,1)}, bf16[256,2048]{1,0:T(8,128)(2,1)}, u32[]{:S(2)}, u32[]{:S(2)}) collective-permute-start(bf16[256,2048]{1,0:T(8,128)(2,1)} %collective-permute-done.1), channel_id=1, source_target_pairs={{2,3},{6,7},{10,11},{14,15},{18,19},{22,23},{26,27},{30,31}} | collective-permute-start | bytes 3145736 | tf_op jit(solution)/shard_map/ppermute | solution.py:55
  54.4 941.0 %reduce-scatter.5.cloned.1.call-start = ((), (), s32[]{:S(2)}) async-start(), calls=%async_computation.12 | async-start | bytes 14155776 | tf_op jit(solution)/shard_map/reduce_scatter | solution.py:233
  130.2 74.9 %collective-permute-start.9 = (bf16[256,2048]{1,0:T(8,128)(2,1)S(1)}, bf16[256,2048]{1,0:T(8,128)(2,1)}, u32[]{:S(2)}, u32[]{:S(2)}) collective-permute-start(bf16[256,2048]{1,0:T(8,128)(2,1)S(1)} %copy-done.28), channel_id=1, source_target_pairs={{1,0},{2,1},{3,2},{5,4},{6,5},{7,6},{9,8},{10,9},{11,10},{13,12},{... | collective-permute-start | bytes 3145736 | tf_op jit(solution)/shard_map/ppermute | solution.py:58
  131.5 58.0 %collective-permute-start.6 = (bf16[256,2048]{1,0:T(8,128)(2,1)S(1)}, bf16[256,2048]{1,0:T(8,128)(2,1)}, u32[]{:S(2)}, u32[]{:S(2)}) collective-permute-start(bf16[256,2048]{1,0:T(8,128)(2,1)S(1)} %copy-done.28), channel_id=1, source_target_pairs={{0,1},{1,2},{2,3},{4,5},{5,6},{6,7},{8,9},{9,10},{10,11},{12,13},{... | collective-permute-start | bytes 3145736 | tf_op jit(solution)/shard_map/ppermute | solution.py:55
  328.3 34.3 %collective-permute-start.17 = (bf16[256,2048]{1,0:T(8,128)(2,1)S(1)}, bf16[256,2048]{1,0:T(8,128)(2,1)}, u32[]{:S(2)}, u32[]{:S(2)}) collective-permute-start(bf16[256,2048]{1,0:T(8,128)(2,1)S(1)} %fusion.36), channel_id=1, source_target_pairs={{1,0},{2,1},{3,2},{5,4},{6,5},{7,6},{9,8},{10,9},{11,10},{13,12},{... | collective-permute-start | bytes 3145736 | tf_op jit(solution)/shard_map/ppermute | solution.py:86
  533.1 465.8 %reduce-scatter.7.cloned.1.call-start = ((), (), s32[]{:S(2)}) async-start(), calls=%async_computation.13 | async-start | bytes 14155776 | tf_op jit(solution)/shard_map/reduce_scatter | solution.py:233
  552.8 449.5 %reduce-scatter.9.cloned.1.call-start = ((), (), s32[]{:S(2)}) async-start(), calls=%async_computation.14 | async-start | bytes 14155776 | tf_op jit(solution)/shard_map/reduce_scatter | solution.py:233
  638.5 38.7 %collective-permute-start.29 = (bf16[256,2048]{1,0:T(8,128)(2,1)S(1)}, bf16[256,2048]{1,0:T(8,128)(2,1)S(1)}, u32[]{:S(2)}, u32[]{:S(2)}) collective-permute-start(bf16[256,2048]{1,0:T(8,128)(2,1)S(1)} %fusion.31), channel_id=1, source_target_pairs={{1,0},{2,1},{3,2},{5,4},{6,5},{7,6},{9,8},{10,9},{11,10},{13,12},{... | collective-permute-start | bytes 3145736 | tf_op jit(solution)/shard_map/ppermute | solution.py:86
  714.8 35.4 %collective-permute-start.34 = (bf16[256,2048]{1,0:T(8,128)(2,1)}, bf16[256,2048]{1,0:T(8,128)(2,1)}, u32[]{:S(2)}, u32[]{:S(2)}) collective-permute-start(bf16[256,2048]{1,0:T(8,128)(2,1)} %collective-permute-done.33), channel_id=1, source_target_pairs={{1,0},{2,1},{5,4},{6,5},{9,8},{10,9},{13,12},{14,13},{17,16},{18,1... | collective-permute-start | bytes 3145736 | tf_op jit(solution)/shard_map/ppermute | solution.py:58
  716.1 35.4 %collective-permute-start.32 = (bf16[256,2048]{1,0:T(8,128)(2,1)}, bf16[256,2048]{1,0:T(8,128)(2,1)}, u32[]{:S(2)}, u32[]{:S(2)}) collective-permute-start(bf16[256,2048]{1,0:T(8,128)(2,1)} %collective-permute-done.31), channel_id=1, source_target_pairs={{2,3},{6,7},{10,11},{14,15},{18,19},{22,23},{26,27},{30,31}} | collective-permute-start | bytes 3145736 | tf_op jit(solution)/shard_map/ppermute | solution.py:55
  775.9 273.4 %all-to-all-start.2 = ((bf16[8,1024,256]{2,1,0:T(8,128)(2,1)}), bf16[8,1024,256]{2,1,0:T(8,128)(2,1)}, u32[]{:S(2)}, u32[]{:S(2)}) async-start(bf16[8,1024,256]{2,1,0:T(8,128)(2,1)} %bitcast.349), calls=%async_computation.6 | async-start | bytes 8388608 | tf_op jit(solution)/shard_map/all_to_all | solution.py:319
  780.5 306.8 %reduce-scatter.11.cloned.1.call-start = ((), (), s32[]{:S(2)}) async-start(), calls=%async_computation.15 | async-start | bytes 2433024 | tf_op jit(solution)/shard_map/reduce_scatter | solution.py:347
  784.7 120.2 %collective-permute-start.36 = (bf16[256,2048]{1,0:T(8,128)(2,1)}, bf16[256,2048]{1,0:T(8,128)(2,1)}, u32[]{:S(2)}, u32[]{:S(2)}) collective-permute-start(bf16[256,2048]{1,0:T(8,128)(2,1)} %get-tuple-element.118), channel_id=1, source_target_pairs={{0,1},{4,5},{8,9},{12,13},{16,17},{20,21},{24,25},{28,29}} | collective-permute-start | bytes 3145736 | tf_op jit(solution)/shard_map/ppermute | solution.py:80
  787.5 128.2 %collective-permute-start.39 = (bf16[256,2048]{1,0:T(8,128)(2,1)}, bf16[256,2048]{1,0:T(8,128)(2,1)}, u32[]{:S(2)}, u32[]{:S(2)}) collective-permute-start(bf16[256,2048]{1,0:T(8,128)(2,1)} %get-tuple-element.119), channel_id=1, source_target_pairs={{3,2},{7,6},{11,10},{15,14},{19,18},{23,22},{27,26},{31,30}} | collective-permute-start | bytes 3145736 | tf_op jit(solution)/shard_map/ppermute | solution.py:86
  1049.2 56.6 %all-to-all-start = ((bf16[8,256,1024]{2,1,0:T(8,128)(2,1)}), bf16[8,256,1024]{2,1,0:T(8,128)(2,1)}, u32[]{:S(2)}, u32[]{:S(2)}) async-start(bf16[8,256,1024]{2,1,0:T(8,128)(2,1)} %bitcast.365), calls=%async_computation.3 | async-start | bytes 8388608 | tf_op jit(solution)/shard_map/all_to_all | solution.py:309
  1066.3 53.5 %collective-permute-start.44 = (bf16[256,2048]{1,0:T(8,128)(2,1)}, bf16[256,2048]{1,0:T(8,128)(2,1)}, u32[]{:S(2)}, u32[]{:S(2)}) collective-permute-start(bf16[256,2048]{1,0:T(8,128)(2,1)} %get-tuple-element.112), channel_id=1, source_target_pairs={{0,1},{1,2},{2,3},{4,5},{5,6},{6,7},{8,9},{9,10},{10,11},{12,13},{... | collective-permute-start | bytes 3145736 | tf_op jit(solution)/shard_map/ppermute | solution.py:80
  1071.7 37.6 %collective-permute-start.46 = (bf16[256,2048]{1,0:T(8,128)(2,1)S(1)}, bf16[256,2048]{1,0:T(8,128)(2,1)S(1)}, u32[]{:S(2)}, u32[]{:S(2)}) collective-permute-start(bf16[256,2048]{1,0:T(8,128)(2,1)S(1)} %get-tuple-element.113), channel_id=1, source_target_pairs={{2,1},{3,2},{6,5},{7,6},{10,9},{11,10},{14,13},{15,14},{18,17},{19... | collective-permute-start | bytes 3145736 | tf_op jit(solution)/shard_map/ppermute | solution.py:86
  (132 other events, 2699.5 us)
Sparse Core Ops, SparseCore 0:
  11.4 73.0 all-gather.17
  86.4 35.6 all-gather.7
  123.9 37.3 all-gather.9
  163.0 71.9 all-gather.15
  236.8 71.9 all-gather.13
  310.6 71.9 all-gather.11
  533.2 89.5 reduce-scatter.4
  626.3 92.2 reduce-scatter.6
  722.1 131.1 reduce-scatter.8
  1026.1 61.1 reduce-scatter.10

commit v7 on v5

--- a/solution.py
+++ b/solution.py
@@ -195,38 +195,84 @@
     )
     residual = tokens_f + attn_out
     ffn_in = rms_norm(residual, gain_ffn).astype(jnp.bfloat16)
-    ffn_rows = tp_gather(ffn_in, tp_size)
     expert_count = gate_w.shape[0]
     chosen = routes[:, :, None] == lax.iota(jnp.int32, expert_count)[None, None, :]
-    share = jnp.sum(jnp.where(chosen, route_weights[:, :, None], 0.0), axis=1)
-    gate_val = jnp.einsum("td,edf->tef", ffn_rows, gate_w, preferred_element_type=jnp.float32)
-    up_val = jnp.einsum("td,edf->tef", ffn_rows, up_w, preferred_element_type=jnp.float32)
-    sigma = jax.nn.sigmoid(gate_val)
-    active = gate_val * sigma
-    hidden = (active * up_val).astype(jnp.bfloat16)
-    hidden_share = (hidden.astype(jnp.float32) * share[:, :, None]).astype(jnp.bfloat16)
-    mixture = jnp.einsum(
-        "tef,efd->td", hidden_share, down_w, preferred_element_type=jnp.float32
-    )
-    mixture_own = tp_scatter_sum(mixture, tp_size, jnp.bfloat16)
+    share_all = jnp.sum(jnp.where(chosen, route_weights[:, :, None], 0.0), axis=1)
     grad_out = out_grad.astype(jnp.float32)
-    hidden_grad = (
-        jnp.einsum("td,efd->tef", grad_rows, down_w, preferred_element_type=jnp.float32)
-        * share[:, :, None]
-    )
-    gate_back = (hidden_grad * up_val * sigma * (1.0 + gate_val * (1.0 - sigma))).astype(
-        jnp.bfloat16
-    )
-    up_back = (hidden_grad * active).astype(jnp.bfloat16)
-    ffn_in_grad = jnp.einsum(
-        "tef,edf->td", gate_back, gate_w, preferred_element_type=jnp.float32
-    ) + jnp.einsum("tef,edf->td", up_back, up_w, preferred_element_type=jnp.float32)
+    chunks = 2
+    chunk_rows = tok_rows // chunks
+
+    def chunk_of(rows_all, index):
+        split = rows_all.reshape((tp_size, chunks, chunk_rows) + rows_all.shape[1:])
+        return split[:, index].reshape((tp_size * chunk_rows,) + rows_all.shape[1:])
+
+    rows_list = []
+    share_list = []
+    grad_list = []
+    hidden_list = []
+    gate_list = []
+    up_list = []
+    mixture_list = []
+    in_grad_list = []
+    previous_rows = None
+    previous_grad = None
+    for index in range(chunks):
+        ffn_piece = ffn_in[index * chunk_rows : (index + 1) * chunk_rows]
+        if previous_rows is not None:
+            ffn_piece, previous_rows = lax.optimization_barrier((ffn_piece, previous_rows))
+            rows_list[-1] = previous_rows
+        ffn_rows = tp_gather(ffn_piece, tp_size)
+        if previous_grad is not None:
+            ffn_rows, previous_grad = lax.optimization_barrier((ffn_rows, previous_grad))
+            in_grad_list[-1] = tp_scatter_sum(previous_grad, tp_size, jnp.bfloat16)
+        share = chunk_of(share_all, index)
+        grad_part = chunk_of(grad_rows, index)
+        gate_val = jnp.einsum(
+            "td,edf->tef", ffn_rows, gate_w, preferred_element_type=jnp.float32
+        )
+        up_val = jnp.einsum("td,edf->tef", ffn_rows, up_w, preferred_element_type=jnp.float32)
+        sigma = jax.nn.sigmoid(gate_val)
+        active = gate_val * sigma
+        hidden = (active * up_val).astype(jnp.bfloat16)
+        hidden_share = (hidden.astype(jnp.float32) * share[:, :, None]).astype(jnp.bfloat16)
+        mixture = jnp.einsum(
+            "tef,efd->td", hidden_share, down_w, preferred_element_type=jnp.float32
+        )
+        hidden_grad = (
+            jnp.einsum("td,efd->tef", grad_part, down_w, preferred_element_type=jnp.float32)
+            * share[:, :, None]
+        )
+        gate_back = (hidden_grad * up_val * sigma * (1.0 + gate_val * (1.0 - sigma))).astype(
+            jnp.bfloat16
+        )
+        up_back = (hidden_grad * active).astype(jnp.bfloat16)
+        ffn_in_grad = jnp.einsum(
+            "tef,edf->td", gate_back, gate_w, preferred_element_type=jnp.float32
+        ) + jnp.einsum("tef,edf->td", up_back, up_w, preferred_element_type=jnp.float32)
+        in_grad_list.append(None)
+        previous_grad = ffn_in_grad
+        mixture_list.append(mixture)
+        rows_list.append(ffn_rows)
+        previous_rows = ffn_rows
+        grad_list.append(grad_part)
+        hidden_list.append(hidden_share)
+        gate_list.append(gate_back)
+        up_list.append(up_back)
+    in_grad_list[-1] = tp_scatter_sum(previous_grad, tp_size, jnp.bfloat16)
+    ffn_rows = jnp.concatenate(rows_list, axis=0)
+    gate_back = jnp.concatenate(gate_list, axis=0)
+    up_back = jnp.concatenate(up_list, axis=0)
+    hidden_share = jnp.concatenate(hidden_list, axis=0)
+    grad_part = jnp.concatenate(grad_list, axis=0)
     gate_part = jnp.einsum("td,tef->edf", ffn_rows, gate_back, preferred_element_type=jnp.float32)
     up_part = jnp.einsum("td,tef->edf", ffn_rows, up_back, preferred_element_type=jnp.float32)
     down_part = jnp.einsum(
-        "tef,td->efd", hidden_share, grad_rows, preferred_element_type=jnp.float32
-    )
-    ffn_in_own = tp_scatter_sum(ffn_in_grad, tp_size, jnp.bfloat16)
+        "tef,td->efd", hidden_share, grad_part, preferred_element_type=jnp.float32
+    )
+    mixture_own = jnp.concatenate(
+        [tp_scatter_sum(part, tp_size, jnp.bfloat16) for part in mixture_list], axis=0
+    )
+    ffn_in_own = jnp.concatenate(in_grad_list, axis=0)
     _, second_back = jax.vjp(rms_norm, residual, gain_ffn)
     residual_norm_grad, ffn_gain_part = second_back(ffn_in_own)
     residual_grad = grad_out + residual_norm_grad

time: 1160 us -> 1190 us (1.026)
  starting transfers between devices: 136 us -> 169 us
  waiting for transfers between devices: 435 us -> 405 us
  matrix products: 332 us -> 356 us
  local copies, waits for them, and re-layouts: 64.7 us -> 78.3 us
    ppermute x12 -> x18, waiting for transfers between devices: 140 us -> 98 us  [tp_scatter_sum(): lax.ppermute(outgoing.astype(send_type), 'tp', [(i, i + 1) for i in range...]
    ppermute x12 -> x18, starting transfers between devices: 46.4 us -> 77.1 us  [tp_scatter_sum(): lax.ppermute(outgoing.astype(send_type), 'tp', [(i, i + 1) for i in range...]
    convert_element_type x1, other arithmetic: 20.4 us -> 5.62 us  [body(): (hidden.astype(jnp.float32) * share[:, :, None]).astype(jnp.bfloat16)]
    ppermute x12 -> x18, waiting for transfers between devices: 45.7 us -> 58.1 us  [tp_scatter_sum(): lax.ppermute(outgoing.astype(send_type), 'tp', [(i, i - 1) for i in range...]
    dot_general x2 -> x3, matrix products: 38.4 us -> 48.4 us  [the longest x2 29.6 us: body(): jnp.einsum('td,efd->tef', grad_part, down_w, preferred_element_type=jnp.f...]
    ppermute x12 -> x15, waiting for transfers between devices: 57.7 us -> 48.4 us  [tp_gather(): lax.ppermute(going_right, 'tp', [(i, i + 1) for i in range(step - 1, coun...]
    ppermute x12 -> x15, waiting for transfers between devices: 161 us -> 170 us  [tp_gather(): lax.ppermute(going_left, 'tp', [(i + 1, i) for i in range(0, count - step)])]
    ppermute x12 -> x15, starting transfers between devices: 47.3 us -> 39.2 us  [tp_gather(): lax.ppermute(going_right, 'tp', [(i, i + 1) for i in range(step - 1, coun...]
  transfers between devices with their start and end apart: 61 -> 79, of which waited for: 30 -> 35; matrix products, arithmetic and copies ran while one was open for 42% -> 40% of each run, Pallas kernels for 0% -> 0%
where the time goes in v7:
time: 1190 us; the launch traced here: 1180 us
  waiting for transfers between devices  405 us (34%)
  matrix products  356 us (30%)
  starting transfers between devices  169 us (14%)
  other arithmetic  154 us (13%)
  local copies, waits for them, and re-layouts  78.3 us (7%)
  between operations  17.7 us (1%)
    ppermute x15, waiting for transfers between devices, tp_gather(): lax.ppermute(going_left, 'tp', [(i + 1, i) for i in range(0, count - step)])  170 us
    ppermute x18, waiting for transfers between devices, tp_scatter_sum(): lax.ppermute(outgoing.astype(send_type), 'tp', [(i, i + 1) for i in range...  98 us
    ppermute x18, starting transfers between devices, tp_scatter_sum(): lax.ppermute(outgoing.astype(send_type), 'tp', [(i, i + 1) for i in range...  77.1 us
    ppermute x18, waiting for transfers between devices, tp_scatter_sum(): lax.ppermute(outgoing.astype(send_type), 'tp', [(i, i - 1) for i in range...  58.1 us
    ppermute x15, waiting for transfers between devices, tp_gather(): lax.ppermute(going_right, 'tp', [(i, i + 1) for i in range(step - 1, coun...  48.4 us
    unnamed x4, matrix products  43.3 us
    ppermute x15, starting transfers between devices, tp_gather(): lax.ppermute(going_right, 'tp', [(i, i + 1) for i in range(step - 1, coun...  39.2 us
    unnamed x221, local copies, waits for them, and re-layouts  29.9 us
  transfers between devices with their start and end apart: 79, of which 35 were waited for; matrix products, arithmetic and copies ran while one was open for 40% of the time, Pallas kernels for 0%

profile of v7, /device:TPU:0, one launch (start us, length us, event | category | flops | bytes accessed | tf_op | source)
XLA Modules:
  0.0 1180.8 jit_solution(3010894049716289091)
XLA Ops:
  18.7 27.4 %collective-permute-done = bf16[256,2048]{1,0:T(8,128)(2,1)S(1)} collective-permute-done((bf16[256,2048]{1,0:T(8,128)(2,1)S(1)}, bf16[256,2048]{1,0:T(8,128)(2,1)S(1)}, u32[]{:S(2)}, u32[]{:S(2)}) %collective-permute-start) | collective-permute-done | bytes 1048608 | tf_op jit(solution)/shard_map/ppermute | solution.py:55
  55.5 34.1 %collective-permute-done.4 = bf16[256,2048]{1,0:T(8,128)(2,1)} collective-permute-done((bf16[256,2048]{1,0:T(8,128)(2,1)S(1)}, bf16[256,2048]{1,0:T(8,128)(2,1)}, u32[]{:S(2)}, u32[]{:S(2)}) %collective-permute-start.4) | collective-permute-done | bytes 1048608 | tf_op jit(solution)/shard_map/ppermute | solution.py:58
  95.3 19.1 %collective-permute-done.5 = bf16[256,2048]{1,0:T(8,128)(2,1)S(1)} collective-permute-done((bf16[256,2048]{1,0:T(8,128)(2,1)}, bf16[256,2048]{1,0:T(8,128)(2,1)S(1)}, u32[]{:S(2)}, u32[]{:S(2)}) %collective-permute-start.5) | collective-permute-done | bytes 1048608 | tf_op jit(solution)/shard_map/ppermute | solution.py:58
  172.5 14.6 %fusion.126 = (f32[8,1024]{1,0:T(8,128)S(1)}, f32[8,1024,1024]{1,2,0:T(8,128)}) fusion(bf16[1024,8,64]{2,0,1:T(8,128)(2,1)S(1)} %get-tuple-element.133, bf16[1024,8,64]{2,0,1:T(8,128)(2,1)S(1)} %get-tuple-element.132, bf16[1024,64]{0,1:T(8,128)(2,1)S(1)} %get-tuple-element.159, bf16[1024,64]{0,1:T(8,128)(2,1)S(1)} %get-tuple-element.158, ...), kind=kOutput, calls=%fused_computation.313 | convolution fusion | flops 2177359872 | bytes 36995072 | tf_op jit(solution)/shard_map/while/body/eval_jaxpr/qhd,kd->hqk/dot_general | solution.py:42
  187.9 14.4 %fusion.3 = f32[8,1024]{1,0:T(8,128)S(1)} fusion(f32[8,1024,1024]{1,2,0:T(8,128)} %get-tuple-element.179, f32[8,1024]{1,0:T(8,128)S(1)} %get-tuple-element.178), kind=kLoop, calls=%fused_computation.9 | loop fusion | flops 16769024 | bytes 33619968 | tf_op jit(solution)/shard_map/while/body/eval_jaxpr/reduce_sum | solution.py:183
  204.6 14.1 %fusion.39 = bf16[128,8,1024]{2,0,1:T(8,128)(2,1)S(1)} fusion(bf16[1024,128,1]{1,0,2:T(8,128)(2,1)S(1)} %copy-done.51, f32[8,1024,1024]{1,2,0:T(8,128)} %get-tuple-element.179, f32[8,1024]{1,0:T(8,128)S(1)} %fusion.3, f32[8,1024]{1,0:T(8,128)S(1)} %get-tuple-element.178), kind=kOutput, calls=%fused_computation.113 | convolution fusion | flops 2173698048 | bytes 35979264 | tf_op jit(solution)/shard_map/while/body/eval_jaxpr/hqk,kd->qhd/dot_general | solution.py:185
  236.1 17.4 %collective-permute-done.11 = bf16[256,2048]{1,0:T(8,128)(2,1)S(1)} collective-permute-done((bf16[256,2048]{1,0:T(8,128)(2,1)S(1)}, bf16[256,2048]{1,0:T(8,128)(2,1)S(1)}, u32[]{:S(2)}, u32[]{:S(2)}) %collective-permute-start.11) | collective-permute-done | bytes 1048608 | tf_op jit(solution)/shard_map/ppermute | solution.py:58
  270.3 16.6 %collective-permute-done.12 = bf16[256,2048]{1,0:T(8,128)(2,1)} collective-permute-done((bf16[256,2048]{1,0:T(8,128)(2,1)}, bf16[256,2048]{1,0:T(8,128)(2,1)}, u32[]{:S(2)}, u32[]{:S(2)}) %collective-permute-start.12) | collective-permute-done | bytes 1048608 | tf_op jit(solution)/shard_map/ppermute | solution.py:80
  295.5 16.5 %collective-permute-done.13 = bf16[256,2048]{1,0:T(8,128)(2,1)} collective-permute-done((bf16[256,2048]{1,0:T(8,128)(2,1)}, bf16[256,2048]{1,0:T(8,128)(2,1)}, u32[]{:S(2)}, u32[]{:S(2)}) %collective-permute-start.13) | collective-permute-done | bytes 1048608 | tf_op jit(solution)/shard_map/ppermute | solution.py:80
  338.3 22.1 %collective-permute-done.17 = bf16[256,2048]{1,0:T(8,128)(2,1)} collective-permute-done((bf16[256,2048]{1,0:T(8,128)(2,1)S(1)}, bf16[256,2048]{1,0:T(8,128)(2,1)}, u32[]{:S(2)}, u32[]{:S(2)}) %collective-permute-start.17) | collective-permute-done | bytes 1048608 | tf_op jit(solution)/shard_map/ppermute | solution.py:86
  385.4 14.6 %collective-permute-done.22 = bf16[128,2048]{1,0:T(8,128)(2,1)S(1)} collective-permute-done((bf16[128,2048]{1,0:T(8,128)(2,1)S(1)}, bf16[128,2048]{1,0:T(8,128)(2,1)S(1)}, u32[]{:S(2)}, u32[]{:S(2)}) %collective-permute-start.22) | collective-permute-done | bytes 524320 | tf_op jit(solution)/shard_map/ppermute | solution.py:58
  401.5 13.5 %collective-permute-done.23 = bf16[128,2048]{1,0:T(8,128)(2,1)S(1)} collective-permute-done((bf16[128,2048]{1,0:T(8,128)(2,1)S(1)}, bf16[128,2048]{1,0:T(8,128)(2,1)S(1)}, u32[]{:S(2)}, u32[]{:S(2)}) %collective-permute-start.23) | collective-permute-done | bytes 524320 | tf_op jit(solution)/shard_map/ppermute | solution.py:58
  540.8 18.9 %multiply_convert_fusion.1 = (bf16[512,16,192]{0,2,1:T(8,128)(2,1)}, bf16[512,16,192]{0,2,1:T(8,128)(2,1)}, bf16[512,16,192]{0,2,1:T(8,128)(2,1)}) fusion(f32[512,16,192]{0,2,1:T(8,128)} %bitcast.516, f32[512,16]{0,1:T(8,128)S(1)} %bitcast.505, f32[512,16,192]{0,2,1:T(8,128)} %bitcast.515, bf16[512,2048,1]{1,0,2:T(8,128)(2,1)S(1)} %bitcast.489, ...), kind=kOutput, calls=%fused_computation.34 | convolution fusion | flops 6472335360 | bytes 36732928 | tf_op jit(solution)/shard_map/td,efd->tef/dot_general | solution.py:242
  559.7 18.8 %convolution_convert_fusion = bf16[16,192,2048]{2,1,0:T(8,128)(2,1)} fusion(bf16[512,16,192]{0,2,1:T(8,128)(2,1)} %get-tuple-element.119, bf16[512,16,192]{0,2,1:T(8,128)(2,1)S(1)} %copy-done.33, bf16[512,2048]{1,0:T(8,128)(2,1)} %bitcast.488, bf16[512,2048]{1,0:T(8,128)(2,1)} %bitcast.491), kind=kOutput, calls=%fused_computation.23 | convolution fusion | flops 12912164864 | bytes 23068672 | tf_op jit(solution)/shard_map/tef,td->efd/dot_general | solution.py:269
  603.0 18.2 %convert_bitcast_fusion.1 = bf16[16,2048,192]{1,2,0:T(8,128)(2,1)} fusion(bf16[512,16,192]{0,2,1:T(8,128)(2,1)} %get-tuple-element.120, bf16[512,16,192]{0,2,1:T(8,128)(2,1)S(1)} %get-tuple-element.117, bf16[512,2048]{1,0:T(8,128)(2,1)} %bitcast.482, bf16[512,2048]{1,0:T(8,128)(2,1)S(1)} %bitcast.481), kind=kOutput, calls=%fused_computation.15 | convolution fusion | flops 12912164864 | bytes 23068672 | tf_op jit(solution)/shard_map/td,tef->edf/dot_general | solution.py:267
  737.1 14.2 %collective-permute-start.50 = (bf16[128,2048]{1,0:T(8,128)(2,1)S(1)}, bf16[128,2048]{1,0:T(8,128)(2,1)S(1)}, u32[]{:S(2)}, u32[]{:S(2)}) collective-permute-start(bf16[128,2048]{1,0:T(8,128)(2,1)S(1)} %get-tuple-element.138), channel_id=1, source_target_pairs={{0,1},{1,2},{2,3},{4,5},{5,6},{6,7},{8,9},{9,10},{10,11},{12,13},{... | collective-permute-start | bytes 1572872 | tf_op jit(solution)/shard_map/ppermute | solution.py:80
  814.2 18.8 %convert_bitcast_fusion = bf16[16,2048,192]{1,2,0:T(8,128)(2,1)} fusion(bf16[512,16,192]{0,2,1:T(8,128)(2,1)} %get-tuple-element.121, bf16[512,16,192]{0,2,1:T(8,128)(2,1)S(1)} %copy-done.32, bf16[512,2048]{1,0:T(8,128)(2,1)} %bitcast.483, bf16[512,2048]{1,0:T(8,128)(2,1)} %bitcast.480), kind=kOutput, calls=%fused_computation.14 | convolution fusion | flops 12912164864 | bytes 23068672 | tf_op jit(solution)/shard_map/td,tef->edf/dot_general | solution.py:268
  841.2 17.0 %collective-permute-done.59 = bf16[256,2048]{1,0:T(8,128)(2,1)S(1)} collective-permute-done((bf16[256,2048]{1,0:T(8,128)(2,1)}, bf16[256,2048]{1,0:T(8,128)(2,1)S(1)}, u32[]{:S(2)}, u32[]{:S(2)}) %collective-permute-start.59) | collective-permute-done | bytes 1048608 | tf_op jit(solution)/shard_map/ppermute | solution.py:58
  880.3 26.4 %fusion = (f32[8,1024]{1,0:T(8,128)S(1)}, f32[1024,1024,8]{1,0,2:T(8,128)}) fusion(f32[8,1024,1024]{1,2,0:T(8,128)} %get-tuple-element.179, f32[8,1024]{1,0:T(8,128)S(1)} %log_add_fusion, bf16[1024,128,1]{1,0,2:T(8,128)(2,1)S(1)} %copy-done.52, bf16[1024,8,128]{0,2,1:T(8,128)(2,1)S(1)} %bitcast.445), kind=kOutput, calls=%fused_computation.2 | convolution fusion | flops 2172641280 | bytes 69533696 | tf_op jit(solution)/shard_map/while/body/eval_jaxpr/qhd,kd->hqk/dot_general | solution.py:307
  906.7 29.6 %fusion.2 = bf16[8,1024,1024]{1,2,0:T(8,128)(2,1)} fusion(f32[1024,1024,8]{1,0,2:T(8,128)} %get-tuple-element.181, f32[8,1024,1024]{1,2,0:T(8,128)} %get-tuple-element.179, f32[8,1024]{1,0:T(8,128)S(1)} %get-tuple-element.180, f32[8,1024]{1,0:T(8,128)S(1)} %log_add_fusion), kind=kLoop, calls=%fused_computation.4 | loop fusion | flops 33554432 | bytes 83951616 | tf_op jit(solution)/shard_map/while/body/eval_jaxpr/convert_element_type | solution.py:312
  994.0 15.0 %fusion.44 = bf16[1024,128]{1,0:T(8,128)(2,1)S(1)} fusion(bf16[1024,8,128]{0,2,1:T(8,128)(2,1)S(1)} %bitcast.446, f32[8,1024,1024]{1,2,0:T(8,128)} %get-tuple-element.179, f32[8,1024]{1,0:T(8,128)S(1)} %log_add_fusion), kind=kOutput, calls=%fused_computation.119 | convolution fusion | flops 2164391936 | bytes 35946496 | tf_op jit(solution)/shard_map/while/body/eval_jaxpr/hqk,qhd->kd/dot_general | solution.py:301
  1102.4 13.1 %reduce-scatter.11.cloned.1.call-done = f32[264,256]{1,0:T(8,128)} async-done(((f32[2112,256]{1,0:T(8,128)}), f32[264,256]{1,0:T(8,128)}) %reduce-scatter.11.cloned.1.call-update) | async-done | bytes 270352 | tf_op jit(solution)/shard_map/reduce_scatter | solution.py:393
  1118.4 15.5 %all-to-all-done = bf16[8,256,1024]{2,1,0:T(8,128)(2,1)} async-done(((bf16[8,256,1024]{2,1,0:T(8,128)(2,1)}), bf16[8,256,1024]{2,1,0:T(8,128)(2,1)}, u32[]{:S(2)}, u32[]{:S(2)}) %all-to-all-start) | async-done | bytes 4194336 | tf_op jit(solution)/shard_map/all_to_all | solution.py:355
  1147.9 18.1 %collective-permute-done.65 = bf16[256,2048]{1,0:T(8,128)(2,1)} collective-permute-done((bf16[256,2048]{1,0:T(8,128)(2,1)}, bf16[256,2048]{1,0:T(8,128)(2,1)}, u32[]{:S(2)}, u32[]{:S(2)}) %collective-permute-start.65) | collective-permute-done | bytes 1048608 | tf_op jit(solution)/shard_map/ppermute | solution.py:86
  (524 shorter events, 715.0 us)
Async XLA Ops:
  7.2 111.3 %all-gather.18.cloned.1.call-start = ((), (), s32[]{:S(2)}) async-start(), calls=%async_computation.16 | async-start | bytes 4866048 | tf_op jit(solution)/shard_map/all_gather | solution.py:125
  9.7 141.8 %all-gather.8.cloned.1.call-start = ((), (), s32[]{:S(2)}) async-start(), calls=%async_computation.7 | async-start | bytes 4718592 | tf_op jit(solution)/shard_map/all_gather | solution.py:141
  10.4 245.5 %all-gather.10.cloned.1.call-start = ((), (), s32[]{:S(2)}) async-start(), calls=%async_computation.8 | async-start | bytes 4718592 | tf_op jit(solution)/shard_map/all_gather | solution.py:142
  11.2 447.3 %all-gather.16.cloned.1.call-start = ((), (), s32[]{:S(2)}) async-start(), calls=%async_computation.11 | async-start | bytes 14155776 | tf_op jit(solution)/shard_map/all_gather | solution.py:143
  11.7 458.1 %all-gather.14.cloned.1.call-start = ((), (), s32[]{:S(2)}) async-start(), calls=%async_computation.10 | async-start | bytes 14155776 | tf_op jit(solution)/shard_map/all_gather | solution.py:144
  12.3 469.0 %all-gather.12.cloned.1.call-start = ((), (), s32[]{:S(2)}) async-start(), calls=%async_computation.9 | async-start | bytes 14155776 | tf_op jit(solution)/shard_map/all_gather | solution.py:145
  51.4 38.2 %collective-permute-start.4 = (bf16[256,2048]{1,0:T(8,128)(2,1)S(1)}, bf16[256,2048]{1,0:T(8,128)(2,1)}, u32[]{:S(2)}, u32[]{:S(2)}) collective-permute-start(bf16[256,2048]{1,0:T(8,128)(2,1)S(1)} %collective-permute-done.3), channel_id=1, source_target_pairs={{1,0},{2,1},{5,4},{6,5},{9,8},{10,9},{13,12},{14,13},{17,16},{18,1... | collective-permute-start | bytes 3145736 | tf_op jit(solution)/shard_map/ppermute | solution.py:58
  52.7 38.2 %collective-permute-start.2 = (bf16[256,2048]{1,0:T(8,128)(2,1)}, bf16[256,2048]{1,0:T(8,128)(2,1)}, u32[]{:S(2)}, u32[]{:S(2)}) collective-permute-start(bf16[256,2048]{1,0:T(8,128)(2,1)} %collective-permute-done.1), channel_id=1, source_target_pairs={{2,3},{6,7},{10,11},{14,15},{18,19},{22,23},{26,27},{30,31}} | collective-permute-start | bytes 3145736 | tf_op jit(solution)/shard_map/ppermute | solution.py:55
  54.4 966.8 %reduce-scatter.5.cloned.1.call-start = ((), (), s32[]{:S(2)}) async-start(), calls=%async_computation.12 | async-start | bytes 14155776 | tf_op jit(solution)/shard_map/reduce_scatter | solution.py:281
  130.2 72.1 %collective-permute-start.9 = (bf16[256,2048]{1,0:T(8,128)(2,1)}, bf16[256,2048]{1,0:T(8,128)(2,1)}, u32[]{:S(2)}, u32[]{:S(2)}) collective-permute-start(bf16[256,2048]{1,0:T(8,128)(2,1)} %param.33), channel_id=1, source_target_pairs={{1,0},{2,1},{3,2},{5,4},{6,5},{7,6},{9,8},{10,9},{11,10},{13,12},{... | collective-permute-start | bytes 3145736 | tf_op jit(solution)/shard_map/ppermute | solution.py:58
  131.5 55.6 %collective-permute-start.6 = (bf16[256,2048]{1,0:T(8,128)(2,1)}, bf16[256,2048]{1,0:T(8,128)(2,1)}, u32[]{:S(2)}, u32[]{:S(2)}) collective-permute-start(bf16[256,2048]{1,0:T(8,128)(2,1)} %param.33), channel_id=1, source_target_pairs={{0,1},{1,2},{2,3},{4,5},{5,6},{6,7},{8,9},{9,10},{10,11},{12,13},{... | collective-permute-start | bytes 3145736 | tf_op jit(solution)/shard_map/ppermute | solution.py:55
  578.6 446.1 %reduce-scatter.7.cloned.1.call-start = ((), (), s32[]{:S(2)}) async-start(), calls=%async_computation.13 | async-start | bytes 14155776 | tf_op jit(solution)/shard_map/reduce_scatter | solution.py:281
  593.0 60.8 %collective-permute-start.42 = (bf16[128,2048]{1,0:T(8,128)(2,1)}, bf16[128,2048]{1,0:T(8,128)(2,1)}, u32[]{:S(2)}, u32[]{:S(2)}) collective-permute-start(bf16[128,2048]{1,0:T(8,128)(2,1)} %get-tuple-element.136), channel_id=1, source_target_pairs={{0,1},{4,5},{8,9},{12,13},{16,17},{20,21},{24,25},{28,29}} | collective-permute-start | bytes 1572872 | tf_op jit(solution)/shard_map/ppermute | solution.py:80
  595.2 79.0 %collective-permute-start.45 = (bf16[128,2048]{1,0:T(8,128)(2,1)}, bf16[128,2048]{1,0:T(8,128)(2,1)}, u32[]{:S(2)}, u32[]{:S(2)}) collective-permute-start(bf16[128,2048]{1,0:T(8,128)(2,1)} %get-tuple-element.137), channel_id=1, source_target_pairs={{3,2},{7,6},{11,10},{15,14},{19,18},{23,22},{27,26},{31,30}} | collective-permute-start | bytes 1572872 | tf_op jit(solution)/shard_map/ppermute | solution.py:86
  599.5 56.6 %collective-permute-start.30 = (bf16[128,2048]{1,0:T(8,128)(2,1)}, bf16[128,2048]{1,0:T(8,128)(2,1)}, u32[]{:S(2)}, u32[]{:S(2)}) collective-permute-start(bf16[128,2048]{1,0:T(8,128)(2,1)} %get-tuple-element.144), channel_id=1, source_target_pairs={{0,1},{4,5},{8,9},{12,13},{16,17},{20,21},{24,25},{28,29}} | collective-permute-start | bytes 1572872 | tf_op jit(solution)/shard_map/ppermute | solution.py:80
  601.6 85.4 %collective-permute-start.33 = (bf16[128,2048]{1,0:T(8,128)(2,1)}, bf16[128,2048]{1,0:T(8,128)(2,1)}, u32[]{:S(2)}, u32[]{:S(2)}) collective-permute-start(bf16[128,2048]{1,0:T(8,128)(2,1)} %get-tuple-element.145), channel_id=1, source_target_pairs={{3,2},{7,6},{11,10},{15,14},{19,18},{23,22},{27,26},{31,30}} | collective-permute-start | bytes 1572872 | tf_op jit(solution)/shard_map/ppermute | solution.py:86
  621.2 406.9 %reduce-scatter.9.cloned.1.call-start = ((), (), s32[]{:S(2)}) async-start(), calls=%async_computation.14 | async-start | bytes 14155776 | tf_op jit(solution)/shard_map/reduce_scatter | solution.py:281
  653.8 44.1 %collective-permute-start.39 = (bf16[128,2048]{1,0:T(8,128)(2,1)S(1)}, bf16[128,2048]{1,0:T(8,128)(2,1)S(1)}, u32[]{:S(2)}, u32[]{:S(2)}) collective-permute-start(bf16[128,2048]{1,0:T(8,128)(2,1)S(1)} %get-tuple-element.149), channel_id=1, source_target_pairs={{3,2},{7,6},{11,10},{15,14},{19,18},{23,22},{27,26},{31,30}} | collective-permute-start | bytes 1572872 | tf_op jit(solution)/shard_map/ppermute | solution.py:86
  692.2 70.7 %collective-permute-start.44 = (bf16[128,2048]{1,0:T(8,128)(2,1)S(1)}, bf16[128,2048]{1,0:T(8,128)(2,1)S(1)}, u32[]{:S(2)}, u32[]{:S(2)}) collective-permute-start(bf16[128,2048]{1,0:T(8,128)(2,1)S(1)} %get-tuple-element.134), channel_id=1, source_target_pairs={{0,1},{1,2},{2,3},{4,5},{5,6},{6,7},{8,9},{9,10},{10,11},{12,13},{... | collective-permute-start | bytes 1572872 | tf_op jit(solution)/shard_map/ppermute | solution.py:80
  722.6 39.4 %collective-permute-start.41 = (bf16[128,2048]{1,0:T(8,128)(2,1)S(1)}, bf16[128,2048]{1,0:T(8,128)(2,1)S(1)}, u32[]{:S(2)}, u32[]{:S(2)}) collective-permute-start(bf16[128,2048]{1,0:T(8,128)(2,1)S(1)} %fusion.63), channel_id=1, source_target_pairs={{1,0},{2,1},{3,2},{5,4},{6,5},{7,6},{9,8},{10,9},{11,10},{13,12},{... | collective-permute-start | bytes 1572872 | tf_op jit(solution)/shard_map/ppermute | solution.py:86
  867.5 209.7 %all-to-all-start.2 = ((bf16[8,1024,256]{2,1,0:T(8,128)(2,1)}), bf16[8,1024,256]{2,1,0:T(8,128)(2,1)}, u32[]{:S(2)}, u32[]{:S(2)}) async-start(bf16[8,1024,256]{2,1,0:T(8,128)(2,1)} %bitcast.443), calls=%async_computation.6 | async-start | bytes 8388608 | tf_op jit(solution)/shard_map/all_to_all | solution.py:365
  872.1 243.3 %reduce-scatter.11.cloned.1.call-start = ((), (), s32[]{:S(2)}) async-start(), calls=%async_computation.15 | async-start | bytes 2433024 | tf_op jit(solution)/shard_map/reduce_scatter | solution.py:393
  1077.2 56.7 %all-to-all-start = ((bf16[8,256,1024]{2,1,0:T(8,128)(2,1)}), bf16[8,256,1024]{2,1,0:T(8,128)(2,1)}, u32[]{:S(2)}, u32[]{:S(2)}) async-start(bf16[8,256,1024]{2,1,0:T(8,128)(2,1)} %bitcast.471), calls=%async_computation.3 | async-start | bytes 8388608 | tf_op jit(solution)/shard_map/all_to_all | solution.py:355
  1096.3 51.6 %collective-permute-start.62 = (bf16[256,2048]{1,0:T(8,128)(2,1)}, bf16[256,2048]{1,0:T(8,128)(2,1)}, u32[]{:S(2)}, u32[]{:S(2)}) collective-permute-start(bf16[256,2048]{1,0:T(8,128)(2,1)} %get-tuple-element.122), channel_id=1, source_target_pairs={{0,1},{1,2},{2,3},{4,5},{5,6},{6,7},{8,9},{9,10},{10,11},{12,13},{... | collective-permute-start | bytes 3145736 | tf_op jit(solution)/shard_map/ppermute | solution.py:80
  (146 other events, 2794.3 us)
Sparse Core Ops, SparseCore 0:
  11.4 73.0 all-gather.17
  86.4 35.6 all-gather.7
  123.9 37.4 all-gather.9
  163.1 71.9 all-gather.15
  236.8 71.9 all-gather.13
  310.6 71.9 all-gather.11
  578.7 90.8 reduce-scatter.4
  673.1 92.2 reduce-scatter.6
  833.1 150.5 reduce-scatter.8
  1051.2 64.1 reduce-scatter.10

commit v8 on v5

--- a/solution.py
+++ b/solution.py
@@ -218,9 +218,10 @@
         jnp.bfloat16
     )
     up_back = (hidden_grad * active).astype(jnp.bfloat16)
+    gate_tied, up_tied, mixture_own = lax.optimization_barrier((gate_back, up_back, mixture_own))
     ffn_in_grad = jnp.einsum(
-        "tef,edf->td", gate_back, gate_w, preferred_element_type=jnp.float32
-    ) + jnp.einsum("tef,edf->td", up_back, up_w, preferred_element_type=jnp.float32)
+        "tef,edf->td", gate_tied, gate_w, preferred_element_type=jnp.float32
+    ) + jnp.einsum("tef,edf->td", up_tied, up_w, preferred_element_type=jnp.float32)
     gate_part = jnp.einsum("td,tef->edf", ffn_rows, gate_back, preferred_element_type=jnp.float32)
     up_part = jnp.einsum("td,tef->edf", ffn_rows, up_back, preferred_element_type=jnp.float32)
     down_part = jnp.einsum(

time: 1160 us -> 1170 us (level)
  waiting for transfers between devices: 435 us -> 465 us
  starting transfers between devices: 136 us -> 121 us
    ppermute x12, waiting for transfers between devices: 45.7 us -> 75.5 us  [tp_scatter_sum(): lax.ppermute(outgoing.astype(send_type), 'tp', [(i, i - 1) for i in range...]
    ppermute x12, starting transfers between devices: 47.3 us -> 27.4 us  [tp_gather(): lax.ppermute(going_right, 'tp', [(i, i + 1) for i in range(step - 1, coun...]
    unnamed x180 -> x190, local copies, waits for them, and re-layouts: 25.1 us -> 26 us
  transfers between devices with their start and end apart: 61 -> 61, of which waited for: 30 -> 31; matrix products, arithmetic and copies ran while one was open for 42% -> 42% of each run, Pallas kernels for 0% -> 0%
where the time goes in v8:
time: 1170 us
  waiting for transfers between devices  465 us (40%)
  matrix products  330 us (28%)
  other arithmetic  168 us (14%)
  starting transfers between devices  121 us (10%)
  local copies, waits for them, and re-layouts  65.6 us (6%)
  between operations  17.2 us (1%)
    ppermute x12, waiting for transfers between devices, tp_gather(): lax.ppermute(going_left, 'tp', [(i + 1, i) for i in range(0, count - step)])  158 us
    ppermute x12, waiting for transfers between devices, tp_scatter_sum(): lax.ppermute(outgoing.astype(send_type), 'tp', [(i, i + 1) for i in range...  149 us
    ppermute x12, waiting for transfers between devices, tp_scatter_sum(): lax.ppermute(outgoing.astype(send_type), 'tp', [(i, i - 1) for i in range...  75.5 us
    ppermute x12, waiting for transfers between devices, tp_gather(): lax.ppermute(going_right, 'tp', [(i, i + 1) for i in range(step - 1, coun...  51.9 us
    ppermute x12, starting transfers between devices, tp_scatter_sum(): lax.ppermute(outgoing.astype(send_type), 'tp', [(i, i + 1) for i in range...  51.6 us
    unnamed x2, matrix products  38.2 us
    convert_element_type x1, other arithmetic, attend_back(): scores_grad = (attn_probs * (probs_grad - jnp.sum(attn_probs * probs_grad...  28.8 us
    ppermute x12, starting transfers between devices, tp_gather(): lax.ppermute(going_right, 'tp', [(i, i + 1) for i in range(step - 1, coun...  27.4 us
  transfers between devices with their start and end apart: 61, of which 31 were waited for; matrix products, arithmetic and copies ran while one was open for 42% of the time, Pallas kernels for 0%

profile of v8, /device:TPU:0, one launch (start us, length us, event | category | flops | bytes accessed | tf_op | source)
XLA Modules:
  0.0 1166.1 jit_solution(2701675980163585465)
XLA Ops:
  18.7 27.4 %collective-permute-done = bf16[256,2048]{1,0:T(8,128)(2,1)S(1)} collective-permute-done((bf16[256,2048]{1,0:T(8,128)(2,1)S(1)}, bf16[256,2048]{1,0:T(8,128)(2,1)S(1)}, u32[]{:S(2)}, u32[]{:S(2)}) %collective-permute-start) | collective-permute-done | bytes 1048608 | tf_op jit(solution)/shard_map/ppermute | solution.py:55
  55.6 34.0 %collective-permute-done.4 = bf16[256,2048]{1,0:T(8,128)(2,1)} collective-permute-done((bf16[256,2048]{1,0:T(8,128)(2,1)S(1)}, bf16[256,2048]{1,0:T(8,128)(2,1)}, u32[]{:S(2)}, u32[]{:S(2)}) %collective-permute-start.4) | collective-permute-done | bytes 1048608 | tf_op jit(solution)/shard_map/ppermute | solution.py:58
  95.3 19.1 %collective-permute-done.5 = bf16[256,2048]{1,0:T(8,128)(2,1)S(1)} collective-permute-done((bf16[256,2048]{1,0:T(8,128)(2,1)}, bf16[256,2048]{1,0:T(8,128)(2,1)S(1)}, u32[]{:S(2)}, u32[]{:S(2)}) %collective-permute-start.5) | collective-permute-done | bytes 1048608 | tf_op jit(solution)/shard_map/ppermute | solution.py:58
  235.4 17.7 %collective-permute-done.11 = bf16[256,2048]{1,0:T(8,128)(2,1)S(1)} collective-permute-done((bf16[256,2048]{1,0:T(8,128)(2,1)S(1)}, bf16[256,2048]{1,0:T(8,128)(2,1)S(1)}, u32[]{:S(2)}, u32[]{:S(2)}) %collective-permute-start.11) | collective-permute-done | bytes 1048608 | tf_op jit(solution)/shard_map/ppermute | solution.py:58
  269.8 16.8 %collective-permute-done.12 = bf16[256,2048]{1,0:T(8,128)(2,1)} collective-permute-done((bf16[256,2048]{1,0:T(8,128)(2,1)}, bf16[256,2048]{1,0:T(8,128)(2,1)}, u32[]{:S(2)}, u32[]{:S(2)}) %collective-permute-start.12) | collective-permute-done | bytes 1048608 | tf_op jit(solution)/shard_map/ppermute | solution.py:80
  338.2 22.2 %collective-permute-done.17 = bf16[256,2048]{1,0:T(8,128)(2,1)} collective-permute-done((bf16[256,2048]{1,0:T(8,128)(2,1)S(1)}, bf16[256,2048]{1,0:T(8,128)(2,1)}, u32[]{:S(2)}, u32[]{:S(2)}) %collective-permute-start.17) | collective-permute-done | bytes 1048608 | tf_op jit(solution)/shard_map/ppermute | solution.py:86
  392.7 21.2 %collective-permute-done.22 = bf16[256,2048]{1,0:T(8,128)(2,1)S(1)} collective-permute-done((bf16[256,2048]{1,0:T(8,128)(2,1)S(1)}, bf16[256,2048]{1,0:T(8,128)(2,1)S(1)}, u32[]{:S(2)}, u32[]{:S(2)}) %collective-permute-start.22) | collective-permute-done | bytes 1048608 | tf_op jit(solution)/shard_map/ppermute | solution.py:58
  433.7 19.1 %fusion.102 = f32[1024,3072]{0,1} fusion(bf16[1024,2048]{1,0:T(8,128)(2,1)} %bitcast.359, bf16[2048,3072]{0,1:T(8,128)(2,1)} %bitcast.385), kind=kOutput, calls=%fused_computation.252 | convolution fusion | flops 12884901888 | bytes 29360128
  452.8 19.1 %fusion.101 = f32[1024,3072]{0,1} fusion(bf16[1024,2048]{1,0:T(8,128)(2,1)} %bitcast.360, bf16[2048,3072]{0,1:T(8,128)(2,1)} %bitcast.386), kind=kOutput, calls=%fused_computation.251 | convolution fusion | flops 12884901888 | bytes 29360128
  471.9 19.3 %fusion.12 = f32[1024,16,192]{0,2,1:T(8,128)} fusion(bf16[16,192,2048]{2,1,0:T(8,128)(2,1)} %all-gather.12.cloned.1.call-done, bf16[1024,2048]{1,0:T(8,128)(2,1)} %bitcast.363), kind=kOutput, calls=%fused_computation.35 | convolution fusion | flops 12884901888 | bytes 29360128 | tf_op jit(solution)/shard_map/td,efd->tef/dot_general | solution.py:214
  491.2 20.3 %multiply_convert_fusion = (bf16[1024,16,192]{0,2,1:T(8,128)(2,1)}, bf16[1024,16,192]{0,2,1:T(8,128)(2,1)}, bf16[1024,16,192]{0,2,1:T(8,128)(2,1)}) fusion(f32[1024,16,192]{0,2,1:T(8,128)} %bitcast.350, f32[1024,16]{0,1:T(8,128)S(1)} %select_reduce_fusion, f32[1024,16,192]{0,2,1:T(8,128)S(1)} %bitcast.349, f32[1024,16,192]{0,2,1:T(8,128)} %fusion.12), kind=kLoop, calls=%fused_computation.16 | loop fusion | flops 59768832 | bytes 56688640 | tf_op jit(solution)/shard_map/convert_element_type | solution.py:207
  511.5 19.2 %convolution_convert_fusion = bf16[16,192,2048]{2,1,0:T(8,128)(2,1)} fusion(bf16[1024,16,192]{0,2,1:T(8,128)(2,1)} %get-tuple-element.113, bf16[1024,2048]{1,0:T(8,128)(2,1)} %bitcast.364), kind=kOutput, calls=%fused_computation.30 | convolution fusion | flops 12891193344 | bytes 23068672 | tf_op jit(solution)/shard_map/tef,td->efd/dot_general | solution.py:227
  530.8 17.8 %fusion.103 = f32[1024,2048,1]{1,0,2:T(8,128)S(1)} fusion(bf16[1024,16,192]{0,2,1:T(8,128)(2,1)} %get-tuple-element.113, bf16[16,192,2048]{2,1,0:T(8,128)(2,1)} %all-gather.12.cloned.1.call-done), kind=kOutput, calls=%fused_computation.253 | convolution fusion | flops 12884901888 | bytes 27262976 | tf_op jit(solution)/shard_map/tef,efd->td/dot_general | solution.py:208
  551.2 17.8 %collective-permute-done.24 = bf16[256,2048]{1,0:T(8,128)(2,1)S(1)} collective-permute-done((bf16[256,2048]{1,0:T(8,128)(2,1)S(1)}, bf16[256,2048]{1,0:T(8,128)(2,1)S(1)}, u32[]{:S(2)}, u32[]{:S(2)}) %collective-permute-start.24) | collective-permute-done | bytes 1048608 | tf_op jit(solution)/shard_map/ppermute | solution.py:80
  631.5 20.7 %fusion.104 = f32[1024,2048,1]{1,0,2:T(8,128)} fusion(bf16[1024,16,192]{0,2,1:T(8,128)(2,1)} %get-tuple-element.93, bf16[16,2048,192]{1,2,0:T(8,128)(2,1)} %all-gather.16.cloned.1.call-done), kind=kOutput, calls=%fused_computation.254 | convolution fusion | flops 12884901888 | bytes 27262976 | tf_op jit(solution)/shard_map/tef,edf->td/dot_general | solution.py:222
  652.2 17.3 %bitcast_add_fusion = f32[1024,2048]{1,0:T(8,128)S(1)} fusion(f32[1024,2048,1]{1,0,2:T(8,128)} %fusion.104, bf16[1024,16,192]{0,2,1:T(8,128)(2,1)S(1)} %bitcast.356, bf16[16,2048,192]{1,2,0:T(8,128)(2,1)} %all-gather.14.cloned.1.call-done), kind=kOutput, calls=%fused_computation.22 | convolution fusion | flops 12886999040 | bytes 35651584 | tf_op jit(solution)/shard_map/tef,edf->td/dot_general | solution.py:224
  674.8 20.6 %collective-permute-done.30 = bf16[256,2048]{1,0:T(8,128)(2,1)S(1)} collective-permute-done((bf16[256,2048]{1,0:T(8,128)(2,1)S(1)}, bf16[256,2048]{1,0:T(8,128)(2,1)S(1)}, u32[]{:S(2)}, u32[]{:S(2)}) %collective-permute-start.30) | collective-permute-done | bytes 1048608 | tf_op jit(solution)/shard_map/ppermute | solution.py:80
  700.2 20.6 %collective-permute-done.31 = bf16[256,2048]{1,0:T(8,128)(2,1)S(1)} collective-permute-done((bf16[256,2048]{1,0:T(8,128)(2,1)S(1)}, bf16[256,2048]{1,0:T(8,128)(2,1)S(1)}, u32[]{:S(2)}, u32[]{:S(2)}) %collective-permute-start.31) | collective-permute-done | bytes 1048608 | tf_op jit(solution)/shard_map/ppermute | solution.py:80
  739.7 28.3 %collective-permute-done.35 = bf16[256,2048]{1,0:T(8,128)(2,1)S(1)} collective-permute-done((bf16[256,2048]{1,0:T(8,128)(2,1)S(1)}, bf16[256,2048]{1,0:T(8,128)(2,1)S(1)}, u32[]{:S(2)}, u32[]{:S(2)}) %collective-permute-start.35) | collective-permute-done | bytes 1048608 | tf_op jit(solution)/shard_map/ppermute | solution.py:86
  796.6 18.5 %convert_bitcast_fusion = bf16[16,2048,192]{1,2,0:T(8,128)(2,1)} fusion(bf16[1024,16,192]{0,2,1:T(8,128)(2,1)} %get-tuple-element.94, bf16[1024,2048,1]{1,0,2:T(8,128)(2,1)S(1)} %bitcast.362), kind=kOutput, calls=%fused_computation.14 | convolution fusion | flops 12891193344 | bytes 23068672 | tf_op jit(solution)/shard_map/td,tef->edf/dot_general | solution.py:226
  823.4 22.3 %collective-permute-done.41 = bf16[256,2048]{1,0:T(8,128)(2,1)S(1)} collective-permute-done((bf16[256,2048]{1,0:T(8,128)(2,1)}, bf16[256,2048]{1,0:T(8,128)(2,1)S(1)}, u32[]{:S(2)}, u32[]{:S(2)}) %collective-permute-start.41) | collective-permute-done | bytes 1048608 | tf_op jit(solution)/shard_map/ppermute | solution.py:58
  868.5 26.2 %fusion = (f32[8,1024]{1,0:T(8,128)S(1)}, f32[1024,1024,8]{1,0,2:T(8,128)}) fusion(f32[8,1024,1024]{1,2,0:T(8,128)} %get-tuple-element.161, f32[8,1024]{1,0:T(8,128)S(1)} %log_add_fusion, bf16[1024,128,1]{1,0,2:T(8,128)(2,1)S(1)} %copy-done.44, bf16[1024,8,128]{0,2,1:T(8,128)(2,1)S(1)} %bitcast.351), kind=kOutput, calls=%fused_computation.2 | convolution fusion | flops 2172641280 | bytes 69533696 | tf_op jit(solution)/shard_map/while/body/eval_jaxpr/qhd,kd->hqk/dot_general | solution.py:262
  894.7 28.8 %fusion.2 = bf16[8,1024,1024]{1,2,0:T(8,128)(2,1)} fusion(f32[1024,1024,8]{1,0,2:T(8,128)} %get-tuple-element.163, f32[8,1024,1024]{1,2,0:T(8,128)} %get-tuple-element.161, f32[8,1024]{1,0:T(8,128)S(1)} %get-tuple-element.162, f32[8,1024]{1,0:T(8,128)S(1)} %log_add_fusion), kind=kLoop, calls=%fused_computation.4 | loop fusion | flops 33554432 | bytes 83951616 | tf_op jit(solution)/shard_map/while/body/eval_jaxpr/convert_element_type | solution.py:267
  1133.2 18.1 %collective-permute-done.47 = bf16[256,2048]{1,0:T(8,128)(2,1)} collective-permute-done((bf16[256,2048]{1,0:T(8,128)(2,1)}, bf16[256,2048]{1,0:T(8,128)(2,1)}, u32[]{:S(2)}, u32[]{:S(2)}) %collective-permute-start.47) | collective-permute-done | bytes 1048608 | tf_op jit(solution)/shard_map/ppermute | solution.py:86
  (434 shorter events, 636.6 us)
Async XLA Ops:
  7.2 111.2 %all-gather.18.cloned.1.call-start = ((), (), s32[]{:S(2)}) async-start(), calls=%async_computation.16 | async-start | bytes 4866048 | tf_op jit(solution)/shard_map/all_gather | solution.py:125
  9.7 141.4 %all-gather.8.cloned.1.call-start = ((), (), s32[]{:S(2)}) async-start(), calls=%async_computation.7 | async-start | bytes 4718592 | tf_op jit(solution)/shard_map/all_gather | solution.py:141
  10.4 245.2 %all-gather.10.cloned.1.call-start = ((), (), s32[]{:S(2)}) async-start(), calls=%async_computation.8 | async-start | bytes 4718592 | tf_op jit(solution)/shard_map/all_gather | solution.py:142
  11.2 422.6 %all-gather.16.cloned.1.call-start = ((), (), s32[]{:S(2)}) async-start(), calls=%async_computation.11 | async-start | bytes 14155776 | tf_op jit(solution)/shard_map/all_gather | solution.py:143
  11.7 441.1 %all-gather.14.cloned.1.call-start = ((), (), s32[]{:S(2)}) async-start(), calls=%async_computation.10 | async-start | bytes 14155776 | tf_op jit(solution)/shard_map/all_gather | solution.py:144
  12.3 459.6 %all-gather.12.cloned.1.call-start = ((), (), s32[]{:S(2)}) async-start(), calls=%async_computation.9 | async-start | bytes 14155776 | tf_op jit(solution)/shard_map/all_gather | solution.py:145
  12.4 33.7 %collective-permute-start = (bf16[256,2048]{1,0:T(8,128)(2,1)S(1)}, bf16[256,2048]{1,0:T(8,128)(2,1)S(1)}, u32[]{:S(2)}, u32[]{:S(2)}) collective-permute-start(bf16[256,2048]{1,0:T(8,128)(2,1)S(1)} %copy-done.15), channel_id=1, source_target_pairs={{0,1},{1,2},{2,3},{4,5},{5,6},{6,7},{8,9},{9,10},{10,11},{12,13},{... | collective-permute-start | bytes 3145736 | tf_op jit(solution)/shard_map/ppermute | solution.py:55
  17.4 34.0 %collective-permute-start.3 = (bf16[256,2048]{1,0:T(8,128)(2,1)S(1)}, bf16[256,2048]{1,0:T(8,128)(2,1)S(1)}, u32[]{:S(2)}, u32[]{:S(2)}) collective-permute-start(bf16[256,2048]{1,0:T(8,128)(2,1)S(1)} %copy-done.15), channel_id=1, source_target_pairs={{1,0},{2,1},{3,2},{5,4},{6,5},{7,6},{9,8},{10,9},{11,10},{13,12},{... | collective-permute-start | bytes 3145736 | tf_op jit(solution)/shard_map/ppermute | solution.py:58
  51.4 38.2 %collective-permute-start.4 = (bf16[256,2048]{1,0:T(8,128)(2,1)S(1)}, bf16[256,2048]{1,0:T(8,128)(2,1)}, u32[]{:S(2)}, u32[]{:S(2)}) collective-permute-start(bf16[256,2048]{1,0:T(8,128)(2,1)S(1)} %collective-permute-done.3), channel_id=1, source_target_pairs={{1,0},{2,1},{5,4},{6,5},{9,8},{10,9},{13,12},{14,13},{17,16},{18,1... | collective-permute-start | bytes 3145736 | tf_op jit(solution)/shard_map/ppermute | solution.py:58
  52.7 38.2 %collective-permute-start.2 = (bf16[256,2048]{1,0:T(8,128)(2,1)}, bf16[256,2048]{1,0:T(8,128)(2,1)}, u32[]{:S(2)}, u32[]{:S(2)}) collective-permute-start(bf16[256,2048]{1,0:T(8,128)(2,1)} %collective-permute-done.1), channel_id=1, source_target_pairs={{2,3},{6,7},{10,11},{14,15},{18,19},{22,23},{26,27},{30,31}} | collective-permute-start | bytes 3145736 | tf_op jit(solution)/shard_map/ppermute | solution.py:55
  54.5 953.8 %reduce-scatter.5.cloned.1.call-start = ((), (), s32[]{:S(2)}) async-start(), calls=%async_computation.12 | async-start | bytes 14155776 | tf_op jit(solution)/shard_map/reduce_scatter | solution.py:236
  130.1 71.8 %collective-permute-start.9 = (bf16[256,2048]{1,0:T(8,128)(2,1)}, bf16[256,2048]{1,0:T(8,128)(2,1)}, u32[]{:S(2)}, u32[]{:S(2)}) collective-permute-start(bf16[256,2048]{1,0:T(8,128)(2,1)} %param.33), channel_id=1, source_target_pairs={{1,0},{2,1},{3,2},{5,4},{6,5},{7,6},{9,8},{10,9},{11,10},{13,12},{... | collective-permute-start | bytes 3145736 | tf_op jit(solution)/shard_map/ppermute | solution.py:58
  131.4 55.1 %collective-permute-start.6 = (bf16[256,2048]{1,0:T(8,128)(2,1)}, bf16[256,2048]{1,0:T(8,128)(2,1)}, u32[]{:S(2)}, u32[]{:S(2)}) collective-permute-start(bf16[256,2048]{1,0:T(8,128)(2,1)} %param.33), channel_id=1, source_target_pairs={{0,1},{1,2},{2,3},{4,5},{5,6},{6,7},{8,9},{9,10},{10,11},{12,13},{... | collective-permute-start | bytes 3145736 | tf_op jit(solution)/shard_map/ppermute | solution.py:55
  324.8 35.7 %collective-permute-start.17 = (bf16[256,2048]{1,0:T(8,128)(2,1)S(1)}, bf16[256,2048]{1,0:T(8,128)(2,1)}, u32[]{:S(2)}, u32[]{:S(2)}) collective-permute-start(bf16[256,2048]{1,0:T(8,128)(2,1)S(1)} %fusion.36), channel_id=1, source_target_pairs={{1,0},{2,1},{3,2},{5,4},{6,5},{7,6},{9,8},{10,9},{11,10},{13,12},{... | collective-permute-start | bytes 3145736 | tf_op jit(solution)/shard_map/ppermute | solution.py:86
  530.7 481.0 %reduce-scatter.7.cloned.1.call-start = ((), (), s32[]{:S(2)}) async-start(), calls=%async_computation.13 | async-start | bytes 14155776 | tf_op jit(solution)/shard_map/reduce_scatter | solution.py:236
  603.6 411.5 %reduce-scatter.9.cloned.1.call-start = ((), (), s32[]{:S(2)}) async-start(), calls=%async_computation.14 | async-start | bytes 14155776 | tf_op jit(solution)/shard_map/reduce_scatter | solution.py:236
  727.8 40.1 %collective-permute-start.35 = (bf16[256,2048]{1,0:T(8,128)(2,1)S(1)}, bf16[256,2048]{1,0:T(8,128)(2,1)S(1)}, u32[]{:S(2)}, u32[]{:S(2)}) collective-permute-start(bf16[256,2048]{1,0:T(8,128)(2,1)S(1)} %fusion.26), channel_id=1, source_target_pairs={{1,0},{2,1},{3,2},{5,4},{6,5},{7,6},{9,8},{10,9},{11,10},{13,12},{... | collective-permute-start | bytes 3145736 | tf_op jit(solution)/shard_map/ppermute | solution.py:86
  815.5 30.2 %collective-permute-start.41 = (bf16[256,2048]{1,0:T(8,128)(2,1)}, bf16[256,2048]{1,0:T(8,128)(2,1)S(1)}, u32[]{:S(2)}, u32[]{:S(2)}) collective-permute-start(bf16[256,2048]{1,0:T(8,128)(2,1)} %collective-permute-done.40), channel_id=1, source_target_pairs={{1,0},{5,4},{9,8},{13,12},{17,16},{21,20},{25,24},{29,28}} | collective-permute-start | bytes 3145736 | tf_op jit(solution)/shard_map/ppermute | solution.py:58
  855.8 206.7 %all-to-all-start.2 = ((bf16[8,1024,256]{2,1,0:T(8,128)(2,1)}), bf16[8,1024,256]{2,1,0:T(8,128)(2,1)}, u32[]{:S(2)}, u32[]{:S(2)}) async-start(bf16[8,1024,256]{2,1,0:T(8,128)(2,1)} %bitcast.347), calls=%async_computation.6 | async-start | bytes 8388608 | tf_op jit(solution)/shard_map/all_to_all | solution.py:320
  860.4 240.4 %reduce-scatter.11.cloned.1.call-start = ((), (), s32[]{:S(2)}) async-start(), calls=%async_computation.15 | async-start | bytes 2433024 | tf_op jit(solution)/shard_map/reduce_scatter | solution.py:348
  1036.4 37.5 %collective-permute-start.45 = (bf16[256,2048]{1,0:T(8,128)(2,1)S(1)}, bf16[256,2048]{1,0:T(8,128)(2,1)}, u32[]{:S(2)}, u32[]{:S(2)}) collective-permute-start(bf16[256,2048]{1,0:T(8,128)(2,1)S(1)} %get-tuple-element.119), channel_id=1, source_target_pairs={{3,2},{7,6},{11,10},{15,14},{19,18},{23,22},{27,26},{31,30}} | collective-permute-start | bytes 3145736 | tf_op jit(solution)/shard_map/ppermute | solution.py:86
  1062.6 56.7 %all-to-all-start = ((bf16[8,256,1024]{2,1,0:T(8,128)(2,1)}), bf16[8,256,1024]{2,1,0:T(8,128)(2,1)}, u32[]{:S(2)}, u32[]{:S(2)}) async-start(bf16[8,256,1024]{2,1,0:T(8,128)(2,1)} %bitcast.365), calls=%async_computation.3 | async-start | bytes 8388608 | tf_op jit(solution)/shard_map/all_to_all | solution.py:310
  1081.9 51.4 %collective-permute-start.44 = (bf16[256,2048]{1,0:T(8,128)(2,1)}, bf16[256,2048]{1,0:T(8,128)(2,1)}, u32[]{:S(2)}, u32[]{:S(2)}) collective-permute-start(bf16[256,2048]{1,0:T(8,128)(2,1)} %get-tuple-element.116), channel_id=1, source_target_pairs={{0,1},{1,2},{2,3},{4,5},{5,6},{6,7},{8,9},{9,10},{10,11},{12,13},{... | collective-permute-start | bytes 3145736 | tf_op jit(solution)/shard_map/ppermute | solution.py:80
  1087.3 35.4 %collective-permute-start.46 = (bf16[256,2048]{1,0:T(8,128)(2,1)S(1)}, bf16[256,2048]{1,0:T(8,128)(2,1)S(1)}, u32[]{:S(2)}, u32[]{:S(2)}) collective-permute-start(bf16[256,2048]{1,0:T(8,128)(2,1)S(1)} %get-tuple-element.117), channel_id=1, source_target_pairs={{2,1},{3,2},{6,5},{7,6},{10,9},{11,10},{14,13},{15,14},{18,17},{19... | collective-permute-start | bytes 3145736 | tf_op jit(solution)/shard_map/ppermute | solution.py:86
  (117 other events, 2482.4 us)
Sparse Core Ops, SparseCore 0:
  11.4 73.0 all-gather.17
  86.4 35.5 all-gather.7
  123.9 37.3 all-gather.9
  163.1 72.0 all-gather.15
  236.9 71.9 all-gather.13
  310.7 71.9 all-gather.11
  530.8 90.8 reduce-scatter.4
  625.2 92.2 reduce-scatter.6
  815.2 151.8 reduce-scatter.8
  1036.5 64.1 reduce-scatter.10

commit v9 on v5

--- a/solution.py
+++ b/solution.py
@@ -181,13 +181,16 @@
         highest = jnp.max(scores, axis=-1, keepdims=True)
         expo = jnp.exp(scores - highest)
         denom = jnp.sum(expo, axis=-1, keepdims=True)
-        attn_probs = (expo / denom).astype(jnp.bfloat16)
+        probs_full = expo / denom
         context = jnp.einsum(
-            "hqk,kd->qhd", attn_probs, values_b, preferred_element_type=jnp.float32
-        )
-        return (context, (highest + jnp.log(denom))[..., 0])
-
-    context_all, log_sums = lax.map(attend, (query_seq, key_seq, value_seq, prefix_len))
+            "hqk,kd->qhd",
+            probs_full.astype(jnp.bfloat16),
+            values_b,
+            preferred_element_type=jnp.float32,
+        )
+        return (context, probs_full)
+
+    context_all, probs_all = lax.map(attend, (query_seq, key_seq, value_seq, prefix_len))
     context_b = context_all.reshape(group_rows, per_dev * HD).astype(jnp.bfloat16)
     context_b, grad_rows = lax.optimization_barrier((context_b, grad_rows))
     attn_out = tp_scatter_sum(
@@ -249,9 +252,7 @@
     )
 
     def attend_back(operands):
-        queries, keys_b, values_b, prefix_end, log_sum, ctx_grad = operands
-        scores = masked_scores(queries, keys_b, prefix_end, factor)
-        attn_probs = jnp.exp(scores - log_sum[..., None])
+        queries, keys_b, values_b, attn_probs, ctx_grad = operands
         value_grad = jnp.einsum(
             "hqk,qhd->kd",
             attn_probs.astype(jnp.bfloat16),
@@ -275,7 +276,7 @@
         return (query_grad, key_grad, value_grad)
 
     query_norm_grad, key_norm_grad, value_grad = lax.map(
-        attend_back, (query_seq, key_seq, value_seq, prefix_len, log_sums, context_grad)
+        attend_back, (query_seq, key_seq, value_seq, probs_all, context_grad)
     )
     query_raw_grad, key_raw_grad, query_gain_part, key_gain_part = prepare_back(
         (query_norm_grad.reshape(group_rows, per_dev, HD), key_norm_grad.reshape(group_rows, HD))

time: 1160 us -> 1150 us (level)
  other arithmetic: 164 us -> 151 us
    sub x0 -> x1, matrix products: none -> 20.4 us  [attend(): expo = jnp.exp(scores - highest)]
    dot_general x2 -> x1, matrix products: 28.7 us -> 12.2 us  [attend(): jnp.einsum('hqk,kd->qhd', probs_full.astype(jnp.bfloat16), values_b, pref...]
    reduce_sum x1 -> x0, other arithmetic: 14.7 us -> none  [attend(): denom = jnp.sum(expo, axis=-1, keepdims=True)]
    unnamed x180 -> x170, local copies, waits for them, and re-layouts: 25.1 us -> 24.2 us
  transfers between devices with their start and end apart: 61 -> 61, of which waited for: 30 -> 29; matrix products, arithmetic and copies ran while one was open for 42% -> 41% of each run, Pallas kernels for 0% -> 0%
where the time goes in v9:
time: 1150 us; the launch traced here: 1140 us
  waiting for transfers between devices  434 us (38%)
  matrix products  337 us (29%)
  other arithmetic  151 us (13%)
  starting transfers between devices  138 us (12%)
  local copies, waits for them, and re-layouts  62.8 us (5%)
  between operations  16.8 us (1%)
    ppermute x12, waiting for transfers between devices, tp_gather(): lax.ppermute(going_left, 'tp', [(i + 1, i) for i in range(0, count - step)])  163 us
    ppermute x12, waiting for transfers between devices, tp_scatter_sum(): lax.ppermute(outgoing.astype(send_type), 'tp', [(i, i + 1) for i in range...  135 us
    ppermute x12, waiting for transfers between devices, tp_gather(): lax.ppermute(going_right, 'tp', [(i, i + 1) for i in range(step - 1, coun...  57.8 us
    ppermute x12, starting transfers between devices, tp_gather(): lax.ppermute(going_right, 'tp', [(i, i + 1) for i in range(step - 1, coun...  49 us
    ppermute x12, waiting for transfers between devices, tp_scatter_sum(): lax.ppermute(outgoing.astype(send_type), 'tp', [(i, i - 1) for i in range...  46.9 us
    ppermute x12, starting transfers between devices, tp_scatter_sum(): lax.ppermute(outgoing.astype(send_type), 'tp', [(i, i + 1) for i in range...  46.8 us
    unnamed x2, matrix products  38.2 us
    convert_element_type x1, other arithmetic, attend_back(): scores_grad = (attn_probs * (probs_grad - jnp.sum(attn_probs * probs_grad...  28.6 us
  transfers between devices with their start and end apart: 61, of which 29 were waited for; matrix products, arithmetic and copies ran while one was open for 41% of the time, Pallas kernels for 0%

profile of v9, /device:TPU:0, one launch (start us, length us, event | category | flops | bytes accessed | tf_op | source)
XLA Modules:
  0.0 1139.2 jit_solution(2240131641863318879)
XLA Ops:
  18.7 27.4 %collective-permute-done = bf16[256,2048]{1,0:T(8,128)(2,1)S(1)} collective-permute-done((bf16[256,2048]{1,0:T(8,128)(2,1)S(1)}, bf16[256,2048]{1,0:T(8,128)(2,1)S(1)}, u32[]{:S(2)}, u32[]{:S(2)}) %collective-permute-start) | collective-permute-done | bytes 1048608 | tf_op jit(solution)/shard_map/ppermute | solution.py:55
  56.6 33.1 %collective-permute-done.4 = bf16[256,2048]{1,0:T(8,128)(2,1)} collective-permute-done((bf16[256,2048]{1,0:T(8,128)(2,1)S(1)}, bf16[256,2048]{1,0:T(8,128)(2,1)}, u32[]{:S(2)}, u32[]{:S(2)}) %collective-permute-start.4) | collective-permute-done | bytes 1048608 | tf_op jit(solution)/shard_map/ppermute | solution.py:58
  95.3 19.4 %collective-permute-done.5 = bf16[256,2048]{1,0:T(8,128)(2,1)S(1)} collective-permute-done((bf16[256,2048]{1,0:T(8,128)(2,1)}, bf16[256,2048]{1,0:T(8,128)(2,1)S(1)}, u32[]{:S(2)}, u32[]{:S(2)}) %collective-permute-start.5) | collective-permute-done | bytes 1048608 | tf_op jit(solution)/shard_map/ppermute | solution.py:58
  172.0 20.4 %fusion.111 = (f32[8,1024]{1,0:T(8,128)S(1)}, f32[8,1024,1024]{1,2,0:T(8,128)}) fusion(pred[1024,1024]{0,1:T(8,128)(4,1)} %fusion.17, bf16[1024,64]{0,1:T(8,128)(2,1)S(1)} %get-tuple-element.141, bf16[1024,64]{0,1:T(8,128)(2,1)S(1)} %get-tuple-element.142, bf16[1024,8,64]{2,0,1:T(8,128)(2,1)} %get-tuple-element.126, ...), kind=kOutput, calls=%fused_computation.255 | convolution fusion | flops 2185757696 | bytes 36995072 | tf_op jit(solution)/shard_map/while/body/eval_jaxpr/sub | solution.py:182
  263.7 16.4 %collective-permute-done.12 = bf16[256,2048]{1,0:T(8,128)(2,1)} collective-permute-done((bf16[256,2048]{1,0:T(8,128)(2,1)}, bf16[256,2048]{1,0:T(8,128)(2,1)}, u32[]{:S(2)}, u32[]{:S(2)}) %collective-permute-start.12) | collective-permute-done | bytes 1048608 | tf_op jit(solution)/shard_map/ppermute | solution.py:80
  330.9 21.4 %collective-permute-done.17 = bf16[256,2048]{1,0:T(8,128)(2,1)} collective-permute-done((bf16[256,2048]{1,0:T(8,128)(2,1)S(1)}, bf16[256,2048]{1,0:T(8,128)(2,1)}, u32[]{:S(2)}, u32[]{:S(2)}) %collective-permute-start.17) | collective-permute-done | bytes 1048608 | tf_op jit(solution)/shard_map/ppermute | solution.py:86
  385.2 21.2 %collective-permute-done.22 = bf16[256,2048]{1,0:T(8,128)(2,1)S(1)} collective-permute-done((bf16[256,2048]{1,0:T(8,128)(2,1)S(1)}, bf16[256,2048]{1,0:T(8,128)(2,1)S(1)}, u32[]{:S(2)}, u32[]{:S(2)}) %collective-permute-start.22) | collective-permute-done | bytes 1048608 | tf_op jit(solution)/shard_map/ppermute | solution.py:58
  426.8 19.1 %fusion.114 = f32[1024,3072]{0,1} fusion(bf16[1024,2048]{1,0:T(8,128)(2,1)} %bitcast.371, bf16[2048,3072]{0,1:T(8,128)(2,1)} %bitcast.397), kind=kOutput, calls=%fused_computation.258 | convolution fusion | flops 12884901888 | bytes 29360128
  445.9 19.1 %fusion.113 = f32[1024,3072]{0,1} fusion(bf16[1024,2048]{1,0:T(8,128)(2,1)} %bitcast.372, bf16[2048,3072]{0,1:T(8,128)(2,1)} %bitcast.398), kind=kOutput, calls=%fused_computation.257 | convolution fusion | flops 12884901888 | bytes 29360128
  465.0 19.3 %fusion.15 = f32[1024,16,192]{0,2,1:T(8,128)} fusion(bf16[16,192,2048]{2,1,0:T(8,128)(2,1)} %all-gather.12.cloned.1.call-done, bf16[1024,2048]{1,0:T(8,128)(2,1)} %bitcast.375), kind=kOutput, calls=%fused_computation.38 | convolution fusion | flops 12884901888 | bytes 29360128 | tf_op jit(solution)/shard_map/td,efd->tef/dot_general | solution.py:217
  484.4 20.5 %multiply_convert_fusion = (bf16[1024,16,192]{0,2,1:T(8,128)(2,1)}, bf16[1024,16,192]{0,2,1:T(8,128)(2,1)}, bf16[1024,16,192]{0,2,1:T(8,128)(2,1)}) fusion(f32[1024,16,192]{0,2,1:T(8,128)} %bitcast.366, f32[1024,16]{0,1:T(8,128)S(1)} %select_reduce_fusion, f32[1024,16,192]{0,2,1:T(8,128)S(1)} %bitcast.365, f32[1024,16,192]{0,2,1:T(8,128)} %fusion.15), kind=kLoop, calls=%fused_computation.15 | loop fusion | flops 59768832 | bytes 56688640 | tf_op jit(solution)/shard_map/convert_element_type | solution.py:210
  504.9 19.2 %convolution_convert_fusion = bf16[16,192,2048]{2,1,0:T(8,128)(2,1)} fusion(bf16[1024,16,192]{0,2,1:T(8,128)(2,1)} %get-tuple-element.104, bf16[1024,2048]{1,0:T(8,128)(2,1)} %bitcast.376), kind=kOutput, calls=%fused_computation.33 | convolution fusion | flops 12891193344 | bytes 23068672 | tf_op jit(solution)/shard_map/tef,td->efd/dot_general | solution.py:229
  524.2 19.3 %convert_bitcast_fusion.1 = bf16[16,2048,192]{1,2,0:T(8,128)(2,1)} fusion(bf16[1024,16,192]{0,2,1:T(8,128)(2,1)} %get-tuple-element.105, bf16[1024,2048,1]{1,0,2:T(8,128)(2,1)} %bitcast.373), kind=kOutput, calls=%fused_computation.14 | convolution fusion | flops 12891193344 | bytes 23068672 | tf_op jit(solution)/shard_map/td,tef->edf/dot_general | solution.py:227
  543.5 17.7 %fusion.115 = f32[1024,2048,1]{1,0,2:T(8,128)S(1)} fusion(bf16[1024,16,192]{0,2,1:T(8,128)(2,1)} %get-tuple-element.105, bf16[16,2048,192]{1,2,0:T(8,128)(2,1)} %all-gather.16.cloned.1.call-done), kind=kOutput, calls=%fused_computation.259 | convolution fusion | flops 12884901888 | bytes 27262976 | tf_op jit(solution)/shard_map/tef,edf->td/dot_general | solution.py:224
  561.2 19.3 %bitcast_add_fusion = f32[1024,2048]{1,0:T(8,128)S(1)} fusion(f32[1024,2048,1]{1,0,2:T(8,128)S(1)} %fusion.115, bf16[1024,16,192]{0,2,1:T(8,128)(2,1)} %get-tuple-element.106, bf16[16,2048,192]{1,2,0:T(8,128)(2,1)} %all-gather.14.cloned.1.call-done), kind=kOutput, calls=%fused_computation.21 | convolution fusion | flops 12886999040 | bytes 35651584 | tf_op jit(solution)/shard_map/tef,edf->td/dot_general | solution.py:226
  583.3 17.8 %fusion.116 = f32[1024,2048,1]{1,0,2:T(8,128)S(1)} fusion(bf16[1024,16,192]{0,2,1:T(8,128)(2,1)} %get-tuple-element.104, bf16[16,192,2048]{2,1,0:T(8,128)(2,1)} %all-gather.12.cloned.1.call-done), kind=kOutput, calls=%fused_computation.260 | convolution fusion | flops 12884901888 | bytes 27262976 | tf_op jit(solution)/shard_map/tef,efd->td/dot_general | solution.py:211
  606.1 20.1 %collective-permute-done.30 = bf16[256,2048]{1,0:T(8,128)(2,1)S(1)} collective-permute-done((bf16[256,2048]{1,0:T(8,128)(2,1)S(1)}, bf16[256,2048]{1,0:T(8,128)(2,1)S(1)}, u32[]{:S(2)}, u32[]{:S(2)}) %collective-permute-start.30) | collective-permute-done | bytes 1048608 | tf_op jit(solution)/shard_map/ppermute | solution.py:80
  630.9 17.7 %collective-permute-done.25 = bf16[256,2048]{1,0:T(8,128)(2,1)S(1)} collective-permute-done((bf16[256,2048]{1,0:T(8,128)(2,1)S(1)}, bf16[256,2048]{1,0:T(8,128)(2,1)S(1)}, u32[]{:S(2)}, u32[]{:S(2)}) %collective-permute-start.25) | collective-permute-done | bytes 1048608 | tf_op jit(solution)/shard_map/ppermute | solution.py:80
  719.8 22.2 %collective-permute-start.36 = (bf16[256,2048]{1,0:T(8,128)(2,1)S(1)}, bf16[256,2048]{1,0:T(8,128)(2,1)S(1)}, u32[]{:S(2)}, u32[]{:S(2)}) collective-permute-start(bf16[256,2048]{1,0:T(8,128)(2,1)S(1)} %convert_element_type.434), channel_id=1, source_target_pairs={{0,1},{1,2},{2,3},{4,5},{5,6},{6,7},{8,9},{9,10},{10,11},{12,13},{... | collective-permute-start | bytes 3145736 | tf_op jit(solution)/shard_map/ppermute | solution.py:55
  768.7 17.6 %convert_bitcast_fusion = bf16[16,2048,192]{1,2,0:T(8,128)(2,1)} fusion(bf16[1024,16,192]{0,2,1:T(8,128)(2,1)S(1)} %bitcast.370, bf16[1024,2048,1]{1,0,2:T(8,128)(2,1)} %bitcast.374), kind=kOutput, calls=%fused_computation.13 | convolution fusion | flops 12891193344 | bytes 23068672 | tf_op jit(solution)/shard_map/td,tef->edf/dot_general | solution.py:228
  792.7 28.8 %collective-permute-done.41 = bf16[256,2048]{1,0:T(8,128)(2,1)S(1)} collective-permute-done((bf16[256,2048]{1,0:T(8,128)(2,1)}, bf16[256,2048]{1,0:T(8,128)(2,1)S(1)}, u32[]{:S(2)}, u32[]{:S(2)}) %collective-permute-start.41) | collective-permute-done | bytes 1048608 | tf_op jit(solution)/shard_map/ppermute | solution.py:58
  843.9 25.6 %fusion.1 = (f32[8,1024]{1,0:T(8,128)S(1)}, f32[1024,1024,8]{1,0,2:T(8,128)}) fusion(f32[8,1024,1024]{1,2,0:T(8,128)} %get-tuple-element.154, f32[8,1024]{1,0:T(8,128)S(1)} %copy-done.49, bf16[1024,128,1]{1,0,2:T(8,128)(2,1)S(1)} %copy-done.67, bf16[1024,8,128]{0,2,1:T(8,128)(2,1)S(1)} %bitcast.401), kind=kOutput, calls=%fused_computation.3 | convolution fusion | flops 2172641280 | bytes 69533696 | tf_op jit(solution)/shard_map/while/body/eval_jaxpr/qhd,kd->hqk/dot_general | solution.py:262
  869.5 28.6 %fusion.3 = bf16[8,1024,1024]{1,2,0:T(8,128)(2,1)} fusion(f32[1024,1024,8]{1,0,2:T(8,128)} %get-tuple-element.156, f32[8,1024]{1,0:T(8,128)S(1)} %get-tuple-element.155, f32[8,1024,1024]{1,2,0:T(8,128)} %get-tuple-element.154, f32[8,1024]{1,0:T(8,128)S(1)} %copy-done.49), kind=kLoop, calls=%fused_computation.5 | loop fusion | flops 33554432 | bytes 83951616 | tf_op jit(solution)/shard_map/while/body/eval_jaxpr/convert_element_type | solution.py:267
  1106.6 18.1 %collective-permute-done.47 = bf16[256,2048]{1,0:T(8,128)(2,1)} collective-permute-done((bf16[256,2048]{1,0:T(8,128)(2,1)}, bf16[256,2048]{1,0:T(8,128)(2,1)}, u32[]{:S(2)}, u32[]{:S(2)}) %collective-permute-start.47) | collective-permute-done | bytes 1048608 | tf_op jit(solution)/shard_map/ppermute | solution.py:86
  (411 shorter events, 613.0 us)
Async XLA Ops:
  7.2 111.5 %all-gather.18.cloned.1.call-start = ((), (), s32[]{:S(2)}) async-start(), calls=%async_computation.16 | async-start | bytes 4866048 | tf_op jit(solution)/shard_map/all_gather | solution.py:125
  9.7 138.1 %all-gather.8.cloned.1.call-start = ((), (), s32[]{:S(2)}) async-start(), calls=%async_computation.7 | async-start | bytes 4718592 | tf_op jit(solution)/shard_map/all_gather | solution.py:141
  10.4 239.0 %all-gather.10.cloned.1.call-start = ((), (), s32[]{:S(2)}) async-start(), calls=%async_computation.8 | async-start | bytes 4718592 | tf_op jit(solution)/shard_map/all_gather | solution.py:142
  11.2 415.6 %all-gather.16.cloned.1.call-start = ((), (), s32[]{:S(2)}) async-start(), calls=%async_computation.11 | async-start | bytes 14155776 | tf_op jit(solution)/shard_map/all_gather | solution.py:143
  11.7 434.2 %all-gather.14.cloned.1.call-start = ((), (), s32[]{:S(2)}) async-start(), calls=%async_computation.10 | async-start | bytes 14155776 | tf_op jit(solution)/shard_map/all_gather | solution.py:144
  12.3 452.7 %all-gather.12.cloned.1.call-start = ((), (), s32[]{:S(2)}) async-start(), calls=%async_computation.9 | async-start | bytes 14155776 | tf_op jit(solution)/shard_map/all_gather | solution.py:145
  51.4 38.2 %collective-permute-start.4 = (bf16[256,2048]{1,0:T(8,128)(2,1)S(1)}, bf16[256,2048]{1,0:T(8,128)(2,1)}, u32[]{:S(2)}, u32[]{:S(2)}) collective-permute-start(bf16[256,2048]{1,0:T(8,128)(2,1)S(1)} %collective-permute-done.3), channel_id=1, source_target_pairs={{1,0},{2,1},{5,4},{6,5},{9,8},{10,9},{13,12},{14,13},{17,16},{18,1... | collective-permute-start | bytes 3145736 | tf_op jit(solution)/shard_map/ppermute | solution.py:58
  52.7 38.2 %collective-permute-start.2 = (bf16[256,2048]{1,0:T(8,128)(2,1)}, bf16[256,2048]{1,0:T(8,128)(2,1)}, u32[]{:S(2)}, u32[]{:S(2)}) collective-permute-start(bf16[256,2048]{1,0:T(8,128)(2,1)} %collective-permute-done.1), channel_id=1, source_target_pairs={{2,3},{6,7},{10,11},{14,15},{18,19},{22,23},{26,27},{30,31}} | collective-permute-start | bytes 3145736 | tf_op jit(solution)/shard_map/ppermute | solution.py:55
  54.5 927.6 %reduce-scatter.5.cloned.1.call-start = ((), (), s32[]{:S(2)}) async-start(), calls=%async_computation.12 | async-start | bytes 14155776 | tf_op jit(solution)/shard_map/reduce_scatter | solution.py:238
  130.4 65.6 %collective-permute-start.9 = (bf16[256,2048]{1,0:T(8,128)(2,1)}, bf16[256,2048]{1,0:T(8,128)(2,1)}, u32[]{:S(2)}, u32[]{:S(2)}) collective-permute-start(bf16[256,2048]{1,0:T(8,128)(2,1)} %param.33), channel_id=1, source_target_pairs={{1,0},{2,1},{3,2},{5,4},{6,5},{7,6},{9,8},{10,9},{11,10},{13,12},{... | collective-permute-start | bytes 3145736 | tf_op jit(solution)/shard_map/ppermute | solution.py:58
  131.7 38.1 %collective-permute-start.6 = (bf16[256,2048]{1,0:T(8,128)(2,1)}, bf16[256,2048]{1,0:T(8,128)(2,1)}, u32[]{:S(2)}, u32[]{:S(2)}) collective-permute-start(bf16[256,2048]{1,0:T(8,128)(2,1)} %param.33), channel_id=1, source_target_pairs={{0,1},{1,2},{2,3},{4,5},{5,6},{6,7},{8,9},{9,10},{10,11},{12,13},{... | collective-permute-start | bytes 3145736 | tf_op jit(solution)/shard_map/ppermute | solution.py:55
  524.1 461.4 %reduce-scatter.7.cloned.1.call-start = ((), (), s32[]{:S(2)}) async-start(), calls=%async_computation.13 | async-start | bytes 14155776 | tf_op jit(solution)/shard_map/reduce_scatter | solution.py:238
  543.5 445.4 %reduce-scatter.9.cloned.1.call-start = ((), (), s32[]{:S(2)}) async-start(), calls=%async_computation.14 | async-start | bytes 14155776 | tf_op jit(solution)/shard_map/reduce_scatter | solution.py:238
  603.8 44.8 %collective-permute-start.25 = (bf16[256,2048]{1,0:T(8,128)(2,1)S(1)}, bf16[256,2048]{1,0:T(8,128)(2,1)S(1)}, u32[]{:S(2)}, u32[]{:S(2)}) collective-permute-start(bf16[256,2048]{1,0:T(8,128)(2,1)S(1)} %fusion.37), channel_id=1, source_target_pairs={{0,1},{1,2},{4,5},{5,6},{8,9},{9,10},{12,13},{13,14},{16,17},{17,1... | collective-permute-start | bytes 3145736 | tf_op jit(solution)/shard_map/ppermute | solution.py:80
  605.3 44.9 %collective-permute-start.33 = (bf16[256,2048]{1,0:T(8,128)(2,1)S(1)}, bf16[256,2048]{1,0:T(8,128)(2,1)S(1)}, u32[]{:S(2)}, u32[]{:S(2)}) collective-permute-start(bf16[256,2048]{1,0:T(8,128)(2,1)S(1)} %get-tuple-element.114), channel_id=1, source_target_pairs={{3,2},{7,6},{11,10},{15,14},{19,18},{23,22},{27,26},{31,30}} | collective-permute-start | bytes 3145736 | tf_op jit(solution)/shard_map/ppermute | solution.py:86
  626.5 38.5 %collective-permute-start.31 = (bf16[256,2048]{1,0:T(8,128)(2,1)S(1)}, bf16[256,2048]{1,0:T(8,128)(2,1)S(1)}, u32[]{:S(2)}, u32[]{:S(2)}) collective-permute-start(bf16[256,2048]{1,0:T(8,128)(2,1)S(1)} %fusion.32), channel_id=1, source_target_pairs={{0,1},{1,2},{4,5},{5,6},{8,9},{9,10},{12,13},{13,14},{16,17},{17,1... | collective-permute-start | bytes 3145736 | tf_op jit(solution)/shard_map/ppermute | solution.py:80
  673.3 37.2 %collective-permute-start.32 = (bf16[256,2048]{1,0:T(8,128)(2,1)S(1)}, bf16[256,2048]{1,0:T(8,128)(2,1)S(1)}, u32[]{:S(2)}, u32[]{:S(2)}) collective-permute-start(bf16[256,2048]{1,0:T(8,128)(2,1)S(1)} %get-tuple-element.111), channel_id=1, source_target_pairs={{0,1},{1,2},{2,3},{4,5},{5,6},{6,7},{8,9},{9,10},{10,11},{12,13},{... | collective-permute-start | bytes 3145736 | tf_op jit(solution)/shard_map/ppermute | solution.py:80
  678.7 37.1 %collective-permute-start.35 = (bf16[256,2048]{1,0:T(8,128)(2,1)S(1)}, bf16[256,2048]{1,0:T(8,128)(2,1)S(1)}, u32[]{:S(2)}, u32[]{:S(2)}) collective-permute-start(bf16[256,2048]{1,0:T(8,128)(2,1)S(1)} %fusion.31), channel_id=1, source_target_pairs={{1,0},{2,1},{3,2},{5,4},{6,5},{7,6},{9,8},{10,9},{11,10},{13,12},{... | collective-permute-start | bytes 3145736 | tf_op jit(solution)/shard_map/ppermute | solution.py:86
  719.8 39.9 %collective-permute-start.36 = (bf16[256,2048]{1,0:T(8,128)(2,1)S(1)}, bf16[256,2048]{1,0:T(8,128)(2,1)S(1)}, u32[]{:S(2)}, u32[]{:S(2)}) collective-permute-start(bf16[256,2048]{1,0:T(8,128)(2,1)S(1)} %convert_element_type.434), channel_id=1, source_target_pairs={{0,1},{1,2},{2,3},{4,5},{5,6},{6,7},{8,9},{9,10},{10,11},{12,13},{... | collective-permute-start | bytes 3145736 | tf_op jit(solution)/shard_map/ppermute | solution.py:55
  831.1 204.8 %all-to-all-start.2 = ((bf16[8,1024,256]{2,1,0:T(8,128)(2,1)}), bf16[8,1024,256]{2,1,0:T(8,128)(2,1)}, u32[]{:S(2)}, u32[]{:S(2)}) async-start(bf16[8,1024,256]{2,1,0:T(8,128)(2,1)} %bitcast.363), calls=%async_computation.6 | async-start | bytes 8388608 | tf_op jit(solution)/shard_map/all_to_all | solution.py:320
  835.8 238.3 %reduce-scatter.11.cloned.1.call-start = ((), (), s32[]{:S(2)}) async-start(), calls=%async_computation.15 | async-start | bytes 2433024 | tf_op jit(solution)/shard_map/reduce_scatter | solution.py:348
  1010.2 37.0 %collective-permute-start.45 = (bf16[256,2048]{1,0:T(8,128)(2,1)S(1)}, bf16[256,2048]{1,0:T(8,128)(2,1)}, u32[]{:S(2)}, u32[]{:S(2)}) collective-permute-start(bf16[256,2048]{1,0:T(8,128)(2,1)S(1)} %get-tuple-element.110), channel_id=1, source_target_pairs={{3,2},{7,6},{11,10},{15,14},{19,18},{23,22},{27,26},{31,30}} | collective-permute-start | bytes 3145736 | tf_op jit(solution)/shard_map/ppermute | solution.py:86
  1035.9 56.7 %all-to-all-start = ((bf16[8,256,1024]{2,1,0:T(8,128)(2,1)}), bf16[8,256,1024]{2,1,0:T(8,128)(2,1)}, u32[]{:S(2)}, u32[]{:S(2)}) async-start(bf16[8,256,1024]{2,1,0:T(8,128)(2,1)} %bitcast.377), calls=%async_computation.3 | async-start | bytes 8388608 | tf_op jit(solution)/shard_map/all_to_all | solution.py:310
  1054.9 51.7 %collective-permute-start.44 = (bf16[256,2048]{1,0:T(8,128)(2,1)}, bf16[256,2048]{1,0:T(8,128)(2,1)}, u32[]{:S(2)}, u32[]{:S(2)}) collective-permute-start(bf16[256,2048]{1,0:T(8,128)(2,1)} %get-tuple-element.107), channel_id=1, source_target_pairs={{0,1},{1,2},{2,3},{4,5},{5,6},{6,7},{8,9},{9,10},{10,11},{12,13},{... | collective-permute-start | bytes 3145736 | tf_op jit(solution)/shard_map/ppermute | solution.py:80
  (107 other events, 2345.4 us)
Sparse Core Ops, SparseCore 0:
  11.4 73.0 all-gather.17
  86.4 35.5 all-gather.7
  123.9 37.3 all-gather.9
  163.0 71.9 all-gather.15
  236.8 71.9 all-gather.13
  310.6 71.9 all-gather.11
  524.2 91.0 reduce-scatter.4
  618.8 92.2 reduce-scatter.6
  786.5 153.2 reduce-scatter.8
  1010.3 63.7 reduce-scatter.10

commit v10 on v9

--- a/solution.py
+++ b/solution.py
@@ -190,7 +190,12 @@
         )
         return (context, probs_full)
 
-    context_all, probs_all = lax.map(attend, (query_seq, key_seq, value_seq, prefix_len))
+    forward_parts = [
+        attend((query_seq[index], key_seq[index], value_seq[index], prefix_len[index]))
+        for index in range(seq_count)
+    ]
+    context_all = jnp.stack([part[0] for part in forward_parts])
+    probs_all = [part[1] for part in forward_parts]
     context_b = context_all.reshape(group_rows, per_dev * HD).astype(jnp.bfloat16)
     context_b, grad_rows = lax.optimization_barrier((context_b, grad_rows))
     attn_out = tp_scatter_sum(
@@ -275,8 +280,20 @@
         )
         return (query_grad, key_grad, value_grad)
 
-    query_norm_grad, key_norm_grad, value_grad = lax.map(
-        attend_back, (query_seq, key_seq, value_seq, probs_all, context_grad)
+    backward_parts = [
+        attend_back(
+            (
+                query_seq[index],
+                key_seq[index],
+                value_seq[index],
+                probs_all[index],
+                context_grad[index],
+            )
+        )
+        for index in range(seq_count)
+    ]
+    query_norm_grad, key_norm_grad, value_grad = (
+        jnp.stack([part[slot] for part in backward_parts]) for slot in range(3)
     )
     query_raw_grad, key_raw_grad, query_gain_part, key_gain_part = prepare_back(
         (query_norm_grad.reshape(group_rows, per_dev, HD), key_norm_grad.reshape(group_rows, HD))

time: 1150 us -> 1150 us (level)
  no operation moved by 1% of the time
where the time goes in v10:
time: 1150 us; the launch traced here: 1140 us
  waiting for transfers between devices  434 us (38%)
  matrix products  337 us (29%)
  other arithmetic  151 us (13%)
  starting transfers between devices  138 us (12%)
  local copies, waits for them, and re-layouts  62.8 us (5%)
  between operations  16.8 us (1%)
    ppermute x12, waiting for transfers between devices, tp_gather(): lax.ppermute(going_left, 'tp', [(i + 1, i) for i in range(0, count - step)])  163 us
    ppermute x12, waiting for transfers between devices, tp_scatter_sum(): lax.ppermute(outgoing.astype(send_type), 'tp', [(i, i + 1) for i in range...  135 us
    ppermute x12, waiting for transfers between devices, tp_gather(): lax.ppermute(going_right, 'tp', [(i, i + 1) for i in range(step - 1, coun...  57.8 us
    ppermute x12, starting transfers between devices, tp_gather(): lax.ppermute(going_right, 'tp', [(i, i + 1) for i in range(step - 1, coun...  49 us
    ppermute x12, waiting for transfers between devices, tp_scatter_sum(): lax.ppermute(outgoing.astype(send_type), 'tp', [(i, i - 1) for i in range...  46.9 us
    ppermute x12, starting transfers between devices, tp_scatter_sum(): lax.ppermute(outgoing.astype(send_type), 'tp', [(i, i + 1) for i in range...  46.8 us
    unnamed x2, matrix products  38.2 us
    convert_element_type x1, other arithmetic, attend_back(): scores_grad = (attn_probs * (probs_grad - jnp.sum(attn_probs * probs_grad...  28.6 us
  transfers between devices with their start and end apart: 61, of which 29 were waited for; matrix products, arithmetic and copies ran while one was open for 41% of the time, Pallas kernels for 0%

profile of v10, /device:TPU:0, one launch (start us, length us, event | category | flops | bytes accessed | tf_op | source)
XLA Modules:
  0.0 1139.2 jit_solution(2240131641863318879)
XLA Ops:
  18.7 27.4 %collective-permute-done = bf16[256,2048]{1,0:T(8,128)(2,1)S(1)} collective-permute-done((bf16[256,2048]{1,0:T(8,128)(2,1)S(1)}, bf16[256,2048]{1,0:T(8,128)(2,1)S(1)}, u32[]{:S(2)}, u32[]{:S(2)}) %collective-permute-start) | collective-permute-done | bytes 1048608 | tf_op jit(solution)/shard_map/ppermute | solution.py:55
  56.6 33.1 %collective-permute-done.4 = bf16[256,2048]{1,0:T(8,128)(2,1)} collective-permute-done((bf16[256,2048]{1,0:T(8,128)(2,1)S(1)}, bf16[256,2048]{1,0:T(8,128)(2,1)}, u32[]{:S(2)}, u32[]{:S(2)}) %collective-permute-start.4) | collective-permute-done | bytes 1048608 | tf_op jit(solution)/shard_map/ppermute | solution.py:58
  95.3 19.4 %collective-permute-done.5 = bf16[256,2048]{1,0:T(8,128)(2,1)S(1)} collective-permute-done((bf16[256,2048]{1,0:T(8,128)(2,1)}, bf16[256,2048]{1,0:T(8,128)(2,1)S(1)}, u32[]{:S(2)}, u32[]{:S(2)}) %collective-permute-start.5) | collective-permute-done | bytes 1048608 | tf_op jit(solution)/shard_map/ppermute | solution.py:58
  172.0 20.4 %fusion.111 = (f32[8,1024]{1,0:T(8,128)S(1)}, f32[8,1024,1024]{1,2,0:T(8,128)}) fusion(pred[1024,1024]{0,1:T(8,128)(4,1)} %fusion.17, bf16[1024,64]{0,1:T(8,128)(2,1)S(1)} %get-tuple-element.93, bf16[1024,64]{0,1:T(8,128)(2,1)S(1)} %get-tuple-element.94, bf16[1024,8,64]{2,0,1:T(8,128)(2,1)} %get-tuple-element.78, ...), kind=kOutput, calls=%fused_computation.255 | convolution fusion | flops 2185757696 | bytes 36995072 | tf_op jit(solution)/shard_map/sub | solution.py:182
  263.7 16.4 %collective-permute-done.12 = bf16[256,2048]{1,0:T(8,128)(2,1)} collective-permute-done((bf16[256,2048]{1,0:T(8,128)(2,1)}, bf16[256,2048]{1,0:T(8,128)(2,1)}, u32[]{:S(2)}, u32[]{:S(2)}) %collective-permute-start.12) | collective-permute-done | bytes 1048608 | tf_op jit(solution)/shard_map/ppermute | solution.py:80
  330.9 21.4 %collective-permute-done.17 = bf16[256,2048]{1,0:T(8,128)(2,1)} collective-permute-done((bf16[256,2048]{1,0:T(8,128)(2,1)S(1)}, bf16[256,2048]{1,0:T(8,128)(2,1)}, u32[]{:S(2)}, u32[]{:S(2)}) %collective-permute-start.17) | collective-permute-done | bytes 1048608 | tf_op jit(solution)/shard_map/ppermute | solution.py:86
  385.2 21.2 %collective-permute-done.22 = bf16[256,2048]{1,0:T(8,128)(2,1)S(1)} collective-permute-done((bf16[256,2048]{1,0:T(8,128)(2,1)S(1)}, bf16[256,2048]{1,0:T(8,128)(2,1)S(1)}, u32[]{:S(2)}, u32[]{:S(2)}) %collective-permute-start.22) | collective-permute-done | bytes 1048608 | tf_op jit(solution)/shard_map/ppermute | solution.py:58
  426.8 19.1 %fusion.114 = f32[1024,3072]{0,1} fusion(bf16[1024,2048]{1,0:T(8,128)(2,1)} %bitcast.371, bf16[2048,3072]{0,1:T(8,128)(2,1)} %bitcast.397), kind=kOutput, calls=%fused_computation.258 | convolution fusion | flops 12884901888 | bytes 29360128
  445.9 19.1 %fusion.113 = f32[1024,3072]{0,1} fusion(bf16[1024,2048]{1,0:T(8,128)(2,1)} %bitcast.372, bf16[2048,3072]{0,1:T(8,128)(2,1)} %bitcast.398), kind=kOutput, calls=%fused_computation.257 | convolution fusion | flops 12884901888 | bytes 29360128
  465.0 19.3 %fusion.15 = f32[1024,16,192]{0,2,1:T(8,128)} fusion(bf16[16,192,2048]{2,1,0:T(8,128)(2,1)} %all-gather.12.cloned.1.call-done, bf16[1024,2048]{1,0:T(8,128)(2,1)} %bitcast.375), kind=kOutput, calls=%fused_computation.38 | convolution fusion | flops 12884901888 | bytes 29360128 | tf_op jit(solution)/shard_map/td,efd->tef/dot_general | solution.py:222
  484.4 20.5 %multiply_convert_fusion = (bf16[1024,16,192]{0,2,1:T(8,128)(2,1)}, bf16[1024,16,192]{0,2,1:T(8,128)(2,1)}, bf16[1024,16,192]{0,2,1:T(8,128)(2,1)}) fusion(f32[1024,16,192]{0,2,1:T(8,128)} %bitcast.366, f32[1024,16]{0,1:T(8,128)S(1)} %select_reduce_fusion, f32[1024,16,192]{0,2,1:T(8,128)S(1)} %bitcast.365, f32[1024,16,192]{0,2,1:T(8,128)} %fusion.15), kind=kLoop, calls=%fused_computation.15 | loop fusion | flops 59768832 | bytes 56688640 | tf_op jit(solution)/shard_map/convert_element_type | solution.py:215
  504.9 19.2 %convolution_convert_fusion = bf16[16,192,2048]{2,1,0:T(8,128)(2,1)} fusion(bf16[1024,16,192]{0,2,1:T(8,128)(2,1)} %get-tuple-element.56, bf16[1024,2048]{1,0:T(8,128)(2,1)} %bitcast.376), kind=kOutput, calls=%fused_computation.33 | convolution fusion | flops 12891193344 | bytes 23068672 | tf_op jit(solution)/shard_map/tef,td->efd/dot_general | solution.py:234
  524.2 19.3 %convert_bitcast_fusion.1 = bf16[16,2048,192]{1,2,0:T(8,128)(2,1)} fusion(bf16[1024,16,192]{0,2,1:T(8,128)(2,1)} %get-tuple-element.57, bf16[1024,2048,1]{1,0,2:T(8,128)(2,1)} %bitcast.373), kind=kOutput, calls=%fused_computation.14 | convolution fusion | flops 12891193344 | bytes 23068672 | tf_op jit(solution)/shard_map/td,tef->edf/dot_general | solution.py:232
  543.5 17.7 %fusion.115 = f32[1024,2048,1]{1,0,2:T(8,128)S(1)} fusion(bf16[1024,16,192]{0,2,1:T(8,128)(2,1)} %get-tuple-element.57, bf16[16,2048,192]{1,2,0:T(8,128)(2,1)} %all-gather.16.cloned.1.call-done), kind=kOutput, calls=%fused_computation.259 | convolution fusion | flops 12884901888 | bytes 27262976 | tf_op jit(solution)/shard_map/tef,edf->td/dot_general | solution.py:229
  561.2 19.3 %bitcast_add_fusion = f32[1024,2048]{1,0:T(8,128)S(1)} fusion(f32[1024,2048,1]{1,0,2:T(8,128)S(1)} %fusion.115, bf16[1024,16,192]{0,2,1:T(8,128)(2,1)} %get-tuple-element.58, bf16[16,2048,192]{1,2,0:T(8,128)(2,1)} %all-gather.14.cloned.1.call-done), kind=kOutput, calls=%fused_computation.21 | convolution fusion | flops 12886999040 | bytes 35651584 | tf_op jit(solution)/shard_map/tef,edf->td/dot_general | solution.py:231
  583.3 17.8 %fusion.116 = f32[1024,2048,1]{1,0,2:T(8,128)S(1)} fusion(bf16[1024,16,192]{0,2,1:T(8,128)(2,1)} %get-tuple-element.56, bf16[16,192,2048]{2,1,0:T(8,128)(2,1)} %all-gather.12.cloned.1.call-done), kind=kOutput, calls=%fused_computation.260 | convolution fusion | flops 12884901888 | bytes 27262976 | tf_op jit(solution)/shard_map/tef,efd->td/dot_general | solution.py:216
  606.1 20.1 %collective-permute-done.30 = bf16[256,2048]{1,0:T(8,128)(2,1)S(1)} collective-permute-done((bf16[256,2048]{1,0:T(8,128)(2,1)S(1)}, bf16[256,2048]{1,0:T(8,128)(2,1)S(1)}, u32[]{:S(2)}, u32[]{:S(2)}) %collective-permute-start.30) | collective-permute-done | bytes 1048608 | tf_op jit(solution)/shard_map/ppermute | solution.py:80
  630.9 17.7 %collective-permute-done.25 = bf16[256,2048]{1,0:T(8,128)(2,1)S(1)} collective-permute-done((bf16[256,2048]{1,0:T(8,128)(2,1)S(1)}, bf16[256,2048]{1,0:T(8,128)(2,1)S(1)}, u32[]{:S(2)}, u32[]{:S(2)}) %collective-permute-start.25) | collective-permute-done | bytes 1048608 | tf_op jit(solution)/shard_map/ppermute | solution.py:80
  719.8 22.2 %collective-permute-start.36 = (bf16[256,2048]{1,0:T(8,128)(2,1)S(1)}, bf16[256,2048]{1,0:T(8,128)(2,1)S(1)}, u32[]{:S(2)}, u32[]{:S(2)}) collective-permute-start(bf16[256,2048]{1,0:T(8,128)(2,1)S(1)} %convert_element_type.431), channel_id=1, source_target_pairs={{0,1},{1,2},{2,3},{4,5},{5,6},{6,7},{8,9},{9,10},{10,11},{12,13},{... | collective-permute-start | bytes 3145736 | tf_op jit(solution)/shard_map/ppermute | solution.py:55
  768.7 17.6 %convert_bitcast_fusion = bf16[16,2048,192]{1,2,0:T(8,128)(2,1)} fusion(bf16[1024,16,192]{0,2,1:T(8,128)(2,1)S(1)} %bitcast.370, bf16[1024,2048,1]{1,0,2:T(8,128)(2,1)} %bitcast.374), kind=kOutput, calls=%fused_computation.13 | convolution fusion | flops 12891193344 | bytes 23068672 | tf_op jit(solution)/shard_map/td,tef->edf/dot_general | solution.py:233
  792.7 28.8 %collective-permute-done.41 = bf16[256,2048]{1,0:T(8,128)(2,1)S(1)} collective-permute-done((bf16[256,2048]{1,0:T(8,128)(2,1)}, bf16[256,2048]{1,0:T(8,128)(2,1)S(1)}, u32[]{:S(2)}, u32[]{:S(2)}) %collective-permute-start.41) | collective-permute-done | bytes 1048608 | tf_op jit(solution)/shard_map/ppermute | solution.py:58
  843.9 25.6 %fusion.1 = (f32[8,1024]{1,0:T(8,128)S(1)}, f32[1024,1024,8]{1,0,2:T(8,128)}) fusion(f32[8,1024,1024]{1,2,0:T(8,128)} %get-tuple-element.106, f32[8,1024]{1,0:T(8,128)S(1)} %copy-done.49, bf16[1024,128,1]{1,0,2:T(8,128)(2,1)S(1)} %copy-done.67, bf16[1024,8,128]{0,2,1:T(8,128)(2,1)S(1)} %bitcast.401), kind=kOutput, calls=%fused_computation.3 | convolution fusion | flops 2172641280 | bytes 69533696 | tf_op jit(solution)/shard_map/qhd,kd->hqk/dot_general | solution.py:267
  869.5 28.6 %fusion.3 = bf16[8,1024,1024]{1,2,0:T(8,128)(2,1)} fusion(f32[1024,1024,8]{1,0,2:T(8,128)} %get-tuple-element.108, f32[8,1024]{1,0:T(8,128)S(1)} %get-tuple-element.107, f32[8,1024,1024]{1,2,0:T(8,128)} %get-tuple-element.106, f32[8,1024]{1,0:T(8,128)S(1)} %copy-done.49), kind=kLoop, calls=%fused_computation.5 | loop fusion | flops 33554432 | bytes 83951616 | tf_op jit(solution)/shard_map/convert_element_type | solution.py:272
  1106.6 18.1 %collective-permute-done.47 = bf16[256,2048]{1,0:T(8,128)(2,1)} collective-permute-done((bf16[256,2048]{1,0:T(8,128)(2,1)}, bf16[256,2048]{1,0:T(8,128)(2,1)}, u32[]{:S(2)}, u32[]{:S(2)}) %collective-permute-start.47) | collective-permute-done | bytes 1048608 | tf_op jit(solution)/shard_map/ppermute | solution.py:86
  (411 shorter events, 613.0 us)
Async XLA Ops:
  7.2 111.5 %all-gather.18.cloned.1.call-start = ((), (), s32[]{:S(2)}) async-start(), calls=%async_computation.16 | async-start | bytes 4866048 | tf_op jit(solution)/shard_map/all_gather | solution.py:125
  9.7 138.1 %all-gather.8.cloned.1.call-start = ((), (), s32[]{:S(2)}) async-start(), calls=%async_computation.7 | async-start | bytes 4718592 | tf_op jit(solution)/shard_map/all_gather | solution.py:141
  10.4 239.0 %all-gather.10.cloned.1.call-start = ((), (), s32[]{:S(2)}) async-start(), calls=%async_computation.8 | async-start | bytes 4718592 | tf_op jit(solution)/shard_map/all_gather | solution.py:142
  11.2 415.6 %all-gather.16.cloned.1.call-start = ((), (), s32[]{:S(2)}) async-start(), calls=%async_computation.11 | async-start | bytes 14155776 | tf_op jit(solution)/shard_map/all_gather | solution.py:143
  11.7 434.2 %all-gather.14.cloned.1.call-start = ((), (), s32[]{:S(2)}) async-start(), calls=%async_computation.10 | async-start | bytes 14155776 | tf_op jit(solution)/shard_map/all_gather | solution.py:144
  12.3 452.7 %all-gather.12.cloned.1.call-start = ((), (), s32[]{:S(2)}) async-start(), calls=%async_computation.9 | async-start | bytes 14155776 | tf_op jit(solution)/shard_map/all_gather | solution.py:145
  51.4 38.2 %collective-permute-start.4 = (bf16[256,2048]{1,0:T(8,128)(2,1)S(1)}, bf16[256,2048]{1,0:T(8,128)(2,1)}, u32[]{:S(2)}, u32[]{:S(2)}) collective-permute-start(bf16[256,2048]{1,0:T(8,128)(2,1)S(1)} %collective-permute-done.3), channel_id=1, source_target_pairs={{1,0},{2,1},{5,4},{6,5},{9,8},{10,9},{13,12},{14,13},{17,16},{18,1... | collective-permute-start | bytes 3145736 | tf_op jit(solution)/shard_map/ppermute | solution.py:58
  52.7 38.2 %collective-permute-start.2 = (bf16[256,2048]{1,0:T(8,128)(2,1)}, bf16[256,2048]{1,0:T(8,128)(2,1)}, u32[]{:S(2)}, u32[]{:S(2)}) collective-permute-start(bf16[256,2048]{1,0:T(8,128)(2,1)} %collective-permute-done.1), channel_id=1, source_target_pairs={{2,3},{6,7},{10,11},{14,15},{18,19},{22,23},{26,27},{30,31}} | collective-permute-start | bytes 3145736 | tf_op jit(solution)/shard_map/ppermute | solution.py:55
  54.5 927.6 %reduce-scatter.5.cloned.1.call-start = ((), (), s32[]{:S(2)}) async-start(), calls=%async_computation.12 | async-start | bytes 14155776 | tf_op jit(solution)/shard_map/reduce_scatter | solution.py:243
  130.4 65.6 %collective-permute-start.9 = (bf16[256,2048]{1,0:T(8,128)(2,1)}, bf16[256,2048]{1,0:T(8,128)(2,1)}, u32[]{:S(2)}, u32[]{:S(2)}) collective-permute-start(bf16[256,2048]{1,0:T(8,128)(2,1)} %param.33), channel_id=1, source_target_pairs={{1,0},{2,1},{3,2},{5,4},{6,5},{7,6},{9,8},{10,9},{11,10},{13,12},{... | collective-permute-start | bytes 3145736 | tf_op jit(solution)/shard_map/ppermute | solution.py:58
  131.7 38.1 %collective-permute-start.6 = (bf16[256,2048]{1,0:T(8,128)(2,1)}, bf16[256,2048]{1,0:T(8,128)(2,1)}, u32[]{:S(2)}, u32[]{:S(2)}) collective-permute-start(bf16[256,2048]{1,0:T(8,128)(2,1)} %param.33), channel_id=1, source_target_pairs={{0,1},{1,2},{2,3},{4,5},{5,6},{6,7},{8,9},{9,10},{10,11},{12,13},{... | collective-permute-start | bytes 3145736 | tf_op jit(solution)/shard_map/ppermute | solution.py:55
  524.1 461.4 %reduce-scatter.7.cloned.1.call-start = ((), (), s32[]{:S(2)}) async-start(), calls=%async_computation.13 | async-start | bytes 14155776 | tf_op jit(solution)/shard_map/reduce_scatter | solution.py:243
  543.5 445.4 %reduce-scatter.9.cloned.1.call-start = ((), (), s32[]{:S(2)}) async-start(), calls=%async_computation.14 | async-start | bytes 14155776 | tf_op jit(solution)/shard_map/reduce_scatter | solution.py:243
  603.8 44.8 %collective-permute-start.25 = (bf16[256,2048]{1,0:T(8,128)(2,1)S(1)}, bf16[256,2048]{1,0:T(8,128)(2,1)S(1)}, u32[]{:S(2)}, u32[]{:S(2)}) collective-permute-start(bf16[256,2048]{1,0:T(8,128)(2,1)S(1)} %fusion.37), channel_id=1, source_target_pairs={{0,1},{1,2},{4,5},{5,6},{8,9},{9,10},{12,13},{13,14},{16,17},{17,1... | collective-permute-start | bytes 3145736 | tf_op jit(solution)/shard_map/ppermute | solution.py:80
  605.3 44.9 %collective-permute-start.33 = (bf16[256,2048]{1,0:T(8,128)(2,1)S(1)}, bf16[256,2048]{1,0:T(8,128)(2,1)S(1)}, u32[]{:S(2)}, u32[]{:S(2)}) collective-permute-start(bf16[256,2048]{1,0:T(8,128)(2,1)S(1)} %get-tuple-element.66), channel_id=1, source_target_pairs={{3,2},{7,6},{11,10},{15,14},{19,18},{23,22},{27,26},{31,30}} | collective-permute-start | bytes 3145736 | tf_op jit(solution)/shard_map/ppermute | solution.py:86
  626.5 38.5 %collective-permute-start.31 = (bf16[256,2048]{1,0:T(8,128)(2,1)S(1)}, bf16[256,2048]{1,0:T(8,128)(2,1)S(1)}, u32[]{:S(2)}, u32[]{:S(2)}) collective-permute-start(bf16[256,2048]{1,0:T(8,128)(2,1)S(1)} %fusion.32), channel_id=1, source_target_pairs={{0,1},{1,2},{4,5},{5,6},{8,9},{9,10},{12,13},{13,14},{16,17},{17,1... | collective-permute-start | bytes 3145736 | tf_op jit(solution)/shard_map/ppermute | solution.py:80
  673.3 37.2 %collective-permute-start.32 = (bf16[256,2048]{1,0:T(8,128)(2,1)S(1)}, bf16[256,2048]{1,0:T(8,128)(2,1)S(1)}, u32[]{:S(2)}, u32[]{:S(2)}) collective-permute-start(bf16[256,2048]{1,0:T(8,128)(2,1)S(1)} %get-tuple-element.63), channel_id=1, source_target_pairs={{0,1},{1,2},{2,3},{4,5},{5,6},{6,7},{8,9},{9,10},{10,11},{12,13},{... | collective-permute-start | bytes 3145736 | tf_op jit(solution)/shard_map/ppermute | solution.py:80
  678.7 37.1 %collective-permute-start.35 = (bf16[256,2048]{1,0:T(8,128)(2,1)S(1)}, bf16[256,2048]{1,0:T(8,128)(2,1)S(1)}, u32[]{:S(2)}, u32[]{:S(2)}) collective-permute-start(bf16[256,2048]{1,0:T(8,128)(2,1)S(1)} %fusion.31), channel_id=1, source_target_pairs={{1,0},{2,1},{3,2},{5,4},{6,5},{7,6},{9,8},{10,9},{11,10},{13,12},{... | collective-permute-start | bytes 3145736 | tf_op jit(solution)/shard_map/ppermute | solution.py:86
  719.8 39.9 %collective-permute-start.36 = (bf16[256,2048]{1,0:T(8,128)(2,1)S(1)}, bf16[256,2048]{1,0:T(8,128)(2,1)S(1)}, u32[]{:S(2)}, u32[]{:S(2)}) collective-permute-start(bf16[256,2048]{1,0:T(8,128)(2,1)S(1)} %convert_element_type.431), channel_id=1, source_target_pairs={{0,1},{1,2},{2,3},{4,5},{5,6},{6,7},{8,9},{9,10},{10,11},{12,13},{... | collective-permute-start | bytes 3145736 | tf_op jit(solution)/shard_map/ppermute | solution.py:55
  831.1 204.8 %all-to-all-start.2 = ((bf16[8,1024,256]{2,1,0:T(8,128)(2,1)}), bf16[8,1024,256]{2,1,0:T(8,128)(2,1)}, u32[]{:S(2)}, u32[]{:S(2)}) async-start(bf16[8,1024,256]{2,1,0:T(8,128)(2,1)} %bitcast.363), calls=%async_computation.6 | async-start | bytes 8388608 | tf_op jit(solution)/shard_map/all_to_all | solution.py:337
  835.8 238.3 %reduce-scatter.11.cloned.1.call-start = ((), (), s32[]{:S(2)}) async-start(), calls=%async_computation.15 | async-start | bytes 2433024 | tf_op jit(solution)/shard_map/reduce_scatter | solution.py:365
  1010.2 37.0 %collective-permute-start.45 = (bf16[256,2048]{1,0:T(8,128)(2,1)S(1)}, bf16[256,2048]{1,0:T(8,128)(2,1)}, u32[]{:S(2)}, u32[]{:S(2)}) collective-permute-start(bf16[256,2048]{1,0:T(8,128)(2,1)S(1)} %get-tuple-element.62), channel_id=1, source_target_pairs={{3,2},{7,6},{11,10},{15,14},{19,18},{23,22},{27,26},{31,30}} | collective-permute-start | bytes 3145736 | tf_op jit(solution)/shard_map/ppermute | solution.py:86
  1035.9 56.7 %all-to-all-start = ((bf16[8,256,1024]{2,1,0:T(8,128)(2,1)}), bf16[8,256,1024]{2,1,0:T(8,128)(2,1)}, u32[]{:S(2)}, u32[]{:S(2)}) async-start(bf16[8,256,1024]{2,1,0:T(8,128)(2,1)} %bitcast.377), calls=%async_computation.3 | async-start | bytes 8388608 | tf_op jit(solution)/shard_map/all_to_all | solution.py:327
  1054.9 51.7 %collective-permute-start.44 = (bf16[256,2048]{1,0:T(8,128)(2,1)}, bf16[256,2048]{1,0:T(8,128)(2,1)}, u32[]{:S(2)}, u32[]{:S(2)}) collective-permute-start(bf16[256,2048]{1,0:T(8,128)(2,1)} %get-tuple-element.59), channel_id=1, source_target_pairs={{0,1},{1,2},{2,3},{4,5},{5,6},{6,7},{8,9},{9,10},{10,11},{12,13},{... | collective-permute-start | bytes 3145736 | tf_op jit(solution)/shard_map/ppermute | solution.py:80
  (107 other events, 2345.4 us)
Sparse Core Ops, SparseCore 0:
  11.4 73.0 all-gather.17
  86.4 35.5 all-gather.7
  123.9 37.3 all-gather.9
  163.0 71.9 all-gather.15
  236.8 71.9 all-gather.13
  310.6 71.9 all-gather.11
  524.2 91.0 reduce-scatter.4
  618.8 92.2 reduce-scatter.6
  786.5 153.2 reduce-scatter.8
  1010.3 63.7 reduce-scatter.10

commit v11 on v9

--- a/solution.py
+++ b/solution.py
@@ -211,7 +211,6 @@
     mixture = jnp.einsum(
         "tef,efd->td", hidden_share, down_w, preferred_element_type=jnp.float32
     )
-    mixture_own = tp_scatter_sum(mixture, tp_size, jnp.bfloat16)
     grad_out = out_grad.astype(jnp.float32)
     hidden_grad = (
         jnp.einsum("td,efd->tef", grad_rows, down_w, preferred_element_type=jnp.float32)
@@ -233,15 +232,16 @@
     _, second_back = jax.vjp(rms_norm, residual, gain_ffn)
     residual_norm_grad, ffn_gain_part = second_back(ffn_in_own)
     residual_grad = grad_out + residual_norm_grad
-    residual_grad, mixture_own = lax.optimization_barrier((residual_grad, mixture_own))
     gate_grad, up_grad, down_grad = (
         lax.psum_scatter(
             part.astype(jnp.bfloat16), "fsdp", scatter_dimension=0, tiled=True
         ).astype(jnp.float32)
         for part in (gate_part, up_part, down_part)
     )
+    attn_out_grad = tp_gather(residual_grad.astype(jnp.bfloat16), tp_size)
+    attn_out_grad, mixture = lax.optimization_barrier((attn_out_grad, mixture))
+    mixture_own = tp_scatter_sum(mixture, tp_size, jnp.bfloat16)
     layer_out = (residual + mixture_own).astype(jnp.bfloat16)
-    attn_out_grad = tp_gather(residual_grad.astype(jnp.bfloat16), tp_size)
     output_part = jnp.einsum(
         "gq,gd->qd", context_b, attn_out_grad, preferred_element_type=jnp.float32
     )

time: 1150 us -> 1100 us (0.957)
  waiting for transfers between devices: 434 us -> 404 us
  starting transfers between devices: 138 us -> 120 us
    ppermute x12, waiting for transfers between devices: 135 us -> 103 us  [tp_scatter_sum(): lax.ppermute(outgoing.astype(send_type), 'tp', [(i, i + 1) for i in range...]
    ppermute x12, waiting for transfers between devices: 46.9 us -> 73 us  [tp_scatter_sum(): lax.ppermute(outgoing.astype(send_type), 'tp', [(i, i - 1) for i in range...]
    ppermute x12, starting transfers between devices: 49 us -> 30.5 us  [tp_gather(): lax.ppermute(going_right, 'tp', [(i, i + 1) for i in range(step - 1, coun...]
    ppermute x12, waiting for transfers between devices: 163 us -> 147 us  [tp_gather(): lax.ppermute(going_left, 'tp', [(i + 1, i) for i in range(0, count - step)])]
    reduce_scatter x1, waiting for transfers between devices: 13.1 us -> 0.02 us  [body(): summed = lax.psum_scatter(combined, 'fsdp', scatter_dimension=0, tiled=True)]
    unnamed x170 -> x181, local copies, waits for them, and re-layouts: 24.2 us -> 23.3 us
  transfers between devices with their start and end apart: 61 -> 61, of which waited for: 29 -> 25; matrix products, arithmetic and copies ran while one was open for 41% -> 43% of each run, Pallas kernels for 0% -> 0%
where the time goes in v11:
time: 1100 us; the launch traced here: 1090 us
  waiting for transfers between devices  404 us (37%)
  matrix products  328 us (30%)
  other arithmetic  158 us (14%)
  starting transfers between devices  120 us (11%)
  local copies, waits for them, and re-layouts  65.6 us (6%)
  between operations  16.9 us (2%)
    ppermute x12, waiting for transfers between devices, tp_gather(): lax.ppermute(going_left, 'tp', [(i + 1, i) for i in range(0, count - step)])  147 us
    ppermute x12, waiting for transfers between devices, tp_scatter_sum(): lax.ppermute(outgoing.astype(send_type), 'tp', [(i, i + 1) for i in range...  103 us
    ppermute x12, waiting for transfers between devices, tp_scatter_sum(): lax.ppermute(outgoing.astype(send_type), 'tp', [(i, i - 1) for i in range...  73 us
    ppermute x12, waiting for transfers between devices, tp_gather(): lax.ppermute(going_right, 'tp', [(i, i + 1) for i in range(step - 1, coun...  51.3 us
    ppermute x12, starting transfers between devices, tp_scatter_sum(): lax.ppermute(outgoing.astype(send_type), 'tp', [(i, i + 1) for i in range...  45.7 us
    unnamed x2, matrix products  38.2 us
    convert_element_type x12, other arithmetic, tp_scatter_sum(): outgoing.astype(send_type)  33 us
    ppermute x12, starting transfers between devices, tp_gather(): lax.ppermute(going_right, 'tp', [(i, i + 1) for i in range(step - 1, coun...  30.5 us
  transfers between devices with their start and end apart: 61, of which 25 were waited for; matrix products, arithmetic and copies ran while one was open for 43% of the time, Pallas kernels for 0%

profile of v11, /device:TPU:0, one launch (start us, length us, event | category | flops | bytes accessed | tf_op | source)
XLA Modules:
  0.0 1091.7 jit_solution(7240575363157727297)
XLA Ops:
  18.7 27.4 %collective-permute-done = bf16[256,2048]{1,0:T(8,128)(2,1)S(1)} collective-permute-done((bf16[256,2048]{1,0:T(8,128)(2,1)S(1)}, bf16[256,2048]{1,0:T(8,128)(2,1)S(1)}, u32[]{:S(2)}, u32[]{:S(2)}) %collective-permute-start) | collective-permute-done | bytes 1048608 | tf_op jit(solution)/shard_map/ppermute | solution.py:55
  57.6 32.0 %collective-permute-done.4 = bf16[256,2048]{1,0:T(8,128)(2,1)} collective-permute-done((bf16[256,2048]{1,0:T(8,128)(2,1)S(1)}, bf16[256,2048]{1,0:T(8,128)(2,1)}, u32[]{:S(2)}, u32[]{:S(2)}) %collective-permute-start.4) | collective-permute-done | bytes 1048608 | tf_op jit(solution)/shard_map/ppermute | solution.py:58
  95.3 20.5 %collective-permute-done.5 = bf16[256,2048]{1,0:T(8,128)(2,1)S(1)} collective-permute-done((bf16[256,2048]{1,0:T(8,128)(2,1)}, bf16[256,2048]{1,0:T(8,128)(2,1)S(1)}, u32[]{:S(2)}, u32[]{:S(2)}) %collective-permute-start.5) | collective-permute-done | bytes 1048608 | tf_op jit(solution)/shard_map/ppermute | solution.py:58
  172.6 20.9 %fusion.114 = (f32[8,1024]{1,0:T(8,128)S(1)}, f32[8,1024,1024]{1,2,0:T(8,128)}) fusion(pred[1024,1024]{0,1:T(8,128)(4,1)} %fusion.17, bf16[1024,64]{0,1:T(8,128)(2,1)S(1)} %get-tuple-element.143, bf16[1024,64]{0,1:T(8,128)(2,1)S(1)} %copy-done.32, bf16[1024,8,64]{2,0,1:T(8,128)(2,1)} %get-tuple-element.126, bf16[1024,8,64]{2,0,1:T(8,128)(2,1)} %get-tuple-element.125), kind=kOutput, calls=%fused_computation.258 | convolution fusion | flops 2185757696 | bytes 36995072 | tf_op jit(solution)/shard_map/while/body/eval_jaxpr/sub | solution.py:182
  229.0 18.2 %collective-permute-done.11 = bf16[256,2048]{1,0:T(8,128)(2,1)S(1)} collective-permute-done((bf16[256,2048]{1,0:T(8,128)(2,1)S(1)}, bf16[256,2048]{1,0:T(8,128)(2,1)S(1)}, u32[]{:S(2)}, u32[]{:S(2)}) %collective-permute-start.11) | collective-permute-done | bytes 1048608 | tf_op jit(solution)/shard_map/ppermute | solution.py:58
  264.4 16.7 %collective-permute-done.12 = bf16[256,2048]{1,0:T(8,128)(2,1)} collective-permute-done((bf16[256,2048]{1,0:T(8,128)(2,1)}, bf16[256,2048]{1,0:T(8,128)(2,1)}, u32[]{:S(2)}, u32[]{:S(2)}) %collective-permute-start.12) | collective-permute-done | bytes 1048608 | tf_op jit(solution)/shard_map/ppermute | solution.py:80
  289.7 16.4 %collective-permute-done.13 = bf16[256,2048]{1,0:T(8,128)(2,1)} collective-permute-done((bf16[256,2048]{1,0:T(8,128)(2,1)}, bf16[256,2048]{1,0:T(8,128)(2,1)}, u32[]{:S(2)}, u32[]{:S(2)}) %collective-permute-start.13) | collective-permute-done | bytes 1048608 | tf_op jit(solution)/shard_map/ppermute | solution.py:80
  332.3 21.8 %collective-permute-done.17 = bf16[256,2048]{1,0:T(8,128)(2,1)} collective-permute-done((bf16[256,2048]{1,0:T(8,128)(2,1)S(1)}, bf16[256,2048]{1,0:T(8,128)(2,1)}, u32[]{:S(2)}, u32[]{:S(2)}) %collective-permute-start.17) | collective-permute-done | bytes 1048608 | tf_op jit(solution)/shard_map/ppermute | solution.py:86
  386.4 21.2 %collective-permute-done.22 = bf16[256,2048]{1,0:T(8,128)(2,1)S(1)} collective-permute-done((bf16[256,2048]{1,0:T(8,128)(2,1)S(1)}, bf16[256,2048]{1,0:T(8,128)(2,1)S(1)}, u32[]{:S(2)}, u32[]{:S(2)}) %collective-permute-start.22) | collective-permute-done | bytes 1048608 | tf_op jit(solution)/shard_map/ppermute | solution.py:58
  427.4 19.1 %fusion.117 = f32[1024,3072]{0,1} fusion(bf16[1024,2048]{1,0:T(8,128)(2,1)} %bitcast.377, bf16[2048,3072]{0,1:T(8,128)(2,1)} %bitcast.401), kind=kOutput, calls=%fused_computation.261 | convolution fusion | flops 12884901888 | bytes 29360128
  446.4 19.1 %fusion.116 = f32[1024,3072]{0,1} fusion(bf16[1024,2048]{1,0:T(8,128)(2,1)} %bitcast.378, bf16[2048,3072]{0,1:T(8,128)(2,1)} %bitcast.402), kind=kOutput, calls=%fused_computation.260 | convolution fusion | flops 12884901888 | bytes 29360128
  465.5 19.2 %fusion.15 = f32[1024,16,192]{0,2,1:T(8,128)} fusion(bf16[16,192,2048]{2,1,0:T(8,128)(2,1)} %all-gather.12.cloned.1.call-done, bf16[1024,2048]{1,0:T(8,128)(2,1)} %bitcast.375), kind=kOutput, calls=%fused_computation.39 | convolution fusion | flops 12884901888 | bytes 29360128 | tf_op jit(solution)/shard_map/td,efd->tef/dot_general | solution.py:216
  484.7 20.4 %multiply_convert_fusion = (bf16[1024,16,192]{0,2,1:T(8,128)(2,1)}, bf16[1024,16,192]{0,2,1:T(8,128)(2,1)}, bf16[1024,16,192]{0,2,1:T(8,128)(2,1)}) fusion(f32[1024,16,192]{0,2,1:T(8,128)} %bitcast.370, f32[1024,16]{0,1:T(8,128)S(1)} %select_reduce_fusion, f32[1024,16,192]{0,2,1:T(8,128)S(1)} %bitcast.369, f32[1024,16,192]{0,2,1:T(8,128)} %fusion.15), kind=kLoop, calls=%fused_computation.15 | loop fusion | flops 59768832 | bytes 56688640 | tf_op jit(solution)/shard_map/convert_element_type | solution.py:210
  505.1 19.2 %convolution_convert_fusion = bf16[16,192,2048]{2,1,0:T(8,128)(2,1)} fusion(bf16[1024,16,192]{0,2,1:T(8,128)(2,1)} %get-tuple-element.104, bf16[1024,2048]{1,0:T(8,128)(2,1)} %bitcast.376), kind=kOutput, calls=%fused_computation.33 | convolution fusion | flops 12891193344 | bytes 23068672 | tf_op jit(solution)/shard_map/tef,td->efd/dot_general | solution.py:228
  524.4 19.4 %convert_bitcast_fusion.1 = bf16[16,2048,192]{1,2,0:T(8,128)(2,1)} fusion(bf16[1024,16,192]{0,2,1:T(8,128)(2,1)} %get-tuple-element.105, bf16[1024,2048,1]{1,0,2:T(8,128)(2,1)} %bitcast.379), kind=kOutput, calls=%fused_computation.14 | convolution fusion | flops 12891193344 | bytes 23068672 | tf_op jit(solution)/shard_map/td,tef->edf/dot_general | solution.py:226
  543.9 17.8 %fusion.118 = f32[1024,2048,1]{1,0,2:T(8,128)S(1)} fusion(bf16[1024,16,192]{0,2,1:T(8,128)(2,1)} %get-tuple-element.105, bf16[16,2048,192]{1,2,0:T(8,128)(2,1)} %all-gather.16.cloned.1.call-done), kind=kOutput, calls=%fused_computation.262 | convolution fusion | flops 12884901888 | bytes 27262976 | tf_op jit(solution)/shard_map/tef,edf->td/dot_general | solution.py:223
  561.7 19.3 %bitcast_add_fusion = f32[1024,2048]{1,0:T(8,128)S(1)} fusion(f32[1024,2048,1]{1,0,2:T(8,128)S(1)} %fusion.118, bf16[1024,16,192]{0,2,1:T(8,128)(2,1)} %get-tuple-element.106, bf16[16,2048,192]{1,2,0:T(8,128)(2,1)} %all-gather.14.cloned.1.call-done), kind=kOutput, calls=%fused_computation.21 | convolution fusion | flops 12886999040 | bytes 35651584 | tf_op jit(solution)/shard_map/tef,edf->td/dot_general | solution.py:225
  584.5 17.7 %collective-permute-done.24 = bf16[256,2048]{1,0:T(8,128)(2,1)S(1)} collective-permute-done((bf16[256,2048]{1,0:T(8,128)(2,1)S(1)}, bf16[256,2048]{1,0:T(8,128)(2,1)S(1)}, u32[]{:S(2)}, u32[]{:S(2)}) %collective-permute-start.24) | collective-permute-done | bytes 1048608 | tf_op jit(solution)/shard_map/ppermute | solution.py:80
  642.6 32.7 %collective-permute-done.29 = bf16[256,2048]{1,0:T(8,128)(2,1)S(1)} collective-permute-done((bf16[256,2048]{1,0:T(8,128)(2,1)S(1)}, bf16[256,2048]{1,0:T(8,128)(2,1)S(1)}, u32[]{:S(2)}, u32[]{:S(2)}) %collective-permute-start.29) | collective-permute-done | bytes 1048608 | tf_op jit(solution)/shard_map/ppermute | solution.py:86
  715.8 19.1 %convolution_bitcast_fusion = f32[1024,2048]{1,0:T(8,128)} fusion(bf16[1024,16,192]{0,2,1:T(8,128)(2,1)} %get-tuple-element.104, bf16[16,192,2048]{2,1,0:T(8,128)(2,1)} %all-gather.12.cloned.1.call-done), kind=kOutput, calls=%fused_computation.35 | convolution fusion | flops 12884901888 | bytes 27262976 | tf_op jit(solution)/shard_map/tef,efd->td/dot_general | solution.py:211
  788.2 25.6 %fusion.1 = (f32[8,1024]{1,0:T(8,128)S(1)}, f32[1024,1024,8]{1,0,2:T(8,128)}) fusion(f32[8,1024,1024]{1,2,0:T(8,128)} %get-tuple-element.156, f32[8,1024]{1,0:T(8,128)S(1)} %copy-done.54, bf16[1024,128,1]{1,0,2:T(8,128)(2,1)S(1)} %copy-done.72, bf16[1024,8,128]{0,2,1:T(8,128)(2,1)S(1)} %bitcast.405), kind=kOutput, calls=%fused_computation.3 | convolution fusion | flops 2172641280 | bytes 69533696 | tf_op jit(solution)/shard_map/while/body/eval_jaxpr/qhd,kd->hqk/dot_general | solution.py:262
  813.8 28.9 %fusion.3 = bf16[8,1024,1024]{1,2,0:T(8,128)(2,1)} fusion(f32[1024,1024,8]{1,0,2:T(8,128)} %get-tuple-element.158, f32[8,1024]{1,0:T(8,128)S(1)} %get-tuple-element.157, f32[8,1024,1024]{1,2,0:T(8,128)} %get-tuple-element.156, f32[8,1024]{1,0:T(8,128)S(1)} %copy-done.54), kind=kLoop, calls=%fused_computation.5 | loop fusion | flops 33554432 | bytes 83951616 | tf_op jit(solution)/shard_map/while/body/eval_jaxpr/convert_element_type | solution.py:267
  1017.0 26.3 %all-to-all-done = bf16[8,256,1024]{2,1,0:T(8,128)(2,1)} async-done(((bf16[8,256,1024]{2,1,0:T(8,128)(2,1)}), bf16[8,256,1024]{2,1,0:T(8,128)(2,1)}, u32[]{:S(2)}, u32[]{:S(2)}) %all-to-all-start) | async-done | bytes 4194336 | tf_op jit(solution)/shard_map/all_to_all | solution.py:310
  1057.5 18.4 %collective-permute-done.47 = bf16[256,2048]{1,0:T(8,128)(2,1)} collective-permute-done((bf16[256,2048]{1,0:T(8,128)(2,1)}, bf16[256,2048]{1,0:T(8,128)(2,1)}, u32[]{:S(2)}, u32[]{:S(2)}) %collective-permute-start.47) | collective-permute-done | bytes 1048608 | tf_op jit(solution)/shard_map/ppermute | solution.py:86
  (418 shorter events, 557.5 us)
Async XLA Ops:
  7.2 112.6 %all-gather.18.cloned.1.call-start = ((), (), s32[]{:S(2)}) async-start(), calls=%async_computation.16 | async-start | bytes 4866048 | tf_op jit(solution)/shard_map/all_gather | solution.py:125
  9.7 138.9 %all-gather.8.cloned.1.call-start = ((), (), s32[]{:S(2)}) async-start(), calls=%async_computation.7 | async-start | bytes 4718592 | tf_op jit(solution)/shard_map/all_gather | solution.py:141
  10.4 239.3 %all-gather.10.cloned.1.call-start = ((), (), s32[]{:S(2)}) async-start(), calls=%async_computation.8 | async-start | bytes 4718592 | tf_op jit(solution)/shard_map/all_gather | solution.py:142
  11.2 416.2 %all-gather.16.cloned.1.call-start = ((), (), s32[]{:S(2)}) async-start(), calls=%async_computation.11 | async-start | bytes 14155776 | tf_op jit(solution)/shard_map/all_gather | solution.py:143
  11.7 434.7 %all-gather.14.cloned.1.call-start = ((), (), s32[]{:S(2)}) async-start(), calls=%async_computation.10 | async-start | bytes 14155776 | tf_op jit(solution)/shard_map/all_gather | solution.py:144
  12.3 453.2 %all-gather.12.cloned.1.call-start = ((), (), s32[]{:S(2)}) async-start(), calls=%async_computation.9 | async-start | bytes 14155776 | tf_op jit(solution)/shard_map/all_gather | solution.py:145
  51.4 38.2 %collective-permute-start.4 = (bf16[256,2048]{1,0:T(8,128)(2,1)S(1)}, bf16[256,2048]{1,0:T(8,128)(2,1)}, u32[]{:S(2)}, u32[]{:S(2)}) collective-permute-start(bf16[256,2048]{1,0:T(8,128)(2,1)S(1)} %collective-permute-done.3), channel_id=1, source_target_pairs={{1,0},{2,1},{5,4},{6,5},{9,8},{10,9},{13,12},{14,13},{17,16},{18,1... | collective-permute-start | bytes 3145736 | tf_op jit(solution)/shard_map/ppermute | solution.py:58
  52.7 38.2 %collective-permute-start.2 = (bf16[256,2048]{1,0:T(8,128)(2,1)}, bf16[256,2048]{1,0:T(8,128)(2,1)}, u32[]{:S(2)}, u32[]{:S(2)}) collective-permute-start(bf16[256,2048]{1,0:T(8,128)(2,1)} %collective-permute-done.1), channel_id=1, source_target_pairs={{2,3},{6,7},{10,11},{14,15},{18,19},{22,23},{26,27},{30,31}} | collective-permute-start | bytes 3145736 | tf_op jit(solution)/shard_map/ppermute | solution.py:55
  54.5 873.5 %reduce-scatter.5.cloned.1.call-start = ((), (), s32[]{:S(2)}) async-start(), calls=%async_computation.12 | async-start | bytes 14155776 | tf_op jit(solution)/shard_map/reduce_scatter | solution.py:236
  131.5 65.6 %collective-permute-start.9 = (bf16[256,2048]{1,0:T(8,128)(2,1)S(1)}, bf16[256,2048]{1,0:T(8,128)(2,1)}, u32[]{:S(2)}, u32[]{:S(2)}) collective-permute-start(bf16[256,2048]{1,0:T(8,128)(2,1)S(1)} %copy-done.16), channel_id=1, source_target_pairs={{1,0},{2,1},{3,2},{5,4},{6,5},{7,6},{9,8},{10,9},{11,10},{13,12},{... | collective-permute-start | bytes 3145736 | tf_op jit(solution)/shard_map/ppermute | solution.py:58
  132.8 38.9 %collective-permute-start.6 = (bf16[256,2048]{1,0:T(8,128)(2,1)S(1)}, bf16[256,2048]{1,0:T(8,128)(2,1)}, u32[]{:S(2)}, u32[]{:S(2)}) collective-permute-start(bf16[256,2048]{1,0:T(8,128)(2,1)S(1)} %copy-done.16), channel_id=1, source_target_pairs={{0,1},{1,2},{2,3},{4,5},{5,6},{6,7},{8,9},{9,10},{10,11},{12,13},{... | collective-permute-start | bytes 3145736 | tf_op jit(solution)/shard_map/ppermute | solution.py:55
  524.4 407.0 %reduce-scatter.7.cloned.1.call-start = ((), (), s32[]{:S(2)}) async-start(), calls=%async_computation.13 | async-start | bytes 14155776 | tf_op jit(solution)/shard_map/reduce_scatter | solution.py:236
  543.8 391.0 %reduce-scatter.9.cloned.1.call-start = ((), (), s32[]{:S(2)}) async-start(), calls=%async_computation.14 | async-start | bytes 14155776 | tf_op jit(solution)/shard_map/reduce_scatter | solution.py:236
  630.7 44.6 %collective-permute-start.29 = (bf16[256,2048]{1,0:T(8,128)(2,1)S(1)}, bf16[256,2048]{1,0:T(8,128)(2,1)S(1)}, u32[]{:S(2)}, u32[]{:S(2)}) collective-permute-start(bf16[256,2048]{1,0:T(8,128)(2,1)S(1)} %fusion.38), channel_id=1, source_target_pairs={{1,0},{2,1},{3,2},{5,4},{6,5},{7,6},{9,8},{10,9},{11,10},{13,12},{... | collective-permute-start | bytes 3145736 | tf_op jit(solution)/shard_map/ppermute | solution.py:86
  767.7 219.0 %all-to-all-start.2 = ((bf16[8,1024,256]{2,1,0:T(8,128)(2,1)}), bf16[8,1024,256]{2,1,0:T(8,128)(2,1)}, u32[]{:S(2)}, u32[]{:S(2)}) async-start(bf16[8,1024,256]{2,1,0:T(8,128)(2,1)} %bitcast.367), calls=%async_computation.6 | async-start | bytes 8388608 | tf_op jit(solution)/shard_map/all_to_all | solution.py:320
  772.3 241.7 %reduce-scatter.11.cloned.1.call-start = ((), (), s32[]{:S(2)}) async-start(), calls=%async_computation.15 | async-start | bytes 2433024 | tf_op jit(solution)/shard_map/reduce_scatter | solution.py:348
  776.4 146.1 %collective-permute-start.36 = (bf16[256,2048]{1,0:T(8,128)(2,1)}, bf16[256,2048]{1,0:T(8,128)(2,1)}, u32[]{:S(2)}, u32[]{:S(2)}) collective-permute-start(bf16[256,2048]{1,0:T(8,128)(2,1)} %get-tuple-element.113), channel_id=1, source_target_pairs={{0,1},{4,5},{8,9},{12,13},{16,17},{20,21},{24,25},{28,29}} | collective-permute-start | bytes 3145736 | tf_op jit(solution)/shard_map/ppermute | solution.py:80
  779.3 172.6 %collective-permute-start.39 = (bf16[256,2048]{1,0:T(8,128)(2,1)}, bf16[256,2048]{1,0:T(8,128)(2,1)}, u32[]{:S(2)}, u32[]{:S(2)}) collective-permute-start(bf16[256,2048]{1,0:T(8,128)(2,1)} %get-tuple-element.114), channel_id=1, source_target_pairs={{3,2},{7,6},{11,10},{15,14},{19,18},{23,22},{27,26},{31,30}} | collective-permute-start | bytes 3145736 | tf_op jit(solution)/shard_map/ppermute | solution.py:86
  956.9 37.3 %collective-permute-start.40 = (bf16[256,2048]{1,0:T(8,128)(2,1)}, bf16[256,2048]{1,0:T(8,128)(2,1)}, u32[]{:S(2)}, u32[]{:S(2)}) collective-permute-start(bf16[256,2048]{1,0:T(8,128)(2,1)} %get-tuple-element.112), channel_id=1, source_target_pairs={{2,1},{3,2},{6,5},{7,6},{10,9},{11,10},{14,13},{15,14},{18,17},{19... | collective-permute-start | bytes 3145736 | tf_op jit(solution)/shard_map/ppermute | solution.py:86
  958.6 43.8 %collective-permute-start.45 = (bf16[256,2048]{1,0:T(8,128)(2,1)S(1)}, bf16[256,2048]{1,0:T(8,128)(2,1)S(1)}, u32[]{:S(2)}, u32[]{:S(2)}) collective-permute-start(bf16[256,2048]{1,0:T(8,128)(2,1)S(1)} %get-tuple-element.110), channel_id=1, source_target_pairs={{3,2},{7,6},{11,10},{15,14},{19,18},{23,22},{27,26},{31,30}} | collective-permute-start | bytes 3145736 | tf_op jit(solution)/shard_map/ppermute | solution.py:86
  986.7 56.6 %all-to-all-start = ((bf16[8,256,1024]{2,1,0:T(8,128)(2,1)}), bf16[8,256,1024]{2,1,0:T(8,128)(2,1)}, u32[]{:S(2)}, u32[]{:S(2)}) async-start(bf16[8,256,1024]{2,1,0:T(8,128)(2,1)} %bitcast.381), calls=%async_computation.3 | async-start | bytes 8388608 | tf_op jit(solution)/shard_map/all_to_all | solution.py:310
  991.3 87.7 %collective-permute-start.38 = (bf16[256,2048]{1,0:T(8,128)(2,1)}, bf16[256,2048]{1,0:T(8,128)(2,1)}, u32[]{:S(2)}, u32[]{:S(2)}) collective-permute-start(bf16[256,2048]{1,0:T(8,128)(2,1)} %get-tuple-element.111), channel_id=1, source_target_pairs={{0,1},{1,2},{2,3},{4,5},{5,6},{6,7},{8,9},{9,10},{10,11},{12,13},{... | collective-permute-start | bytes 3145736 | tf_op jit(solution)/shard_map/ppermute | solution.py:80
  997.4 81.6 %collective-permute-start.41 = (bf16[256,2048]{1,0:T(8,128)(2,1)}, bf16[256,2048]{1,0:T(8,128)(2,1)}, u32[]{:S(2)}, u32[]{:S(2)}) collective-permute-start(bf16[256,2048]{1,0:T(8,128)(2,1)} %fusion.31), channel_id=1, source_target_pairs={{1,0},{2,1},{3,2},{5,4},{6,5},{7,6},{9,8},{10,9},{11,10},{13,12},{... | collective-permute-start | bytes 3145736 | tf_op jit(solution)/shard_map/ppermute | solution.py:86
  1008.0 49.5 %collective-permute-start.44 = (bf16[256,2048]{1,0:T(8,128)(2,1)}, bf16[256,2048]{1,0:T(8,128)(2,1)}, u32[]{:S(2)}, u32[]{:S(2)}) collective-permute-start(bf16[256,2048]{1,0:T(8,128)(2,1)} %get-tuple-element.107), channel_id=1, source_target_pairs={{0,1},{1,2},{2,3},{4,5},{5,6},{6,7},{8,9},{9,10},{10,11},{12,13},{... | collective-permute-start | bytes 3145736 | tf_op jit(solution)/shard_map/ppermute | solution.py:80
  (112 other events, 2347.5 us)
Sparse Core Ops, SparseCore 0:
  11.4 73.0 all-gather.17
  86.4 35.5 all-gather.7
  123.9 37.3 all-gather.9
  163.0 71.9 all-gather.15
  236.8 71.9 all-gather.13
  310.6 71.9 all-gather.11
  524.5 91.8 reduce-scatter.4
  619.9 92.2 reduce-scatter.6
  715.7 135.0 reduce-scatter.8
  952.0 54.4 reduce-scatter.10

commit v12 on v11

--- a/solution.py
+++ b/solution.py
@@ -192,7 +192,6 @@
 
     context_all, probs_all = lax.map(attend, (query_seq, key_seq, value_seq, prefix_len))
     context_b = context_all.reshape(group_rows, per_dev * HD).astype(jnp.bfloat16)
-    context_b, grad_rows = lax.optimization_barrier((context_b, grad_rows))
     attn_out = tp_scatter_sum(
         jnp.dot(context_b, out_w, preferred_element_type=jnp.float32), tp_size, jnp.bfloat16
     )

time: 1100 us -> 1110 us (level)
  starting transfers between devices: 120 us -> 136 us
    ppermute x12, starting transfers between devices: 45.7 us -> 57.6 us  [tp_scatter_sum(): lax.ppermute(outgoing.astype(send_type), 'tp', [(i, i + 1) for i in range...]
    unnamed x181 -> x183, local copies, waits for them, and re-layouts: 23.3 us -> 25.1 us
  transfers between devices with their start and end apart: 61 -> 61, of which waited for: 25 -> 24; matrix products, arithmetic and copies ran while one was open for 43% -> 43% of each run, Pallas kernels for 0% -> 0%
where the time goes in v12:
time: 1110 us
  waiting for transfers between devices  404 us (36%)
  matrix products  326 us (29%)
  other arithmetic  155 us (14%)
  starting transfers between devices  136 us (12%)
  local copies, waits for them, and re-layouts  68.3 us (6%)
  between operations  16.9 us (2%)
    ppermute x12, waiting for transfers between devices, tp_gather(): lax.ppermute(going_left, 'tp', [(i + 1, i) for i in range(0, count - step)])  151 us
    ppermute x12, waiting for transfers between devices, tp_scatter_sum(): lax.ppermute(outgoing.astype(send_type), 'tp', [(i, i + 1) for i in range...  97.4 us
    ppermute x12, waiting for transfers between devices, tp_scatter_sum(): lax.ppermute(outgoing.astype(send_type), 'tp', [(i, i - 1) for i in range...  71.9 us
    ppermute x12, starting transfers between devices, tp_scatter_sum(): lax.ppermute(outgoing.astype(send_type), 'tp', [(i, i + 1) for i in range...  57.6 us
    ppermute x12, waiting for transfers between devices, tp_gather(): lax.ppermute(going_right, 'tp', [(i, i + 1) for i in range(step - 1, coun...  54.4 us
    unnamed x2, matrix products  38.2 us
    ppermute x12, starting transfers between devices, tp_gather(): lax.ppermute(going_right, 'tp', [(i, i + 1) for i in range(step - 1, coun...  33.8 us
    convert_element_type x12, other arithmetic, tp_scatter_sum(): outgoing.astype(send_type)  33.7 us
  transfers between devices with their start and end apart: 61, of which 24 were waited for; matrix products, arithmetic and copies ran while one was open for 43% of the time, Pallas kernels for 0%

profile of v12, /device:TPU:0, one launch (start us, length us, event | category | flops | bytes accessed | tf_op | source)
XLA Modules:
  0.0 1105.2 jit_solution(618366804654818515)
XLA Ops:
  18.7 27.4 %collective-permute-done = bf16[256,2048]{1,0:T(8,128)(2,1)S(1)} collective-permute-done((bf16[256,2048]{1,0:T(8,128)(2,1)S(1)}, bf16[256,2048]{1,0:T(8,128)(2,1)S(1)}, u32[]{:S(2)}, u32[]{:S(2)}) %collective-permute-start) | collective-permute-done | bytes 1048608 | tf_op jit(solution)/shard_map/ppermute | solution.py:55
  56.6 33.1 %collective-permute-done.4 = bf16[256,2048]{1,0:T(8,128)(2,1)} collective-permute-done((bf16[256,2048]{1,0:T(8,128)(2,1)S(1)}, bf16[256,2048]{1,0:T(8,128)(2,1)}, u32[]{:S(2)}, u32[]{:S(2)}) %collective-permute-start.4) | collective-permute-done | bytes 1048608 | tf_op jit(solution)/shard_map/ppermute | solution.py:58
  95.3 19.4 %collective-permute-done.5 = bf16[256,2048]{1,0:T(8,128)(2,1)S(1)} collective-permute-done((bf16[256,2048]{1,0:T(8,128)(2,1)}, bf16[256,2048]{1,0:T(8,128)(2,1)S(1)}, u32[]{:S(2)}, u32[]{:S(2)}) %collective-permute-start.5) | collective-permute-done | bytes 1048608 | tf_op jit(solution)/shard_map/ppermute | solution.py:58
  159.7 21.2 %fusion.114 = (f32[8,1024]{1,0:T(8,128)S(1)}, f32[8,1024,1024]{1,2,0:T(8,128)}) fusion(pred[1024,1024]{0,1:T(8,128)(4,1)} %fusion.16, bf16[1024,64]{0,1:T(8,128)(2,1)S(1)} %get-tuple-element.139, bf16[1024,64]{0,1:T(8,128)(2,1)S(1)} %get-tuple-element.140, bf16[1024,8,64]{2,0,1:T(8,128)(2,1)} %get-tuple-element.122, ...), kind=kOutput, calls=%fused_computation.258 | convolution fusion | flops 2185757696 | bytes 36995072 | tf_op jit(solution)/shard_map/while/body/eval_jaxpr/sub | solution.py:182
  240.8 20.6 %collective-permute-done.7 = bf16[256,2048]{1,0:T(8,128)(2,1)} collective-permute-done((bf16[256,2048]{1,0:T(8,128)(2,1)}, bf16[256,2048]{1,0:T(8,128)(2,1)}, u32[]{:S(2)}, u32[]{:S(2)}) %collective-permute-start.7) | collective-permute-done | bytes 1048608 | tf_op jit(solution)/shard_map/ppermute | solution.py:80
  280.7 17.9 %collective-permute-start.8 = (bf16[256,2048]{1,0:T(8,128)(2,1)S(1)}, bf16[256,2048]{1,0:T(8,128)(2,1)}, u32[]{:S(2)}, u32[]{:S(2)}) collective-permute-start(bf16[256,2048]{1,0:T(8,128)(2,1)S(1)} %get-tuple-element.115), channel_id=1, source_target_pairs={{0,1},{1,2},{2,3},{4,5},{5,6},{6,7},{8,9},{9,10},{10,11},{12,13},{... | collective-permute-start | bytes 3145736 | tf_op jit(solution)/shard_map/ppermute | solution.py:80
  305.5 24.7 %collective-permute-done.11 = bf16[256,2048]{1,0:T(8,128)(2,1)} collective-permute-done((bf16[256,2048]{1,0:T(8,128)(2,1)}, bf16[256,2048]{1,0:T(8,128)(2,1)}, u32[]{:S(2)}, u32[]{:S(2)}) %collective-permute-start.11) | collective-permute-done | bytes 1048608 | tf_op jit(solution)/shard_map/ppermute | solution.py:86
  359.7 37.0 %collective-permute-done.21 = bf16[256,2048]{1,0:T(8,128)(2,1)S(1)} collective-permute-done((bf16[256,2048]{1,0:T(8,128)(2,1)S(1)}, bf16[256,2048]{1,0:T(8,128)(2,1)S(1)}, u32[]{:S(2)}, u32[]{:S(2)}) %collective-permute-start.21) | collective-permute-done | bytes 1048608 | tf_op jit(solution)/shard_map/ppermute | solution.py:58
  401.3 18.8 %collective-permute-done.22 = bf16[256,2048]{1,0:T(8,128)(2,1)S(1)} collective-permute-done((bf16[256,2048]{1,0:T(8,128)(2,1)S(1)}, bf16[256,2048]{1,0:T(8,128)(2,1)S(1)}, u32[]{:S(2)}, u32[]{:S(2)}) %collective-permute-start.22) | collective-permute-done | bytes 1048608 | tf_op jit(solution)/shard_map/ppermute | solution.py:58
  440.6 19.1 %fusion.117 = f32[1024,3072]{0,1} fusion(bf16[1024,2048]{1,0:T(8,128)(2,1)} %bitcast.371, bf16[2048,3072]{0,1:T(8,128)(2,1)} %bitcast.399), kind=kOutput, calls=%fused_computation.261 | convolution fusion | flops 12884901888 | bytes 29360128
  459.7 19.1 %fusion.116 = f32[1024,3072]{0,1} fusion(bf16[1024,2048]{1,0:T(8,128)(2,1)} %bitcast.372, bf16[2048,3072]{0,1:T(8,128)(2,1)} %bitcast.400), kind=kOutput, calls=%fused_computation.260 | convolution fusion | flops 12884901888 | bytes 29360128
  478.7 19.2 %fusion.115 = f32[1024,16,192]{0,2,1:T(8,128)} fusion(bf16[1024,2048,1]{1,0,2:T(8,128)(2,1)} %bitcast.376, bf16[16,192,2048]{2,1,0:T(8,128)(2,1)} %all-gather.12.cloned.1.call-done), kind=kOutput, calls=%fused_computation.259 | convolution fusion | flops 12884901888 | bytes 29360128 | tf_op jit(solution)/shard_map/td,efd->tef/dot_general | solution.py:215
  497.9 20.4 %multiply_convert_fusion = (bf16[1024,16,192]{0,2,1:T(8,128)(2,1)}, bf16[1024,16,192]{0,2,1:T(8,128)(2,1)}, bf16[1024,16,192]{0,2,1:T(8,128)(2,1)}) fusion(f32[1024,16,192]{0,2,1:T(8,128)} %bitcast.366, f32[1024,16]{0,1:T(8,128)S(1)} %select_reduce_fusion, f32[1024,16,192]{0,2,1:T(8,128)S(1)} %bitcast.365, f32[1024,16,192]{0,2,1:T(8,128)} %fusion.115), kind=kLoop, calls=%fused_computation.15 | loop fusion | flops 59768832 | bytes 56688640 | tf_op jit(solution)/shard_map/convert_element_type | solution.py:209
  518.4 19.2 %convolution_convert_fusion = bf16[16,192,2048]{2,1,0:T(8,128)(2,1)} fusion(bf16[1024,16,192]{0,2,1:T(8,128)(2,1)} %get-tuple-element.100, bf16[1024,2048,1]{1,0,2:T(8,128)(2,1)} %bitcast.377), kind=kOutput, calls=%fused_computation.33 | convolution fusion | flops 12891193344 | bytes 23068672 | tf_op jit(solution)/shard_map/tef,td->efd/dot_general | solution.py:227
  537.6 19.3 %convert_bitcast_fusion.1 = bf16[16,2048,192]{1,2,0:T(8,128)(2,1)} fusion(bf16[1024,16,192]{0,2,1:T(8,128)(2,1)} %get-tuple-element.101, bf16[1024,2048,1]{1,0,2:T(8,128)(2,1)} %bitcast.373), kind=kOutput, calls=%fused_computation.14 | convolution fusion | flops 12891193344 | bytes 23068672 | tf_op jit(solution)/shard_map/td,tef->edf/dot_general | solution.py:225
  557.0 17.7 %fusion.118 = f32[1024,2048,1]{1,0,2:T(8,128)S(1)} fusion(bf16[1024,16,192]{0,2,1:T(8,128)(2,1)} %get-tuple-element.101, bf16[16,2048,192]{1,2,0:T(8,128)(2,1)} %all-gather.16.cloned.1.call-done), kind=kOutput, calls=%fused_computation.262 | convolution fusion | flops 12884901888 | bytes 27262976 | tf_op jit(solution)/shard_map/tef,edf->td/dot_general | solution.py:222
  574.7 19.3 %bitcast_add_fusion = f32[1024,2048]{1,0:T(8,128)S(1)} fusion(f32[1024,2048,1]{1,0,2:T(8,128)S(1)} %fusion.118, bf16[1024,16,192]{0,2,1:T(8,128)(2,1)} %get-tuple-element.102, bf16[16,2048,192]{1,2,0:T(8,128)(2,1)} %all-gather.14.cloned.1.call-done), kind=kOutput, calls=%fused_computation.21 | convolution fusion | flops 12886999040 | bytes 35651584 | tf_op jit(solution)/shard_map/tef,edf->td/dot_general | solution.py:224
  597.6 17.8 %collective-permute-done.24 = bf16[256,2048]{1,0:T(8,128)(2,1)S(1)} collective-permute-done((bf16[256,2048]{1,0:T(8,128)(2,1)S(1)}, bf16[256,2048]{1,0:T(8,128)(2,1)S(1)}, u32[]{:S(2)}, u32[]{:S(2)}) %collective-permute-start.24) | collective-permute-done | bytes 1048608 | tf_op jit(solution)/shard_map/ppermute | solution.py:80
  656.2 28.8 %collective-permute-done.29 = bf16[256,2048]{1,0:T(8,128)(2,1)S(1)} collective-permute-done((bf16[256,2048]{1,0:T(8,128)(2,1)S(1)}, bf16[256,2048]{1,0:T(8,128)(2,1)S(1)}, u32[]{:S(2)}, u32[]{:S(2)}) %collective-permute-start.29) | collective-permute-done | bytes 1048608 | tf_op jit(solution)/shard_map/ppermute | solution.py:86
  725.5 19.0 %convolution_bitcast_fusion = f32[1024,2048]{1,0:T(8,128)} fusion(bf16[1024,16,192]{0,2,1:T(8,128)(2,1)} %get-tuple-element.100, bf16[16,192,2048]{2,1,0:T(8,128)(2,1)} %all-gather.12.cloned.1.call-done), kind=kOutput, calls=%fused_computation.35 | convolution fusion | flops 12884901888 | bytes 27262976 | tf_op jit(solution)/shard_map/tef,efd->td/dot_general | solution.py:210
  801.6 25.5 %fusion.1 = (f32[8,1024]{1,0:T(8,128)S(1)}, f32[1024,1024,8]{1,0,2:T(8,128)}) fusion(f32[8,1024,1024]{1,2,0:T(8,128)} %get-tuple-element.152, f32[8,1024]{1,0:T(8,128)S(1)} %copy-done.58, bf16[1024,128,1]{1,0,2:T(8,128)(2,1)S(1)} %copy-done.73, bf16[1024,8,128]{0,2,1:T(8,128)(2,1)S(1)} %bitcast.401), kind=kOutput, calls=%fused_computation.3 | convolution fusion | flops 2172641280 | bytes 69533696 | tf_op jit(solution)/shard_map/while/body/eval_jaxpr/qhd,kd->hqk/dot_general | solution.py:261
  827.2 29.3 %fusion.3 = bf16[8,1024,1024]{1,2,0:T(8,128)(2,1)} fusion(f32[1024,1024,8]{1,0,2:T(8,128)} %get-tuple-element.154, f32[8,1024]{1,0:T(8,128)S(1)} %get-tuple-element.153, f32[8,1024,1024]{1,2,0:T(8,128)} %get-tuple-element.152, f32[8,1024]{1,0:T(8,128)S(1)} %copy-done.58), kind=kLoop, calls=%fused_computation.5 | loop fusion | flops 33554432 | bytes 83951616 | tf_op jit(solution)/shard_map/while/body/eval_jaxpr/convert_element_type | solution.py:266
  1030.5 26.3 %all-to-all-done = bf16[8,256,1024]{2,1,0:T(8,128)(2,1)} async-done(((bf16[8,256,1024]{2,1,0:T(8,128)(2,1)}), bf16[8,256,1024]{2,1,0:T(8,128)(2,1)}, u32[]{:S(2)}, u32[]{:S(2)}) %all-to-all-start) | async-done | bytes 4194336 | tf_op jit(solution)/shard_map/all_to_all | solution.py:309
  1071.0 18.4 %collective-permute-done.47 = bf16[256,2048]{1,0:T(8,128)(2,1)} collective-permute-done((bf16[256,2048]{1,0:T(8,128)(2,1)}, bf16[256,2048]{1,0:T(8,128)(2,1)}, u32[]{:S(2)}, u32[]{:S(2)}) %collective-permute-start.47) | collective-permute-done | bytes 1048608 | tf_op jit(solution)/shard_map/ppermute | solution.py:86
  (421 shorter events, 549.8 us)
Async XLA Ops:
  7.2 111.5 %all-gather.18.cloned.1.call-start = ((), (), s32[]{:S(2)}) async-start(), calls=%async_computation.16 | async-start | bytes 4866048 | tf_op jit(solution)/shard_map/all_gather | solution.py:125
  9.7 128.0 %all-gather.8.cloned.1.call-start = ((), (), s32[]{:S(2)}) async-start(), calls=%async_computation.7 | async-start | bytes 4718592 | tf_op jit(solution)/shard_map/all_gather | solution.py:141
  10.4 185.5 %all-gather.10.cloned.1.call-start = ((), (), s32[]{:S(2)}) async-start(), calls=%async_computation.8 | async-start | bytes 4718592 | tf_op jit(solution)/shard_map/all_gather | solution.py:142
  11.2 429.4 %all-gather.16.cloned.1.call-start = ((), (), s32[]{:S(2)}) async-start(), calls=%async_computation.11 | async-start | bytes 14155776 | tf_op jit(solution)/shard_map/all_gather | solution.py:143
  11.7 447.9 %all-gather.14.cloned.1.call-start = ((), (), s32[]{:S(2)}) async-start(), calls=%async_computation.10 | async-start | bytes 14155776 | tf_op jit(solution)/shard_map/all_gather | solution.py:144
  12.3 466.4 %all-gather.12.cloned.1.call-start = ((), (), s32[]{:S(2)}) async-start(), calls=%async_computation.9 | async-start | bytes 14155776 | tf_op jit(solution)/shard_map/all_gather | solution.py:145
  54.5 887.2 %reduce-scatter.5.cloned.1.call-start = ((), (), s32[]{:S(2)}) async-start(), calls=%async_computation.12 | async-start | bytes 14155776 | tf_op jit(solution)/shard_map/reduce_scatter | solution.py:235
  303.3 43.2 %collective-permute-start.16 = (bf16[256,2048]{1,0:T(8,128)(2,1)}, bf16[256,2048]{1,0:T(8,128)(2,1)S(1)}, u32[]{:S(2)}, u32[]{:S(2)}) collective-permute-start(bf16[256,2048]{1,0:T(8,128)(2,1)} %collective-permute-done.15), channel_id=1, source_target_pairs={{1,0},{2,1},{5,4},{6,5},{9,8},{10,9},{13,12},{14,13},{17,16},{18,1... | collective-permute-start | bytes 3145736 | tf_op jit(solution)/shard_map/ppermute | solution.py:58
  304.8 43.1 %collective-permute-start.14 = (bf16[256,2048]{1,0:T(8,128)(2,1)}, bf16[256,2048]{1,0:T(8,128)(2,1)S(1)}, u32[]{:S(2)}, u32[]{:S(2)}) collective-permute-start(bf16[256,2048]{1,0:T(8,128)(2,1)} %collective-permute-done.13), channel_id=1, source_target_pairs={{2,3},{6,7},{10,11},{14,15},{18,19},{22,23},{26,27},{30,31}} | collective-permute-start | bytes 3145736 | tf_op jit(solution)/shard_map/ppermute | solution.py:55
  346.6 52.3 %collective-permute-start.17 = (bf16[256,2048]{1,0:T(8,128)(2,1)S(1)}, bf16[256,2048]{1,0:T(8,128)(2,1)S(1)}, u32[]{:S(2)}, u32[]{:S(2)}) collective-permute-start(bf16[256,2048]{1,0:T(8,128)(2,1)S(1)} %collective-permute-done.16), channel_id=1, source_target_pairs={{1,0},{5,4},{9,8},{13,12},{17,16},{21,20},{25,24},{29,28}} | collective-permute-start | bytes 3145736 | tf_op jit(solution)/shard_map/ppermute | solution.py:58
  349.2 47.5 %collective-permute-start.21 = (bf16[256,2048]{1,0:T(8,128)(2,1)S(1)}, bf16[256,2048]{1,0:T(8,128)(2,1)S(1)}, u32[]{:S(2)}, u32[]{:S(2)}) collective-permute-start(bf16[256,2048]{1,0:T(8,128)(2,1)S(1)} %multiply_convert_fusion.5), channel_id=1, source_target_pairs={{1,0},{2,1},{3,2},{5,4},{6,5},{7,6},{9,8},{10,9},{11,10},{13,12},{... | collective-permute-start | bytes 3145736 | tf_op jit(solution)/shard_map/ppermute | solution.py:58
  356.3 41.7 %collective-permute-start.19 = (bf16[256,2048]{1,0:T(8,128)(2,1)S(1)}, bf16[256,2048]{1,0:T(8,128)(2,1)S(1)}, u32[]{:S(2)}, u32[]{:S(2)}) collective-permute-start(bf16[256,2048]{1,0:T(8,128)(2,1)S(1)} %collective-permute-done.18), channel_id=1, source_target_pairs={{1,2},{2,3},{5,6},{6,7},{9,10},{10,11},{13,14},{14,15},{17,18},{18... | collective-permute-start | bytes 3145736 | tf_op jit(solution)/shard_map/ppermute | solution.py:55
  537.6 407.6 %reduce-scatter.7.cloned.1.call-start = ((), (), s32[]{:S(2)}) async-start(), calls=%async_computation.13 | async-start | bytes 14155776 | tf_op jit(solution)/shard_map/reduce_scatter | solution.py:235
  556.9 391.7 %reduce-scatter.9.cloned.1.call-start = ((), (), s32[]{:S(2)}) async-start(), calls=%async_computation.14 | async-start | bytes 14155776 | tf_op jit(solution)/shard_map/reduce_scatter | solution.py:235
  643.8 41.2 %collective-permute-start.29 = (bf16[256,2048]{1,0:T(8,128)(2,1)S(1)}, bf16[256,2048]{1,0:T(8,128)(2,1)S(1)}, u32[]{:S(2)}, u32[]{:S(2)}) collective-permute-start(bf16[256,2048]{1,0:T(8,128)(2,1)S(1)} %fusion.37), channel_id=1, source_target_pairs={{1,0},{2,1},{3,2},{5,4},{6,5},{7,6},{9,8},{10,9},{11,10},{13,12},{... | collective-permute-start | bytes 3145736 | tf_op jit(solution)/shard_map/ppermute | solution.py:86
  780.9 219.4 %all-to-all-start.2 = ((bf16[8,1024,256]{2,1,0:T(8,128)(2,1)}), bf16[8,1024,256]{2,1,0:T(8,128)(2,1)}, u32[]{:S(2)}, u32[]{:S(2)}) async-start(bf16[8,1024,256]{2,1,0:T(8,128)(2,1)} %bitcast.363), calls=%async_computation.6 | async-start | bytes 8388608 | tf_op jit(solution)/shard_map/all_to_all | solution.py:319
  785.9 241.7 %reduce-scatter.11.cloned.1.call-start = ((), (), s32[]{:S(2)}) async-start(), calls=%async_computation.15 | async-start | bytes 2433024 | tf_op jit(solution)/shard_map/reduce_scatter | solution.py:347
  790.0 146.3 %collective-permute-start.36 = (bf16[256,2048]{1,0:T(8,128)(2,1)}, bf16[256,2048]{1,0:T(8,128)(2,1)}, u32[]{:S(2)}, u32[]{:S(2)}) collective-permute-start(bf16[256,2048]{1,0:T(8,128)(2,1)} %get-tuple-element.109), channel_id=1, source_target_pairs={{0,1},{4,5},{8,9},{12,13},{16,17},{20,21},{24,25},{28,29}} | collective-permute-start | bytes 3145736 | tf_op jit(solution)/shard_map/ppermute | solution.py:80
  792.5 173.1 %collective-permute-start.39 = (bf16[256,2048]{1,0:T(8,128)(2,1)}, bf16[256,2048]{1,0:T(8,128)(2,1)}, u32[]{:S(2)}, u32[]{:S(2)}) collective-permute-start(bf16[256,2048]{1,0:T(8,128)(2,1)} %get-tuple-element.110), channel_id=1, source_target_pairs={{3,2},{7,6},{11,10},{15,14},{19,18},{23,22},{27,26},{31,30}} | collective-permute-start | bytes 3145736 | tf_op jit(solution)/shard_map/ppermute | solution.py:86
  972.4 43.5 %collective-permute-start.45 = (bf16[256,2048]{1,0:T(8,128)(2,1)S(1)}, bf16[256,2048]{1,0:T(8,128)(2,1)S(1)}, u32[]{:S(2)}, u32[]{:S(2)}) collective-permute-start(bf16[256,2048]{1,0:T(8,128)(2,1)S(1)} %get-tuple-element.106), channel_id=1, source_target_pairs={{3,2},{7,6},{11,10},{15,14},{19,18},{23,22},{27,26},{31,30}} | collective-permute-start | bytes 3145736 | tf_op jit(solution)/shard_map/ppermute | solution.py:86
  1000.2 56.6 %all-to-all-start = ((bf16[8,256,1024]{2,1,0:T(8,128)(2,1)}), bf16[8,256,1024]{2,1,0:T(8,128)(2,1)}, u32[]{:S(2)}, u32[]{:S(2)}) async-start(bf16[8,256,1024]{2,1,0:T(8,128)(2,1)} %bitcast.375), calls=%async_computation.3 | async-start | bytes 8388608 | tf_op jit(solution)/shard_map/all_to_all | solution.py:309
  1004.8 87.7 %collective-permute-start.38 = (bf16[256,2048]{1,0:T(8,128)(2,1)}, bf16[256,2048]{1,0:T(8,128)(2,1)}, u32[]{:S(2)}, u32[]{:S(2)}) collective-permute-start(bf16[256,2048]{1,0:T(8,128)(2,1)} %get-tuple-element.107), channel_id=1, source_target_pairs={{0,1},{1,2},{2,3},{4,5},{5,6},{6,7},{8,9},{9,10},{10,11},{12,13},{... | collective-permute-start | bytes 3145736 | tf_op jit(solution)/shard_map/ppermute | solution.py:80
  1010.8 81.7 %collective-permute-start.41 = (bf16[256,2048]{1,0:T(8,128)(2,1)}, bf16[256,2048]{1,0:T(8,128)(2,1)}, u32[]{:S(2)}, u32[]{:S(2)}) collective-permute-start(bf16[256,2048]{1,0:T(8,128)(2,1)} %fusion.30), channel_id=1, source_target_pairs={{1,0},{2,1},{3,2},{5,4},{6,5},{7,6},{9,8},{10,9},{11,10},{13,12},{... | collective-permute-start | bytes 3145736 | tf_op jit(solution)/shard_map/ppermute | solution.py:86
  1021.5 49.5 %collective-permute-start.44 = (bf16[256,2048]{1,0:T(8,128)(2,1)}, bf16[256,2048]{1,0:T(8,128)(2,1)}, u32[]{:S(2)}, u32[]{:S(2)}) collective-permute-start(bf16[256,2048]{1,0:T(8,128)(2,1)} %get-tuple-element.103), channel_id=1, source_target_pairs={{0,1},{1,2},{2,3},{4,5},{5,6},{6,7},{8,9},{9,10},{10,11},{12,13},{... | collective-permute-start | bytes 3145736 | tf_op jit(solution)/shard_map/ppermute | solution.py:80
  (113 other events, 2635.1 us)
Sparse Core Ops, SparseCore 0:
  11.4 73.0 all-gather.17
  86.4 35.5 all-gather.7
  123.9 37.3 all-gather.9
  163.0 71.9 all-gather.15
  236.8 71.9 all-gather.13
  310.6 71.9 all-gather.11
  537.7 91.2 reduce-scatter.4
  632.5 92.2 reduce-scatter.6
  728.3 132.3 reduce-scatter.8
  965.7 53.9 reduce-scatter.10

commit v13 on v11

--- a/solution.py
+++ b/solution.py
@@ -306,16 +306,9 @@
     (attn_gain_part,) = rows_back(attn_in_part)
     in_grad = residual_grad + input_norm_grad
     fsdp_size = lax.axis_size("fsdp")
-    query_proj_grad = jnp.sum(
-        lax.all_to_all(
-            query_part.astype(jnp.bfloat16).reshape(fsdp_size, -1, query_part.shape[1]),
-            "fsdp",
-            split_axis=0,
-            concat_axis=0,
-            tiled=True,
-        ).astype(jnp.float32),
-        axis=0,
-    )
+    query_proj_grad = lax.psum_scatter(
+        query_part.astype(jnp.bfloat16), "fsdp", scatter_dimension=0, tiled=True
+    ).astype(jnp.float32)
     output_proj_grad = jnp.sum(
         lax.all_to_all(
             output_part.astype(jnp.bfloat16)

time: 1100 us -> 1130 us (1.027)
  waiting for transfers between devices: 404 us -> 429 us
    all_to_all x1, waiting for transfers between devices: 0.01 us -> 34 us  [body(): lax.all_to_all(output_part.astype(jnp.bfloat16).reshape(output_part.shape...]
    all_to_all x1 -> x0, waiting for transfers between devices: 26.3 us -> none  [body(): lax.all_to_all(query_part.astype(jnp.bfloat16).reshape(fsdp_size, -1, que...]
    ppermute x12, waiting for transfers between devices: 103 us -> 124 us  [tp_scatter_sum(): lax.ppermute(outgoing.astype(send_type), 'tp', [(i, i + 1) for i in range...]
    unnamed x181 -> x187, local copies, waits for them, and re-layouts: 23.3 us -> 24.9 us
  transfers between devices with their start and end apart: 61 -> 61, of which waited for: 25 -> 26; matrix products, arithmetic and copies ran while one was open for 43% -> 41% of each run, Pallas kernels for 0% -> 0%
where the time goes in v13:
time: 1130 us; the launch traced here: 1120 us
  waiting for transfers between devices  429 us (38%)
  matrix products  328 us (29%)
  other arithmetic  156 us (14%)
  starting transfers between devices  122 us (11%)
  local copies, waits for them, and re-layouts  67.1 us (6%)
  between operations  16.6 us (1%)
    ppermute x12, waiting for transfers between devices, tp_gather(): lax.ppermute(going_left, 'tp', [(i + 1, i) for i in range(0, count - step)])  147 us
    ppermute x12, waiting for transfers between devices, tp_scatter_sum(): lax.ppermute(outgoing.astype(send_type), 'tp', [(i, i + 1) for i in range...  124 us
    ppermute x12, waiting for transfers between devices, tp_scatter_sum(): lax.ppermute(outgoing.astype(send_type), 'tp', [(i, i - 1) for i in range...  69.5 us
    ppermute x12, waiting for transfers between devices, tp_gather(): lax.ppermute(going_right, 'tp', [(i, i + 1) for i in range(step - 1, coun...  51.5 us
    ppermute x12, starting transfers between devices, tp_scatter_sum(): lax.ppermute(outgoing.astype(send_type), 'tp', [(i, i + 1) for i in range...  48.4 us
    unnamed x2, matrix products  38.2 us
    all_to_all x1, waiting for transfers between devices, body(): lax.all_to_all(output_part.astype(jnp.bfloat16).reshape(output_part.shape...  34 us
    convert_element_type x12, other arithmetic, tp_scatter_sum(): outgoing.astype(send_type)  32.6 us
  transfers between devices with their start and end apart: 61, of which 26 were waited for; matrix products, arithmetic and copies ran while one was open for 41% of the time, Pallas kernels for 0%

profile of v13, /device:TPU:0, one launch (start us, length us, event | category | flops | bytes accessed | tf_op | source)
XLA Modules:
  0.0 1118.7 jit_solution(7104994855092514783)
XLA Ops:
  18.7 27.4 %collective-permute-done = bf16[256,2048]{1,0:T(8,128)(2,1)S(1)} collective-permute-done((bf16[256,2048]{1,0:T(8,128)(2,1)S(1)}, bf16[256,2048]{1,0:T(8,128)(2,1)S(1)}, u32[]{:S(2)}, u32[]{:S(2)}) %collective-permute-start) | collective-permute-done | bytes 1048608 | tf_op jit(solution)/shard_map/ppermute | solution.py:55
  57.6 32.0 %collective-permute-done.4 = bf16[256,2048]{1,0:T(8,128)(2,1)} collective-permute-done((bf16[256,2048]{1,0:T(8,128)(2,1)S(1)}, bf16[256,2048]{1,0:T(8,128)(2,1)}, u32[]{:S(2)}, u32[]{:S(2)}) %collective-permute-start.4) | collective-permute-done | bytes 1048608 | tf_op jit(solution)/shard_map/ppermute | solution.py:58
  95.3 20.5 %collective-permute-done.5 = bf16[256,2048]{1,0:T(8,128)(2,1)S(1)} collective-permute-done((bf16[256,2048]{1,0:T(8,128)(2,1)}, bf16[256,2048]{1,0:T(8,128)(2,1)S(1)}, u32[]{:S(2)}, u32[]{:S(2)}) %collective-permute-start.5) | collective-permute-done | bytes 1048608 | tf_op jit(solution)/shard_map/ppermute | solution.py:58
  172.9 20.8 %fusion.114 = (f32[8,1024]{1,0:T(8,128)S(1)}, f32[8,1024,1024]{1,2,0:T(8,128)}) fusion(pred[1024,1024]{0,1:T(8,128)(4,1)} %fusion.17, bf16[1024,64]{0,1:T(8,128)(2,1)S(1)} %get-tuple-element.143, bf16[1024,64]{0,1:T(8,128)(2,1)S(1)} %copy-done.35, bf16[1024,8,64]{2,0,1:T(8,128)(2,1)} %get-tuple-element.126, bf16[1024,8,64]{2,0,1:T(8,128)(2,1)} %get-tuple-element.125), kind=kOutput, calls=%fused_computation.257 | convolution fusion | flops 2185757696 | bytes 36995072 | tf_op jit(solution)/shard_map/while/body/eval_jaxpr/sub | solution.py:182
  229.0 18.2 %collective-permute-done.11 = bf16[256,2048]{1,0:T(8,128)(2,1)S(1)} collective-permute-done((bf16[256,2048]{1,0:T(8,128)(2,1)S(1)}, bf16[256,2048]{1,0:T(8,128)(2,1)S(1)}, u32[]{:S(2)}, u32[]{:S(2)}) %collective-permute-start.11) | collective-permute-done | bytes 1048608 | tf_op jit(solution)/shard_map/ppermute | solution.py:58
  330.4 21.0 %collective-permute-done.17 = bf16[256,2048]{1,0:T(8,128)(2,1)} collective-permute-done((bf16[256,2048]{1,0:T(8,128)(2,1)S(1)}, bf16[256,2048]{1,0:T(8,128)(2,1)}, u32[]{:S(2)}, u32[]{:S(2)}) %collective-permute-start.17) | collective-permute-done | bytes 1048608 | tf_op jit(solution)/shard_map/ppermute | solution.py:86
  384.2 21.2 %collective-permute-done.22 = bf16[256,2048]{1,0:T(8,128)(2,1)S(1)} collective-permute-done((bf16[256,2048]{1,0:T(8,128)(2,1)S(1)}, bf16[256,2048]{1,0:T(8,128)(2,1)S(1)}, u32[]{:S(2)}, u32[]{:S(2)}) %collective-permute-start.22) | collective-permute-done | bytes 1048608 | tf_op jit(solution)/shard_map/ppermute | solution.py:58
  425.5 19.1 %fusion.117 = f32[1024,3072]{0,1} fusion(bf16[1024,2048]{1,0:T(8,128)(2,1)} %bitcast.378, bf16[2048,3072]{0,1:T(8,128)(2,1)} %bitcast.399), kind=kOutput, calls=%fused_computation.260 | convolution fusion | flops 12884901888 | bytes 29360128
  444.6 19.1 %fusion.116 = f32[1024,3072]{0,1} fusion(bf16[1024,2048]{1,0:T(8,128)(2,1)} %bitcast.379, bf16[2048,3072]{0,1:T(8,128)(2,1)} %bitcast.400), kind=kOutput, calls=%fused_computation.259 | convolution fusion | flops 12884901888 | bytes 29360128
  463.7 19.2 %fusion.15 = f32[1024,16,192]{0,2,1:T(8,128)} fusion(bf16[16,192,2048]{2,1,0:T(8,128)(2,1)} %all-gather.12.cloned.1.call-done, bf16[1024,2048]{1,0:T(8,128)(2,1)} %bitcast.376), kind=kOutput, calls=%fused_computation.38 | convolution fusion | flops 12884901888 | bytes 29360128 | tf_op jit(solution)/shard_map/td,efd->tef/dot_general | solution.py:216
  482.9 20.5 %multiply_convert_fusion = (bf16[1024,16,192]{0,2,1:T(8,128)(2,1)}, bf16[1024,16,192]{0,2,1:T(8,128)(2,1)}, bf16[1024,16,192]{0,2,1:T(8,128)(2,1)}) fusion(f32[1024,16,192]{0,2,1:T(8,128)} %bitcast.369, f32[1024,16]{0,1:T(8,128)S(1)} %select_reduce_fusion, f32[1024,16,192]{0,2,1:T(8,128)S(1)} %bitcast.368, f32[1024,16,192]{0,2,1:T(8,128)} %fusion.15), kind=kLoop, calls=%fused_computation.15 | loop fusion | flops 59768832 | bytes 56688640 | tf_op jit(solution)/shard_map/convert_element_type | solution.py:210
  503.4 19.3 %convolution_convert_fusion = bf16[16,192,2048]{2,1,0:T(8,128)(2,1)} fusion(bf16[1024,16,192]{0,2,1:T(8,128)(2,1)} %get-tuple-element.104, bf16[1024,2048]{1,0:T(8,128)(2,1)} %bitcast.377), kind=kOutput, calls=%fused_computation.32 | convolution fusion | flops 12891193344 | bytes 23068672 | tf_op jit(solution)/shard_map/tef,td->efd/dot_general | solution.py:228
  522.7 19.5 %convert_bitcast_fusion.1 = bf16[16,2048,192]{1,2,0:T(8,128)(2,1)} fusion(bf16[1024,16,192]{0,2,1:T(8,128)(2,1)} %get-tuple-element.105, bf16[1024,2048,1]{1,0,2:T(8,128)(2,1)} %bitcast.380), kind=kOutput, calls=%fused_computation.14 | convolution fusion | flops 12891193344 | bytes 23068672 | tf_op jit(solution)/shard_map/td,tef->edf/dot_general | solution.py:226
  542.3 17.8 %fusion.118 = f32[1024,2048,1]{1,0,2:T(8,128)S(1)} fusion(bf16[1024,16,192]{0,2,1:T(8,128)(2,1)} %get-tuple-element.105, bf16[16,2048,192]{1,2,0:T(8,128)(2,1)} %all-gather.16.cloned.1.call-done), kind=kOutput, calls=%fused_computation.261 | convolution fusion | flops 12884901888 | bytes 27262976 | tf_op jit(solution)/shard_map/tef,edf->td/dot_general | solution.py:223
  560.1 19.3 %bitcast_add_fusion = f32[1024,2048]{1,0:T(8,128)S(1)} fusion(f32[1024,2048,1]{1,0,2:T(8,128)S(1)} %fusion.118, bf16[1024,16,192]{0,2,1:T(8,128)(2,1)} %get-tuple-element.106, bf16[16,2048,192]{1,2,0:T(8,128)(2,1)} %all-gather.14.cloned.1.call-done), kind=kOutput, calls=%fused_computation.21 | convolution fusion | flops 12886999040 | bytes 35651584 | tf_op jit(solution)/shard_map/tef,edf->td/dot_general | solution.py:225
  582.9 17.8 %collective-permute-done.24 = bf16[256,2048]{1,0:T(8,128)(2,1)S(1)} collective-permute-done((bf16[256,2048]{1,0:T(8,128)(2,1)S(1)}, bf16[256,2048]{1,0:T(8,128)(2,1)S(1)}, u32[]{:S(2)}, u32[]{:S(2)}) %collective-permute-start.24) | collective-permute-done | bytes 1048608 | tf_op jit(solution)/shard_map/ppermute | solution.py:80
  605.7 16.3 %collective-permute-done.25 = bf16[256,2048]{1,0:T(8,128)(2,1)S(1)} collective-permute-done((bf16[256,2048]{1,0:T(8,128)(2,1)S(1)}, bf16[256,2048]{1,0:T(8,128)(2,1)S(1)}, u32[]{:S(2)}, u32[]{:S(2)}) %collective-permute-start.25) | collective-permute-done | bytes 1048608 | tf_op jit(solution)/shard_map/ppermute | solution.py:80
  641.1 32.1 %collective-permute-done.29 = bf16[256,2048]{1,0:T(8,128)(2,1)S(1)} collective-permute-done((bf16[256,2048]{1,0:T(8,128)(2,1)S(1)}, bf16[256,2048]{1,0:T(8,128)(2,1)S(1)}, u32[]{:S(2)}, u32[]{:S(2)}) %collective-permute-start.29) | collective-permute-done | bytes 1048608 | tf_op jit(solution)/shard_map/ppermute | solution.py:86
  713.7 19.1 %convolution_bitcast_fusion = f32[1024,2048]{1,0:T(8,128)} fusion(bf16[1024,16,192]{0,2,1:T(8,128)(2,1)} %get-tuple-element.104, bf16[16,192,2048]{2,1,0:T(8,128)(2,1)} %all-gather.12.cloned.1.call-done), kind=kOutput, calls=%fused_computation.34 | convolution fusion | flops 12884901888 | bytes 27262976 | tf_op jit(solution)/shard_map/tef,efd->td/dot_general | solution.py:211
  765.6 26.3 %fusion.1 = (f32[8,1024]{1,0:T(8,128)S(1)}, f32[1024,1024,8]{1,0,2:T(8,128)}) fusion(f32[8,1024,1024]{1,2,0:T(8,128)} %get-tuple-element.156, f32[8,1024]{1,0:T(8,128)S(1)} %copy-done.56, bf16[1024,128,1]{1,0,2:T(8,128)(2,1)S(1)} %copy-done.75, bf16[1024,8,128]{0,2,1:T(8,128)(2,1)S(1)} %bitcast.403), kind=kOutput, calls=%fused_computation.3 | convolution fusion | flops 2172641280 | bytes 69533696 | tf_op jit(solution)/shard_map/while/body/eval_jaxpr/qhd,kd->hqk/dot_general | solution.py:262
  791.8 28.5 %fusion.3 = bf16[8,1024,1024]{1,2,0:T(8,128)(2,1)} fusion(f32[1024,1024,8]{1,0,2:T(8,128)} %get-tuple-element.158, f32[8,1024]{1,0:T(8,128)S(1)} %get-tuple-element.157, f32[8,1024,1024]{1,2,0:T(8,128)} %get-tuple-element.156, f32[8,1024]{1,0:T(8,128)S(1)} %copy-done.56), kind=kLoop, calls=%fused_computation.5 | loop fusion | flops 33554432 | bytes 83951616 | tf_op jit(solution)/shard_map/while/body/eval_jaxpr/convert_element_type | solution.py:267
  928.2 22.6 %collective-permute-done.36 = bf16[256,2048]{1,0:T(8,128)(2,1)S(1)} collective-permute-done((bf16[256,2048]{1,0:T(8,128)(2,1)S(1)}, bf16[256,2048]{1,0:T(8,128)(2,1)S(1)}, u32[]{:S(2)}, u32[]{:S(2)}) %collective-permute-start.36) | collective-permute-done | bytes 1048608 | tf_op jit(solution)/shard_map/ppermute | solution.py:80
  1037.1 34.0 %all-to-all-done.1 = bf16[8,1024,256]{2,1,0:T(8,128)(2,1)} async-done(((bf16[8,1024,256]{2,1,0:T(8,128)(2,1)}), bf16[8,1024,256]{2,1,0:T(8,128)(2,1)}, u32[]{:S(2)}, u32[]{:S(2)}) %all-to-all-start.1) | async-done | bytes 4194336 | tf_op jit(solution)/shard_map/all_to_all | solution.py:313
  1086.9 16.3 %collective-permute-done.47 = bf16[256,2048]{1,0:T(8,128)(2,1)} collective-permute-done((bf16[256,2048]{1,0:T(8,128)(2,1)}, bf16[256,2048]{1,0:T(8,128)(2,1)}, u32[]{:S(2)}, u32[]{:S(2)}) %collective-permute-start.47) | collective-permute-done | bytes 1048608 | tf_op jit(solution)/shard_map/ppermute | solution.py:86
  (425 shorter events, 574.3 us)
Async XLA Ops:
  7.2 112.5 %all-gather.18.cloned.1.call-start = ((), (), s32[]{:S(2)}) async-start(), calls=%async_computation.17 | async-start | bytes 4866048 | tf_op jit(solution)/shard_map/all_gather | solution.py:125
  9.7 138.9 %all-gather.8.cloned.1.call-start = ((), (), s32[]{:S(2)}) async-start(), calls=%async_computation.7 | async-start | bytes 4718592 | tf_op jit(solution)/shard_map/all_gather | solution.py:141
  10.4 239.1 %all-gather.10.cloned.1.call-start = ((), (), s32[]{:S(2)}) async-start(), calls=%async_computation.8 | async-start | bytes 4718592 | tf_op jit(solution)/shard_map/all_gather | solution.py:142
  11.2 414.4 %all-gather.16.cloned.1.call-start = ((), (), s32[]{:S(2)}) async-start(), calls=%async_computation.11 | async-start | bytes 14155776 | tf_op jit(solution)/shard_map/all_gather | solution.py:143
  11.7 432.9 %all-gather.14.cloned.1.call-start = ((), (), s32[]{:S(2)}) async-start(), calls=%async_computation.10 | async-start | bytes 14155776 | tf_op jit(solution)/shard_map/all_gather | solution.py:144
  12.3 451.4 %all-gather.12.cloned.1.call-start = ((), (), s32[]{:S(2)}) async-start(), calls=%async_computation.9 | async-start | bytes 14155776 | tf_op jit(solution)/shard_map/all_gather | solution.py:145
  51.4 38.2 %collective-permute-start.4 = (bf16[256,2048]{1,0:T(8,128)(2,1)S(1)}, bf16[256,2048]{1,0:T(8,128)(2,1)}, u32[]{:S(2)}, u32[]{:S(2)}) collective-permute-start(bf16[256,2048]{1,0:T(8,128)(2,1)S(1)} %collective-permute-done.3), channel_id=1, source_target_pairs={{1,0},{2,1},{5,4},{6,5},{9,8},{10,9},{13,12},{14,13},{17,16},{18,1... | collective-permute-start | bytes 3145736 | tf_op jit(solution)/shard_map/ppermute | solution.py:58
  52.7 38.2 %collective-permute-start.2 = (bf16[256,2048]{1,0:T(8,128)(2,1)}, bf16[256,2048]{1,0:T(8,128)(2,1)}, u32[]{:S(2)}, u32[]{:S(2)}) collective-permute-start(bf16[256,2048]{1,0:T(8,128)(2,1)} %collective-permute-done.1), channel_id=1, source_target_pairs={{2,3},{6,7},{10,11},{14,15},{18,19},{22,23},{26,27},{30,31}} | collective-permute-start | bytes 3145736 | tf_op jit(solution)/shard_map/ppermute | solution.py:55
  54.5 849.6 %reduce-scatter.6.cloned.1.call-start = ((), (), s32[]{:S(2)}) async-start(), calls=%async_computation.12 | async-start | bytes 14155776 | tf_op jit(solution)/shard_map/reduce_scatter | solution.py:236
  131.4 65.9 %collective-permute-start.9 = (bf16[256,2048]{1,0:T(8,128)(2,1)S(1)}, bf16[256,2048]{1,0:T(8,128)(2,1)}, u32[]{:S(2)}, u32[]{:S(2)}) collective-permute-start(bf16[256,2048]{1,0:T(8,128)(2,1)S(1)} %copy-done.16), channel_id=1, source_target_pairs={{1,0},{2,1},{3,2},{5,4},{6,5},{7,6},{9,8},{10,9},{11,10},{13,12},{... | collective-permute-start | bytes 3145736 | tf_op jit(solution)/shard_map/ppermute | solution.py:58
  132.7 38.9 %collective-permute-start.6 = (bf16[256,2048]{1,0:T(8,128)(2,1)S(1)}, bf16[256,2048]{1,0:T(8,128)(2,1)}, u32[]{:S(2)}, u32[]{:S(2)}) collective-permute-start(bf16[256,2048]{1,0:T(8,128)(2,1)S(1)} %copy-done.16), channel_id=1, source_target_pairs={{0,1},{1,2},{2,3},{4,5},{5,6},{6,7},{8,9},{9,10},{10,11},{12,13},{... | collective-permute-start | bytes 3145736 | tf_op jit(solution)/shard_map/ppermute | solution.py:55
  522.7 384.8 %reduce-scatter.8.cloned.1.call-start = ((), (), s32[]{:S(2)}) async-start(), calls=%async_computation.13 | async-start | bytes 14155776 | tf_op jit(solution)/shard_map/reduce_scatter | solution.py:236
  542.2 368.7 %reduce-scatter.10.cloned.1.call-start = ((), (), s32[]{:S(2)}) async-start(), calls=%async_computation.14 | async-start | bytes 14155776 | tf_op jit(solution)/shard_map/reduce_scatter | solution.py:236
  629.2 44.0 %collective-permute-start.29 = (bf16[256,2048]{1,0:T(8,128)(2,1)S(1)}, bf16[256,2048]{1,0:T(8,128)(2,1)S(1)}, u32[]{:S(2)}, u32[]{:S(2)}) collective-permute-start(bf16[256,2048]{1,0:T(8,128)(2,1)S(1)} %fusion.38), channel_id=1, source_target_pairs={{1,0},{2,1},{3,2},{5,4},{6,5},{7,6},{9,8},{10,9},{11,10},{13,12},{... | collective-permute-start | bytes 3145736 | tf_op jit(solution)/shard_map/ppermute | solution.py:86
  710.7 323.4 %reduce-scatter.14.cloned.1.call-start = ((), (), s32[]{:S(2)}) async-start(), calls=%async_computation.16 | async-start | bytes 2433024 | tf_op jit(solution)/shard_map/reduce_scatter | solution.py:341
  922.1 160.5 %reduce-scatter.12.cloned.1.call-start = ((), (), s32[]{:S(2)}) async-start(), calls=%async_computation.15 | async-start | bytes 4718592 | tf_op jit(solution)/shard_map/reduce_scatter | solution.py:309
  927.4 43.2 %collective-permute-start.39 = (bf16[256,2048]{1,0:T(8,128)(2,1)}, bf16[256,2048]{1,0:T(8,128)(2,1)S(1)}, u32[]{:S(2)}, u32[]{:S(2)}) collective-permute-start(bf16[256,2048]{1,0:T(8,128)(2,1)} %get-tuple-element.114), channel_id=1, source_target_pairs={{3,2},{7,6},{11,10},{15,14},{19,18},{23,22},{27,26},{31,30}} | collective-permute-start | bytes 3145736 | tf_op jit(solution)/shard_map/ppermute | solution.py:86
  980.1 39.0 %collective-permute-start.40 = (bf16[256,2048]{1,0:T(8,128)(2,1)}, bf16[256,2048]{1,0:T(8,128)(2,1)}, u32[]{:S(2)}, u32[]{:S(2)}) collective-permute-start(bf16[256,2048]{1,0:T(8,128)(2,1)} %get-tuple-element.112), channel_id=1, source_target_pairs={{2,1},{3,2},{6,5},{7,6},{10,9},{11,10},{14,13},{15,14},{18,17},{19... | collective-permute-start | bytes 3145736 | tf_op jit(solution)/shard_map/ppermute | solution.py:86
  981.9 41.7 %collective-permute-start.45 = (bf16[256,2048]{1,0:T(8,128)(2,1)S(1)}, bf16[256,2048]{1,0:T(8,128)(2,1)S(1)}, u32[]{:S(2)}, u32[]{:S(2)}) collective-permute-start(bf16[256,2048]{1,0:T(8,128)(2,1)S(1)} %get-tuple-element.110), channel_id=1, source_target_pairs={{3,2},{7,6},{11,10},{15,14},{19,18},{23,22},{27,26},{31,30}} | collective-permute-start | bytes 3145736 | tf_op jit(solution)/shard_map/ppermute | solution.py:86
  1007.9 63.1 %all-to-all-start.1 = ((bf16[8,1024,256]{2,1,0:T(8,128)(2,1)}), bf16[8,1024,256]{2,1,0:T(8,128)(2,1)}, u32[]{:S(2)}, u32[]{:S(2)}) async-start(bf16[8,1024,256]{2,1,0:T(8,128)(2,1)} %bitcast.366), calls=%async_computation.6 | async-start | bytes 8388608 | tf_op jit(solution)/shard_map/all_to_all | solution.py:313
  1016.3 90.0 %collective-permute-start.38 = (bf16[256,2048]{1,0:T(8,128)(2,1)}, bf16[256,2048]{1,0:T(8,128)(2,1)}, u32[]{:S(2)}, u32[]{:S(2)}) collective-permute-start(bf16[256,2048]{1,0:T(8,128)(2,1)} %get-tuple-element.111), channel_id=1, source_target_pairs={{0,1},{1,2},{2,3},{4,5},{5,6},{6,7},{8,9},{9,10},{10,11},{12,13},{... | collective-permute-start | bytes 3145736 | tf_op jit(solution)/shard_map/ppermute | solution.py:80
  1022.3 83.9 %collective-permute-start.41 = (bf16[256,2048]{1,0:T(8,128)(2,1)}, bf16[256,2048]{1,0:T(8,128)(2,1)}, u32[]{:S(2)}, u32[]{:S(2)}) collective-permute-start(bf16[256,2048]{1,0:T(8,128)(2,1)} %fusion.31), channel_id=1, source_target_pairs={{1,0},{2,1},{3,2},{5,4},{6,5},{7,6},{9,8},{10,9},{11,10},{13,12},{... | collective-permute-start | bytes 3145736 | tf_op jit(solution)/shard_map/ppermute | solution.py:86
  1027.5 59.3 %collective-permute-start.44 = (bf16[256,2048]{1,0:T(8,128)(2,1)}, bf16[256,2048]{1,0:T(8,128)(2,1)}, u32[]{:S(2)}, u32[]{:S(2)}) collective-permute-start(bf16[256,2048]{1,0:T(8,128)(2,1)} %get-tuple-element.107), channel_id=1, source_target_pairs={{0,1},{1,2},{2,3},{4,5},{5,6},{6,7},{8,9},{9,10},{10,11},{12,13},{... | collective-permute-start | bytes 3145736 | tf_op jit(solution)/shard_map/ppermute | solution.py:80
  1033.4 41.1 %collective-permute-start.46 = (bf16[256,2048]{1,0:T(8,128)(2,1)S(1)}, bf16[256,2048]{1,0:T(8,128)(2,1)S(1)}, u32[]{:S(2)}, u32[]{:S(2)}) collective-permute-start(bf16[256,2048]{1,0:T(8,128)(2,1)S(1)} %get-tuple-element.108), channel_id=1, source_target_pairs={{2,1},{3,2},{6,5},{7,6},{10,9},{11,10},{14,13},{15,14},{18,17},{19... | collective-permute-start | bytes 3145736 | tf_op jit(solution)/shard_map/ppermute | solution.py:86
  (115 other events, 2349.5 us)
Sparse Core Ops, SparseCore 0:
  11.4 73.0 all-gather.17
  86.4 35.5 all-gather.7
  123.9 37.3 all-gather.9
  163.0 71.9 all-gather.15
  236.8 71.9 all-gather.13
  310.6 71.9 all-gather.11
  522.8 91.9 reduce-scatter.5
  618.3 92.2 reduce-scatter.7
  714.2 94.6 reduce-scatter.9
  922.2 41.7 reduce-scatter.13
  970.6 80.9 reduce-scatter.11
